TPU v7x, 512 devices: a whole 4x8x8 slice. The times are simulated.
512 devices in a mesh: dp: 32 (over y, z_lo), band: 16 (over x, z_hi, core).
Axes of the slice: x: 4, y: 8, z: 8 (z_hi: 2, z_lo: 4; z = z_hi * 4 + z_lo), core: 2. Of those that a mesh axis runs over, the one named last changes fastest.
Arguments:
- cell_states: bfloat16 [64, 32, 128, 768], P('dp', 'band'), may hold values from -6 to 6
- head_grads: bfloat16 [64, 32, 128, 384], P('dp', 'band'), may hold values from -6 to 6
- group_ids: int32 [64, 128, 32], P('dp', 'band'), may hold values from 0 to 7, never falling along the last dimension, each value on 1 to 8 neighbouring positions
- proj_weights: bfloat16 [768, 1152], replicated, may hold values from -0.8694895 to 0.8694895
Outputs:
- input_grad: bfloat16 [64, 32, 128, 768], P('dp', 'band')
- weight_grad: float32 [768, 1152], P('band', 'dp')
Inputs may be any that keep to these rules, and one draw needn't show every extreme that they name: `group_ids`: group numbers never fall down the rows of a column; a cell sees the header row 0 and the cells of its own group.
All inputs are finite; a program needn't handle non-finite values.
Results may differ from a plain program's by a relative error of at most 0.008.
Values may be sent and summed in bfloat16 or wider, within the bound.
No kernel may reach another device: no remote copies, remote signals or barrier semaphores. Data moves between devices by JAX's collectives and lax.ppermute only.
A program may use at most 64 MiB of HBM per device.

v0:
```python
import jax
import jax.numpy as jnp
from jax import lax
from jax.sharding import PartitionSpec as P

HD = 64


SCALE = 0.125
EPSILON = 1e-06


def normalize(states):
    widened = states.astype(jnp.float32)
    meansq = jnp.mean(widened * widened, axis=-1, keepdims=True)
    inverse = lax.rsqrt(meansq + EPSILON)
    scaled = widened * inverse
    return (scaled, inverse, scaled.astype(jnp.bfloat16))


def project(normed, weights):
    width = weights.shape[1] // 3
    flat = normed.reshape(-1, normed.shape[-1])
    mixed = jnp.dot(flat, weights, preferred_element_type=jnp.float32).astype(jnp.bfloat16)
    mixed = mixed.reshape(normed.shape[:-1] + (3 * width,))
    return (mixed[..., :width], mixed[..., width : 2 * width], mixed[..., 2 * width :])


def attend_back(query_rows, key_rows, value_rows, grad_rows, groups):
    shape = query_rows.shape
    split = shape[:-1] + (shape[-1] // HD, HD)
    query_five = query_rows.reshape(split)
    key_five = key_rows.reshape(split)
    value_five = value_rows.reshape(split)
    grad_five = grad_rows.reshape(split)
    scores = (
        jnp.einsum("bichd,bjchd->bchij", query_five, key_five, preferred_element_type=jnp.float32)
        * SCALE
    )
    header = lax.broadcasted_iota(jnp.int32, (shape[1], shape[1]), 1) == 0
    visible = (groups[:, :, :, None] == groups[:, :, None, :]) | header
    scores = jnp.where(visible[:, :, None], scores, -1e30)
    peak = jnp.max(scores, axis=-1, keepdims=True)
    expsc = jnp.exp(scores - peak)
    probs = expsc / jnp.sum(expsc, axis=-1, keepdims=True)
    probs_low = probs.astype(jnp.bfloat16)
    value_grad = jnp.einsum(
        "bchij,bichd->bjchd", probs_low, grad_five, preferred_element_type=jnp.float32
    ).astype(jnp.bfloat16)
    prob_grad = jnp.einsum(
        "bichd,bjchd->bchij", grad_five, value_five, preferred_element_type=jnp.float32
    )
    score_grad = probs * (prob_grad - jnp.sum(probs * prob_grad, axis=-1, keepdims=True))
    score_low = (score_grad * SCALE).astype(jnp.bfloat16)
    query_grad = jnp.einsum(
        "bchij,bjchd->bichd", score_low, key_five, preferred_element_type=jnp.float32
    ).astype(jnp.bfloat16)
    key_grad = jnp.einsum(
        "bchij,bichd->bjchd", score_low, query_five, preferred_element_type=jnp.float32
    ).astype(jnp.bfloat16)
    return (query_grad.reshape(shape), key_grad.reshape(shape), value_grad.reshape(shape))


def finish(scaled, inverse, normed, all_grads, weights):
    flat_norm = normed.reshape(-1, normed.shape[-1])
    flat_grad = all_grads.reshape(-1, all_grads.shape[-1])
    partial_w = lax.dot_general(
        flat_norm, flat_grad, (((0,), (0,)), ((), ())), preferred_element_type=jnp.float32
    )
    normed_grad = lax.dot_general(
        flat_grad, weights, (((1,), (1,)), ((), ())), preferred_element_type=jnp.float32
    )
    normed_grad = normed_grad.reshape(scaled.shape)
    coupling = jnp.mean(normed_grad * scaled, axis=-1, keepdims=True)
    state_grad = (inverse * (normed_grad - scaled * coupling)).astype(jnp.bfloat16)
    return (partial_w, state_grad)


def body(cell_states, head_grads, group_ids, proj_weights):
    scaled, inverse, normed = normalize(cell_states)
    query_rows, key_rows, value_rows = project(normed, proj_weights)
    query_cols, key_cols, value_cols, grad_cols = (
        lax.all_to_all(query_rows, "band", split_axis=2, concat_axis=1, tiled=True),
        lax.all_to_all(key_rows, "band", split_axis=2, concat_axis=1, tiled=True),
        lax.all_to_all(value_rows, "band", split_axis=2, concat_axis=1, tiled=True),
        lax.all_to_all(head_grads, "band", split_axis=2, concat_axis=1, tiled=True),
    )
    query_grad, key_grad, value_grad = attend_back(
        query_cols, key_cols, value_cols, grad_cols, group_ids
    )
    query_home, key_home, value_home = (
        lax.all_to_all(query_grad, "band", split_axis=1, concat_axis=2, tiled=True),
        lax.all_to_all(key_grad, "band", split_axis=1, concat_axis=2, tiled=True),
        lax.all_to_all(value_grad, "band", split_axis=1, concat_axis=2, tiled=True),
    )
    all_grads = jnp.concatenate((query_home, key_home, value_home), axis=-1)
    partial_w, input_grad = finish(scaled, inverse, normed, all_grads, proj_weights)
    shared = lax.psum_scatter(partial_w, "dp", scatter_dimension=1, tiled=True)
    weight_grad = lax.psum_scatter(shared, "band", scatter_dimension=0, tiled=True)
    return (input_grad, weight_grad)


def solution(mesh):
    return jax.shard_map(
        body,
        mesh=mesh,
        in_specs=(
            P("dp", "band", None, None),
            P("dp", "band", None, None),
            P("dp", "band", None),
            P(),
        ),
        out_specs=(P("dp", "band", None, None), P("band", "dp")),
        check_vma=False,
    )
```

profile of v0, /device:TPU:1, one launch (start us, length us, event | category | flops | bytes accessed | tf_op | source)
XLA Modules:
  0.0 393.6 jit_solution(13017459943249130709)
XLA Ops:
  9.5 14.3 %all-to-all-start.3 = ((bf16[2,2,128,384]{3,1,0,2:T(2,128)(2,1)}), bf16[2,2,128,384]{3,1,0,2:T(2,128)(2,1)S(1)}, u32[]{:S(2)}, u32[]{:S(2)}) async-start(bf16[2,2,128,384]{3,1,0,2:T(2,128)(2,1)} %copy.54), calls=%async_computation.3 | async-start | bytes 786432 | tf_op jit(solution)/shard_map/all_to_all | solution.py:86
  27.6 8.5 %all-to-all-done.3 = bf16[2,2,128,384]{3,1,0,2:T(2,128)(2,1)S(1)} async-done(((bf16[2,2,128,384]{3,1,0,2:T(2,128)(2,1)}), bf16[2,2,128,384]{3,1,0,2:T(2,128)(2,1)S(1)}, u32[]{:S(2)}, u32[]{:S(2)}) %all-to-all-start.3) | async-done | bytes 393248 | tf_op jit(solution)/shard_map/all_to_all | solution.py:86
  36.2 5.9 %all-to-all-start.2 = ((bf16[2,2,128,384]{3,1,0,2:T(2,128)(2,1)}), bf16[2,2,128,384]{3,1,0,2:T(2,128)(2,1)S(1)}, u32[]{:S(2)}, u32[]{:S(2)}) async-start(bf16[2,2,128,384]{3,1,0,2:T(2,128)(2,1)} %copy.92), calls=%async_computation.2 | async-start | bytes 786432 | tf_op jit(solution)/shard_map/all_to_all | solution.py:85
  44.2 10.2 %all-to-all-done.2 = bf16[2,2,128,384]{3,1,0,2:T(2,128)(2,1)S(1)} async-done(((bf16[2,2,128,384]{3,1,0,2:T(2,128)(2,1)}), bf16[2,2,128,384]{3,1,0,2:T(2,128)(2,1)S(1)}, u32[]{:S(2)}, u32[]{:S(2)}) %all-to-all-start.2) | async-done | bytes 393248 | tf_op jit(solution)/shard_map/all_to_all | solution.py:85
  54.5 5.9 %all-to-all-start.1 = ((bf16[2,2,128,384]{3,1,0,2:T(2,128)(2,1)}), bf16[2,2,128,384]{3,1,0,2:T(2,128)(2,1)}, u32[]{:S(2)}, u32[]{:S(2)}) async-start(bf16[2,2,128,384]{3,1,0,2:T(2,128)(2,1)} %copy.91), calls=%async_computation.1 | async-start | bytes 786432 | tf_op jit(solution)/shard_map/all_to_all | solution.py:83
  62.6 10.3 %all-to-all-done.1 = bf16[2,2,128,384]{3,1,0,2:T(2,128)(2,1)} async-done(((bf16[2,2,128,384]{3,1,0,2:T(2,128)(2,1)}), bf16[2,2,128,384]{3,1,0,2:T(2,128)(2,1)}, u32[]{:S(2)}, u32[]{:S(2)}) %all-to-all-start.1) | async-done | bytes 393248 | tf_op jit(solution)/shard_map/all_to_all | solution.py:83
  72.8 6.0 %all-to-all-start = ((bf16[2,2,128,384]{3,1,0,2:T(2,128)(2,1)}), bf16[2,2,128,384]{3,1,0,2:T(2,128)(2,1)}, u32[]{:S(2)}, u32[]{:S(2)}) async-start(bf16[2,2,128,384]{3,1,0,2:T(2,128)(2,1)} %copy.90), calls=%async_computation | async-start | bytes 786432 | tf_op jit(solution)/shard_map/all_to_all | solution.py:84
  83.4 7.9 %all-to-all-done = bf16[2,2,128,384]{3,1,0,2:T(2,128)(2,1)} async-done(((bf16[2,2,128,384]{3,1,0,2:T(2,128)(2,1)}), bf16[2,2,128,384]{3,1,0,2:T(2,128)(2,1)}, u32[]{:S(2)}, u32[]{:S(2)}) %all-to-all-start) | async-done | bytes 393248 | tf_op jit(solution)/shard_map/all_to_all | solution.py:84
  98.6 3.7 fusion.22
  102.3 4.1 %fusion.40 = (f32[2,8,6,32]{3,2,1,0:T(8,128)S(1)}, f32[2,8,6,32,32]{3,4,2,1,0:T(8,128)}) fusion(pred[2,8,32,32]{2,3,1,0:T(8,128)(4,1)S(1)} %compare_or_fusion, bf16[2,32,8,6,64]{4,3,2,1,0:T(8,128)(2,1)} %reshape.72, bf16[2,32,8,6,64]{4,3,2,1,0:T(8,128)(2,1)} %reshape.73), kind=kOutput, calls=%fused_computation.63 | convolution fusion | flops 12976159 | bytes 1208320 | tf_op jit(solution)/shard_map/sub | solution.py:44
  106.4 4.3 %fusion.18 = bf16[2,32,8,6,64]{4,1,3,2,0:T(8,128)(2,1)S(1)} fusion(f32[2,8,6,32,32]{4,3,2,1,0:T(8,128)} %fusion.22, bf16[2,32,8,6,64]{4,3,2,1,0:T(8,128)(2,1)} %reshape.72, f32[2,8,6,32,32]{3,4,2,1,0:T(8,128)} %get-tuple-element.6, f32[2,8,6,32]{3,2,1,0:T(8,128)S(1)} %get-tuple-element.5), kind=kOutput, calls=%fused_computation.27 | convolution fusion | flops 13470751 | bytes 1585152 | tf_op jit(solution)/shard_map/bchij,bjchd->bichd/dot_general | solution.py:55
  114.5 6.0 %all-to-all-start.4 = ((bf16[2,32,8,384]{3,2,0,1:T(8,128)(2,1)}), bf16[2,32,8,384]{3,2,0,1:T(8,128)(2,1)S(1)}, u32[]{:S(2)}, u32[]{:S(2)}) async-start(bf16[2,32,8,384]{3,2,0,1:T(8,128)(2,1)} %reshape.81), calls=%async_computation.4 | async-start | bytes 786432 | tf_op jit(solution)/shard_map/all_to_all | solution.py:92
  120.5 5.1 %fusion.20 = bf16[2,32,8,6,64]{4,1,3,2,0:T(8,128)(2,1)} fusion(f32[2,8,6,32,32]{4,3,2,1,0:T(8,128)} %fusion.22, bf16[2,32,8,6,64]{4,3,2,1,0:T(8,128)(2,1)} %reshape.73, f32[2,8,6,32,32]{3,4,2,1,0:T(8,128)} %get-tuple-element.6, f32[2,8,6,32]{3,2,1,0:T(8,128)S(1)} %get-tuple-element.5), kind=kOutput, calls=%fused_computation.29 | convolution fusion | flops 13470751 | bytes 1585152 | tf_op jit(solution)/shard_map/bchij,bichd->bjchd/dot_general | solution.py:58
  132.9 7.3 %all-to-all-start.5 = ((bf16[2,32,8,384]{3,2,0,1:T(8,128)(2,1)}), bf16[2,32,8,384]{3,2,0,1:T(8,128)(2,1)S(1)}, u32[]{:S(2)}, u32[]{:S(2)}) async-start(bf16[2,32,8,384]{3,2,0,1:T(8,128)(2,1)} %reshape.82), calls=%async_computation.5 | async-start | bytes 786432 | tf_op jit(solution)/shard_map/all_to_all | solution.py:93
  146.4 6.2 %all-to-all-done.5 = bf16[2,32,8,384]{3,2,0,1:T(8,128)(2,1)S(1)} async-done(((bf16[2,32,8,384]{3,2,0,1:T(8,128)(2,1)}), bf16[2,32,8,384]{3,2,0,1:T(8,128)(2,1)S(1)}, u32[]{:S(2)}, u32[]{:S(2)}) %all-to-all-start.5) | async-done | bytes 393248 | tf_op jit(solution)/shard_map/all_to_all | solution.py:93
  152.7 6.2 %all-to-all-start.6 = ((bf16[2,32,8,384]{3,2,0,1:T(8,128)(2,1)}), bf16[2,32,8,384]{3,2,0,1:T(8,128)(2,1)}, u32[]{:S(2)}, u32[]{:S(2)}) async-start(bf16[2,32,8,384]{3,2,0,1:T(8,128)(2,1)} %reshape.83), calls=%async_computation.6 | async-start | bytes 786432 | tf_op jit(solution)/shard_map/all_to_all | solution.py:94
  162.3 8.9 %all-to-all-done.6 = bf16[2,32,8,384]{3,2,0,1:T(8,128)(2,1)} async-done(((bf16[2,32,8,384]{3,2,0,1:T(8,128)(2,1)}), bf16[2,32,8,384]{3,2,0,1:T(8,128)(2,1)}, u32[]{:S(2)}, u32[]{:S(2)}) %all-to-all-start.6) | async-done | bytes 393248 | tf_op jit(solution)/shard_map/all_to_all | solution.py:94
  172.3 3.5 fusion.9
  178.7 96.1 %fusion = f32[768,40]{0,1:T(8,128)S(1)} fusion(f32[768,1152]{0,1:T(8,128)} %convolution_bitcast_fusion), kind=kCustom, calls=%all-reduce-scatter | all-reduce-scatter fusion | flops 983041 | bytes 3663872
  274.9 4.8 %collective-permute-start.2 = (f32[768,40]{0,1:T(8,128)S(1)}, f32[768,40]{0,1:T(8,128)S(1)}, u32[]{:S(2)}, u32[]{:S(2)}) collective-permute-start(f32[768,40]{0,1:T(8,128)S(1)} %fusion), channel_id=1, source_target_pairs={{0,48},{16,64},{32,80},{48,96},{64,112},{80,128},{96,144},{112,160... | collective-permute-start | bytes 368648
  279.7 3.0 collective-permute-start.1
  282.7 4.1 %collective-permute-start = (f32[768,40]{0,1:T(8,128)S(1)}, f32[768,40]{0,1:T(8,128)}, u32[]{:S(2)}, u32[]{:S(2)}) collective-permute-start(f32[768,40]{0,1:T(8,128)S(1)} %fusion), channel_id=1, source_target_pairs={{0,16},{16,32},{32,48},{48,64},{64,80},{80,96},{96,112},{112,128},... | collective-permute-start | bytes 368648
  286.8 3.5 collective-permute-start.3
  296.3 89.1 %reduce-scatter.6.cloned.1.call-done = f32[48,36]{1,0:T(8,128)} async-done(((f32[768,36]{1,0:T(8,128)}), f32[48,36]{1,0:T(8,128)}) %reduce-scatter.6.cloned.1.call-update) | async-done | bytes 6928
  (62 shorter events, 53.7 us)
Async XLA Ops:
  7.2 17.1 %copy-start = (bf16[768,1152]{1,0:T(8,128)(2,1)S(1)}, bf16[768,1152]{1,0:T(8,128)(2,1)}, u32[]{:S(2)}) copy-start(bf16[768,1152]{1,0:T(8,128)(2,1)} %param.7) | copy-start | bytes 5308420
  7.2 16.6 %copy-start.1 = (bf16[2,2,128,768]{3,2,1,0:T(8,128)(2,1)S(1)}, bf16[2,2,128,768]{3,2,1,0:T(8,128)(2,1)}, u32[]{:S(2)}) copy-start(bf16[2,2,128,768]{3,2,1,0:T(8,128)(2,1)} %param.4) | copy-start | bytes 2359300
  9.5 26.7 %all-to-all-start.3 = ((bf16[2,2,128,384]{3,1,0,2:T(2,128)(2,1)}), bf16[2,2,128,384]{3,1,0,2:T(2,128)(2,1)S(1)}, u32[]{:S(2)}, u32[]{:S(2)}) async-start(bf16[2,2,128,384]{3,1,0,2:T(2,128)(2,1)} %copy.54), calls=%async_computation.3 | async-start | bytes 786432 | tf_op jit(solution)/shard_map/all_to_all | solution.py:86
  24.2 1.2 copy-start.2
  36.2 18.3 %all-to-all-start.2 = ((bf16[2,2,128,384]{3,1,0,2:T(2,128)(2,1)}), bf16[2,2,128,384]{3,1,0,2:T(2,128)(2,1)S(1)}, u32[]{:S(2)}, u32[]{:S(2)}) async-start(bf16[2,2,128,384]{3,1,0,2:T(2,128)(2,1)} %copy.92), calls=%async_computation.2 | async-start | bytes 786432 | tf_op jit(solution)/shard_map/all_to_all | solution.py:85
  42.1 36.8 %copy-start.6 = (s32[2,8,32]{2,1,0:T(8,128)S(1)}, s32[2,8,32]{2,1,0:T(8,128)}, u32[]{:S(2)}) copy-start(s32[2,8,32]{2,1,0:T(8,128)} %param.6) | copy-start | bytes 6148
  54.5 18.4 %all-to-all-start.1 = ((bf16[2,2,128,384]{3,1,0,2:T(2,128)(2,1)}), bf16[2,2,128,384]{3,1,0,2:T(2,128)(2,1)}, u32[]{:S(2)}, u32[]{:S(2)}) async-start(bf16[2,2,128,384]{3,1,0,2:T(2,128)(2,1)} %copy.91), calls=%async_computation.1 | async-start | bytes 786432 | tf_op jit(solution)/shard_map/all_to_all | solution.py:83
  72.8 18.5 %all-to-all-start = ((bf16[2,2,128,384]{3,1,0,2:T(2,128)(2,1)}), bf16[2,2,128,384]{3,1,0,2:T(2,128)(2,1)}, u32[]{:S(2)}, u32[]{:S(2)}) async-start(bf16[2,2,128,384]{3,1,0,2:T(2,128)(2,1)} %copy.90), calls=%async_computation | async-start | bytes 786432 | tf_op jit(solution)/shard_map/all_to_all | solution.py:84
  114.5 18.4 %all-to-all-start.4 = ((bf16[2,32,8,384]{3,2,0,1:T(8,128)(2,1)}), bf16[2,32,8,384]{3,2,0,1:T(8,128)(2,1)S(1)}, u32[]{:S(2)}, u32[]{:S(2)}) async-start(bf16[2,32,8,384]{3,2,0,1:T(8,128)(2,1)} %reshape.81), calls=%async_computation.4 | async-start | bytes 786432 | tf_op jit(solution)/shard_map/all_to_all | solution.py:92
  132.9 19.7 %all-to-all-start.5 = ((bf16[2,32,8,384]{3,2,0,1:T(8,128)(2,1)}), bf16[2,32,8,384]{3,2,0,1:T(8,128)(2,1)S(1)}, u32[]{:S(2)}, u32[]{:S(2)}) async-start(bf16[2,32,8,384]{3,2,0,1:T(8,128)(2,1)} %reshape.82), calls=%async_computation.5 | async-start | bytes 786432 | tf_op jit(solution)/shard_map/all_to_all | solution.py:93
  152.7 18.6 %all-to-all-start.6 = ((bf16[2,32,8,384]{3,2,0,1:T(8,128)(2,1)}), bf16[2,32,8,384]{3,2,0,1:T(8,128)(2,1)}, u32[]{:S(2)}, u32[]{:S(2)}) async-start(bf16[2,32,8,384]{3,2,0,1:T(8,128)(2,1)} %reshape.83), calls=%async_computation.6 | async-start | bytes 786432 | tf_op jit(solution)/shard_map/all_to_all | solution.py:94
  158.8 226.6 %reduce-scatter.6.cloned.1.call-start = ((), (), s32[]{:S(2)}) async-start(), calls=%async_computation.8 | async-start | bytes 417792
  161.6 10.7 %copy-start.4 = (bf16[2,2,16,8,384]{4,3,2,1,0:T(8,128)(2,1)S(1)}, bf16[2,2,16,8,384]{4,3,2,1,0:T(8,128)(2,1)}, u32[]{:S(2)}) copy-start(bf16[2,2,16,8,384]{4,3,2,1,0:T(8,128)(2,1)} %copy.120) | copy-start | bytes 1179652
  172.3 3.5 copy-start.3
  172.3 3.5 copy-start.5
  274.9 16.3 %collective-permute-start.2 = (f32[768,40]{0,1:T(8,128)S(1)}, f32[768,40]{0,1:T(8,128)S(1)}, u32[]{:S(2)}, u32[]{:S(2)}) collective-permute-start(f32[768,40]{0,1:T(8,128)S(1)} %fusion), channel_id=1, source_target_pairs={{0,48},{16,64},{32,80},{48,96},{64,112},{80,128},{96,144},{112,160... | collective-permute-start | bytes 368648
  279.7 11.4 %collective-permute-start.1 = (f32[768,40]{0,1:T(8,128)S(1)}, f32[768,40]{0,1:T(8,128)S(1)}, u32[]{:S(2)}, u32[]{:S(2)}) collective-permute-start(f32[768,40]{0,1:T(8,128)S(1)} %fusion), channel_id=1, source_target_pairs={{0,32},{16,48},{32,64},{48,80},{64,96},{80,112},{96,128},{112,144}... | collective-permute-start | bytes 368648
  282.7 8.4 %collective-permute-start = (f32[768,40]{0,1:T(8,128)S(1)}, f32[768,40]{0,1:T(8,128)}, u32[]{:S(2)}, u32[]{:S(2)}) collective-permute-start(f32[768,40]{0,1:T(8,128)S(1)} %fusion), channel_id=1, source_target_pairs={{0,16},{16,32},{32,48},{48,64},{64,80},{80,96},{96,112},{112,128},... | collective-permute-start | bytes 368648
  286.8 4.3 %collective-permute-start.3 = (f32[768,4]{0,1:T(4,128)S(1)}, f32[768,4]{0,1:T(4,128)S(1)}, u32[]{:S(2)}, u32[]{:S(2)}) collective-permute-start(f32[768,4]{0,1:T(4,128)S(1)} %slice.15), channel_id=1, source_target_pairs={{0,64},{16,80},{32,96},{48,112},{64,128},{80,144},{96,160},{112,17... | collective-permute-start | bytes 36872
Sparse Core Ops, SparseCore 0:
  293.8 91.5 reduce-scatter.5
where the time goes:
time: 396 us; the launch traced here: 394 us
  waiting for transfers between devices  144 us (36%)
  blocking collectives  96.1 us (24%)
  starting transfers between devices  67.1 us (17%)
  local copies, waits for them, and re-layouts  40.9 us (10%)
  matrix products  27.2 us (7%)
  between operations  14.9 us (4%)
    unnamed x1, blocking collectives  96.1 us
    unnamed x6, waiting for transfers between devices  89.9 us
    unnamed x5, starting transfers between devices  15.5 us
    all_to_all x1, starting transfers between devices, body(): lax.all_to_all(head_grads, 'band', split_axis=2, concat_axis=1, tiled=True)  14.3 us
    unnamed x24, local copies, waits for them, and re-layouts  12.9 us
    all_to_all x1, waiting for transfers between devices, body(): lax.all_to_all(query_rows, 'band', split_axis=2, concat_axis=1, tiled=True)  10.3 us
    all_to_all x1, waiting for transfers between devices, body(): lax.all_to_all(value_rows, 'band', split_axis=2, concat_axis=1, tiled=True)  10.2 us
    all_to_all x1, waiting for transfers between devices, body(): lax.all_to_all(value_grad, 'band', split_axis=1, concat_axis=2, tiled=True)  8.9 us
  transfers between devices with their start and end apart: 12, of which 9 were waited for; matrix products, arithmetic and copies ran while one was open for 9% of the time, Pallas kernels for 0%

commit v1 on v0

--- a/solution.py
+++ b/solution.py
@@ -77,26 +77,27 @@
 
 
 def body(cell_states, head_grads, group_ids, proj_weights):
-    scaled, inverse, normed = normalize(cell_states)
-    query_rows, key_rows, value_rows = project(normed, proj_weights)
-    query_cols, key_cols, value_cols, grad_cols = (
-        lax.all_to_all(query_rows, "band", split_axis=2, concat_axis=1, tiled=True),
-        lax.all_to_all(key_rows, "band", split_axis=2, concat_axis=1, tiled=True),
-        lax.all_to_all(value_rows, "band", split_axis=2, concat_axis=1, tiled=True),
-        lax.all_to_all(head_grads, "band", split_axis=2, concat_axis=1, tiled=True),
-    )
+    tables, rows_here, cols, width = cell_states.shape
+    heads_width = head_grads.shape[-1]
+    both = jnp.concatenate((cell_states, head_grads), axis=-1)
+    both_cols = lax.all_to_all(both, "band", split_axis=2, concat_axis=1, tiled=True)
+    states_cols = both_cols[..., :width]
+    grad_cols = both_cols[..., width:]
+    scaled, inverse, normed = normalize(states_cols)
+    query_cols, key_cols, value_cols = project(normed, proj_weights)
     query_grad, key_grad, value_grad = attend_back(
         query_cols, key_cols, value_cols, grad_cols, group_ids
     )
-    query_home, key_home, value_home = (
-        lax.all_to_all(query_grad, "band", split_axis=1, concat_axis=2, tiled=True),
-        lax.all_to_all(key_grad, "band", split_axis=1, concat_axis=2, tiled=True),
-        lax.all_to_all(value_grad, "band", split_axis=1, concat_axis=2, tiled=True),
-    )
-    all_grads = jnp.concatenate((query_home, key_home, value_home), axis=-1)
-    partial_w, input_grad = finish(scaled, inverse, normed, all_grads, proj_weights)
-    shared = lax.psum_scatter(partial_w, "dp", scatter_dimension=1, tiled=True)
-    weight_grad = lax.psum_scatter(shared, "band", scatter_dimension=0, tiled=True)
+    all_grads = jnp.concatenate((query_grad, key_grad, value_grad), axis=-1)
+    partial_w, input_cols = finish(scaled, inverse, normed, all_grads, proj_weights)
+    input_grad = lax.all_to_all(input_cols, "band", split_axis=1, concat_axis=2, tiled=True)
+    n_band = lax.axis_size("band")
+    n_dp = lax.axis_size("dp")
+    d_in, d_out = partial_w.shape
+    blocks = partial_w.reshape(n_band, d_in // n_band, n_dp, d_out // n_dp)
+    blocks = blocks.transpose(0, 2, 1, 3).reshape(n_band * n_dp, d_in // n_band, d_out // n_dp)
+    weight_grad = lax.psum_scatter(blocks, ("band", "dp"), scatter_dimension=0, tiled=True)
+    weight_grad = weight_grad.reshape(d_in // n_band, d_out // n_dp)
     return (input_grad, weight_grad)
 
 

time: 396 us -> 452 us (1.14)
  waiting for transfers between devices: 144 us -> 327 us
  blocking collectives: 96.1 us -> 0 us
  starting transfers between devices: 67.1 us -> 21.5 us
  local copies, waits for them, and re-layouts: 40.9 us -> 48 us
  matrix products: 27.2 us -> 33.1 us
    unnamed x6 -> x2, waiting for transfers between devices: 89.9 us -> 291 us
    unnamed x1 -> x0, blocking collectives: 96.1 us -> none
    all_to_all x7 -> x2, starting transfers between devices: 51.6 us -> 21.4 us  [the longest x1 14.4 us: body(): lax.all_to_all(both, 'band', split_axis=2, concat_axis=1, tiled=True)]
    all_to_all x7 -> x2, waiting for transfers between devices: 54.4 us -> 36.5 us  [the longest x1 21 us: body(): lax.all_to_all(both, 'band', split_axis=2, concat_axis=1, tiled=True)]
    concatenate x0 -> x7, local copies, waits for them, and re-layouts: none -> 16.5 us  [the longest x6 14.3 us: body(): all_grads = jnp.concatenate((query_grad, key_grad, value_grad), axis=-1)]
    unnamed x5 -> x1, starting transfers between devices: 15.5 us -> 0.04 us
    reshape x6 -> x1, local copies, waits for them, and re-layouts: 12.6 us -> 1.94 us  [body(): weight_grad = weight_grad.reshape(d_in // n_band, d_out // n_dp)]
    unnamed x24 -> x9, local copies, waits for them, and re-layouts: 12.9 us -> 2.32 us
  transfers between devices with their start and end apart: 12 -> 3, of which waited for: 9 -> 3; matrix products, arithmetic and copies ran while one was open for 9% -> 1% of each run, Pallas kernels for 0% -> 0%
where the time goes in v1:
time: 452 us; the launch traced here: 450 us
  waiting for transfers between devices  327 us (72%)
  local copies, waits for them, and re-layouts  48 us (11%)
  matrix products  33.1 us (7%)
  starting transfers between devices  21.5 us (5%)
  between operations  14.2 us (3%)
  other arithmetic  6.05 us (1%)
    unnamed x2, waiting for transfers between devices  291 us
    all_to_all x1, waiting for transfers between devices, body(): lax.all_to_all(both, 'band', split_axis=2, concat_axis=1, tiled=True)  21 us
    all_to_all x1, waiting for transfers between devices, body(): lax.all_to_all(input_cols, 'band', split_axis=1, concat_axis=2, tiled=True)  15.5 us
    all_to_all x1, starting transfers between devices, body(): lax.all_to_all(both, 'band', split_axis=2, concat_axis=1, tiled=True)  14.4 us
    concatenate x6, local copies, waits for them, and re-layouts, body(): all_grads = jnp.concatenate((query_grad, key_grad, value_grad), axis=-1)  14.3 us
  transfers between devices with their start and end apart: 3, of which 3 were waited for; matrix products, arithmetic and copies ran while one was open for 1% of the time, Pallas kernels for 0%

profile of v1, /device:TPU:1, one launch (start us, length us, event | category | flops | bytes accessed | tf_op | source)
XLA Modules:
  0.0 449.9 jit_solution(11299459925265378232)
XLA Ops:
  10.9 14.4 %all-to-all-start = ((bf16[2,2,128,1152]{3,1,0,2:T(2,128)(2,1)}), bf16[2,2,128,1152]{3,1,0,2:T(2,128)(2,1)S(1)}, u32[]{:S(2)}, u32[]{:S(2)}) async-start(bf16[2,2,128,1152]{3,1,0,2:T(2,128)(2,1)} %copy.49), calls=%async_computation | async-start | bytes 2359296 | tf_op jit(solution)/shard_map/all_to_all | solution.py:83
  25.5 21.0 %all-to-all-done = bf16[2,2,128,1152]{3,1,0,2:T(2,128)(2,1)S(1)} async-done(((bf16[2,2,128,1152]{3,1,0,2:T(2,128)(2,1)}), bf16[2,2,128,1152]{3,1,0,2:T(2,128)(2,1)S(1)}, u32[]{:S(2)}, u32[]{:S(2)}) %all-to-all-start) | async-done | bytes 1179680 | tf_op jit(solution)/shard_map/all_to_all | solution.py:83
  53.2 2.4 reshape.71
  55.6 2.4 reshape.72
  59.6 3.8 fusion.41
  63.3 4.1 fusion.58
  67.5 3.2 fusion.35
  70.7 5.1 %fusion.29 = bf16[2,32,8,6,64]{4,1,3,2,0:T(8,128)(2,1)} fusion(f32[2,8,6,32,32]{3,4,2,1,0:T(8,128)} %fusion.41, bf16[2,32,8,6,64]{4,3,2,1,0:T(8,128)(2,1)} %reshape.72, f32[2,8,6,32,32]{3,4,2,1,0:T(8,128)} %get-tuple-element.6, f32[2,8,6,32]{3,2,1,0:T(8,128)S(1)} %get-tuple-element.5), kind=kOutput, calls=%fused_computation.26 | convolution fusion | flops 13470751 | bytes 1585152 | tf_op jit(solution)/shard_map/bchij,bichd->bjchd/dot_general | solution.py:58
  75.8 5.1 %fusion.32 = bf16[2,32,8,6,64]{4,1,3,2,0:T(8,128)(2,1)} fusion(f32[2,8,6,32,32]{3,4,2,1,0:T(8,128)} %fusion.41, bf16[2,32,8,6,64]{4,3,2,1,0:T(8,128)(2,1)} %reshape.71, f32[2,8,6,32,32]{3,4,2,1,0:T(8,128)} %get-tuple-element.6, f32[2,8,6,32]{3,2,1,0:T(8,128)S(1)} %get-tuple-element.5), kind=kOutput, calls=%fused_computation.27 | convolution fusion | flops 13470751 | bytes 1585152 | tf_op jit(solution)/shard_map/bchij,bjchd->bichd/dot_general | solution.py:55
  80.9 2.5 copy.61
  83.4 2.5 concatenate.25
  87.7 2.5 copy.59
  90.2 2.5 concatenate.24
  92.7 2.5 concatenate.28
  95.2 2.5 copy.57
  97.6 2.5 concatenate.23
  100.1 2.5 concatenate.27
  102.6 3.6 fusion.8
  110.8 2.4 copy.68
  113.2 2.9 reshape.79
  116.1 6.9 %fusion.63 = f32[16,48,32,36]{1,3,2,0:T(8,128)} fusion(bf16[16,48,512,1]{2,1,3,0:T(8,128)(2,1)} %bitcast.64, bf16[32,36,512,1]{2,1,0,3:T(8,128)(2,1)} %reshape.79), kind=kOutput, calls=%fused_computation.61 | convolution fusion | flops 905969664 | bytes 5505024 | tf_op jit(solution)/shard_map/dot_general | solution.py:67
  125.8 7.1 %all-to-all-start.1 = ((bf16[2,32,8,768]{3,2,0,1:T(8,128)(2,1)}), bf16[2,32,8,768]{3,2,0,1:T(8,128)(2,1)S(1)}, u32[]{:S(2)}, u32[]{:S(2)}) async-start(bf16[2,32,8,768]{3,2,0,1:T(8,128)(2,1)} %copy.62), calls=%async_computation.1 | async-start | bytes 1572864 | tf_op jit(solution)/shard_map/all_to_all | solution.py:93
  134.1 15.5 %all-to-all-done.1 = bf16[2,32,8,768]{3,2,0,1:T(8,128)(2,1)S(1)} async-done(((bf16[2,32,8,768]{3,2,0,1:T(8,128)(2,1)}), bf16[2,32,8,768]{3,2,0,1:T(8,128)(2,1)S(1)}, u32[]{:S(2)}, u32[]{:S(2)}) %all-to-all-start.1) | async-done | bytes 786464 | tf_op jit(solution)/shard_map/all_to_all | solution.py:93
  150.6 290.5 %all-reduce.3.cloned.1.call-done = f32[512,48,36]{1,2,0:T(8,128)} async-done(((f32[512,48,36]{1,2,0:T(8,128)}), f32[512,48,36]{1,2,0:T(8,128)}) %all-reduce.3.cloned.1.call-update) | async-done | bytes 3538960
  (32 shorter events, 25.3 us)
Async XLA Ops:
  7.2 43.8 %copy-start = (bf16[768,1152]{1,0:T(8,128)(2,1)S(1)}, bf16[768,1152]{1,0:T(8,128)(2,1)}, u32[]{:S(2)}) copy-start(bf16[768,1152]{1,0:T(8,128)(2,1)} %param.7) | copy-start | bytes 5308420
  10.9 14.5 %copy-start.3 = (s32[2,8,32]{2,1,0:T(8,128)S(1)}, s32[2,8,32]{2,1,0:T(8,128)}, u32[]{:S(2)}) copy-start(s32[2,8,32]{2,1,0:T(8,128)} %param.6) | copy-start | bytes 6148
  10.9 35.6 %all-to-all-start = ((bf16[2,2,128,1152]{3,1,0,2:T(2,128)(2,1)}), bf16[2,2,128,1152]{3,1,0,2:T(2,128)(2,1)S(1)}, u32[]{:S(2)}, u32[]{:S(2)}) async-start(bf16[2,2,128,1152]{3,1,0,2:T(2,128)(2,1)} %copy.49), calls=%async_computation | async-start | bytes 2359296 | tf_op jit(solution)/shard_map/all_to_all | solution.py:83
  25.3 415.8 %all-reduce.3.cloned.1.call-start = ((), (), s32[]{:S(2)}) async-start(), calls=%async_computation.2 | async-start | bytes 20971520
  46.5 1.0 copy-start.1
  51.0 1.2 copy-start.2
  125.8 23.9 %all-to-all-start.1 = ((bf16[2,32,8,768]{3,2,0,1:T(8,128)(2,1)}), bf16[2,32,8,768]{3,2,0,1:T(8,128)(2,1)S(1)}, u32[]{:S(2)}, u32[]{:S(2)}) async-start(bf16[2,32,8,768]{3,2,0,1:T(8,128)(2,1)} %copy.62), calls=%async_computation.1 | async-start | bytes 1572864 | tf_op jit(solution)/shard_map/all_to_all | solution.py:93
Sparse Core Ops, SparseCore 0:
  123.2 317.8 all-reduce.2

commit v2 on v1

--- a/solution.py
+++ b/solution.py
@@ -76,6 +76,36 @@
     return (partial_w, state_grad)
 
 
+def exchange(blocks, dim, band, digit, stride, n):
+    mine = lax.dynamic_index_in_dim(blocks, digit, axis=dim, keepdims=False)
+    total = mine.astype(jnp.float32)
+    n_band = lax.axis_size("band")
+    for shift in range(1, n):
+        part = lax.dynamic_index_in_dim(blocks, (digit + shift) % n, axis=dim, keepdims=False)
+        pairs = []
+        for source in range(n_band):
+            d = (source // stride) % n
+            pairs.append((source, source + (((d + shift) % n) - d) * stride))
+        total = total + lax.ppermute(part, "band", pairs)
+    return total
+
+
+def reduce_weight_grad(partial_w):
+    n_band = lax.axis_size("band")
+    n_dp = lax.axis_size("dp")
+    d_in, d_out = partial_w.shape
+    rows = d_in // n_band
+    band = lax.axis_index("band")
+    blocks = partial_w.reshape(n_band // 4, 2, 2, rows, d_out)
+    blocks = exchange(blocks, 2, band, band % 2, 1, 2)
+    blocks = exchange(blocks, 0, band, band // 4, 4, n_band // 4)
+    blocks = exchange(blocks, 0, band, (band // 2) % 2, 2, 2)
+    cols = d_out // n_dp
+    blocks = blocks.reshape(rows, n_dp, cols).transpose(1, 0, 2)
+    blocks = lax.all_to_all(blocks, "dp", 0, 0, tiled=True)
+    return blocks.sum(axis=0)
+
+
 def body(cell_states, head_grads, group_ids, proj_weights):
     tables, rows_here, cols, width = cell_states.shape
     heads_width = head_grads.shape[-1]
@@ -91,13 +121,7 @@
     all_grads = jnp.concatenate((query_grad, key_grad, value_grad), axis=-1)
     partial_w, input_cols = finish(scaled, inverse, normed, all_grads, proj_weights)
     input_grad = lax.all_to_all(input_cols, "band", split_axis=1, concat_axis=2, tiled=True)
-    n_band = lax.axis_size("band")
-    n_dp = lax.axis_size("dp")
-    d_in, d_out = partial_w.shape
-    blocks = partial_w.reshape(n_band, d_in // n_band, n_dp, d_out // n_dp)
-    blocks = blocks.transpose(0, 2, 1, 3).reshape(n_band * n_dp, d_in // n_band, d_out // n_dp)
-    weight_grad = lax.psum_scatter(blocks, ("band", "dp"), scatter_dimension=0, tiled=True)
-    weight_grad = weight_grad.reshape(d_in // n_band, d_out // n_dp)
+    weight_grad = reduce_weight_grad(partial_w)
     return (input_grad, weight_grad)
 
 

time: 452 us -> 200 us (0.44)
  waiting for transfers between devices: 327 us -> 54.3 us
  starting transfers between devices: 21.5 us -> 58.8 us
  between operations: 14.2 us -> 1 us
  matrix products: 33.1 us -> 27.7 us
    unnamed x2 -> x0, waiting for transfers between devices: 291 us -> none
    ppermute x0 -> x5, waiting for transfers between devices: none -> 23.3 us  [exchange(): total = total + lax.ppermute(part, 'band', pairs)]
    all_to_all x0 -> x1, starting transfers between devices: none -> 21.4 us  [reduce_weight_grad(): blocks = lax.all_to_all(blocks, 'dp', 0, 0, tiled=True)]
    ppermute x0 -> x5, starting transfers between devices: none -> 18.6 us  [exchange(): total = total + lax.ppermute(part, 'band', pairs)]
    all_to_all x1, waiting for transfers between devices: 15.5 us -> 0.01 us  [body(): lax.all_to_all(input_cols, 'band', split_axis=1, concat_axis=2, tiled=True)]
    all_to_all x0 -> x1, waiting for transfers between devices: none -> 9.88 us  [reduce_weight_grad(): blocks = lax.all_to_all(blocks, 'dp', 0, 0, tiled=True)]
    dot_general x3 -> x1, local copies, waits for them, and re-layouts: 7.66 us -> 2.29 us  [finish(): lax.dot_general(flat_norm, flat_grad, (((0,), (0,)), ((), ())), preferred...]
  transfers between devices with their start and end apart: 3 -> 8, of which waited for: 3 -> 5; matrix products, arithmetic and copies ran while one was open for 1% -> 10% of each run, Pallas kernels for 0% -> 0%
where the time goes in v2:
time: 200 us; the launch traced here: 197 us
  starting transfers between devices  58.8 us (29%)
  waiting for transfers between devices  54.3 us (27%)
  local copies, waits for them, and re-layouts  46.8 us (23%)
  matrix products  27.7 us (14%)
  other arithmetic  8.07 us (4%)
    ppermute x5, waiting for transfers between devices, exchange(): total = total + lax.ppermute(part, 'band', pairs)  23.3 us
    all_to_all x1, starting transfers between devices, reduce_weight_grad(): blocks = lax.all_to_all(blocks, 'dp', 0, 0, tiled=True)  21.4 us
    all_to_all x1, waiting for transfers between devices, body(): lax.all_to_all(both, 'band', split_axis=2, concat_axis=1, tiled=True)  21.1 us
    ppermute x5, starting transfers between devices, exchange(): total = total + lax.ppermute(part, 'band', pairs)  18.6 us
    all_to_all x1, starting transfers between devices, body(): lax.all_to_all(both, 'band', split_axis=2, concat_axis=1, tiled=True)  14.4 us
    concatenate x6, local copies, waits for them, and re-layouts, body(): all_grads = jnp.concatenate((query_grad, key_grad, value_grad), axis=-1)  13.9 us
    all_to_all x1, waiting for transfers between devices, reduce_weight_grad(): blocks = lax.all_to_all(blocks, 'dp', 0, 0, tiled=True)  9.88 us
    dot_general x1, matrix products, attend_back(): jnp.einsum('bchij,bjchd->bichd', score_low, key_five, preferred_element_t...  5.16 us
  transfers between devices with their start and end apart: 8, of which 5 were waited for; matrix products, arithmetic and copies ran while one was open for 10% of the time, Pallas kernels for 0%

profile of v2, /device:TPU:1, one launch (start us, length us, event | category | flops | bytes accessed | tf_op | source)
XLA Modules:
  0.0 196.7 jit_solution(7420546486905091427)
XLA Ops:
  4.4 14.4 %all-to-all-start = ((bf16[2,2,128,1152]{3,1,0,2:T(2,128)(2,1)}), bf16[2,2,128,1152]{3,1,0,2:T(2,128)(2,1)S(1)}, u32[]{:S(2)}, u32[]{:S(2)}) async-start(bf16[2,2,128,1152]{3,1,0,2:T(2,128)(2,1)} %copy.50), calls=%async_computation | async-start | bytes 2359296 | tf_op jit(solution)/shard_map/all_to_all | solution.py:113
  18.9 21.1 %all-to-all-done = bf16[2,2,128,1152]{3,1,0,2:T(2,128)(2,1)S(1)} async-done(((bf16[2,2,128,1152]{3,1,0,2:T(2,128)(2,1)}), bf16[2,2,128,1152]{3,1,0,2:T(2,128)(2,1)S(1)}, u32[]{:S(2)}, u32[]{:S(2)}) %all-to-all-start) | async-done | bytes 1179680 | tf_op jit(solution)/shard_map/all_to_all | solution.py:113
  53.1 3.8 %fusion.46 = f32[2,8,6,32,32]{3,4,2,1,0:T(8,128)} fusion(bf16[2,32,8,6,64]{4,3,2,1,0:T(8,128)(2,1)} %reshape.70, bf16[2,32,8,6,64]{4,3,2,1,0:T(8,128)(2,1)} %reshape.69), kind=kOutput, calls=%fused_computation.44 | convolution fusion | flops 12582912 | bytes 1179648 | tf_op jit(solution)/shard_map/bichd,bjchd->bchij/dot_general | solution.py:50
  56.8 4.1 %fusion.66 = (f32[2,8,6,32]{3,2,1,0:T(8,128)S(1)}, f32[2,8,6,32,32]{3,4,2,1,0:T(8,128)}) fusion(pred[2,8,32,32]{2,3,1,0:T(8,128)(4,1)S(1)} %compare_or_fusion, bf16[2,32,8,6,64]{4,3,2,1,0:T(8,128)(2,1)} %reshape.67, bf16[2,32,8,6,64]{4,3,2,1,0:T(8,128)(2,1)} %reshape.68), kind=kOutput, calls=%fused_computation.75 | convolution fusion | flops 12976159 | bytes 1208320 | tf_op jit(solution)/shard_map/sub | solution.py:44
  61.0 3.2 %fusion.35 = bf16[2,32,8,6,64]{4,1,3,2,0:T(8,128)(2,1)} fusion(bf16[2,32,8,6,64]{4,3,2,1,0:T(8,128)(2,1)} %reshape.69, f32[2,8,6,32,32]{3,4,2,1,0:T(8,128)} %get-tuple-element.13, f32[2,8,6,32]{3,2,1,0:T(8,128)S(1)} %get-tuple-element.12), kind=kOutput, calls=%fused_computation.30 | convolution fusion | flops 12976128 | bytes 1191936 | tf_op jit(solution)/shard_map/bchij,bichd->bjchd/dot_general | solution.py:47
  64.2 5.2 %fusion.29 = bf16[2,32,8,6,64]{4,1,3,2,0:T(8,128)(2,1)} fusion(f32[2,8,6,32,32]{3,4,2,1,0:T(8,128)} %fusion.46, bf16[2,32,8,6,64]{4,3,2,1,0:T(8,128)(2,1)} %reshape.68, f32[2,8,6,32,32]{3,4,2,1,0:T(8,128)} %get-tuple-element.13, f32[2,8,6,32]{3,2,1,0:T(8,128)S(1)} %get-tuple-element.12), kind=kOutput, calls=%fused_computation.28 | convolution fusion | flops 13470751 | bytes 1585152 | tf_op jit(solution)/shard_map/bchij,bichd->bjchd/dot_general | solution.py:58
  69.3 5.2 %fusion.32 = bf16[2,32,8,6,64]{4,1,3,2,0:T(8,128)(2,1)} fusion(f32[2,8,6,32,32]{3,4,2,1,0:T(8,128)} %fusion.46, bf16[2,32,8,6,64]{4,3,2,1,0:T(8,128)(2,1)} %reshape.67, f32[2,8,6,32,32]{3,4,2,1,0:T(8,128)} %get-tuple-element.13, f32[2,8,6,32]{3,2,1,0:T(8,128)S(1)} %get-tuple-element.12), kind=kOutput, calls=%fused_computation.29 | convolution fusion | flops 13470751 | bytes 1585152 | tf_op jit(solution)/shard_map/bchij,bjchd->bichd/dot_general | solution.py:55
  76.8 2.6 %copy.58 = bf16[2,32,8,6,64]{4,3,2,1,0:T(8,128)(2,1)} copy(bf16[2,32,8,6,64]{4,1,3,2,0:T(8,128)(2,1)} %fusion.32) | data formatting | bytes 786432 | tf_op jit(solution)/shard_map/convert_element_type | solution.py:57
  83.9 2.7 %concatenate.28 = bf16[512,384]{1,0:T(8,128)(2,1)} reshape(bf16[2,32,8,6,64]{4,3,2,1,0:T(8,128)(2,1)} %copy.60) | data formatting | bytes 786432 | tf_op jit(solution)/shard_map/concatenate | solution.py:121
  86.6 2.5 %concatenate.27 = bf16[512,384]{1,0:T(8,128)(2,1)} reshape(bf16[2,32,8,6,64]{4,3,2,1,0:T(8,128)(2,1)} %copy.58) | data formatting | bytes 786432 | tf_op jit(solution)/shard_map/concatenate | solution.py:121
  89.1 2.5 %fusion.41 = f32[4,2,2,48,1152]{4,3,2,1,0:T(8,128)S(1)} fusion(bf16[4,2,2,48,512]{4,3,2,1,0:T(8,128)(2,1)} %bitcast.81, bf16[512,384]{1,0:T(8,128)(2,1)S(1)} %concatenate.29, bf16[512,384]{1,0:T(8,128)(2,1)} %concatenate.28, bf16[512,384]{1,0:T(8,128)(2,1)} %concatenate.27), kind=kOutput, calls=%fused_computation.38 | convolution fusion | flops 909508608 | bytes 5505024 | tf_op jit(solution)/shard_map/dot_general | solution.py:67
  93.9 2.7 %collective-permute-start = (f32[4,2,48,1152]{3,2,1,0:T(8,128)}, f32[4,2,48,1152]{3,2,1,0:T(8,128)}, u32[]{:S(2)}, u32[]{:S(2)}) collective-permute-start(f32[4,2,48,1152]{3,2,1,0:T(8,128)} %dynamic-slice_bitcast_fusion), channel_id=1, source_target_pairs={{0,1},{1,0},{2,3},{3,2},{4,5},{5,4},{6,7},{7,6},{8,9},{9,8},{10,11... | collective-permute-start | bytes 5308424 | tf_op jit(solution)/shard_map/ppermute | solution.py:89
  98.6 2.5 %concatenate.24 = bf16[2,32,8,384]{3,2,1,0:T(8,128)(2,1)} reshape(bf16[2,32,8,6,64]{4,3,2,1,0:T(8,128)(2,1)} %copy.60) | data formatting | bytes 786432 | tf_op jit(solution)/shard_map/concatenate | solution.py:121
  101.1 2.5 %concatenate.23 = bf16[2,32,8,384]{3,2,1,0:T(8,128)(2,1)} reshape(bf16[2,32,8,6,64]{4,3,2,1,0:T(8,128)(2,1)} %copy.58) | data formatting | bytes 786432 | tf_op jit(solution)/shard_map/concatenate | solution.py:121
  103.6 2.6 %fusion.8 = (f32[2,32,8]{2,1,0:T(8,128)S(1)}, f32[2,32,8,768]{3,2,1,0:T(8,128)S(1)}) fusion(f32[2,32,8]{2,1,0:T(8,128)S(1)} %add_rsqrt_fusion, bf16[2,32,8,1152]{3,2,1,0:T(8,128)(2,1)S(1)} %bitcast.71, bf16[768,1152]{1,0:T(8,128)(2,1)S(1)} %copy-done, bf16[2,32,8,384]{3,2,1,0:T(8,128)(2,1)S(1)} %concatenate.25, bf16[2,32,8,384]{3,2,1,0:T(8,128)(2,1)} %concatenate.24, ...), kind=kOutput, calls=%fused_computation.13 | convolution fusion | flops 911080960 | bytes 5312512 | tf_op jit(solution)/shard_map/dot_general | solution.py:70
  109.1 6.6 %collective-permute-start.1 = (f32[2,48,1152]{2,1,0:T(8,128)}, f32[2,48,1152]{2,1,0:T(8,128)S(1)}, u32[]{:S(2)}, u32[]{:S(2)}) collective-permute-start(f32[2,48,1152]{2,1,0:T(8,128)} %get-tuple-element.6), channel_id=1, source_target_pairs={{0,4},{1,5},{2,6},{3,7},{4,8},{5,9},{6,10},{7,11},{8,12},{9,13},{1... | collective-permute-start | bytes 1327112 | tf_op jit(solution)/shard_map/ppermute | solution.py:89
  117.6 3.7 %collective-permute-start.2 = (f32[2,48,1152]{2,1,0:T(8,128)}, f32[2,48,1152]{2,1,0:T(8,128)}, u32[]{:S(2)}, u32[]{:S(2)}) collective-permute-start(f32[2,48,1152]{2,1,0:T(8,128)} %get-tuple-element.8), channel_id=1, source_target_pairs={{0,8},{1,9},{2,10},{3,11},{4,12},{5,13},{6,14},{7,15},{8,0},{9,1},... | collective-permute-start | bytes 1327112 | tf_op jit(solution)/shard_map/ppermute | solution.py:89
  122.7 4.5 %all-to-all-start.1 = ((bf16[2,32,8,768]{3,2,0,1:T(8,128)(2,1)}), bf16[2,32,8,768]{3,2,0,1:T(8,128)(2,1)S(1)}, u32[]{:S(2)}, u32[]{:S(2)}) async-start(bf16[2,32,8,768]{3,2,0,1:T(8,128)(2,1)} %copy.63), calls=%async_computation.1 | async-start | bytes 1572864 | tf_op jit(solution)/shard_map/all_to_all | solution.py:123
  127.1 6.3 %collective-permute-done.1 = f32[2,48,1152]{2,1,0:T(8,128)S(1)} collective-permute-done((f32[2,48,1152]{2,1,0:T(8,128)}, f32[2,48,1152]{2,1,0:T(8,128)S(1)}, u32[]{:S(2)}, u32[]{:S(2)}) %collective-permute-start.1) | collective-permute-done | bytes 442400 | tf_op jit(solution)/shard_map/ppermute | solution.py:89
  133.4 2.8 %collective-permute-done.2 = f32[2,48,1152]{2,1,0:T(8,128)} collective-permute-done((f32[2,48,1152]{2,1,0:T(8,128)}, f32[2,48,1152]{2,1,0:T(8,128)}, u32[]{:S(2)}, u32[]{:S(2)}) %collective-permute-start.2) | collective-permute-done | bytes 442400 | tf_op jit(solution)/shard_map/ppermute | solution.py:89
  137.6 3.7 %collective-permute-start.4 = (f32[48,1152]{1,0:T(8,128)S(1)}, f32[48,1152]{1,0:T(8,128)S(1)}, u32[]{:S(2)}, u32[]{:S(2)}) collective-permute-start(f32[48,1152]{1,0:T(8,128)S(1)} %dynamic-slice_bitcast_fusion.4), channel_id=1, source_target_pairs={{0,2},{1,3},{2,0},{3,1},{4,6},{5,7},{6,4},{7,5},{8,10},{9,11},{10,... | collective-permute-start | bytes 663560 | tf_op jit(solution)/shard_map/ppermute | solution.py:89
  141.3 14.3 %collective-permute-done.4 = f32[48,1152]{1,0:T(8,128)S(1)} collective-permute-done((f32[48,1152]{1,0:T(8,128)S(1)}, f32[48,1152]{1,0:T(8,128)S(1)}, u32[]{:S(2)}, u32[]{:S(2)}) %collective-permute-start.4) | collective-permute-done | bytes 221216 | tf_op jit(solution)/shard_map/ppermute | solution.py:89
  161.9 21.4 %all-to-all-start.2 = ((f32[32,1,1728]{2,1,0:T(1,128)}), f32[32,1,1728]{2,1,0:T(1,128)S(1)}, u32[]{:S(2)}, u32[]{:S(2)}) async-start(f32[32,1,1728]{2,1,0:T(1,128)} %reshape.74), calls=%async_computation.2 | async-start | bytes 458752 | tf_op jit(solution)/shard_map/all_to_all | solution.py:105
  184.2 9.9 %all-to-all-done.2 = f32[32,1,1728]{2,1,0:T(1,128)S(1)} async-done(((f32[32,1,1728]{2,1,0:T(1,128)}), f32[32,1,1728]{2,1,0:T(1,128)S(1)}, u32[]{:S(2)}, u32[]{:S(2)}) %all-to-all-start.2) | async-done | bytes 221216 | tf_op jit(solution)/shard_map/all_to_all | solution.py:105
  (59 shorter events, 45.2 us)
Async XLA Ops:
  0.6 43.8 %copy-start = (bf16[768,1152]{1,0:T(8,128)(2,1)S(1)}, bf16[768,1152]{1,0:T(8,128)(2,1)}, u32[]{:S(2)}) copy-start(bf16[768,1152]{1,0:T(8,128)(2,1)} %param.7) | copy-start | bytes 5308420
  4.4 14.4 %copy-start.8 = (s32[2,8,32]{2,1,0:T(8,128)S(1)}, s32[2,8,32]{2,1,0:T(8,128)}, u32[]{:S(2)}) copy-start(s32[2,8,32]{2,1,0:T(8,128)} %param.6) | copy-start | bytes 6148
  4.4 35.6 %all-to-all-start = ((bf16[2,2,128,1152]{3,1,0,2:T(2,128)(2,1)}), bf16[2,2,128,1152]{3,1,0,2:T(2,128)(2,1)S(1)}, u32[]{:S(2)}, u32[]{:S(2)}) async-start(bf16[2,2,128,1152]{3,1,0,2:T(2,128)(2,1)} %copy.50), calls=%async_computation | async-start | bytes 2359296 | tf_op jit(solution)/shard_map/all_to_all | solution.py:113
  40.0 1.0 copy-start.2
  44.5 1.2 copy-start.5
  76.8 2.6 %copy-start.7 = (bf16[2,32,8,6,64]{4,1,3,2,0:T(8,128)(2,1)S(1)}, bf16[2,32,8,6,64]{4,1,3,2,0:T(8,128)(2,1)}, u32[]{:S(2)}) copy-start(bf16[2,32,8,6,64]{4,1,3,2,0:T(8,128)(2,1)} %fusion.29) | copy-start | bytes 1179652
  76.8 4.0 %copy-start.6 = (bf16[2,32,8,6,64]{4,1,3,2,0:T(8,128)(2,1)S(1)}, bf16[2,32,8,6,64]{4,1,3,2,0:T(8,128)(2,1)}, u32[]{:S(2)}) copy-start(bf16[2,32,8,6,64]{4,1,3,2,0:T(8,128)(2,1)} %fusion.35) | copy-start | bytes 1179652
  91.6 2.3 %copy-start.3 = (f32[4,2,2,48,1152]{4,3,2,1,0:T(8,128)}, f32[4,2,2,48,1152]{4,3,2,1,0:T(8,128)S(1)}, u32[]{:S(2)}) copy-start(f32[4,2,2,48,1152]{4,3,2,1,0:T(8,128)S(1)} %fusion.41) | copy-start | bytes 10616836
  93.9 12.3 %collective-permute-start = (f32[4,2,48,1152]{3,2,1,0:T(8,128)}, f32[4,2,48,1152]{3,2,1,0:T(8,128)}, u32[]{:S(2)}, u32[]{:S(2)}) collective-permute-start(f32[4,2,48,1152]{3,2,1,0:T(8,128)} %dynamic-slice_bitcast_fusion), channel_id=1, source_target_pairs={{0,1},{1,0},{2,3},{3,2},{4,5},{5,4},{6,7},{7,6},{8,9},{9,8},{10,11... | collective-permute-start | bytes 5308424 | tf_op jit(solution)/shard_map/ppermute | solution.py:89
  103.6 2.6 %copy-start.4 = (f32[4,2,2,48,1152]{4,3,2,1,0:T(8,128)S(1)}, f32[4,2,2,48,1152]{4,3,2,1,0:T(8,128)}, u32[]{:S(2)}) copy-start(f32[4,2,2,48,1152]{4,3,2,1,0:T(8,128)} %copy-done.3) | copy-start | bytes 10616836
  107.9 13.8 %copy-start.1 = (f32[4,2,48,1152]{3,2,1,0:T(8,128)}, f32[4,2,48,1152]{3,2,1,0:T(8,128)S(1)}, u32[]{:S(2)}) copy-start(f32[4,2,48,1152]{3,2,1,0:T(8,128)S(1)} %bitcast_add_fusion) | copy-start | bytes 5308420
  109.1 24.2 %collective-permute-start.1 = (f32[2,48,1152]{2,1,0:T(8,128)}, f32[2,48,1152]{2,1,0:T(8,128)S(1)}, u32[]{:S(2)}, u32[]{:S(2)}) collective-permute-start(f32[2,48,1152]{2,1,0:T(8,128)} %get-tuple-element.6), channel_id=1, source_target_pairs={{0,4},{1,5},{2,6},{3,7},{4,8},{5,9},{6,10},{7,11},{8,12},{9,13},{1... | collective-permute-start | bytes 1327112 | tf_op jit(solution)/shard_map/ppermute | solution.py:89
  115.7 17.7 %collective-permute-start.3 = (f32[2,48,1152]{2,1,0:T(8,128)}, f32[2,48,1152]{2,1,0:T(8,128)}, u32[]{:S(2)}, u32[]{:S(2)}) collective-permute-start(f32[2,48,1152]{2,1,0:T(8,128)} %get-tuple-element.7), channel_id=1, source_target_pairs={{0,12},{1,13},{2,14},{3,15},{4,0},{5,1},{6,2},{7,3},{8,4},{9,5},{1... | collective-permute-start | bytes 1327112 | tf_op jit(solution)/shard_map/ppermute | solution.py:89
  117.6 18.6 %collective-permute-start.2 = (f32[2,48,1152]{2,1,0:T(8,128)}, f32[2,48,1152]{2,1,0:T(8,128)}, u32[]{:S(2)}, u32[]{:S(2)}) collective-permute-start(f32[2,48,1152]{2,1,0:T(8,128)} %get-tuple-element.8), channel_id=1, source_target_pairs={{0,8},{1,9},{2,10},{3,11},{4,12},{5,13},{6,14},{7,15},{8,0},{9,1},... | collective-permute-start | bytes 1327112 | tf_op jit(solution)/shard_map/ppermute | solution.py:89
  122.7 39.2 %all-to-all-start.1 = ((bf16[2,32,8,768]{3,2,0,1:T(8,128)(2,1)}), bf16[2,32,8,768]{3,2,0,1:T(8,128)(2,1)S(1)}, u32[]{:S(2)}, u32[]{:S(2)}) async-start(bf16[2,32,8,768]{3,2,0,1:T(8,128)(2,1)} %copy.63), calls=%async_computation.1 | async-start | bytes 1572864 | tf_op jit(solution)/shard_map/all_to_all | solution.py:123
  137.6 18.0 %collective-permute-start.4 = (f32[48,1152]{1,0:T(8,128)S(1)}, f32[48,1152]{1,0:T(8,128)S(1)}, u32[]{:S(2)}, u32[]{:S(2)}) collective-permute-start(f32[48,1152]{1,0:T(8,128)S(1)} %dynamic-slice_bitcast_fusion.4), channel_id=1, source_target_pairs={{0,2},{1,3},{2,0},{3,1},{4,6},{5,7},{6,4},{7,5},{8,10},{9,11},{10,... | collective-permute-start | bytes 663560 | tf_op jit(solution)/shard_map/ppermute | solution.py:89
  161.9 32.2 %all-to-all-start.2 = ((f32[32,1,1728]{2,1,0:T(1,128)}), f32[32,1,1728]{2,1,0:T(1,128)S(1)}, u32[]{:S(2)}, u32[]{:S(2)}) async-start(f32[32,1,1728]{2,1,0:T(1,128)} %reshape.74), calls=%async_computation.2 | async-start | bytes 458752 | tf_op jit(solution)/shard_map/all_to_all | solution.py:105

commit v3 on v2

--- a/solution.py
+++ b/solution.py
@@ -106,21 +106,34 @@
     return blocks.sum(axis=0)
 
 
-def body(cell_states, head_grads, group_ids, proj_weights):
-    tables, rows_here, cols, width = cell_states.shape
-    heads_width = head_grads.shape[-1]
-    both = jnp.concatenate((cell_states, head_grads), axis=-1)
+def column_part(both, groups, proj_weights, width):
     both_cols = lax.all_to_all(both, "band", split_axis=2, concat_axis=1, tiled=True)
     states_cols = both_cols[..., :width]
     grad_cols = both_cols[..., width:]
     scaled, inverse, normed = normalize(states_cols)
     query_cols, key_cols, value_cols = project(normed, proj_weights)
     query_grad, key_grad, value_grad = attend_back(
-        query_cols, key_cols, value_cols, grad_cols, group_ids
+        query_cols, key_cols, value_cols, grad_cols, groups
     )
     all_grads = jnp.concatenate((query_grad, key_grad, value_grad), axis=-1)
     partial_w, input_cols = finish(scaled, inverse, normed, all_grads, proj_weights)
     input_grad = lax.all_to_all(input_cols, "band", split_axis=1, concat_axis=2, tiled=True)
+    return partial_w, input_grad
+
+
+def body(cell_states, head_grads, group_ids, proj_weights):
+    tables = cell_states.shape[0]
+    width = cell_states.shape[-1]
+    both = jnp.concatenate((cell_states, head_grads), axis=-1)
+    partial_w = None
+    pieces = []
+    for t in range(tables):
+        part_w, input_part = column_part(
+            both[t : t + 1], group_ids[t : t + 1], proj_weights, width
+        )
+        partial_w = part_w if partial_w is None else partial_w + part_w
+        pieces.append(input_part)
+    input_grad = jnp.concatenate(pieces, axis=0)
     weight_grad = reduce_weight_grad(partial_w)
     return (input_grad, weight_grad)
 

time: 200 us -> 217 us (1.085)
  starting transfers between devices: 58.8 us -> 72 us
  matrix products: 27.7 us -> 35.1 us
    all_to_all x2 -> x4, starting transfers between devices: 18.9 us -> 39.3 us  [the longest x2 22.2 us: column_part(): lax.all_to_all(both, 'band', split_axis=2, concat_axis=1, tiled=True)]
    another operation x0 -> x8, local copies, waits for them, and re-layouts: none -> 14.7 us
    ppermute x5, waiting for transfers between devices: 23.3 us -> 33 us  [exchange(): total = total + lax.ppermute(part, 'band', pairs)]
    all_to_all x2 -> x4, waiting for transfers between devices: 21.1 us -> 12.4 us  [the longest x2 12.4 us: column_part(): lax.all_to_all(both, 'band', split_axis=2, concat_axis=1, tiled=True)]
    reshape x4 -> x0, local copies, waits for them, and re-layouts: 7.9 us -> none  [the longest x1 2.43 us: attend_back(): query_five = query_rows.reshape(split)]
    concatenate x6, local copies, waits for them, and re-layouts: 13.9 us -> 6.04 us  [column_part(): all_grads = jnp.concatenate((query_grad, key_grad, value_grad), axis=-1)]
    all_to_all x1, starting transfers between devices: 21.4 us -> 14 us  [reduce_weight_grad(): blocks = lax.all_to_all(blocks, 'dp', 0, 0, tiled=True)]
    unnamed x20 -> x41, local copies, waits for them, and re-layouts: 4.38 us -> 7.68 us
  transfers between devices with their start and end apart: 8 -> 10, of which waited for: 5 -> 6; matrix products, arithmetic and copies ran while one was open for 10% -> 18% of each run, Pallas kernels for 0% -> 0%
where the time goes in v3:
time: 217 us; the launch traced here: 214 us
  starting transfers between devices  72 us (33%)
  waiting for transfers between devices  53.5 us (25%)
  local copies, waits for them, and re-layouts  44.7 us (21%)
  matrix products  35.1 us (16%)
  other arithmetic  7.59 us (3%)
    ppermute x5, waiting for transfers between devices, exchange(): total = total + lax.ppermute(part, 'band', pairs)  33 us
    all_to_all x2, starting transfers between devices, column_part(): lax.all_to_all(both, 'band', split_axis=2, concat_axis=1, tiled=True)  22.2 us
    ppermute x5, starting transfers between devices, exchange(): total = total + lax.ppermute(part, 'band', pairs)  18.7 us
    all_to_all x2, starting transfers between devices, column_part(): lax.all_to_all(input_cols, 'band', split_axis=1, concat_axis=2, tiled=True)  17.1 us
    another operation x8, local copies, waits for them, and re-layouts  14.7 us
    all_to_all x1, starting transfers between devices, reduce_weight_grad(): blocks = lax.all_to_all(blocks, 'dp', 0, 0, tiled=True)  14 us
    all_to_all x2, waiting for transfers between devices, column_part(): lax.all_to_all(both, 'band', split_axis=2, concat_axis=1, tiled=True)  12.4 us
    all_to_all x1, waiting for transfers between devices, reduce_weight_grad(): blocks = lax.all_to_all(blocks, 'dp', 0, 0, tiled=True)  8.15 us
  transfers between devices with their start and end apart: 10, of which 6 were waited for; matrix products, arithmetic and copies ran while one was open for 18% of the time, Pallas kernels for 0%

profile of v3, /device:TPU:1, one launch (start us, length us, event | category | flops | bytes accessed | tf_op | source)
XLA Modules:
  0.0 214.0 jit_solution(13795832891653729559)
XLA Ops:
  3.6 14.3 %all-to-all-start.2 = ((bf16[1,2,128,1152]{3,1,0,2:T(2,128)(2,1)}), bf16[1,2,128,1152]{3,1,0,2:T(2,128)(2,1)S(1)}, u32[]{:S(2)}, u32[]{:S(2)}) async-start(bf16[1,2,128,1152]{3,1,0,2:T(2,128)(2,1)} %copy.116), calls=%async_computation.2 | async-start | bytes 1179648 | tf_op jit(solution)/shard_map/all_to_all | solution.py:110
  20.1 12.4 %all-to-all-done.2 = bf16[1,2,128,1152]{3,1,0,2:T(2,128)(2,1)S(1)} async-done(((bf16[1,2,128,1152]{3,1,0,2:T(2,128)(2,1)}), bf16[1,2,128,1152]{3,1,0,2:T(2,128)(2,1)S(1)}, u32[]{:S(2)}, u32[]{:S(2)}) %all-to-all-start.2) | async-done | bytes 589856 | tf_op jit(solution)/shard_map/all_to_all | solution.py:110
  32.5 7.9 %all-to-all-start = ((bf16[1,2,128,1152]{3,1,0,2:T(2,128)(2,1)}), bf16[1,2,128,1152]{3,1,0,2:T(2,128)(2,1)S(1)}, u32[]{:S(2)}, u32[]{:S(2)}) async-start(bf16[1,2,128,1152]{3,1,0,2:T(2,128)(2,1)} %copy.115), calls=%async_computation | async-start | bytes 1179648 | tf_op jit(solution)/shard_map/all_to_all | solution.py:110
  50.3 2.5 %fusion.71 = f32[8,6,32,32]{2,3,1,0:T(8,128)} fusion(bf16[32,8,6,64]{3,2,1,0:T(8,128)(2,1)} %reshape.290, bf16[32,8,6,64]{3,2,1,0:T(8,128)(2,1)S(1)} %reshape.289), kind=kOutput, calls=%fused_computation.87 | convolution fusion | flops 6291456 | bytes 589824 | tf_op jit(solution)/shard_map/bichd,bjchd->bchij/dot_general | solution.py:50
  52.8 2.8 %fusion.116 = (f32[8,6,32]{2,1,0:T(8,128)S(1)}, f32[8,6,32,32]{2,3,1,0:T(8,128)}) fusion(pred[8,32,32]{1,2,0:T(8,128)(4,1)S(1)} %copy-done.16, bf16[32,8,6,64]{3,2,1,0:T(8,128)(2,1)} %reshape.287, bf16[32,8,6,64]{3,2,1,0:T(8,128)(2,1)} %reshape.288), kind=kOutput, calls=%fused_computation.144 | convolution fusion | flops 6488095 | bytes 604160 | tf_op jit(solution)/shard_map/sub | solution.py:44
  55.6 3.3 %fusion.32 = bf16[1,32,8,6,64]{4,1,3,2,0:T(8,128)(2,1)} fusion(f32[8,6,32,32]{2,3,1,0:T(8,128)} %fusion.71, bf16[32,8,6,64]{3,2,1,0:T(8,128)(2,1)} %reshape.287, f32[8,6,32,32]{2,3,1,0:T(8,128)} %get-tuple-element.22, f32[8,6,32]{2,1,0:T(8,128)S(1)} %get-tuple-element.21), kind=kOutput, calls=%fused_computation.42 | convolution fusion | flops 6735391 | bytes 792576 | tf_op jit(solution)/shard_map/bchij,bjchd->bichd/dot_general | solution.py:55
  59.0 3.3 %fusion.35 = bf16[1,32,8,6,64]{4,1,3,2,0:T(8,128)(2,1)} fusion(f32[8,6,32,32]{2,3,1,0:T(8,128)} %fusion.71, bf16[32,8,6,64]{3,2,1,0:T(8,128)(2,1)} %reshape.288, f32[8,6,32,32]{2,3,1,0:T(8,128)} %get-tuple-element.22, f32[8,6,32]{2,1,0:T(8,128)S(1)} %get-tuple-element.21), kind=kOutput, calls=%fused_computation.45 | convolution fusion | flops 6735391 | bytes 792576 | tf_op jit(solution)/shard_map/bchij,bichd->bjchd/dot_general | solution.py:58
  62.3 2.3 %fusion.36 = bf16[1,32,8,6,64]{4,1,3,2,0:T(8,128)(2,1)} fusion(bf16[32,8,6,64]{3,2,1,0:T(8,128)(2,1)S(1)} %reshape.289, f32[8,6,32,32]{2,3,1,0:T(8,128)} %get-tuple-element.22, f32[8,6,32]{2,1,0:T(8,128)S(1)} %get-tuple-element.21), kind=kOutput, calls=%fused_computation.46 | convolution fusion | flops 6488064 | bytes 595968 | tf_op jit(solution)/shard_map/bchij,bichd->bjchd/dot_general | solution.py:47
  74.5 2.5 %fusion.73 = f32[8,6,32,32]{2,3,1,0:T(8,128)} fusion(bf16[32,8,6,64]{3,2,1,0:T(8,128)(2,1)} %reshape.283, bf16[32,8,6,64]{3,2,1,0:T(8,128)(2,1)S(1)} %reshape.282), kind=kOutput, calls=%fused_computation.90 | convolution fusion | flops 6291456 | bytes 589824 | tf_op jit(solution)/shard_map/bichd,bjchd->bchij/dot_general | solution.py:50
  77.0 2.8 %fusion.117 = (f32[8,6,32]{2,1,0:T(8,128)S(1)}, f32[8,6,32,32]{2,3,1,0:T(8,128)}) fusion(pred[8,32,32]{1,2,0:T(8,128)(4,1)S(1)} %copy-done.15, bf16[32,8,6,64]{3,2,1,0:T(8,128)(2,1)} %reshape.280, bf16[32,8,6,64]{3,2,1,0:T(8,128)(2,1)} %reshape.281), kind=kOutput, calls=%fused_computation.145 | convolution fusion | flops 6488095 | bytes 604160 | tf_op jit(solution)/shard_map/sub | solution.py:44
  82.1 3.4 %fusion.33 = bf16[1,32,8,6,64]{4,1,3,2,0:T(8,128)(2,1)} fusion(f32[8,6,32,32]{2,3,1,0:T(8,128)} %fusion.73, bf16[32,8,6,64]{3,2,1,0:T(8,128)(2,1)} %reshape.281, f32[8,6,32,32]{2,3,1,0:T(8,128)} %get-tuple-element.26, f32[8,6,32]{2,1,0:T(8,128)S(1)} %get-tuple-element.25), kind=kOutput, calls=%fused_computation.43 | convolution fusion | flops 6735391 | bytes 792576 | tf_op jit(solution)/shard_map/bchij,bichd->bjchd/dot_general | solution.py:58
  85.4 3.1 %fusion.31 = bf16[1,32,8,6,64]{4,1,3,2,0:T(8,128)(2,1)} fusion(f32[8,6,32,32]{2,3,1,0:T(8,128)} %fusion.73, bf16[32,8,6,64]{3,2,1,0:T(8,128)(2,1)S(1)} %copy-done.4, f32[8,6,32,32]{2,3,1,0:T(8,128)} %get-tuple-element.26, f32[8,6,32]{2,1,0:T(8,128)S(1)} %get-tuple-element.25), kind=kOutput, calls=%fused_computation.41 | convolution fusion | flops 6735391 | bytes 792576 | tf_op jit(solution)/shard_map/bchij,bjchd->bichd/dot_general | solution.py:55
  111.7 9.7 %all-to-all-start.3 = ((bf16[1,32,8,768]{3,2,0,1:T(8,128)(2,1)}), bf16[1,32,8,768]{3,2,0,1:T(8,128)(2,1)S(1)}, u32[]{:S(2)}, u32[]{:S(2)}) async-start(bf16[1,32,8,768]{3,2,0,1:T(8,128)(2,1)} %fusion.65), calls=%async_computation.3 | async-start | bytes 786432 | tf_op jit(solution)/shard_map/all_to_all | solution.py:120
  125.2 4.5 %collective-permute-start.3 = (f32[2,48,1152]{2,1,0:T(8,128)S(1)}, f32[2,48,1152]{2,1,0:T(8,128)S(1)}, u32[]{:S(2)}, u32[]{:S(2)}) collective-permute-start(f32[2,48,1152]{2,1,0:T(8,128)S(1)} %get-tuple-element.7), channel_id=1, source_target_pairs={{0,12},{1,13},{2,14},{3,15},{4,0},{5,1},{6,2},{7,3},{8,4},{9,5},{1... | collective-permute-start | bytes 1327112 | tf_op jit(solution)/shard_map/ppermute | solution.py:89
  129.7 2.5 %collective-permute-start.2 = (f32[2,48,1152]{2,1,0:T(8,128)S(1)}, f32[2,48,1152]{2,1,0:T(8,128)S(1)}, u32[]{:S(2)}, u32[]{:S(2)}) collective-permute-start(f32[2,48,1152]{2,1,0:T(8,128)S(1)} %get-tuple-element.8), channel_id=1, source_target_pairs={{0,8},{1,9},{2,10},{3,11},{4,12},{5,13},{6,14},{7,15},{8,0},{9,1},... | collective-permute-start | bytes 1327112 | tf_op jit(solution)/shard_map/ppermute | solution.py:89
  132.2 2.5 %collective-permute-start.1 = (f32[2,48,1152]{2,1,0:T(8,128)S(1)}, f32[2,48,1152]{2,1,0:T(8,128)S(1)}, u32[]{:S(2)}, u32[]{:S(2)}) collective-permute-start(f32[2,48,1152]{2,1,0:T(8,128)S(1)} %get-tuple-element.6), channel_id=1, source_target_pairs={{0,4},{1,5},{2,6},{3,7},{4,8},{5,9},{6,10},{7,11},{8,12},{9,13},{1... | collective-permute-start | bytes 1327112 | tf_op jit(solution)/shard_map/ppermute | solution.py:89
  135.7 4.7 %collective-permute-done.3 = f32[2,48,1152]{2,1,0:T(8,128)S(1)} collective-permute-done((f32[2,48,1152]{2,1,0:T(8,128)S(1)}, f32[2,48,1152]{2,1,0:T(8,128)S(1)}, u32[]{:S(2)}, u32[]{:S(2)}) %collective-permute-start.3) | collective-permute-done | bytes 442400 | tf_op jit(solution)/shard_map/ppermute | solution.py:89
  140.4 3.7 %collective-permute-done.2 = f32[2,48,1152]{2,1,0:T(8,128)S(1)} collective-permute-done((f32[2,48,1152]{2,1,0:T(8,128)S(1)}, f32[2,48,1152]{2,1,0:T(8,128)S(1)}, u32[]{:S(2)}, u32[]{:S(2)}) %collective-permute-start.2) | collective-permute-done | bytes 442400 | tf_op jit(solution)/shard_map/ppermute | solution.py:89
  144.2 10.5 %collective-permute-done.1 = f32[2,48,1152]{2,1,0:T(8,128)S(1)} collective-permute-done((f32[2,48,1152]{2,1,0:T(8,128)S(1)}, f32[2,48,1152]{2,1,0:T(8,128)S(1)}, u32[]{:S(2)}, u32[]{:S(2)}) %collective-permute-start.1) | collective-permute-done | bytes 442400 | tf_op jit(solution)/shard_map/ppermute | solution.py:89
  154.8 7.5 %all-to-all-start.1 = ((bf16[1,32,8,768]{3,2,0,1:T(8,128)(2,1)}), bf16[1,32,8,768]{3,2,0,1:T(8,128)(2,1)}, u32[]{:S(2)}, u32[]{:S(2)}) async-start(bf16[1,32,8,768]{3,2,0,1:T(8,128)(2,1)} %fusion.66), calls=%async_computation.1 | async-start | bytes 786432 | tf_op jit(solution)/shard_map/all_to_all | solution.py:120
  162.3 7.2 %collective-permute-start.4 = (f32[48,1152]{1,0:T(8,128)S(1)}, f32[48,1152]{1,0:T(8,128)S(1)}, u32[]{:S(2)}, u32[]{:S(2)}) collective-permute-start(f32[48,1152]{1,0:T(8,128)S(1)} %dynamic-slice_bitcast_fusion.4), channel_id=1, source_target_pairs={{0,2},{1,3},{2,0},{3,1},{4,6},{5,7},{6,4},{7,5},{8,10},{9,11},{10,... | collective-permute-start | bytes 663560 | tf_op jit(solution)/shard_map/ppermute | solution.py:89
  169.5 13.9 %collective-permute-done.4 = f32[48,1152]{1,0:T(8,128)S(1)} collective-permute-done((f32[48,1152]{1,0:T(8,128)S(1)}, f32[48,1152]{1,0:T(8,128)S(1)}, u32[]{:S(2)}, u32[]{:S(2)}) %collective-permute-start.4) | collective-permute-done | bytes 221216 | tf_op jit(solution)/shard_map/ppermute | solution.py:89
  186.2 14.0 %all-to-all-start.4 = ((f32[32,1,1728]{2,1,0:T(1,128)}), f32[32,1,1728]{2,1,0:T(1,128)S(1)}, u32[]{:S(2)}, u32[]{:S(2)}) async-start(f32[32,1,1728]{2,1,0:T(1,128)} %reshape.299), calls=%async_computation.4 | async-start | bytes 458752 | tf_op jit(solution)/shard_map/all_to_all | solution.py:105
  203.3 8.2 %all-to-all-done.4 = f32[32,1,1728]{2,1,0:T(1,128)S(1)} async-done(((f32[32,1,1728]{2,1,0:T(1,128)}), f32[32,1,1728]{2,1,0:T(1,128)S(1)}, u32[]{:S(2)}, u32[]{:S(2)}) %all-to-all-start.4) | async-done | bytes 221216 | tf_op jit(solution)/shard_map/all_to_all | solution.py:105
  (106 shorter events, 63.2 us)
Async XLA Ops:
  0.6 40.0 %copy-start = (bf16[768,1152]{1,0:T(8,128)(2,1)S(1)}, bf16[768,1152]{1,0:T(8,128)(2,1)}, u32[]{:S(2)}) copy-start(bf16[768,1152]{1,0:T(8,128)(2,1)} %param.7) | copy-start | bytes 5308420
  2.2 17.1 %copy-start.17 = (s32[2,8,32]{2,1,0:T(8,128)S(1)}, s32[2,8,32]{2,1,0:T(8,128)}, u32[]{:S(2)}) copy-start(s32[2,8,32]{2,1,0:T(8,128)} %param.6) | copy-start | bytes 6148
  3.6 28.9 %all-to-all-start.2 = ((bf16[1,2,128,1152]{3,1,0,2:T(2,128)(2,1)}), bf16[1,2,128,1152]{3,1,0,2:T(2,128)(2,1)S(1)}, u32[]{:S(2)}, u32[]{:S(2)}) async-start(bf16[1,2,128,1152]{3,1,0,2:T(2,128)(2,1)} %copy.116), calls=%async_computation.2 | async-start | bytes 1179648 | tf_op jit(solution)/shard_map/all_to_all | solution.py:110
  32.5 32.1 %all-to-all-start = ((bf16[1,2,128,1152]{3,1,0,2:T(2,128)(2,1)}), bf16[1,2,128,1152]{3,1,0,2:T(2,128)(2,1)S(1)}, u32[]{:S(2)}, u32[]{:S(2)}) async-start(bf16[1,2,128,1152]{3,1,0,2:T(2,128)(2,1)} %copy.115), calls=%async_computation | async-start | bytes 1179648 | tf_op jit(solution)/shard_map/all_to_all | solution.py:110
  44.2 8.7 %copy-start.16 = (pred[8,32,32]{1,2,0:T(8,128)(4,1)S(1)}, pred[8,32,32]{1,2,0:T(8,128)(4,1)}, u32[]{:S(2)}) copy-start(pred[8,32,32]{1,2,0:T(8,128)(4,1)} %get-tuple-element.20) | copy-start | bytes 24580
  68.3 8.7 %copy-start.15 = (pred[8,32,32]{1,2,0:T(8,128)(4,1)S(1)}, pred[8,32,32]{1,2,0:T(8,128)(4,1)}, u32[]{:S(2)}) copy-start(pred[8,32,32]{1,2,0:T(8,128)(4,1)} %get-tuple-element.19) | copy-start | bytes 24580
  82.1 3.4 %copy-start.4 = (bf16[32,8,6,64]{3,2,1,0:T(8,128)(2,1)S(1)}, bf16[32,8,6,64]{3,2,1,0:T(8,128)(2,1)}, u32[]{:S(2)}) copy-start(bf16[32,8,6,64]{3,2,1,0:T(8,128)(2,1)} %reshape.280) | copy-start | bytes 589828
  101.8 2.0 copy-start.10
  101.8 2.0 copy-start.11
  101.8 2.0 copy-start.13
  104.7 2.3 %copy-start.1 = (f32[768,1152]{1,0:T(8,128)}, f32[768,1152]{1,0:T(8,128)S(1)}, u32[]{:S(2)}) copy-start(f32[768,1152]{1,0:T(8,128)S(1)} %fusion.4) | copy-start | bytes 10616836
  107.0 15.3 %collective-permute-start = (f32[4,2,48,1152]{3,2,1,0:T(8,128)}, f32[4,2,48,1152]{3,2,1,0:T(8,128)}, u32[]{:S(2)}, u32[]{:S(2)}) collective-permute-start(f32[4,2,48,1152]{3,2,1,0:T(8,128)} %dynamic-slice_bitcast_fusion), channel_id=1, source_target_pairs={{0,1},{1,0},{2,3},{3,2},{4,5},{5,4},{6,7},{7,6},{8,9},{9,8},{10,11... | collective-permute-start | bytes 5308424 | tf_op jit(solution)/shard_map/ppermute | solution.py:89
  110.7 10.7 %copy-start.6 = (bf16[1,32,8,384]{3,2,1,0:T(8,128)(2,1)S(1)}, bf16[1,32,8,384]{3,2,1,0:T(8,128)(2,1)}, u32[]{:S(2)}) copy-start(bf16[1,32,8,384]{3,2,1,0:T(8,128)(2,1)} %concatenate.31) | copy-start | bytes 589828
  110.7 10.7 %copy-start.7 = (bf16[1,32,8,384]{3,2,1,0:T(8,128)(2,1)S(1)}, bf16[1,32,8,384]{3,2,1,0:T(8,128)(2,1)}, u32[]{:S(2)}) copy-start(bf16[1,32,8,384]{3,2,1,0:T(8,128)(2,1)} %concatenate.30) | copy-start | bytes 589828
  110.7 10.7 %copy-start.8 = (bf16[1,32,8,384]{3,2,1,0:T(8,128)(2,1)S(1)}, bf16[1,32,8,384]{3,2,1,0:T(8,128)(2,1)}, u32[]{:S(2)}) copy-start(bf16[1,32,8,384]{3,2,1,0:T(8,128)(2,1)} %concatenate.29) | copy-start | bytes 589828
  111.7 43.0 %all-to-all-start.3 = ((bf16[1,32,8,768]{3,2,0,1:T(8,128)(2,1)}), bf16[1,32,8,768]{3,2,0,1:T(8,128)(2,1)S(1)}, u32[]{:S(2)}, u32[]{:S(2)}) async-start(bf16[1,32,8,768]{3,2,0,1:T(8,128)(2,1)} %fusion.65), calls=%async_computation.3 | async-start | bytes 786432 | tf_op jit(solution)/shard_map/all_to_all | solution.py:120
  121.4 2.0 copy-start.2
  125.2 15.2 %collective-permute-start.3 = (f32[2,48,1152]{2,1,0:T(8,128)S(1)}, f32[2,48,1152]{2,1,0:T(8,128)S(1)}, u32[]{:S(2)}, u32[]{:S(2)}) collective-permute-start(f32[2,48,1152]{2,1,0:T(8,128)S(1)} %get-tuple-element.7), channel_id=1, source_target_pairs={{0,12},{1,13},{2,14},{3,15},{4,0},{5,1},{6,2},{7,3},{8,4},{9,5},{1... | collective-permute-start | bytes 1327112 | tf_op jit(solution)/shard_map/ppermute | solution.py:89
  129.7 14.4 %collective-permute-start.2 = (f32[2,48,1152]{2,1,0:T(8,128)S(1)}, f32[2,48,1152]{2,1,0:T(8,128)S(1)}, u32[]{:S(2)}, u32[]{:S(2)}) collective-permute-start(f32[2,48,1152]{2,1,0:T(8,128)S(1)} %get-tuple-element.8), channel_id=1, source_target_pairs={{0,8},{1,9},{2,10},{3,11},{4,12},{5,13},{6,14},{7,15},{8,0},{9,1},... | collective-permute-start | bytes 1327112 | tf_op jit(solution)/shard_map/ppermute | solution.py:89
  132.2 22.5 %collective-permute-start.1 = (f32[2,48,1152]{2,1,0:T(8,128)S(1)}, f32[2,48,1152]{2,1,0:T(8,128)S(1)}, u32[]{:S(2)}, u32[]{:S(2)}) collective-permute-start(f32[2,48,1152]{2,1,0:T(8,128)S(1)} %get-tuple-element.6), channel_id=1, source_target_pairs={{0,4},{1,5},{2,6},{3,7},{4,8},{5,9},{6,10},{7,11},{8,12},{9,13},{1... | collective-permute-start | bytes 1327112 | tf_op jit(solution)/shard_map/ppermute | solution.py:89
  154.8 28.7 %copy-start.3 = (bf16[1,32,8,768]{3,2,0,1:T(8,128)(2,1)}, bf16[1,32,8,768]{3,2,0,1:T(8,128)(2,1)S(1)}, u32[]{:S(2)}) copy-start(bf16[1,32,8,768]{3,2,0,1:T(8,128)(2,1)S(1)} %all-to-all-done.3) | copy-start | bytes 1179652
  154.8 31.4 %all-to-all-start.1 = ((bf16[1,32,8,768]{3,2,0,1:T(8,128)(2,1)}), bf16[1,32,8,768]{3,2,0,1:T(8,128)(2,1)}, u32[]{:S(2)}, u32[]{:S(2)}) async-start(bf16[1,32,8,768]{3,2,0,1:T(8,128)(2,1)} %fusion.66), calls=%async_computation.1 | async-start | bytes 786432 | tf_op jit(solution)/shard_map/all_to_all | solution.py:120
  162.3 21.2 %collective-permute-start.4 = (f32[48,1152]{1,0:T(8,128)S(1)}, f32[48,1152]{1,0:T(8,128)S(1)}, u32[]{:S(2)}, u32[]{:S(2)}) collective-permute-start(f32[48,1152]{1,0:T(8,128)S(1)} %dynamic-slice_bitcast_fusion.4), channel_id=1, source_target_pairs={{0,2},{1,3},{2,0},{3,1},{4,6},{5,7},{6,4},{7,5},{8,10},{9,11},{10,... | collective-permute-start | bytes 663560 | tf_op jit(solution)/shard_map/ppermute | solution.py:89
  186.2 25.2 %all-to-all-start.4 = ((f32[32,1,1728]{2,1,0:T(1,128)}), f32[32,1,1728]{2,1,0:T(1,128)S(1)}, u32[]{:S(2)}, u32[]{:S(2)}) async-start(f32[32,1,1728]{2,1,0:T(1,128)} %reshape.299), calls=%async_computation.4 | async-start | bytes 458752 | tf_op jit(solution)/shard_map/all_to_all | solution.py:105
  (4 other events, 6.6 us)

commit v4 on v2

--- a/solution.py
+++ b/solution.py
@@ -26,39 +26,46 @@
     return (mixed[..., :width], mixed[..., width : 2 * width], mixed[..., 2 * width :])
 
 
-def attend_back(query_rows, key_rows, value_rows, grad_rows, groups):
-    shape = query_rows.shape
-    split = shape[:-1] + (shape[-1] // HD, HD)
-    query_five = query_rows.reshape(split)
-    key_five = key_rows.reshape(split)
-    value_five = value_rows.reshape(split)
-    grad_five = grad_rows.reshape(split)
+def attend_back(query, key, value, grads, groups):
+    batch, rows, features = query.shape
+    heads = features // HD
+    own = (
+        lax.broadcasted_iota(jnp.int32, (heads, features), 1) // HD
+        == lax.broadcasted_iota(jnp.int32, (heads, features), 0)
+    )
+
+    def by_head(x):
+        return jnp.where(own[None, :, None, :], x[:, None], jnp.zeros((), x.dtype))
+
+    query_heads = by_head(query)
+    key_heads = by_head(key)
+    grad_heads = by_head(grads)
     scores = (
-        jnp.einsum("bichd,bjchd->bchij", query_five, key_five, preferred_element_type=jnp.float32)
+        jnp.einsum("bhid,bjd->bhij", query_heads, key, preferred_element_type=jnp.float32)
         * SCALE
     )
-    header = lax.broadcasted_iota(jnp.int32, (shape[1], shape[1]), 1) == 0
-    visible = (groups[:, :, :, None] == groups[:, :, None, :]) | header
-    scores = jnp.where(visible[:, :, None], scores, -1e30)
+    header = lax.broadcasted_iota(jnp.int32, (rows, rows), 1) == 0
+    visible = (groups[:, :, None] == groups[:, None, :]) | header
+    scores = jnp.where(visible[:, None], scores, -1e30)
     peak = jnp.max(scores, axis=-1, keepdims=True)
     expsc = jnp.exp(scores - peak)
     probs = expsc / jnp.sum(expsc, axis=-1, keepdims=True)
     probs_low = probs.astype(jnp.bfloat16)
     value_grad = jnp.einsum(
-        "bchij,bichd->bjchd", probs_low, grad_five, preferred_element_type=jnp.float32
+        "bhij,bhid->bjd", probs_low, grad_heads, preferred_element_type=jnp.float32
     ).astype(jnp.bfloat16)
     prob_grad = jnp.einsum(
-        "bichd,bjchd->bchij", grad_five, value_five, preferred_element_type=jnp.float32
+        "bhid,bjd->bhij", grad_heads, value, preferred_element_type=jnp.float32
     )
     score_grad = probs * (prob_grad - jnp.sum(probs * prob_grad, axis=-1, keepdims=True))
     score_low = (score_grad * SCALE).astype(jnp.bfloat16)
     query_grad = jnp.einsum(
-        "bchij,bjchd->bichd", score_low, key_five, preferred_element_type=jnp.float32
+        "bhij,bhjd->bid", score_low, key_heads, preferred_element_type=jnp.float32
     ).astype(jnp.bfloat16)
     key_grad = jnp.einsum(
-        "bchij,bichd->bjchd", score_low, query_five, preferred_element_type=jnp.float32
+        "bhij,bhid->bjd", score_low, query_heads, preferred_element_type=jnp.float32
     ).astype(jnp.bfloat16)
-    return (query_grad.reshape(shape), key_grad.reshape(shape), value_grad.reshape(shape))
+    return (query_grad, key_grad, value_grad)
 
 
 def finish(scaled, inverse, normed, all_grads, weights):
@@ -107,19 +114,22 @@
 
 
 def body(cell_states, head_grads, group_ids, proj_weights):
-    tables, rows_here, cols, width = cell_states.shape
-    heads_width = head_grads.shape[-1]
+    width = cell_states.shape[-1]
     both = jnp.concatenate((cell_states, head_grads), axis=-1)
     both_cols = lax.all_to_all(both, "band", split_axis=2, concat_axis=1, tiled=True)
+    tables, rows, cols, features = both_cols.shape
+    both_cols = both_cols.transpose(0, 2, 1, 3).reshape(tables * cols, rows, features)
+    groups = group_ids.reshape(tables * cols, rows)
     states_cols = both_cols[..., :width]
     grad_cols = both_cols[..., width:]
     scaled, inverse, normed = normalize(states_cols)
     query_cols, key_cols, value_cols = project(normed, proj_weights)
     query_grad, key_grad, value_grad = attend_back(
-        query_cols, key_cols, value_cols, grad_cols, group_ids
+        query_cols, key_cols, value_cols, grad_cols, groups
     )
     all_grads = jnp.concatenate((query_grad, key_grad, value_grad), axis=-1)
     partial_w, input_cols = finish(scaled, inverse, normed, all_grads, proj_weights)
+    input_cols = input_cols.reshape(tables, cols, rows, width).transpose(0, 2, 1, 3)
     input_grad = lax.all_to_all(input_cols, "band", split_axis=1, concat_axis=2, tiled=True)
     weight_grad = reduce_weight_grad(partial_w)
     return (input_grad, weight_grad)

time: 200 us -> 178 us (0.89)
  the two profiles are of different devices: /device:TPU:1 before, /device:TPU:2 now
where the time goes in v4:
time: 178 us; the launch traced here: 177 us
  waiting for transfers between devices  65.1 us (37%)
  starting transfers between devices  51.6 us (29%)
  matrix products  26.4 us (15%)
  local copies, waits for them, and re-layouts  22.6 us (13%)
  other arithmetic  10.3 us (6%)
    ppermute x5, waiting for transfers between devices, exchange(): total = total + lax.ppermute(part, 'band', pairs)  28.4 us
    all_to_all x1, waiting for transfers between devices, body(): lax.all_to_all(both, 'band', split_axis=2, concat_axis=1, tiled=True)  24.8 us
    all_to_all x1, starting transfers between devices, reduce_weight_grad(): blocks = lax.all_to_all(blocks, 'dp', 0, 0, tiled=True)  20.4 us
    all_to_all x1, starting transfers between devices, body(): lax.all_to_all(both, 'band', split_axis=2, concat_axis=1, tiled=True)  13.4 us
    all_to_all x1, waiting for transfers between devices, reduce_weight_grad(): blocks = lax.all_to_all(blocks, 'dp', 0, 0, tiled=True)  11.9 us
    ppermute x5, starting transfers between devices, exchange(): total = total + lax.ppermute(part, 'band', pairs)  11.8 us
    all_to_all x1, starting transfers between devices, body(): lax.all_to_all(input_cols, 'band', split_axis=1, concat_axis=2, tiled=True)  5.98 us
    sub x1, matrix products, attend_back(): expsc = jnp.exp(scores - peak)  4.88 us
  transfers between devices with their start and end apart: 8, of which 5 were waited for; matrix products, arithmetic and copies ran while one was open for 7% of the time, Pallas kernels for 0%

profile of v4, /device:TPU:2, one launch (start us, length us, event | category | flops | bytes accessed | tf_op | source)
XLA Modules:
  0.0 177.0 jit_solution(346414766773094631)
XLA Ops:
  2.1 2.2 %copy.24 = bf16[2,2,128,1152]{3,1,0,2:T(2,128)(2,1)} copy(bf16[2,2,128,1152]{3,2,1,0:T(8,128)(2,1)S(1)} %pad_maximum_fusion) | data formatting | bytes 2359296 | tf_op jit(solution)/shard_map/concatenate | solution.py:118
  4.4 13.4 %all-to-all-start = ((bf16[2,2,128,1152]{3,1,0,2:T(2,128)(2,1)}), bf16[2,2,128,1152]{3,1,0,2:T(2,128)(2,1)S(1)}, u32[]{:S(2)}, u32[]{:S(2)}) async-start(bf16[2,2,128,1152]{3,1,0,2:T(2,128)(2,1)} %copy.24), calls=%async_computation | async-start | bytes 2359296 | tf_op jit(solution)/shard_map/all_to_all | solution.py:119
  18.0 24.8 %all-to-all-done = bf16[2,2,128,1152]{3,1,0,2:T(2,128)(2,1)S(1)} async-done(((bf16[2,2,128,1152]{3,1,0,2:T(2,128)(2,1)}), bf16[2,2,128,1152]{3,1,0,2:T(2,128)(2,1)S(1)}, u32[]{:S(2)}, u32[]{:S(2)}) %all-to-all-start) | async-done | bytes 1179680 | tf_op jit(solution)/shard_map/all_to_all | solution.py:119
  44.6 2.9 %all_to_all.32 = bf16[2,32,8,1152]{3,1,2,0:T(8,128)(2,1)S(1)} reshape(bf16[2,16,2,8,1152]{4,2,1,3,0:T(2,128)(2,1)} %copy.25) | data formatting | bytes 2359296 | tf_op jit(solution)/shard_map/all_to_all | solution.py:119
  48.9 2.3 %copy.29 = bf16[768,512]{1,0:T(8,128)(2,1)} copy(bf16[768,512]{0,1:T(8,128)(2,1)} %bitcast.97) | data formatting | bytes 1572864 | tf_op jit(solution)/shard_map/dot_general | solution.py:74
  51.2 2.3 %convolution_convert_fusion = bf16[512,1152]{1,0:T(8,128)(2,1)S(1)} fusion(bf16[512,768]{1,0:T(8,128)(2,1)} %bitcast.98, bf16[768,1152]{1,0:T(8,128)(2,1)S(1)} %copy-done), kind=kOutput, calls=%fused_computation.10 | convolution fusion | flops 906559488 | bytes 3735552 | tf_op jit(solution)/shard_map/dot_general | solution.py:24
  54.6 3.7 %fusion.4 = f32[16,6,32,32]{2,3,1,0:T(8,128)} fusion(pred[6,384]{1,0:T(8,128)(4,1)S(1)} %iota_compare_fusion, bf16[16,32,384]{2,1,0:T(8,128)(2,1)S(1)} %slice.23, bf16[16,32,1152]{2,1,0:T(8,128)(2,1)S(1)} %bitcast.105), kind=kOutput, calls=%fused_computation.4 | convolution fusion | flops 76677120 | bytes 1182720 | tf_op jit(solution)/shard_map/bhid,bjd->bhij/dot_general | solution.py:57
  58.3 4.9 %fusion.86 = (f32[16,6,32]{2,1,0:T(8,128)S(1)}, f32[16,6,32,32]{2,3,1,0:T(8,128)}) fusion(pred[6,384]{1,0:T(8,128)(4,1)S(1)} %iota_compare_fusion, bf16[16,32,384]{2,1,0:T(8,128)(2,1)} %get-tuple-element.10, pred[16,32,32]{1,2,0:T(8,128)(4,1)S(1)} %compare_or_fusion, bf16[16,32,1152]{2,1,0:T(8,128)(2,1)} %bitcast.106), kind=kOutput, calls=%fused_computation.95 | convolution fusion | flops 77070368 | bytes 1210624 | tf_op jit(solution)/shard_map/sub | solution.py:51
  63.2 2.3 %fusion.46 = bf16[16,32,384]{2,1,0:T(8,128)(2,1)S(1)} fusion(pred[6,384]{1,0:T(8,128)(4,1)S(1)} %iota_compare_fusion, bf16[16,32,384]{2,1,0:T(8,128)(2,1)} %copy-done.6, f32[16,6,32,32]{2,3,1,0:T(8,128)} %get-tuple-element.12, f32[16,6,32]{2,1,0:T(8,128)S(1)} %get-tuple-element.11), kind=kOutput, calls=%fused_computation.42 | convolution fusion | flops 77070336 | bytes 1194240 | tf_op jit(solution)/shard_map/bhij,bhid->bjd/dot_general | solution.py:54
  65.5 4.8 %fusion.49 = bf16[16,32,384]{2,1,0:T(8,128)(2,1)} fusion(pred[6,384]{1,0:T(8,128)(4,1)S(1)} %iota_compare_fusion, bf16[16,32,384]{2,1,0:T(8,128)(2,1)} %get-tuple-element.10, f32[16,6,32,32]{2,3,1,0:T(8,128)} %fusion.4, f32[16,6,32,32]{2,3,1,0:T(8,128)} %get-tuple-element.12, f32[16,6,32]{2,1,0:T(8,128)S(1)} %get-tuple-element.11), kind=kOutput, calls=%fused_computation.43 | convolution fusion | flops 77564960 | bytes 1587456 | tf_op jit(solution)/shard_map/bhij,bhid->bjd/dot_general | solution.py:65
  70.3 4.7 %fusion.43 = bf16[16,32,384]{2,1,0:T(8,128)(2,1)} fusion(pred[6,384]{1,0:T(8,128)(4,1)S(1)} %iota_compare_fusion, bf16[16,32,384]{2,1,0:T(8,128)(2,1)} %get-tuple-element.9, f32[16,6,32,32]{2,3,1,0:T(8,128)} %fusion.4, f32[16,6,32,32]{2,3,1,0:T(8,128)} %get-tuple-element.12, f32[16,6,32]{2,1,0:T(8,128)S(1)} %get-tuple-element.11), kind=kOutput, calls=%fused_computation.41 | convolution fusion | flops 77564960 | bytes 1587456 | tf_op jit(solution)/shard_map/bhij,bhjd->bid/dot_general | solution.py:62
  79.9 1.9 %collective-permute-start = (f32[4,2,48,1152]{3,2,1,0:T(8,128)}, f32[4,2,48,1152]{3,2,1,0:T(8,128)}, u32[]{:S(2)}, u32[]{:S(2)}) collective-permute-start(f32[4,2,48,1152]{3,2,1,0:T(8,128)} %dynamic-slice_bitcast_fusion), channel_id=1, source_target_pairs={{0,1},{1,0},{2,3},{3,2},{4,5},{5,4},{6,7},{7,6},{8,9},{9,8},{10,11... | collective-permute-start | bytes 5308424 | tf_op jit(solution)/shard_map/ppermute | solution.py:96
  81.9 2.6 %fusion.23 = (f32[16,32]{1,0:T(8,128)S(1)}, f32[16,32,768]{2,1,0:T(8,128)S(1)}) fusion(f32[16,32]{1,0:T(8,128)S(1)} %add_rsqrt_fusion, bf16[16,32,1152]{2,1,0:T(8,128)(2,1)S(1)} %bitcast.92, bf16[768,1152]{1,0:T(8,128)(2,1)S(1)} %copy-done, bf16[16,32,384]{2,1,0:T(8,128)(2,1)S(1)} %fusion.46, bf16[16,32,384]{2,1,0:T(8,128)(2,1)} %fusion.49, ...), kind=kOutput, calls=%fused_computation.28 | convolution fusion | flops 911080960 | bytes 5312512 | tf_op jit(solution)/shard_map/dot_general | solution.py:77
  88.7 1.9 %collective-permute-start.1 = (f32[2,48,1152]{2,1,0:T(8,128)}, f32[2,48,1152]{2,1,0:T(8,128)S(1)}, u32[]{:S(2)}, u32[]{:S(2)}) collective-permute-start(f32[2,48,1152]{2,1,0:T(8,128)} %get-tuple-element.6), channel_id=1, source_target_pairs={{0,4},{1,5},{2,6},{3,7},{4,8},{5,9},{6,10},{7,11},{8,12},{9,13},{1... | collective-permute-start | bytes 1327112 | tf_op jit(solution)/shard_map/ppermute | solution.py:96
  90.6 3.9 %collective-permute-start.3 = (f32[2,48,1152]{2,1,0:T(8,128)}, f32[2,48,1152]{2,1,0:T(8,128)}, u32[]{:S(2)}, u32[]{:S(2)}) collective-permute-start(f32[2,48,1152]{2,1,0:T(8,128)} %get-tuple-element.7), channel_id=1, source_target_pairs={{0,12},{1,13},{2,14},{3,15},{4,0},{5,1},{6,2},{7,3},{8,4},{9,5},{1... | collective-permute-start | bytes 1327112 | tf_op jit(solution)/shard_map/ppermute | solution.py:96
  94.6 2.1 %collective-permute-start.2 = (f32[2,48,1152]{2,1,0:T(8,128)}, f32[2,48,1152]{2,1,0:T(8,128)}, u32[]{:S(2)}, u32[]{:S(2)}) collective-permute-start(f32[2,48,1152]{2,1,0:T(8,128)} %get-tuple-element.8), channel_id=1, source_target_pairs={{0,8},{1,9},{2,10},{3,11},{4,12},{5,13},{6,14},{7,15},{8,0},{9,1},... | collective-permute-start | bytes 1327112 | tf_op jit(solution)/shard_map/ppermute | solution.py:96
  98.4 6.0 %all-to-all-start.1 = ((bf16[2,32,8,768]{3,2,0,1:T(8,128)(2,1)}), bf16[2,32,8,768]{3,2,0,1:T(8,128)(2,1)S(1)}, u32[]{:S(2)}, u32[]{:S(2)}) async-start(bf16[2,32,8,768]{3,2,0,1:T(8,128)(2,1)} %bitcast.88), calls=%async_computation.1 | async-start | bytes 1572864 | tf_op jit(solution)/shard_map/all_to_all | solution.py:133
  104.4 17.3 %collective-permute-done.3 = f32[2,48,1152]{2,1,0:T(8,128)} collective-permute-done((f32[2,48,1152]{2,1,0:T(8,128)}, f32[2,48,1152]{2,1,0:T(8,128)}, u32[]{:S(2)}, u32[]{:S(2)}) %collective-permute-start.3) | collective-permute-done | bytes 442400 | tf_op jit(solution)/shard_map/ppermute | solution.py:96
  123.1 1.9 %collective-permute-start.4 = (f32[48,1152]{1,0:T(8,128)S(1)}, f32[48,1152]{1,0:T(8,128)S(1)}, u32[]{:S(2)}, u32[]{:S(2)}) collective-permute-start(f32[48,1152]{1,0:T(8,128)S(1)} %dynamic-slice_bitcast_fusion.4), channel_id=1, source_target_pairs={{0,2},{1,3},{2,0},{3,1},{4,6},{5,7},{6,4},{7,5},{8,10},{9,11},{10,... | collective-permute-start | bytes 663560 | tf_op jit(solution)/shard_map/ppermute | solution.py:96
  125.0 9.8 %collective-permute-done.4 = f32[48,1152]{1,0:T(8,128)S(1)} collective-permute-done((f32[48,1152]{1,0:T(8,128)S(1)}, f32[48,1152]{1,0:T(8,128)S(1)}, u32[]{:S(2)}, u32[]{:S(2)}) %collective-permute-start.4) | collective-permute-done | bytes 221216 | tf_op jit(solution)/shard_map/ppermute | solution.py:96
  135.5 1.9 %reshape.101 = f32[48,32,36]{2,1,0:T(8,128)S(1)} reshape(f32[48,1152]{1,0:T(8,128)} %bitcast_add_fusion.2) | data formatting | bytes 442368 | tf_op jit(solution)/shard_map/reshape | solution.py:111
  138.8 2.3 %reshape.109 = f32[32,1,1728]{2,1,0:T(1,128)} reshape(f32[32,36,48]{2,1,0:T(8,128)} %bitcast.102) | data formatting | bytes 442368
  141.1 20.4 %all-to-all-start.2 = ((f32[32,1,1728]{2,1,0:T(1,128)}), f32[32,1,1728]{2,1,0:T(1,128)S(1)}, u32[]{:S(2)}, u32[]{:S(2)}) async-start(f32[32,1,1728]{2,1,0:T(1,128)} %reshape.109), calls=%async_computation.2 | async-start | bytes 458752 | tf_op jit(solution)/shard_map/all_to_all | solution.py:112
  162.5 11.9 %all-to-all-done.2 = f32[32,1,1728]{2,1,0:T(1,128)S(1)} async-done(((f32[32,1,1728]{2,1,0:T(1,128)}), f32[32,1,1728]{2,1,0:T(1,128)S(1)}, u32[]{:S(2)}, u32[]{:S(2)}) %all-to-all-start.2) | async-done | bytes 221216 | tf_op jit(solution)/shard_map/all_to_all | solution.py:112
  (49 shorter events, 23.7 us)
Async XLA Ops:
  0.6 50.6 %copy-start = (bf16[768,1152]{1,0:T(8,128)(2,1)S(1)}, bf16[768,1152]{1,0:T(8,128)(2,1)}, u32[]{:S(2)}) copy-start(bf16[768,1152]{1,0:T(8,128)(2,1)} %param.7) | copy-start | bytes 5308420
  4.4 13.5 %copy-start.7 = (s32[2,8,32]{2,1,0:T(8,128)S(1)}, s32[2,8,32]{2,1,0:T(8,128)}, u32[]{:S(2)}) copy-start(s32[2,8,32]{2,1,0:T(8,128)} %param.6) | copy-start | bytes 6148
  4.4 38.4 %all-to-all-start = ((bf16[2,2,128,1152]{3,1,0,2:T(2,128)(2,1)}), bf16[2,2,128,1152]{3,1,0,2:T(2,128)(2,1)S(1)}, u32[]{:S(2)}, u32[]{:S(2)}) async-start(bf16[2,2,128,1152]{3,1,0,2:T(2,128)(2,1)} %copy.24), calls=%async_computation | async-start | bytes 2359296 | tf_op jit(solution)/shard_map/all_to_all | solution.py:119
  47.8 6.8 %copy-start.6 = (bf16[16,32,384]{2,1,0:T(8,128)(2,1)}, bf16[16,32,384]{2,1,0:T(8,128)(2,1)S(1)}, u32[]{:S(2)}) copy-start(bf16[16,32,384]{2,1,0:T(8,128)(2,1)S(1)} %slice.23) | copy-start | bytes 1179652
  53.5 4.8 %copy-start.5 = (bf16[512,1152]{1,0:T(8,128)(2,1)}, bf16[512,1152]{1,0:T(8,128)(2,1)S(1)}, u32[]{:S(2)}) copy-start(bf16[512,1152]{1,0:T(8,128)(2,1)S(1)} %convolution_convert_fusion) | copy-start | bytes 3538948
  75.0 1.4 copy-start.4
  77.6 2.3 %copy-start.1 = (f32[4,2,2,48,1152]{4,3,2,1,0:T(8,128)}, f32[4,2,2,48,1152]{4,3,2,1,0:T(8,128)S(1)}, u32[]{:S(2)}) copy-start(f32[4,2,2,48,1152]{4,3,2,1,0:T(8,128)S(1)} %fusion.91) | copy-start | bytes 10616836
  79.9 5.9 %collective-permute-start = (f32[4,2,48,1152]{3,2,1,0:T(8,128)}, f32[4,2,48,1152]{3,2,1,0:T(8,128)}, u32[]{:S(2)}, u32[]{:S(2)}) collective-permute-start(f32[4,2,48,1152]{3,2,1,0:T(8,128)} %dynamic-slice_bitcast_fusion), channel_id=1, source_target_pairs={{0,1},{1,0},{2,3},{3,2},{4,5},{5,4},{6,7},{7,6},{8,9},{9,8},{10,11... | collective-permute-start | bytes 5308424 | tf_op jit(solution)/shard_map/ppermute | solution.py:96
  81.9 3.9 %copy-start.2 = (f32[4,2,2,48,1152]{4,3,2,1,0:T(8,128)S(1)}, f32[4,2,2,48,1152]{4,3,2,1,0:T(8,128)}, u32[]{:S(2)}) copy-start(f32[4,2,2,48,1152]{4,3,2,1,0:T(8,128)} %copy-done.1) | copy-start | bytes 10616836
  87.5 9.5 %copy-start.3 = (f32[4,2,48,1152]{3,2,1,0:T(8,128)}, f32[4,2,48,1152]{3,2,1,0:T(8,128)S(1)}, u32[]{:S(2)}) copy-start(f32[4,2,48,1152]{3,2,1,0:T(8,128)S(1)} %bitcast_add_fusion) | copy-start | bytes 5308420
  88.7 15.6 %collective-permute-start.1 = (f32[2,48,1152]{2,1,0:T(8,128)}, f32[2,48,1152]{2,1,0:T(8,128)S(1)}, u32[]{:S(2)}, u32[]{:S(2)}) collective-permute-start(f32[2,48,1152]{2,1,0:T(8,128)} %get-tuple-element.6), channel_id=1, source_target_pairs={{0,4},{1,5},{2,6},{3,7},{4,8},{5,9},{6,10},{7,11},{8,12},{9,13},{1... | collective-permute-start | bytes 1327112 | tf_op jit(solution)/shard_map/ppermute | solution.py:96
  90.6 31.0 %collective-permute-start.3 = (f32[2,48,1152]{2,1,0:T(8,128)}, f32[2,48,1152]{2,1,0:T(8,128)}, u32[]{:S(2)}, u32[]{:S(2)}) collective-permute-start(f32[2,48,1152]{2,1,0:T(8,128)} %get-tuple-element.7), channel_id=1, source_target_pairs={{0,12},{1,13},{2,14},{3,15},{4,0},{5,1},{6,2},{7,3},{8,4},{9,5},{1... | collective-permute-start | bytes 1327112 | tf_op jit(solution)/shard_map/ppermute | solution.py:96
  94.6 27.1 %collective-permute-start.2 = (f32[2,48,1152]{2,1,0:T(8,128)}, f32[2,48,1152]{2,1,0:T(8,128)}, u32[]{:S(2)}, u32[]{:S(2)}) collective-permute-start(f32[2,48,1152]{2,1,0:T(8,128)} %get-tuple-element.8), channel_id=1, source_target_pairs={{0,8},{1,9},{2,10},{3,11},{4,12},{5,13},{6,14},{7,15},{8,0},{9,1},... | collective-permute-start | bytes 1327112 | tf_op jit(solution)/shard_map/ppermute | solution.py:96
  98.4 42.7 %all-to-all-start.1 = ((bf16[2,32,8,768]{3,2,0,1:T(8,128)(2,1)}), bf16[2,32,8,768]{3,2,0,1:T(8,128)(2,1)S(1)}, u32[]{:S(2)}, u32[]{:S(2)}) async-start(bf16[2,32,8,768]{3,2,0,1:T(8,128)(2,1)} %bitcast.88), calls=%async_computation.1 | async-start | bytes 1572864 | tf_op jit(solution)/shard_map/all_to_all | solution.py:133
  123.1 11.7 %collective-permute-start.4 = (f32[48,1152]{1,0:T(8,128)S(1)}, f32[48,1152]{1,0:T(8,128)S(1)}, u32[]{:S(2)}, u32[]{:S(2)}) collective-permute-start(f32[48,1152]{1,0:T(8,128)S(1)} %dynamic-slice_bitcast_fusion.4), channel_id=1, source_target_pairs={{0,2},{1,3},{2,0},{3,1},{4,6},{5,7},{6,4},{7,5},{8,10},{9,11},{10,... | collective-permute-start | bytes 663560 | tf_op jit(solution)/shard_map/ppermute | solution.py:96
  141.1 33.3 %all-to-all-start.2 = ((f32[32,1,1728]{2,1,0:T(1,128)}), f32[32,1,1728]{2,1,0:T(1,128)S(1)}, u32[]{:S(2)}, u32[]{:S(2)}) async-start(f32[32,1,1728]{2,1,0:T(1,128)} %reshape.109), calls=%async_computation.2 | async-start | bytes 458752 | tf_op jit(solution)/shard_map/all_to_all | solution.py:112

commit v5 on v4

--- a/solution.py
+++ b/solution.py
@@ -115,13 +115,13 @@
 
 def body(cell_states, head_grads, group_ids, proj_weights):
     width = cell_states.shape[-1]
-    both = jnp.concatenate((cell_states, head_grads), axis=-1)
-    both_cols = lax.all_to_all(both, "band", split_axis=2, concat_axis=1, tiled=True)
-    tables, rows, cols, features = both_cols.shape
-    both_cols = both_cols.transpose(0, 2, 1, 3).reshape(tables * cols, rows, features)
+    states_cols = lax.all_to_all(cell_states, "band", split_axis=2, concat_axis=1, tiled=True)
+    tables, rows, cols, _ = states_cols.shape
+    states_cols = states_cols.transpose(0, 2, 1, 3).reshape(tables * cols, rows, width)
+    states_cols, head_grads = lax.optimization_barrier((states_cols, head_grads))
+    grad_cols = lax.all_to_all(head_grads, "band", split_axis=2, concat_axis=1, tiled=True)
+    grad_cols = grad_cols.transpose(0, 2, 1, 3).reshape(tables * cols, rows, -1)
     groups = group_ids.reshape(tables * cols, rows)
-    states_cols = both_cols[..., :width]
-    grad_cols = both_cols[..., width:]
     scaled, inverse, normed = normalize(states_cols)
     query_cols, key_cols, value_cols = project(normed, proj_weights)
     query_grad, key_grad, value_grad = attend_back(

time: 178 us -> 172 us (0.966)
  the two profiles are of different devices: /device:TPU:2 before, /device:TPU:1 now
where the time goes in v5:
time: 172 us; the launch traced here: 170 us
  starting transfers between devices  62.2 us (36%)
  waiting for transfers between devices  52.2 us (30%)
  matrix products  24 us (14%)
  local copies, waits for them, and re-layouts  23.3 us (14%)
  other arithmetic  7.69 us (4%)
    ppermute x5, waiting for transfers between devices, exchange(): total = total + lax.ppermute(part, 'band', pairs)  22.1 us
    ppermute x5, starting transfers between devices, exchange(): total = total + lax.ppermute(part, 'band', pairs)  20.2 us
    all_to_all x1, waiting for transfers between devices, body(): lax.all_to_all(cell_states, 'band', split_axis=2, concat_axis=1, tiled=True)  16.8 us
    all_to_all x1, starting transfers between devices, body(): lax.all_to_all(cell_states, 'band', split_axis=2, concat_axis=1, tiled=True)  14.3 us
    all_to_all x1, starting transfers between devices, reduce_weight_grad(): blocks = lax.all_to_all(blocks, 'dp', 0, 0, tiled=True)  12.5 us
    all_to_all x1, waiting for transfers between devices, reduce_weight_grad(): blocks = lax.all_to_all(blocks, 'dp', 0, 0, tiled=True)  10.2 us
    all_to_all x1, starting transfers between devices, body(): lax.all_to_all(head_grads, 'band', split_axis=2, concat_axis=1, tiled=True)  9.74 us
    unnamed x23, local copies, waits for them, and re-layouts  8.22 us
  transfers between devices with their start and end apart: 9, of which 7 were waited for; matrix products, arithmetic and copies ran while one was open for 12% of the time, Pallas kernels for 0%

profile of v5, /device:TPU:1, one launch (start us, length us, event | category | flops | bytes accessed | tf_op | source)
XLA Modules:
  0.0 170.4 jit_solution(684765450812399524)
XLA Ops:
  0.7 3.0 %copy.20 = bf16[2,2,128,768]{3,1,0,2:T(2,128)(2,1)} copy(bf16[2,2,128,768]{3,2,1,0:T(8,128)(2,1)} %param.4) | data formatting | bytes 1572864 | tf_op args[0]
  3.6 14.3 %all-to-all-start = ((bf16[2,2,128,768]{3,1,0,2:T(2,128)(2,1)}), bf16[2,2,128,768]{3,1,0,2:T(2,128)(2,1)S(1)}, u32[]{:S(2)}, u32[]{:S(2)}) async-start(bf16[2,2,128,768]{3,1,0,2:T(2,128)(2,1)} %copy.20), calls=%async_computation | async-start | bytes 1572864 | tf_op jit(solution)/shard_map/all_to_all | solution.py:118
  18.1 16.8 %all-to-all-done = bf16[2,2,128,768]{3,1,0,2:T(2,128)(2,1)S(1)} async-done(((bf16[2,2,128,768]{3,1,0,2:T(2,128)(2,1)}), bf16[2,2,128,768]{3,1,0,2:T(2,128)(2,1)S(1)}, u32[]{:S(2)}, u32[]{:S(2)}) %all-to-all-start) | async-done | bytes 786464 | tf_op jit(solution)/shard_map/all_to_all | solution.py:118
  36.1 2.2 %copy.22 = bf16[2,2,128,384]{3,1,0,2:T(2,128)(2,1)} copy(bf16[2,2,128,384]{3,2,1,0:T(8,128)(2,1)} %param.5) | data formatting | bytes 786432 | tf_op jit(solution)/shard_map/optimization_barrier | solution.py:121
  38.3 9.7 %all-to-all-start.1 = ((bf16[2,2,128,384]{3,1,0,2:T(2,128)(2,1)}), bf16[2,2,128,384]{3,1,0,2:T(2,128)(2,1)}, u32[]{:S(2)}, u32[]{:S(2)}) async-start(bf16[2,2,128,384]{3,1,0,2:T(2,128)(2,1)} %copy.22), calls=%async_computation.1 | async-start | bytes 786432 | tf_op jit(solution)/shard_map/all_to_all | solution.py:122
  52.5 4.9 %fusion.86 = (f32[16,6,32]{2,1,0:T(8,128)S(1)}, f32[16,6,32,32]{2,3,1,0:T(8,128)}) fusion(pred[6,384]{1,0:T(8,128)(4,1)S(1)} %iota_compare_fusion, bf16[16,32,384]{2,1,0:T(8,128)(2,1)S(1)} %get-tuple-element.12, pred[16,32,32]{1,2,0:T(8,128)(4,1)S(1)} %compare_or_fusion, bf16[16,32,1152]{2,1,0:T(8,128)(2,1)} %bitcast.115), kind=kOutput, calls=%fused_computation.95 | convolution fusion | flops 77070368 | bytes 1210624 | tf_op jit(solution)/shard_map/sub | solution.py:51
  57.4 3.1 %all-to-all-done.1 = bf16[2,2,128,384]{3,1,0,2:T(2,128)(2,1)} async-done(((bf16[2,2,128,384]{3,1,0,2:T(2,128)(2,1)}), bf16[2,2,128,384]{3,1,0,2:T(2,128)(2,1)}, u32[]{:S(2)}, u32[]{:S(2)}) %all-to-all-start.1) | async-done | bytes 393248 | tf_op jit(solution)/shard_map/all_to_all | solution.py:122
  61.7 4.8 %fusion.4 = f32[16,6,32,32]{2,3,1,0:T(8,128)} fusion(pred[6,384]{1,0:T(8,128)(4,1)S(1)} %iota_compare_fusion, bf16[16,32,384]{2,1,0:T(8,128)(2,1)S(1)} %bitcast.117, bf16[16,32,1152]{2,1,0:T(8,128)(2,1)} %bitcast.116), kind=kOutput, calls=%fused_computation.4 | convolution fusion | flops 76677120 | bytes 1181952 | tf_op jit(solution)/shard_map/bhid,bjd->bhij/dot_general | solution.py:57
  67.3 3.9 %fusion.49 = bf16[16,32,384]{2,1,0:T(8,128)(2,1)S(1)} fusion(pred[6,384]{1,0:T(8,128)(4,1)S(1)} %iota_compare_fusion, bf16[16,32,384]{2,1,0:T(8,128)(2,1)} %copy-done.7, f32[16,6,32,32]{2,3,1,0:T(8,128)} %fusion.4, f32[16,6,32,32]{2,3,1,0:T(8,128)} %get-tuple-element.14, f32[16,6,32]{2,1,0:T(8,128)S(1)} %get-tuple-element.13), kind=kOutput, calls=%fused_computation.43 | convolution fusion | flops 77564960 | bytes 1587456 | tf_op jit(solution)/shard_map/bhij,bhid->bjd/dot_general | solution.py:65
  71.2 4.7 %fusion.43 = bf16[16,32,384]{2,1,0:T(8,128)(2,1)} fusion(pred[6,384]{1,0:T(8,128)(4,1)S(1)} %iota_compare_fusion, bf16[16,32,384]{2,1,0:T(8,128)(2,1)} %get-tuple-element.11, f32[16,6,32,32]{2,3,1,0:T(8,128)} %fusion.4, f32[16,6,32,32]{2,3,1,0:T(8,128)} %get-tuple-element.14, f32[16,6,32]{2,1,0:T(8,128)S(1)} %get-tuple-element.13), kind=kOutput, calls=%fused_computation.41 | convolution fusion | flops 77564960 | bytes 1587456 | tf_op jit(solution)/shard_map/bhij,bhjd->bid/dot_general | solution.py:62
  80.6 3.3 %collective-permute-start = (f32[4,2,48,1152]{3,2,1,0:T(8,128)}, f32[4,2,48,1152]{3,2,1,0:T(8,128)}, u32[]{:S(2)}, u32[]{:S(2)}) collective-permute-start(f32[4,2,48,1152]{3,2,1,0:T(8,128)} %dynamic-slice_bitcast_fusion), channel_id=1, source_target_pairs={{0,1},{1,0},{2,3},{3,2},{4,5},{5,4},{6,7},{7,6},{8,9},{9,8},{10,11... | collective-permute-start | bytes 5308424 | tf_op jit(solution)/shard_map/ppermute | solution.py:96
  84.1 2.4 %fusion.23 = (f32[16,32]{1,0:T(8,128)S(1)}, f32[16,32,768]{2,1,0:T(8,128)S(1)}) fusion(bf16[16,32,768]{2,1,0:T(8,128)(2,1)S(1)} %bitcast.100, f32[16,32]{1,0:T(8,128)S(1)} %add_rsqrt_fusion, bf16[768,1152]{1,0:T(8,128)(2,1)S(1)} %copy-done, bf16[16,32,384]{2,1,0:T(8,128)(2,1)S(1)} %fusion.46, bf16[16,32,384]{2,1,0:T(8,128)(2,1)S(1)} %fusion.49, ...), kind=kOutput, calls=%fused_computation.28 | convolution fusion | flops 911080960 | bytes 5312512 | tf_op jit(solution)/shard_map/dot_general | solution.py:77
  87.4 1.7 bitcast_add_fusion
  90.3 2.5 %collective-permute-start.3 = (f32[2,48,1152]{2,1,0:T(8,128)}, f32[2,48,1152]{2,1,0:T(8,128)S(1)}, u32[]{:S(2)}, u32[]{:S(2)}) collective-permute-start(f32[2,48,1152]{2,1,0:T(8,128)} %get-tuple-element.9), channel_id=1, source_target_pairs={{0,12},{1,13},{2,14},{3,15},{4,0},{5,1},{6,2},{7,3},{8,4},{9,5},{1... | collective-permute-start | bytes 1327112 | tf_op jit(solution)/shard_map/ppermute | solution.py:96
  92.7 6.3 %collective-permute-start.2 = (f32[2,48,1152]{2,1,0:T(8,128)}, f32[2,48,1152]{2,1,0:T(8,128)S(1)}, u32[]{:S(2)}, u32[]{:S(2)}) collective-permute-start(f32[2,48,1152]{2,1,0:T(8,128)} %get-tuple-element.10), channel_id=1, source_target_pairs={{0,8},{1,9},{2,10},{3,11},{4,12},{5,13},{6,14},{7,15},{8,0},{9,1},... | collective-permute-start | bytes 1327112 | tf_op jit(solution)/shard_map/ppermute | solution.py:96
  99.1 1.9 %collective-permute-start.1 = (f32[2,48,1152]{2,1,0:T(8,128)}, f32[2,48,1152]{2,1,0:T(8,128)}, u32[]{:S(2)}, u32[]{:S(2)}) collective-permute-start(f32[2,48,1152]{2,1,0:T(8,128)} %get-tuple-element.8), channel_id=1, source_target_pairs={{0,4},{1,5},{2,6},{3,7},{4,8},{5,9},{6,10},{7,11},{8,12},{9,13},{1... | collective-permute-start | bytes 1327112 | tf_op jit(solution)/shard_map/ppermute | solution.py:96
  102.7 5.5 %all-to-all-start.2 = ((bf16[2,32,8,768]{3,2,0,1:T(8,128)(2,1)}), bf16[2,32,8,768]{3,2,0,1:T(8,128)(2,1)S(1)}, u32[]{:S(2)}, u32[]{:S(2)}) async-start(bf16[2,32,8,768]{3,2,0,1:T(8,128)(2,1)} %bitcast.96), calls=%async_computation.2 | async-start | bytes 1572864 | tf_op jit(solution)/shard_map/all_to_all | solution.py:133
  110.0 11.3 %collective-permute-done.1 = f32[2,48,1152]{2,1,0:T(8,128)} collective-permute-done((f32[2,48,1152]{2,1,0:T(8,128)}, f32[2,48,1152]{2,1,0:T(8,128)}, u32[]{:S(2)}, u32[]{:S(2)}) %collective-permute-start.1) | collective-permute-done | bytes 442400 | tf_op jit(solution)/shard_map/ppermute | solution.py:96
  122.6 6.1 %collective-permute-start.4 = (f32[48,1152]{1,0:T(8,128)S(1)}, f32[48,1152]{1,0:T(8,128)S(1)}, u32[]{:S(2)}, u32[]{:S(2)}) collective-permute-start(f32[48,1152]{1,0:T(8,128)S(1)} %dynamic-slice_bitcast_fusion.4), channel_id=1, source_target_pairs={{0,2},{1,3},{2,0},{3,1},{4,6},{5,7},{6,4},{7,5},{8,10},{9,11},{10,... | collective-permute-start | bytes 663560 | tf_op jit(solution)/shard_map/ppermute | solution.py:96
  128.8 9.0 %collective-permute-done.4 = f32[48,1152]{1,0:T(8,128)S(1)} collective-permute-done((f32[48,1152]{1,0:T(8,128)S(1)}, f32[48,1152]{1,0:T(8,128)S(1)}, u32[]{:S(2)}, u32[]{:S(2)}) %collective-permute-start.4) | collective-permute-done | bytes 221216 | tf_op jit(solution)/shard_map/ppermute | solution.py:96
  138.5 1.9 %reshape.101 = f32[48,32,36]{2,1,0:T(8,128)S(1)} reshape(f32[48,1152]{1,0:T(8,128)} %bitcast_add_fusion.2) | data formatting | bytes 442368 | tf_op jit(solution)/shard_map/reshape | solution.py:111
  141.8 2.3 %reshape.109 = f32[32,1,1728]{2,1,0:T(1,128)} reshape(f32[32,36,48]{2,1,0:T(8,128)} %bitcast.110) | data formatting | bytes 442368
  144.1 12.5 %all-to-all-start.3 = ((f32[32,1,1728]{2,1,0:T(1,128)}), f32[32,1,1728]{2,1,0:T(1,128)S(1)}, u32[]{:S(2)}, u32[]{:S(2)}) async-start(f32[32,1,1728]{2,1,0:T(1,128)} %reshape.109), calls=%async_computation.3 | async-start | bytes 458752 | tf_op jit(solution)/shard_map/all_to_all | solution.py:112
  157.5 10.2 %all-to-all-done.3 = f32[32,1,1728]{2,1,0:T(1,128)S(1)} async-done(((f32[32,1,1728]{2,1,0:T(1,128)}), f32[32,1,1728]{2,1,0:T(1,128)S(1)}, u32[]{:S(2)}, u32[]{:S(2)}) %all-to-all-start.3) | async-done | bytes 221216 | tf_op jit(solution)/shard_map/all_to_all | solution.py:112
  (57 shorter events, 25.0 us)
Async XLA Ops:
  0.6 48.8 %copy-start = (bf16[768,1152]{1,0:T(8,128)(2,1)S(1)}, bf16[768,1152]{1,0:T(8,128)(2,1)}, u32[]{:S(2)}) copy-start(bf16[768,1152]{1,0:T(8,128)(2,1)} %param.7) | copy-start | bytes 5308420
  0.6 17.3 %copy-start.8 = (s32[2,8,32]{2,1,0:T(8,128)S(1)}, s32[2,8,32]{2,1,0:T(8,128)}, u32[]{:S(2)}) copy-start(s32[2,8,32]{2,1,0:T(8,128)} %param.6) | copy-start | bytes 6148
  3.6 31.3 %all-to-all-start = ((bf16[2,2,128,768]{3,1,0,2:T(2,128)(2,1)}), bf16[2,2,128,768]{3,1,0,2:T(2,128)(2,1)S(1)}, u32[]{:S(2)}, u32[]{:S(2)}) async-start(bf16[2,2,128,768]{3,1,0,2:T(2,128)(2,1)} %copy.20), calls=%async_computation | async-start | bytes 1572864 | tf_op jit(solution)/shard_map/all_to_all | solution.py:118
  38.3 22.2 %all-to-all-start.1 = ((bf16[2,2,128,384]{3,1,0,2:T(2,128)(2,1)}), bf16[2,2,128,384]{3,1,0,2:T(2,128)(2,1)}, u32[]{:S(2)}, u32[]{:S(2)}) async-start(bf16[2,2,128,384]{3,1,0,2:T(2,128)(2,1)} %copy.22), calls=%async_computation.1 | async-start | bytes 786432 | tf_op jit(solution)/shard_map/all_to_all | solution.py:122
  50.6 1.0 copy-start.5
  52.5 4.9 %copy-start.7 = (bf16[16,32,384]{2,1,0:T(8,128)(2,1)}, bf16[16,32,384]{2,1,0:T(8,128)(2,1)S(1)}, u32[]{:S(2)}) copy-start(bf16[16,32,384]{2,1,0:T(8,128)(2,1)S(1)} %get-tuple-element.12) | copy-start | bytes 1179652
  61.7 4.8 %copy-start.9 = (f32[16,6,32,32]{2,3,1,0:T(8,128)S(1)}, f32[16,6,32,32]{2,3,1,0:T(8,128)}, u32[]{:S(2)}) copy-start(f32[16,6,32,32]{2,3,1,0:T(8,128)} %get-tuple-element.14) | copy-start | bytes 1179652
  75.9 1.3 copy-start.4
  78.3 2.3 %copy-start.1 = (f32[4,2,2,48,1152]{4,3,2,1,0:T(8,128)}, f32[4,2,2,48,1152]{4,3,2,1,0:T(8,128)S(1)}, u32[]{:S(2)}) copy-start(f32[4,2,2,48,1152]{4,3,2,1,0:T(8,128)S(1)} %fusion.91) | copy-start | bytes 10616836
  80.6 6.8 %collective-permute-start = (f32[4,2,48,1152]{3,2,1,0:T(8,128)}, f32[4,2,48,1152]{3,2,1,0:T(8,128)}, u32[]{:S(2)}, u32[]{:S(2)}) collective-permute-start(f32[4,2,48,1152]{3,2,1,0:T(8,128)} %dynamic-slice_bitcast_fusion), channel_id=1, source_target_pairs={{0,1},{1,0},{2,3},{3,2},{4,5},{5,4},{6,7},{7,6},{8,9},{9,8},{10,11... | collective-permute-start | bytes 5308424 | tf_op jit(solution)/shard_map/ppermute | solution.py:96
  84.0 3.4 %copy-start.2 = (f32[4,2,2,48,1152]{4,3,2,1,0:T(8,128)S(1)}, f32[4,2,2,48,1152]{4,3,2,1,0:T(8,128)}, u32[]{:S(2)}) copy-start(f32[4,2,2,48,1152]{4,3,2,1,0:T(8,128)} %copy-done.1) | copy-start | bytes 10616836
  89.1 12.3 %copy-start.3 = (f32[4,2,48,1152]{3,2,1,0:T(8,128)}, f32[4,2,48,1152]{3,2,1,0:T(8,128)S(1)}, u32[]{:S(2)}) copy-start(f32[4,2,48,1152]{3,2,1,0:T(8,128)S(1)} %bitcast_add_fusion) | copy-start | bytes 5308420
  90.3 18.0 %collective-permute-start.3 = (f32[2,48,1152]{2,1,0:T(8,128)}, f32[2,48,1152]{2,1,0:T(8,128)S(1)}, u32[]{:S(2)}, u32[]{:S(2)}) collective-permute-start(f32[2,48,1152]{2,1,0:T(8,128)} %get-tuple-element.9), channel_id=1, source_target_pairs={{0,12},{1,13},{2,14},{3,15},{4,0},{5,1},{6,2},{7,3},{8,4},{9,5},{1... | collective-permute-start | bytes 1327112 | tf_op jit(solution)/shard_map/ppermute | solution.py:96
  92.7 16.4 %collective-permute-start.2 = (f32[2,48,1152]{2,1,0:T(8,128)}, f32[2,48,1152]{2,1,0:T(8,128)S(1)}, u32[]{:S(2)}, u32[]{:S(2)}) collective-permute-start(f32[2,48,1152]{2,1,0:T(8,128)} %get-tuple-element.10), channel_id=1, source_target_pairs={{0,8},{1,9},{2,10},{3,11},{4,12},{5,13},{6,14},{7,15},{8,0},{9,1},... | collective-permute-start | bytes 1327112 | tf_op jit(solution)/shard_map/ppermute | solution.py:96
  99.1 22.1 %collective-permute-start.1 = (f32[2,48,1152]{2,1,0:T(8,128)}, f32[2,48,1152]{2,1,0:T(8,128)}, u32[]{:S(2)}, u32[]{:S(2)}) collective-permute-start(f32[2,48,1152]{2,1,0:T(8,128)} %get-tuple-element.8), channel_id=1, source_target_pairs={{0,4},{1,5},{2,6},{3,7},{4,8},{5,9},{6,10},{7,11},{8,12},{9,13},{1... | collective-permute-start | bytes 1327112 | tf_op jit(solution)/shard_map/ppermute | solution.py:96
  102.7 41.4 %all-to-all-start.2 = ((bf16[2,32,8,768]{3,2,0,1:T(8,128)(2,1)}), bf16[2,32,8,768]{3,2,0,1:T(8,128)(2,1)S(1)}, u32[]{:S(2)}, u32[]{:S(2)}) async-start(bf16[2,32,8,768]{3,2,0,1:T(8,128)(2,1)} %bitcast.96), calls=%async_computation.2 | async-start | bytes 1572864 | tf_op jit(solution)/shard_map/all_to_all | solution.py:133
  109.2 0.8 copy-start.6
  122.6 15.2 %collective-permute-start.4 = (f32[48,1152]{1,0:T(8,128)S(1)}, f32[48,1152]{1,0:T(8,128)S(1)}, u32[]{:S(2)}, u32[]{:S(2)}) collective-permute-start(f32[48,1152]{1,0:T(8,128)S(1)} %dynamic-slice_bitcast_fusion.4), channel_id=1, source_target_pairs={{0,2},{1,3},{2,0},{3,1},{4,6},{5,7},{6,4},{7,5},{8,10},{9,11},{10,... | collective-permute-start | bytes 663560 | tf_op jit(solution)/shard_map/ppermute | solution.py:96
  144.1 23.7 %all-to-all-start.3 = ((f32[32,1,1728]{2,1,0:T(1,128)}), f32[32,1,1728]{2,1,0:T(1,128)S(1)}, u32[]{:S(2)}, u32[]{:S(2)}) async-start(f32[32,1,1728]{2,1,0:T(1,128)} %reshape.109), calls=%async_computation.3 | async-start | bytes 458752 | tf_op jit(solution)/shard_map/all_to_all | solution.py:112

commit v6 on v5

--- a/solution.py
+++ b/solution.py
@@ -93,7 +93,8 @@
         for source in range(n_band):
             d = (source // stride) % n
             pairs.append((source, source + (((d + shift) % n) - d) * stride))
-        total = total + lax.ppermute(part, "band", pairs)
+        got = lax.ppermute(part.astype(jnp.bfloat16), "band", pairs)
+        total = total + got.astype(jnp.float32)
     return total
 
 
@@ -109,8 +110,8 @@
     blocks = exchange(blocks, 0, band, (band // 2) % 2, 2, 2)
     cols = d_out // n_dp
     blocks = blocks.reshape(rows, n_dp, cols).transpose(1, 0, 2)
-    blocks = lax.all_to_all(blocks, "dp", 0, 0, tiled=True)
-    return blocks.sum(axis=0)
+    blocks = lax.all_to_all(blocks.astype(jnp.bfloat16), "dp", 0, 0, tiled=True)
+    return blocks.astype(jnp.float32).sum(axis=0)
 
 
 def body(cell_states, head_grads, group_ids, proj_weights):

time: 172 us -> 173 us (level)
  waiting for transfers between devices: 52.2 us -> 59.4 us
  local copies, waits for them, and re-layouts: 23.3 us -> 18.6 us
    all_to_all x1, waiting for transfers between devices: 0.01 us -> 20.1 us  [body(): lax.all_to_all(input_cols, 'band', split_axis=1, concat_axis=2, tiled=True)]
    ppermute x5, waiting for transfers between devices: 22.1 us -> 12.7 us  [exchange(): got = lax.ppermute(part.astype(jnp.bfloat16), 'band', pairs)]
    ppermute x5, starting transfers between devices: 20.2 us -> 16.5 us  [exchange(): got = lax.ppermute(part.astype(jnp.bfloat16), 'band', pairs)]
    all_to_all x1, waiting for transfers between devices: 10.2 us -> 6.75 us  [reduce_weight_grad(): blocks = lax.all_to_all(blocks.astype(jnp.bfloat16), 'dp', 0, 0, tiled=True)]
    all_to_all x1, starting transfers between devices: 5.52 us -> 8.86 us  [body(): lax.all_to_all(input_cols, 'band', split_axis=1, concat_axis=2, tiled=True)]
    convert_element_type x0 -> x5, local copies, waits for them, and re-layouts: none -> 2.72 us  [the longest x2 1.61 us: reduce_weight_grad(): blocks = lax.all_to_all(blocks.astype(jnp.bfloat16), 'dp', 0, 0, tiled=True)]
    squeeze x3 -> x0, local copies, waits for them, and re-layouts: 2.7 us -> none  [exchange(): lax.dynamic_index_in_dim(blocks, (digit + shift) % n, axis=dim, keepdims=...]
    add x3 -> x2, other arithmetic: 3.71 us -> 1.73 us  [exchange(): total = total + got.astype(jnp.float32)]
  transfers between devices with their start and end apart: 9 -> 9, of which waited for: 7 -> 8; matrix products, arithmetic and copies ran while one was open for 12% -> 9% of each run, Pallas kernels for 0% -> 0%
where the time goes in v6:
time: 173 us; the launch traced here: 171 us
  starting transfers between devices  61.7 us (36%)
  waiting for transfers between devices  59.4 us (34%)
  matrix products  24 us (14%)
  local copies, waits for them, and re-layouts  18.6 us (11%)
  other arithmetic  5.97 us (3%)
    all_to_all x1, waiting for transfers between devices, body(): lax.all_to_all(input_cols, 'band', split_axis=1, concat_axis=2, tiled=True)  20.1 us
    all_to_all x1, waiting for transfers between devices, body(): lax.all_to_all(cell_states, 'band', split_axis=2, concat_axis=1, tiled=True)  16.8 us
    ppermute x5, starting transfers between devices, exchange(): got = lax.ppermute(part.astype(jnp.bfloat16), 'band', pairs)  16.5 us
    all_to_all x1, starting transfers between devices, body(): lax.all_to_all(cell_states, 'band', split_axis=2, concat_axis=1, tiled=True)  14.3 us
    ppermute x5, waiting for transfers between devices, exchange(): got = lax.ppermute(part.astype(jnp.bfloat16), 'band', pairs)  12.7 us
    all_to_all x1, starting transfers between devices, reduce_weight_grad(): blocks = lax.all_to_all(blocks.astype(jnp.bfloat16), 'dp', 0, 0, tiled=True)  12.3 us
    all_to_all x1, starting transfers between devices, body(): lax.all_to_all(head_grads, 'band', split_axis=2, concat_axis=1, tiled=True)  9.74 us
    all_to_all x1, starting transfers between devices, body(): lax.all_to_all(input_cols, 'band', split_axis=1, concat_axis=2, tiled=True)  8.86 us
  transfers between devices with their start and end apart: 9, of which 8 were waited for; matrix products, arithmetic and copies ran while one was open for 9% of the time, Pallas kernels for 0%

profile of v6, /device:TPU:1, one launch (start us, length us, event | category | flops | bytes accessed | tf_op | source)
XLA Modules:
  0.0 170.7 jit_solution(13392154812574480499)
XLA Ops:
  0.7 3.0 %copy.33 = bf16[2,2,128,768]{3,1,0,2:T(2,128)(2,1)} copy(bf16[2,2,128,768]{3,2,1,0:T(8,128)(2,1)} %param.4) | data formatting | bytes 1572864 | tf_op args[0]
  3.6 14.3 %all-to-all-start = ((bf16[2,2,128,768]{3,1,0,2:T(2,128)(2,1)}), bf16[2,2,128,768]{3,1,0,2:T(2,128)(2,1)S(1)}, u32[]{:S(2)}, u32[]{:S(2)}) async-start(bf16[2,2,128,768]{3,1,0,2:T(2,128)(2,1)} %copy.33), calls=%async_computation | async-start | bytes 1572864 | tf_op jit(solution)/shard_map/all_to_all | solution.py:119
  18.1 16.8 %all-to-all-done = bf16[2,2,128,768]{3,1,0,2:T(2,128)(2,1)S(1)} async-done(((bf16[2,2,128,768]{3,1,0,2:T(2,128)(2,1)}), bf16[2,2,128,768]{3,1,0,2:T(2,128)(2,1)S(1)}, u32[]{:S(2)}, u32[]{:S(2)}) %all-to-all-start) | async-done | bytes 786464 | tf_op jit(solution)/shard_map/all_to_all | solution.py:119
  36.1 2.1 %copy.35 = bf16[2,2,128,384]{3,1,0,2:T(2,128)(2,1)} copy(bf16[2,2,128,384]{3,2,1,0:T(8,128)(2,1)} %param.5) | data formatting | bytes 786432 | tf_op jit(solution)/shard_map/optimization_barrier | solution.py:122
  38.3 9.7 %all-to-all-start.1 = ((bf16[2,2,128,384]{3,1,0,2:T(2,128)(2,1)}), bf16[2,2,128,384]{3,1,0,2:T(2,128)(2,1)}, u32[]{:S(2)}, u32[]{:S(2)}) async-start(bf16[2,2,128,384]{3,1,0,2:T(2,128)(2,1)} %copy.35), calls=%async_computation.1 | async-start | bytes 786432 | tf_op jit(solution)/shard_map/all_to_all | solution.py:123
  52.5 4.9 %fusion.92 = (f32[16,6,32]{2,1,0:T(8,128)S(1)}, f32[16,6,32,32]{2,3,1,0:T(8,128)}) fusion(pred[6,384]{1,0:T(8,128)(4,1)S(1)} %iota_compare_fusion, bf16[16,32,384]{2,1,0:T(8,128)(2,1)S(1)} %get-tuple-element.14, pred[16,32,32]{1,2,0:T(8,128)(4,1)S(1)} %compare_or_fusion, bf16[16,32,1152]{2,1,0:T(8,128)(2,1)} %bitcast.117), kind=kOutput, calls=%fused_computation.102 | convolution fusion | flops 77070368 | bytes 1210624 | tf_op jit(solution)/shard_map/sub | solution.py:51
  57.4 3.1 %all-to-all-done.1 = bf16[2,2,128,384]{3,1,0,2:T(2,128)(2,1)} async-done(((bf16[2,2,128,384]{3,1,0,2:T(2,128)(2,1)}), bf16[2,2,128,384]{3,1,0,2:T(2,128)(2,1)}, u32[]{:S(2)}, u32[]{:S(2)}) %all-to-all-start.1) | async-done | bytes 393248 | tf_op jit(solution)/shard_map/all_to_all | solution.py:123
  61.6 4.8 %fusion.4 = f32[16,6,32,32]{2,3,1,0:T(8,128)} fusion(pred[6,384]{1,0:T(8,128)(4,1)S(1)} %iota_compare_fusion, bf16[16,32,384]{2,1,0:T(8,128)(2,1)S(1)} %bitcast.119, bf16[16,32,1152]{2,1,0:T(8,128)(2,1)} %bitcast.118), kind=kOutput, calls=%fused_computation.4 | convolution fusion | flops 76677120 | bytes 1181952 | tf_op jit(solution)/shard_map/bhid,bjd->bhij/dot_general | solution.py:57
  67.2 4.0 %fusion.49 = bf16[16,32,384]{2,1,0:T(8,128)(2,1)S(1)} fusion(pred[6,384]{1,0:T(8,128)(4,1)S(1)} %iota_compare_fusion, bf16[16,32,384]{2,1,0:T(8,128)(2,1)} %copy-done.9, f32[16,6,32,32]{2,3,1,0:T(8,128)} %fusion.4, f32[16,6,32,32]{2,3,1,0:T(8,128)} %get-tuple-element.16, f32[16,6,32]{2,1,0:T(8,128)S(1)} %get-tuple-element.15), kind=kOutput, calls=%fused_computation.43 | convolution fusion | flops 77564960 | bytes 1587456 | tf_op jit(solution)/shard_map/bhij,bhid->bjd/dot_general | solution.py:65
  71.3 4.7 %fusion.43 = bf16[16,32,384]{2,1,0:T(8,128)(2,1)} fusion(pred[6,384]{1,0:T(8,128)(4,1)S(1)} %iota_compare_fusion, bf16[16,32,384]{2,1,0:T(8,128)(2,1)} %get-tuple-element.13, f32[16,6,32,32]{2,3,1,0:T(8,128)} %fusion.4, f32[16,6,32,32]{2,3,1,0:T(8,128)} %get-tuple-element.16, f32[16,6,32]{2,1,0:T(8,128)S(1)} %get-tuple-element.15), kind=kOutput, calls=%fused_computation.41 | convolution fusion | flops 77564960 | bytes 1587456 | tf_op jit(solution)/shard_map/bhij,bhjd->bid/dot_general | solution.py:62
  81.2 3.1 %collective-permute-start = (bf16[4,2,48,1152]{3,2,1,0:T(8,128)(2,1)}, bf16[4,2,48,1152]{3,2,1,0:T(8,128)(2,1)S(1)}, u32[]{:S(2)}, u32[]{:S(2)}) collective-permute-start(bf16[4,2,48,1152]{3,2,1,0:T(8,128)(2,1)} %fusion.66), channel_id=1, source_target_pairs={{0,1},{1,0},{2,3},{3,2},{4,5},{5,4},{6,7},{7,6},{8,9},{9,8},{10,11... | collective-permute-start | bytes 2654216 | tf_op jit(solution)/shard_map/ppermute | solution.py:96
  84.5 2.1 %collective-permute-done = bf16[4,2,48,1152]{3,2,1,0:T(8,128)(2,1)S(1)} collective-permute-done((bf16[4,2,48,1152]{3,2,1,0:T(8,128)(2,1)}, bf16[4,2,48,1152]{3,2,1,0:T(8,128)(2,1)S(1)}, u32[]{:S(2)}, u32[]{:S(2)}) %collective-permute-start) | collective-permute-done | bytes 884768 | tf_op jit(solution)/shard_map/ppermute | solution.py:96
  88.3 5.3 %collective-permute-start.1 = (bf16[2,48,1152]{2,1,0:T(8,128)(2,1)S(1)}, bf16[2,48,1152]{2,1,0:T(8,128)(2,1)S(1)}, u32[]{:S(2)}, u32[]{:S(2)}) collective-permute-start(bf16[2,48,1152]{2,1,0:T(8,128)(2,1)S(1)} %get-tuple-element.10), channel_id=1, source_target_pairs={{0,4},{1,5},{2,6},{3,7},{4,8},{5,9},{6,10},{7,11},{8,12},{9,13},{1... | collective-permute-start | bytes 663560 | tf_op jit(solution)/shard_map/ppermute | solution.py:96
  93.6 1.9 %collective-permute-start.3 = (bf16[2,48,1152]{2,1,0:T(8,128)(2,1)S(1)}, bf16[2,48,1152]{2,1,0:T(8,128)(2,1)S(1)}, u32[]{:S(2)}, u32[]{:S(2)}) collective-permute-start(bf16[2,48,1152]{2,1,0:T(8,128)(2,1)S(1)} %get-tuple-element.11), channel_id=1, source_target_pairs={{0,12},{1,13},{2,14},{3,15},{4,0},{5,1},{6,2},{7,3},{8,4},{9,5},{1... | collective-permute-start | bytes 663560 | tf_op jit(solution)/shard_map/ppermute | solution.py:96
  95.5 3.7 %collective-permute-start.2 = (bf16[2,48,1152]{2,1,0:T(8,128)(2,1)S(1)}, bf16[2,48,1152]{2,1,0:T(8,128)(2,1)S(1)}, u32[]{:S(2)}, u32[]{:S(2)}) collective-permute-start(bf16[2,48,1152]{2,1,0:T(8,128)(2,1)S(1)} %get-tuple-element.12), channel_id=1, source_target_pairs={{0,8},{1,9},{2,10},{3,11},{4,12},{5,13},{6,14},{7,15},{8,0},{9,1},... | collective-permute-start | bytes 663560 | tf_op jit(solution)/shard_map/ppermute | solution.py:96
  99.3 2.4 %fusion.23 = (f32[16,32]{1,0:T(8,128)S(1)}, f32[16,32,768]{2,1,0:T(8,128)}) fusion(bf16[16,32,768]{2,1,0:T(8,128)(2,1)S(1)} %bitcast.101, f32[16,32]{1,0:T(8,128)S(1)} %add_rsqrt_fusion, bf16[768,1152]{1,0:T(8,128)(2,1)S(1)} %copy-done, bf16[16,32,384]{2,1,0:T(8,128)(2,1)S(1)} %copy-done.5, bf16[16,32,384]{2,1,0:T(8,128)(2,1)S(1)} %copy-done.7, ...), kind=kOutput, calls=%fused_computation.28 | convolution fusion | flops 911080960 | bytes 5312512 | tf_op jit(solution)/shard_map/dot_general | solution.py:77
  101.8 3.4 %collective-permute-done.2 = bf16[2,48,1152]{2,1,0:T(8,128)(2,1)S(1)} collective-permute-done((bf16[2,48,1152]{2,1,0:T(8,128)(2,1)S(1)}, bf16[2,48,1152]{2,1,0:T(8,128)(2,1)S(1)}, u32[]{:S(2)}, u32[]{:S(2)}) %collective-permute-start.2) | collective-permute-done | bytes 221216 | tf_op jit(solution)/shard_map/ppermute | solution.py:96
  105.4 2.4 %collective-permute-start.4 = (bf16[48,1152]{1,0:T(8,128)(2,1)S(1)}, bf16[48,1152]{1,0:T(8,128)(2,1)S(1)}, u32[]{:S(2)}, u32[]{:S(2)}) collective-permute-start(bf16[48,1152]{1,0:T(8,128)(2,1)S(1)} %fusion.77), channel_id=1, source_target_pairs={{0,2},{1,3},{2,0},{3,1},{4,6},{5,7},{6,4},{7,5},{8,10},{9,11},{10,... | collective-permute-start | bytes 331784 | tf_op jit(solution)/shard_map/ppermute | solution.py:96
  107.8 7.0 %collective-permute-done.4 = bf16[48,1152]{1,0:T(8,128)(2,1)S(1)} collective-permute-done((bf16[48,1152]{1,0:T(8,128)(2,1)S(1)}, bf16[48,1152]{1,0:T(8,128)(2,1)S(1)}, u32[]{:S(2)}, u32[]{:S(2)}) %collective-permute-start.4) | collective-permute-done | bytes 110624 | tf_op jit(solution)/shard_map/ppermute | solution.py:96
  117.5 12.3 %all-to-all-start.3 = ((bf16[32,2,864]{2,1,0:T(2,128)(2,1)}), bf16[32,2,864]{2,1,0:T(2,128)(2,1)S(1)}, u32[]{:S(2)}, u32[]{:S(2)}) async-start(bf16[32,2,864]{2,1,0:T(2,128)(2,1)} %reshape.112), calls=%async_computation.3 | async-start | bytes 229376 | tf_op jit(solution)/shard_map/all_to_all | solution.py:113
  129.9 1.8 %fusion.26 = bf16[16,32,768]{2,1,0:T(8,128)(2,1)S(1)} fusion(f32[16,32,768]{2,1,0:T(8,128)} %get-tuple-element.18, bf16[16,32,768]{2,1,0:T(8,128)(2,1)S(1)} %bitcast.102, f32[16,32]{1,0:T(8,128)S(1)} %broadcast_multiply_fusion, f32[16,32]{1,0:T(8,128)S(1)} %add_rsqrt_fusion), kind=kLoop, calls=%fused_computation.31 | loop fusion | flops 2359296 | bytes 3149824 | tf_op jit(solution)/shard_map/convert_element_type | solution.py:82
  132.9 6.8 %all-to-all-done.3 = bf16[32,2,864]{2,1,0:T(2,128)(2,1)S(1)} async-done(((bf16[32,2,864]{2,1,0:T(2,128)(2,1)}), bf16[32,2,864]{2,1,0:T(2,128)(2,1)S(1)}, u32[]{:S(2)}, u32[]{:S(2)}) %all-to-all-start.3) | async-done | bytes 110624 | tf_op jit(solution)/shard_map/all_to_all | solution.py:113
  139.7 8.9 %all-to-all-start.2 = ((bf16[2,32,8,768]{3,2,0,1:T(8,128)(2,1)}), bf16[2,32,8,768]{3,2,0,1:T(8,128)(2,1)S(1)}, u32[]{:S(2)}, u32[]{:S(2)}) async-start(bf16[2,32,8,768]{3,2,0,1:T(8,128)(2,1)} %bitcast.97), calls=%async_computation.2 | async-start | bytes 1572864 | tf_op jit(solution)/shard_map/all_to_all | solution.py:134
  149.7 20.1 %all-to-all-done.2 = bf16[2,32,8,768]{3,2,0,1:T(8,128)(2,1)S(1)} async-done(((bf16[2,32,8,768]{3,2,0,1:T(8,128)(2,1)}), bf16[2,32,8,768]{3,2,0,1:T(8,128)(2,1)S(1)}, u32[]{:S(2)}, u32[]{:S(2)}) %all-to-all-start.2) | async-done | bytes 786464 | tf_op jit(solution)/shard_map/all_to_all | solution.py:134
  (59 shorter events, 21.1 us)
Async XLA Ops:
  0.6 48.8 %copy-start = (bf16[768,1152]{1,0:T(8,128)(2,1)S(1)}, bf16[768,1152]{1,0:T(8,128)(2,1)}, u32[]{:S(2)}) copy-start(bf16[768,1152]{1,0:T(8,128)(2,1)} %param.7) | copy-start | bytes 5308420
  0.6 17.3 %copy-start.10 = (s32[2,8,32]{2,1,0:T(8,128)S(1)}, s32[2,8,32]{2,1,0:T(8,128)}, u32[]{:S(2)}) copy-start(s32[2,8,32]{2,1,0:T(8,128)} %param.6) | copy-start | bytes 6148
  3.6 31.3 %all-to-all-start = ((bf16[2,2,128,768]{3,1,0,2:T(2,128)(2,1)}), bf16[2,2,128,768]{3,1,0,2:T(2,128)(2,1)S(1)}, u32[]{:S(2)}, u32[]{:S(2)}) async-start(bf16[2,2,128,768]{3,1,0,2:T(2,128)(2,1)} %copy.33), calls=%async_computation | async-start | bytes 1572864 | tf_op jit(solution)/shard_map/all_to_all | solution.py:119
  38.3 22.2 %all-to-all-start.1 = ((bf16[2,2,128,384]{3,1,0,2:T(2,128)(2,1)}), bf16[2,2,128,384]{3,1,0,2:T(2,128)(2,1)}, u32[]{:S(2)}, u32[]{:S(2)}) async-start(bf16[2,2,128,384]{3,1,0,2:T(2,128)(2,1)} %copy.35), calls=%async_computation.1 | async-start | bytes 786432 | tf_op jit(solution)/shard_map/all_to_all | solution.py:123
  50.6 1.0 copy-start.3
  52.5 4.9 %copy-start.9 = (bf16[16,32,384]{2,1,0:T(8,128)(2,1)}, bf16[16,32,384]{2,1,0:T(8,128)(2,1)S(1)}, u32[]{:S(2)}) copy-start(bf16[16,32,384]{2,1,0:T(8,128)(2,1)S(1)} %get-tuple-element.14) | copy-start | bytes 1179652
  61.6 4.8 %copy-start.11 = (f32[16,6,32,32]{2,3,1,0:T(8,128)S(1)}, f32[16,6,32,32]{2,3,1,0:T(8,128)}, u32[]{:S(2)}) copy-start(f32[16,6,32,32]{2,3,1,0:T(8,128)} %get-tuple-element.16) | copy-start | bytes 1179652
  67.2 8.8 %copy-start.4 = (bf16[16,32,384]{2,1,0:T(8,128)(2,1)}, bf16[16,32,384]{2,1,0:T(8,128)(2,1)S(1)}, u32[]{:S(2)}) copy-start(bf16[16,32,384]{2,1,0:T(8,128)(2,1)S(1)} %fusion.46) | copy-start | bytes 1179652
  71.2 4.8 %copy-start.6 = (bf16[16,32,384]{2,1,0:T(8,128)(2,1)}, bf16[16,32,384]{2,1,0:T(8,128)(2,1)S(1)}, u32[]{:S(2)}) copy-start(bf16[16,32,384]{2,1,0:T(8,128)(2,1)S(1)} %fusion.49) | copy-start | bytes 1179652
  76.0 1.3 copy-start.2
  78.4 1.8 %copy-start.1 = (f32[4,2,2,48,1152]{4,3,2,1,0:T(8,128)}, f32[4,2,2,48,1152]{4,3,2,1,0:T(8,128)S(1)}, u32[]{:S(2)}) copy-start(f32[4,2,2,48,1152]{4,3,2,1,0:T(8,128)S(1)} %fusion.97) | copy-start | bytes 10616836
  81.2 5.4 %collective-permute-start = (bf16[4,2,48,1152]{3,2,1,0:T(8,128)(2,1)}, bf16[4,2,48,1152]{3,2,1,0:T(8,128)(2,1)S(1)}, u32[]{:S(2)}, u32[]{:S(2)}) collective-permute-start(bf16[4,2,48,1152]{3,2,1,0:T(8,128)(2,1)} %fusion.66), channel_id=1, source_target_pairs={{0,1},{1,0},{2,3},{3,2},{4,5},{5,4},{6,7},{7,6},{8,9},{9,8},{10,11... | collective-permute-start | bytes 2654216 | tf_op jit(solution)/shard_map/ppermute | solution.py:96
  84.4 14.8 %copy-start.5 = (bf16[16,32,384]{2,1,0:T(8,128)(2,1)S(1)}, bf16[16,32,384]{2,1,0:T(8,128)(2,1)}, u32[]{:S(2)}) copy-start(bf16[16,32,384]{2,1,0:T(8,128)(2,1)} %copy-done.4) | copy-start | bytes 1179652
  84.4 14.8 %copy-start.7 = (bf16[16,32,384]{2,1,0:T(8,128)(2,1)S(1)}, bf16[16,32,384]{2,1,0:T(8,128)(2,1)}, u32[]{:S(2)}) copy-start(bf16[16,32,384]{2,1,0:T(8,128)(2,1)} %copy-done.6) | copy-start | bytes 1179652
  84.5 14.8 %copy-start.8 = (bf16[16,32,384]{2,1,0:T(8,128)(2,1)S(1)}, bf16[16,32,384]{2,1,0:T(8,128)(2,1)}, u32[]{:S(2)}) copy-start(bf16[16,32,384]{2,1,0:T(8,128)(2,1)} %fusion.43) | copy-start | bytes 1179652
  88.3 13.4 %collective-permute-start.1 = (bf16[2,48,1152]{2,1,0:T(8,128)(2,1)S(1)}, bf16[2,48,1152]{2,1,0:T(8,128)(2,1)S(1)}, u32[]{:S(2)}, u32[]{:S(2)}) collective-permute-start(bf16[2,48,1152]{2,1,0:T(8,128)(2,1)S(1)} %get-tuple-element.10), channel_id=1, source_target_pairs={{0,4},{1,5},{2,6},{3,7},{4,8},{5,9},{6,10},{7,11},{8,12},{9,13},{1... | collective-permute-start | bytes 663560 | tf_op jit(solution)/shard_map/ppermute | solution.py:96
  93.6 8.2 %collective-permute-start.3 = (bf16[2,48,1152]{2,1,0:T(8,128)(2,1)S(1)}, bf16[2,48,1152]{2,1,0:T(8,128)(2,1)S(1)}, u32[]{:S(2)}, u32[]{:S(2)}) collective-permute-start(bf16[2,48,1152]{2,1,0:T(8,128)(2,1)S(1)} %get-tuple-element.11), channel_id=1, source_target_pairs={{0,12},{1,13},{2,14},{3,15},{4,0},{5,1},{6,2},{7,3},{8,4},{9,5},{1... | collective-permute-start | bytes 663560 | tf_op jit(solution)/shard_map/ppermute | solution.py:96
  95.5 9.7 %collective-permute-start.2 = (bf16[2,48,1152]{2,1,0:T(8,128)(2,1)S(1)}, bf16[2,48,1152]{2,1,0:T(8,128)(2,1)S(1)}, u32[]{:S(2)}, u32[]{:S(2)}) collective-permute-start(bf16[2,48,1152]{2,1,0:T(8,128)(2,1)S(1)} %get-tuple-element.12), channel_id=1, source_target_pairs={{0,8},{1,9},{2,10},{3,11},{4,12},{5,13},{6,14},{7,15},{8,0},{9,1},... | collective-permute-start | bytes 663560 | tf_op jit(solution)/shard_map/ppermute | solution.py:96
  105.4 9.4 %collective-permute-start.4 = (bf16[48,1152]{1,0:T(8,128)(2,1)S(1)}, bf16[48,1152]{1,0:T(8,128)(2,1)S(1)}, u32[]{:S(2)}, u32[]{:S(2)}) collective-permute-start(bf16[48,1152]{1,0:T(8,128)(2,1)S(1)} %fusion.77), channel_id=1, source_target_pairs={{0,2},{1,3},{2,0},{3,1},{4,6},{5,7},{6,4},{7,5},{8,10},{9,11},{10,... | collective-permute-start | bytes 331784 | tf_op jit(solution)/shard_map/ppermute | solution.py:96
  117.5 22.2 %all-to-all-start.3 = ((bf16[32,2,864]{2,1,0:T(2,128)(2,1)}), bf16[32,2,864]{2,1,0:T(2,128)(2,1)S(1)}, u32[]{:S(2)}, u32[]{:S(2)}) async-start(bf16[32,2,864]{2,1,0:T(2,128)(2,1)} %reshape.112), calls=%async_computation.3 | async-start | bytes 229376 | tf_op jit(solution)/shard_map/all_to_all | solution.py:113
  139.7 30.1 %all-to-all-start.2 = ((bf16[2,32,8,768]{3,2,0,1:T(8,128)(2,1)}), bf16[2,32,8,768]{3,2,0,1:T(8,128)(2,1)S(1)}, u32[]{:S(2)}, u32[]{:S(2)}) async-start(bf16[2,32,8,768]{3,2,0,1:T(8,128)(2,1)} %bitcast.97), calls=%async_computation.2 | async-start | bytes 1572864 | tf_op jit(solution)/shard_map/all_to_all | solution.py:134

commit v7 on v5

--- a/solution.py
+++ b/solution.py
@@ -83,7 +83,7 @@
     return (partial_w, state_grad)
 
 
-def exchange(blocks, dim, band, digit, stride, n):
+def exchange(blocks, dim, digit, stride, n, wire=jnp.float32):
     mine = lax.dynamic_index_in_dim(blocks, digit, axis=dim, keepdims=False)
     total = mine.astype(jnp.float32)
     n_band = lax.axis_size("band")
@@ -93,20 +93,25 @@
         for source in range(n_band):
             d = (source // stride) % n
             pairs.append((source, source + (((d + shift) % n) - d) * stride))
-        total = total + lax.ppermute(part, "band", pairs)
+        got = lax.ppermute(part.astype(wire), "band", pairs)
+        total = total + got.astype(jnp.float32)
     return total
 
 
-def reduce_weight_grad(partial_w):
+def band_stages(partial_w):
     n_band = lax.axis_size("band")
-    n_dp = lax.axis_size("dp")
     d_in, d_out = partial_w.shape
     rows = d_in // n_band
     band = lax.axis_index("band")
     blocks = partial_w.reshape(n_band // 4, 2, 2, rows, d_out)
-    blocks = exchange(blocks, 2, band, band % 2, 1, 2)
-    blocks = exchange(blocks, 0, band, band // 4, 4, n_band // 4)
-    blocks = exchange(blocks, 0, band, (band // 2) % 2, 2, 2)
+    blocks = exchange(blocks, 2, band % 2, 1, 2)
+    blocks = exchange(blocks, 0, band // 4, 4, n_band // 4, jnp.bfloat16)
+    return exchange(blocks, 0, (band // 2) % 2, 2, 2)
+
+
+def dp_stage(blocks):
+    n_dp = lax.axis_size("dp")
+    rows, d_out = blocks.shape
     cols = d_out // n_dp
     blocks = blocks.reshape(rows, n_dp, cols).transpose(1, 0, 2)
     blocks = lax.all_to_all(blocks, "dp", 0, 0, tiled=True)
@@ -130,8 +135,11 @@
     all_grads = jnp.concatenate((query_grad, key_grad, value_grad), axis=-1)
     partial_w, input_cols = finish(scaled, inverse, normed, all_grads, proj_weights)
     input_cols = input_cols.reshape(tables, cols, rows, width).transpose(0, 2, 1, 3)
+    input_cols, partial_w = lax.optimization_barrier((input_cols, partial_w))
     input_grad = lax.all_to_all(input_cols, "band", split_axis=1, concat_axis=2, tiled=True)
-    weight_grad = reduce_weight_grad(partial_w)
+    reduced = band_stages(partial_w)
+    reduced, input_grad = lax.optimization_barrier((reduced, input_grad))
+    weight_grad = dp_stage(reduced)
     return (input_grad, weight_grad)
 
 

time: 172 us -> 161 us (0.936)
  blocking collectives: 0 us -> 25.4 us
  waiting for transfers between devices: 52.2 us -> 37.6 us
  starting transfers between devices: 62.2 us -> 47.7 us
  local copies, waits for them, and re-layouts: 23.3 us -> 16.5 us
    all_to_all x0 -> x1, blocking collectives: none -> 25.4 us  [dp_stage(): blocks = lax.all_to_all(blocks, 'dp', 0, 0, tiled=True)]
    all_to_all x1 -> x0, starting transfers between devices: 12.5 us -> none  [reduce_weight_grad(): blocks = lax.all_to_all(blocks, 'dp', 0, 0, tiled=True)]
    all_to_all x1 -> x0, waiting for transfers between devices: 10.2 us -> none  [reduce_weight_grad(): blocks = lax.all_to_all(blocks, 'dp', 0, 0, tiled=True)]
    ppermute x5, waiting for transfers between devices: 22.1 us -> 16.6 us  [exchange(): got = lax.ppermute(part.astype(wire), 'band', pairs)]
    unnamed x23 -> x29, local copies, waits for them, and re-layouts: 8.22 us -> 5.58 us
    squeeze x3 -> x2, local copies, waits for them, and re-layouts: 2.7 us -> 0.13 us  [exchange(): lax.dynamic_index_in_dim(blocks, (digit + shift) % n, axis=dim, keepdims=...]
  transfers between devices with their start and end apart: 9 -> 8, of which waited for: 7 -> 6; matrix products, arithmetic and copies ran while one was open for 12% -> 9% of each run, Pallas kernels for 0% -> 0%
where the time goes in v7:
time: 161 us; the launch traced here: 160 us
  starting transfers between devices  47.7 us (30%)
  waiting for transfers between devices  37.6 us (23%)
  blocking collectives  25.4 us (16%)
  matrix products  25.3 us (16%)
  local copies, waits for them, and re-layouts  16.5 us (10%)
  other arithmetic  6.27 us (4%)
    all_to_all x1, blocking collectives, dp_stage(): blocks = lax.all_to_all(blocks, 'dp', 0, 0, tiled=True)  25.4 us
    ppermute x5, starting transfers between devices, exchange(): got = lax.ppermute(part.astype(wire), 'band', pairs)  18.8 us
    all_to_all x1, waiting for transfers between devices, body(): lax.all_to_all(cell_states, 'band', split_axis=2, concat_axis=1, tiled=True)  16.8 us
    ppermute x5, waiting for transfers between devices, exchange(): got = lax.ppermute(part.astype(wire), 'band', pairs)  16.6 us
    all_to_all x1, starting transfers between devices, body(): lax.all_to_all(cell_states, 'band', split_axis=2, concat_axis=1, tiled=True)  14.3 us
    all_to_all x1, starting transfers between devices, body(): lax.all_to_all(head_grads, 'band', split_axis=2, concat_axis=1, tiled=True)  9.74 us
    unnamed x29, local copies, waits for them, and re-layouts  5.58 us
    all_to_all x1, starting transfers between devices, body(): lax.all_to_all(input_cols, 'band', split_axis=1, concat_axis=2, tiled=True)  4.9 us
  transfers between devices with their start and end apart: 8, of which 6 were waited for; matrix products, arithmetic and copies ran while one was open for 9% of the time, Pallas kernels for 0%

profile of v7, /device:TPU:1, one launch (start us, length us, event | category | flops | bytes accessed | tf_op | source)
XLA Modules:
  0.0 159.9 jit_solution(13897251531697422927)
XLA Ops:
  0.7 3.0 %copy.17 = bf16[2,2,128,768]{3,1,0,2:T(2,128)(2,1)} copy(bf16[2,2,128,768]{3,2,1,0:T(8,128)(2,1)} %param.4) | data formatting | bytes 1572864 | tf_op args[0]
  3.6 14.3 %all-to-all-start = ((bf16[2,2,128,768]{3,1,0,2:T(2,128)(2,1)}), bf16[2,2,128,768]{3,1,0,2:T(2,128)(2,1)S(1)}, u32[]{:S(2)}, u32[]{:S(2)}) async-start(bf16[2,2,128,768]{3,1,0,2:T(2,128)(2,1)} %copy.17), calls=%async_computation | async-start | bytes 1572864 | tf_op jit(solution)/shard_map/all_to_all | solution.py:123
  18.1 16.8 %all-to-all-done = bf16[2,2,128,768]{3,1,0,2:T(2,128)(2,1)S(1)} async-done(((bf16[2,2,128,768]{3,1,0,2:T(2,128)(2,1)}), bf16[2,2,128,768]{3,1,0,2:T(2,128)(2,1)S(1)}, u32[]{:S(2)}, u32[]{:S(2)}) %all-to-all-start) | async-done | bytes 786464 | tf_op jit(solution)/shard_map/all_to_all | solution.py:123
  36.1 2.2 %copy.19 = bf16[2,2,128,384]{3,1,0,2:T(2,128)(2,1)} copy(bf16[2,2,128,384]{3,2,1,0:T(8,128)(2,1)} %param.5) | data formatting | bytes 786432 | tf_op jit(solution)/shard_map/optimization_barrier | solution.py:126
  38.3 9.7 %all-to-all-start.1 = ((bf16[2,2,128,384]{3,1,0,2:T(2,128)(2,1)}), bf16[2,2,128,384]{3,1,0,2:T(2,128)(2,1)S(1)}, u32[]{:S(2)}, u32[]{:S(2)}) async-start(bf16[2,2,128,384]{3,1,0,2:T(2,128)(2,1)} %copy.19), calls=%async_computation.1 | async-start | bytes 786432 | tf_op jit(solution)/shard_map/all_to_all | solution.py:127
  51.4 4.9 %fusion.91 = (f32[16,6,32]{2,1,0:T(8,128)S(1)}, f32[16,6,32,32]{2,3,1,0:T(8,128)}) fusion(pred[6,384]{1,0:T(8,128)(4,1)S(1)} %iota_compare_fusion, bf16[16,32,384]{2,1,0:T(8,128)(2,1)} %get-tuple-element.20, pred[16,32,32]{1,2,0:T(8,128)(4,1)S(1)} %compare_or_fusion, bf16[16,32,1152]{2,1,0:T(8,128)(2,1)} %bitcast.107), kind=kOutput, calls=%fused_computation.101 | convolution fusion | flops 77070368 | bytes 1210624 | tf_op jit(solution)/shard_map/sub | solution.py:51
  56.2 4.2 %all-to-all-done.1 = bf16[2,2,128,384]{3,1,0,2:T(2,128)(2,1)S(1)} async-done(((bf16[2,2,128,384]{3,1,0,2:T(2,128)(2,1)}), bf16[2,2,128,384]{3,1,0,2:T(2,128)(2,1)S(1)}, u32[]{:S(2)}, u32[]{:S(2)}) %all-to-all-start.1) | async-done | bytes 393248 | tf_op jit(solution)/shard_map/all_to_all | solution.py:127
  60.6 4.8 %fusion.4 = f32[16,6,32,32]{2,3,1,0:T(8,128)} fusion(pred[6,384]{1,0:T(8,128)(4,1)S(1)} %iota_compare_fusion, bf16[16,32,384]{2,1,0:T(8,128)(2,1)S(1)} %bitcast.109, bf16[16,32,1152]{2,1,0:T(8,128)(2,1)} %bitcast.108), kind=kOutput, calls=%fused_computation.5 | convolution fusion | flops 76677120 | bytes 1181952 | tf_op jit(solution)/shard_map/bhid,bjd->bhij/dot_general | solution.py:57
  67.0 4.5 %fusion.49 = bf16[16,32,384]{2,1,0:T(8,128)(2,1)} fusion(pred[6,384]{1,0:T(8,128)(4,1)S(1)} %iota_compare_fusion, bf16[16,32,384]{2,1,0:T(8,128)(2,1)S(1)} %copy-done.7, f32[16,6,32,32]{2,3,1,0:T(8,128)} %fusion.4, f32[16,6,32,32]{2,3,1,0:T(8,128)} %get-tuple-element.22, f32[16,6,32]{2,1,0:T(8,128)S(1)} %get-tuple-element.21), kind=kOutput, calls=%fused_computation.44 | convolution fusion | flops 77564960 | bytes 1587456 | tf_op jit(solution)/shard_map/bhij,bhid->bjd/dot_general | solution.py:65
  71.5 4.6 %fusion.43 = bf16[16,32,384]{2,1,0:T(8,128)(2,1)} fusion(pred[6,384]{1,0:T(8,128)(4,1)S(1)} %iota_compare_fusion, bf16[16,32,384]{2,1,0:T(8,128)(2,1)S(1)} %get-tuple-element.19, f32[16,6,32,32]{2,3,1,0:T(8,128)} %fusion.4, f32[16,6,32,32]{2,3,1,0:T(8,128)} %get-tuple-element.22, f32[16,6,32]{2,1,0:T(8,128)S(1)} %get-tuple-element.21), kind=kOutput, calls=%fused_computation.42 | convolution fusion | flops 77564960 | bytes 1587456 | tf_op jit(solution)/shard_map/bhij,bhjd->bid/dot_general | solution.py:62
  76.1 2.5 %fusion.23 = (f32[16,32]{1,0:T(8,128)S(1)}, f32[16,32,768]{2,1,0:T(8,128)S(1)}) fusion(bf16[16,32,768]{2,1,0:T(8,128)(2,1)S(1)} %bitcast.94, f32[16,32]{1,0:T(8,128)S(1)} %add_rsqrt_fusion, bf16[768,1152]{1,0:T(8,128)(2,1)S(1)} %copy-done, bf16[16,32,384]{2,1,0:T(8,128)(2,1)S(1)} %copy-done.10, bf16[16,32,384]{2,1,0:T(8,128)(2,1)} %fusion.49, ...), kind=kOutput, calls=%fused_computation.29 | convolution fusion | flops 911080960 | bytes 5312512 | tf_op jit(solution)/shard_map/dot_general | solution.py:77
  82.1 3.1 %collective-permute-start = (f32[4,2,48,1152]{3,2,1,0:T(8,128)S(1)}, f32[4,2,48,1152]{3,2,1,0:T(8,128)}, u32[]{:S(2)}, u32[]{:S(2)}) collective-permute-start(f32[4,2,48,1152]{3,2,1,0:T(8,128)S(1)} %dynamic-slice_bitcast_fusion), channel_id=1, source_target_pairs={{0,1},{1,0},{2,3},{3,2},{4,5},{5,4},{6,7},{7,6},{8,9},{9,8},{10,11... | collective-permute-start | bytes 5308424 | tf_op jit(solution)/shard_map/ppermute | solution.py:96
  85.2 4.9 %all-to-all-start.2 = ((bf16[2,32,8,768]{3,2,0,1:T(8,128)(2,1)}), bf16[2,32,8,768]{3,2,0,1:T(8,128)(2,1)}, u32[]{:S(2)}, u32[]{:S(2)}) async-start(bf16[2,32,8,768]{3,2,0,1:T(8,128)(2,1)} %bitcast.90), calls=%async_computation.2 | async-start | bytes 1572864 | tf_op jit(solution)/shard_map/all_to_all | solution.py:139
  90.1 2.2 %bitcast_add_fusion = f32[4,2,48,1152]{3,2,1,0:T(8,128)S(1)} fusion(f32[4,2,48,1152]{3,2,1,0:T(8,128)} %collective-permute-done, f32[4,2,2,48,1152]{4,3,2,1,0:T(8,128)} %bitcast.97, s32[]{:T(128)S(6)} %select_n.98), kind=kLoop, calls=%fused_computation.24 | loop fusion | flops 442368 | bytes 5308420 | tf_op jit(solution)/shard_map/add | solution.py:97
  93.2 4.5 %collective-permute-start.3 = (bf16[2,48,1152]{2,1,0:T(8,128)(2,1)}, bf16[2,48,1152]{2,1,0:T(8,128)(2,1)}, u32[]{:S(2)}, u32[]{:S(2)}) collective-permute-start(bf16[2,48,1152]{2,1,0:T(8,128)(2,1)} %get-tuple-element.17), channel_id=1, source_target_pairs={{0,12},{1,13},{2,14},{3,15},{4,0},{5,1},{6,2},{7,3},{8,4},{9,5},{1... | collective-permute-start | bytes 663560 | tf_op jit(solution)/shard_map/ppermute | solution.py:96
  97.7 3.6 %collective-permute-start.2 = (bf16[2,48,1152]{2,1,0:T(8,128)(2,1)}, bf16[2,48,1152]{2,1,0:T(8,128)(2,1)}, u32[]{:S(2)}, u32[]{:S(2)}) collective-permute-start(bf16[2,48,1152]{2,1,0:T(8,128)(2,1)} %get-tuple-element.18), channel_id=1, source_target_pairs={{0,8},{1,9},{2,10},{3,11},{4,12},{5,13},{6,14},{7,15},{8,0},{9,1},... | collective-permute-start | bytes 663560 | tf_op jit(solution)/shard_map/ppermute | solution.py:96
  101.3 1.9 %collective-permute-start.1 = (bf16[2,48,1152]{2,1,0:T(8,128)(2,1)}, bf16[2,48,1152]{2,1,0:T(8,128)(2,1)}, u32[]{:S(2)}, u32[]{:S(2)}) collective-permute-start(bf16[2,48,1152]{2,1,0:T(8,128)(2,1)} %get-tuple-element.16), channel_id=1, source_target_pairs={{0,4},{1,5},{2,6},{3,7},{4,8},{5,9},{6,10},{7,11},{8,12},{9,13},{1... | collective-permute-start | bytes 663560 | tf_op jit(solution)/shard_map/ppermute | solution.py:96
  103.3 3.7 %collective-permute-done.3 = bf16[2,48,1152]{2,1,0:T(8,128)(2,1)} collective-permute-done((bf16[2,48,1152]{2,1,0:T(8,128)(2,1)}, bf16[2,48,1152]{2,1,0:T(8,128)(2,1)}, u32[]{:S(2)}, u32[]{:S(2)}) %collective-permute-start.3) | collective-permute-done | bytes 221216 | tf_op jit(solution)/shard_map/ppermute | solution.py:96
  107.0 3.0 %collective-permute-done.2 = bf16[2,48,1152]{2,1,0:T(8,128)(2,1)} collective-permute-done((bf16[2,48,1152]{2,1,0:T(8,128)(2,1)}, bf16[2,48,1152]{2,1,0:T(8,128)(2,1)}, u32[]{:S(2)}, u32[]{:S(2)}) %collective-permute-start.2) | collective-permute-done | bytes 221216 | tf_op jit(solution)/shard_map/ppermute | solution.py:96
  110.0 5.2 %collective-permute-done.1 = bf16[2,48,1152]{2,1,0:T(8,128)(2,1)} collective-permute-done((bf16[2,48,1152]{2,1,0:T(8,128)(2,1)}, bf16[2,48,1152]{2,1,0:T(8,128)(2,1)}, u32[]{:S(2)}, u32[]{:S(2)}) %collective-permute-start.1) | collective-permute-done | bytes 221216 | tf_op jit(solution)/shard_map/ppermute | solution.py:96
  117.2 5.7 %collective-permute-start.4 = (f32[48,1152]{1,0:T(8,128)S(1)}, f32[48,1152]{1,0:T(8,128)S(1)}, u32[]{:S(2)}, u32[]{:S(2)}) collective-permute-start(f32[48,1152]{1,0:T(8,128)S(1)} %dynamic-slice_bitcast_fusion.1), channel_id=1, source_target_pairs={{0,2},{1,3},{2,0},{3,1},{4,6},{5,7},{6,4},{7,5},{8,10},{9,11},{10,... | collective-permute-start | bytes 663560 | tf_op jit(solution)/shard_map/ppermute | solution.py:96
  122.9 2.1 %copy.39 = bf16[2,2,16,8,768]{4,3,2,1,0:T(8,128)(2,1)} copy(bf16[2,2,16,8,768]{4,3,0,1,2:T(8,128)(2,1)} %bitcast.36) | data formatting | bytes 1572864 | tf_op jit(solution)/shard_map/all_to_all | solution.py:139
  125.0 4.7 %collective-permute-done.4 = f32[48,1152]{1,0:T(8,128)S(1)} collective-permute-done((f32[48,1152]{1,0:T(8,128)S(1)}, f32[48,1152]{1,0:T(8,128)S(1)}, u32[]{:S(2)}, u32[]{:S(2)}) %collective-permute-start.4) | collective-permute-done | bytes 221216 | tf_op jit(solution)/shard_map/ppermute | solution.py:96
  131.8 25.4 %all_to_all.59 = f32[32,1,1728]{2,1,0:T(1,128)S(1)} all-to-all(f32[32,1,1728]{2,1,0:T(1,128)S(1)} %reshape.111), channel_id=1, replica_groups=mesh['dp'=32,'band'=16] {'dp'}, dimensions={0} | all-to-all | bytes 442368 | tf_op jit(solution)/shard_map/all_to_all | solution.py:117
  (60 shorter events, 17.4 us)
Async XLA Ops:
  0.6 47.6 %copy-start = (bf16[768,1152]{1,0:T(8,128)(2,1)S(1)}, bf16[768,1152]{1,0:T(8,128)(2,1)}, u32[]{:S(2)}) copy-start(bf16[768,1152]{1,0:T(8,128)(2,1)} %param.7) | copy-start | bytes 5308420
  0.6 17.3 %copy-start.8 = (s32[2,8,32]{2,1,0:T(8,128)S(1)}, s32[2,8,32]{2,1,0:T(8,128)}, u32[]{:S(2)}) copy-start(s32[2,8,32]{2,1,0:T(8,128)} %param.6) | copy-start | bytes 6148
  3.6 31.3 %all-to-all-start = ((bf16[2,2,128,768]{3,1,0,2:T(2,128)(2,1)}), bf16[2,2,128,768]{3,1,0,2:T(2,128)(2,1)S(1)}, u32[]{:S(2)}, u32[]{:S(2)}) async-start(bf16[2,2,128,768]{3,1,0,2:T(2,128)(2,1)} %copy.17), calls=%async_computation | async-start | bytes 1572864 | tf_op jit(solution)/shard_map/all_to_all | solution.py:123
  38.3 22.1 %all-to-all-start.1 = ((bf16[2,2,128,384]{3,1,0,2:T(2,128)(2,1)}), bf16[2,2,128,384]{3,1,0,2:T(2,128)(2,1)S(1)}, u32[]{:S(2)}, u32[]{:S(2)}) async-start(bf16[2,2,128,384]{3,1,0,2:T(2,128)(2,1)} %copy.19), calls=%async_computation.1 | async-start | bytes 786432 | tf_op jit(solution)/shard_map/all_to_all | solution.py:127
  48.2 1.2 copy-start.4
  49.5 1.0 copy-start.6
  60.6 4.8 %copy-start.9 = (f32[16,6,32,32]{2,3,1,0:T(8,128)S(1)}, f32[16,6,32,32]{2,3,1,0:T(8,128)}, u32[]{:S(2)}) copy-start(f32[16,6,32,32]{2,3,1,0:T(8,128)} %get-tuple-element.22) | copy-start | bytes 1179652
  65.4 1.6 copy-start.7
  71.5 4.6 %copy-start.10 = (bf16[16,32,384]{2,1,0:T(8,128)(2,1)S(1)}, bf16[16,32,384]{2,1,0:T(8,128)(2,1)}, u32[]{:S(2)}) copy-start(bf16[16,32,384]{2,1,0:T(8,128)(2,1)} %fusion.46) | copy-start | bytes 1179652
  76.1 2.6 %copy-start.5 = (bf16[16,32,768]{2,1,0:T(8,128)(2,1)S(1)}, bf16[16,32,768]{2,1,0:T(8,128)(2,1)}, u32[]{:S(2)}) copy-start(bf16[16,32,768]{2,1,0:T(8,128)(2,1)} %copy-done.4) | copy-start | bytes 2359300
  76.1 2.6 %copy-start.11 = (bf16[16,32,384]{2,1,0:T(8,128)(2,1)S(1)}, bf16[16,32,384]{2,1,0:T(8,128)(2,1)}, u32[]{:S(2)}) copy-start(bf16[16,32,384]{2,1,0:T(8,128)(2,1)} %fusion.49) | copy-start | bytes 1179652
  76.1 2.6 %copy-start.12 = (bf16[16,32,384]{2,1,0:T(8,128)(2,1)S(1)}, bf16[16,32,384]{2,1,0:T(8,128)(2,1)}, u32[]{:S(2)}) copy-start(bf16[16,32,384]{2,1,0:T(8,128)(2,1)} %fusion.43) | copy-start | bytes 1179652
  79.9 2.0 %copy-start.1 = (f32[768,1152]{1,0:T(8,128)}, f32[768,1152]{1,0:T(8,128)S(1)}, u32[]{:S(2)}) copy-start(f32[768,1152]{1,0:T(8,128)S(1)} %convolution_bitcast_fusion) | copy-start | bytes 10616836
  82.1 8.1 %collective-permute-start = (f32[4,2,48,1152]{3,2,1,0:T(8,128)S(1)}, f32[4,2,48,1152]{3,2,1,0:T(8,128)}, u32[]{:S(2)}, u32[]{:S(2)}) collective-permute-start(f32[4,2,48,1152]{3,2,1,0:T(8,128)S(1)} %dynamic-slice_bitcast_fusion), channel_id=1, source_target_pairs={{0,1},{1,0},{2,3},{3,2},{4,5},{5,4},{6,7},{7,6},{8,9},{9,8},{10,11... | collective-permute-start | bytes 5308424 | tf_op jit(solution)/shard_map/ppermute | solution.py:96
  85.2 37.7 %all-to-all-start.2 = ((bf16[2,32,8,768]{3,2,0,1:T(8,128)(2,1)}), bf16[2,32,8,768]{3,2,0,1:T(8,128)(2,1)}, u32[]{:S(2)}, u32[]{:S(2)}) async-start(bf16[2,32,8,768]{3,2,0,1:T(8,128)(2,1)} %bitcast.90), calls=%async_computation.2 | async-start | bytes 1572864 | tf_op jit(solution)/shard_map/all_to_all | solution.py:139
  93.2 13.8 %collective-permute-start.3 = (bf16[2,48,1152]{2,1,0:T(8,128)(2,1)}, bf16[2,48,1152]{2,1,0:T(8,128)(2,1)}, u32[]{:S(2)}, u32[]{:S(2)}) collective-permute-start(bf16[2,48,1152]{2,1,0:T(8,128)(2,1)} %get-tuple-element.17), channel_id=1, source_target_pairs={{0,12},{1,13},{2,14},{3,15},{4,0},{5,1},{6,2},{7,3},{8,4},{9,5},{1... | collective-permute-start | bytes 663560 | tf_op jit(solution)/shard_map/ppermute | solution.py:96
  97.7 12.3 %collective-permute-start.2 = (bf16[2,48,1152]{2,1,0:T(8,128)(2,1)}, bf16[2,48,1152]{2,1,0:T(8,128)(2,1)}, u32[]{:S(2)}, u32[]{:S(2)}) collective-permute-start(bf16[2,48,1152]{2,1,0:T(8,128)(2,1)} %get-tuple-element.18), channel_id=1, source_target_pairs={{0,8},{1,9},{2,10},{3,11},{4,12},{5,13},{6,14},{7,15},{8,0},{9,1},... | collective-permute-start | bytes 663560 | tf_op jit(solution)/shard_map/ppermute | solution.py:96
  101.3 13.9 %collective-permute-start.1 = (bf16[2,48,1152]{2,1,0:T(8,128)(2,1)}, bf16[2,48,1152]{2,1,0:T(8,128)(2,1)}, u32[]{:S(2)}, u32[]{:S(2)}) collective-permute-start(bf16[2,48,1152]{2,1,0:T(8,128)(2,1)} %get-tuple-element.16), channel_id=1, source_target_pairs={{0,4},{1,5},{2,6},{3,7},{4,8},{5,9},{6,10},{7,11},{8,12},{9,13},{1... | collective-permute-start | bytes 663560 | tf_op jit(solution)/shard_map/ppermute | solution.py:96
  116.5 0.8 copy-start.2
  117.2 12.5 %copy-start.3 = (f32[2,48,1152]{2,1,0:T(8,128)S(1)}, f32[2,48,1152]{2,1,0:T(8,128)}, u32[]{:S(2)}) copy-start(f32[2,48,1152]{2,1,0:T(8,128)} %copy-done.2) | copy-start | bytes 1327108
  117.2 12.5 %collective-permute-start.4 = (f32[48,1152]{1,0:T(8,128)S(1)}, f32[48,1152]{1,0:T(8,128)S(1)}, u32[]{:S(2)}, u32[]{:S(2)}) collective-permute-start(f32[48,1152]{1,0:T(8,128)S(1)} %dynamic-slice_bitcast_fusion.1), channel_id=1, source_target_pairs={{0,2},{1,3},{2,0},{3,1},{4,6},{5,7},{6,4},{7,5},{8,10},{9,11},{10,... | collective-permute-start | bytes 663560 | tf_op jit(solution)/shard_map/ppermute | solution.py:96

commit v8 on v7

--- a/solution.py
+++ b/solution.py
@@ -123,9 +123,10 @@
     states_cols = lax.all_to_all(cell_states, "band", split_axis=2, concat_axis=1, tiled=True)
     tables, rows, cols, _ = states_cols.shape
     states_cols = states_cols.transpose(0, 2, 1, 3).reshape(tables * cols, rows, width)
-    states_cols, head_grads = lax.optimization_barrier((states_cols, head_grads))
-    grad_cols = lax.all_to_all(head_grads, "band", split_axis=2, concat_axis=1, tiled=True)
-    grad_cols = grad_cols.transpose(0, 2, 1, 3).reshape(tables * cols, rows, -1)
+    grads_by_col = head_grads.transpose(2, 0, 1, 3)
+    states_cols, grads_by_col = lax.optimization_barrier((states_cols, grads_by_col))
+    grad_cols = lax.all_to_all(grads_by_col, "band", split_axis=0, concat_axis=2, tiled=True)
+    grad_cols = grad_cols.transpose(1, 0, 2, 3).reshape(tables * cols, rows, -1)
     groups = group_ids.reshape(tables * cols, rows)
     scaled, inverse, normed = normalize(states_cols)
     query_cols, key_cols, value_cols = project(normed, proj_weights)

time: 161 us -> 159 us (0.988)
    optimization_barrier x1 -> x0, local copies, waits for them, and re-layouts: 2.15 us -> none  [body(): lax.optimization_barrier((states_cols, head_grads))]
    unnamed x29 -> x32, local copies, waits for them, and re-layouts: 5.58 us -> 6.77 us
where the time goes in v8:
time: 159 us; the launch traced here: 158 us
  starting transfers between devices  47.8 us (30%)
  waiting for transfers between devices  36.4 us (23%)
  blocking collectives  25.4 us (16%)
  matrix products  25.3 us (16%)
  local copies, waits for them, and re-layouts  15.5 us (10%)
  other arithmetic  6.26 us (4%)
    all_to_all x1, blocking collectives, dp_stage(): blocks = lax.all_to_all(blocks, 'dp', 0, 0, tiled=True)  25.4 us
    ppermute x5, starting transfers between devices, exchange(): got = lax.ppermute(part.astype(wire), 'band', pairs)  18.8 us
    ppermute x5, waiting for transfers between devices, exchange(): got = lax.ppermute(part.astype(wire), 'band', pairs)  16.6 us
    all_to_all x1, waiting for transfers between devices, body(): lax.all_to_all(cell_states, 'band', split_axis=2, concat_axis=1, tiled=True)  15.6 us
    all_to_all x1, starting transfers between devices, body(): lax.all_to_all(cell_states, 'band', split_axis=2, concat_axis=1, tiled=True)  14.4 us
    all_to_all x1, starting transfers between devices, body(): lax.all_to_all(grads_by_col, 'band', split_axis=0, concat_axis=2, tiled=T...  9.75 us
    unnamed x32, local copies, waits for them, and re-layouts  6.77 us
    all_to_all x1, starting transfers between devices, body(): lax.all_to_all(input_cols, 'band', split_axis=1, concat_axis=2, tiled=True)  4.89 us
  transfers between devices with their start and end apart: 8, of which 6 were waited for; matrix products, arithmetic and copies ran while one was open for 9% of the time, Pallas kernels for 0%

profile of v8, /device:TPU:1, one launch (start us, length us, event | category | flops | bytes accessed | tf_op | source)
XLA Modules:
  0.0 157.9 jit_solution(5112834922300352435)
XLA Ops:
  0.7 3.0 %copy.17 = bf16[2,2,128,768]{3,1,0,2:T(2,128)(2,1)} copy(bf16[2,2,128,768]{3,2,1,0:T(8,128)(2,1)} %param.4) | data formatting | bytes 1572864 | tf_op args[0]
  3.6 14.4 %all-to-all-start = ((bf16[2,2,128,768]{3,1,0,2:T(2,128)(2,1)}), bf16[2,2,128,768]{3,1,0,2:T(2,128)(2,1)S(1)}, u32[]{:S(2)}, u32[]{:S(2)}) async-start(bf16[2,2,128,768]{3,1,0,2:T(2,128)(2,1)} %copy.17), calls=%async_computation | async-start | bytes 1572864 | tf_op jit(solution)/shard_map/all_to_all | solution.py:123
  19.4 15.6 %all-to-all-done = bf16[2,2,128,768]{3,1,0,2:T(2,128)(2,1)S(1)} async-done(((bf16[2,2,128,768]{3,1,0,2:T(2,128)(2,1)}), bf16[2,2,128,768]{3,1,0,2:T(2,128)(2,1)S(1)}, u32[]{:S(2)}, u32[]{:S(2)}) %all-to-all-start) | async-done | bytes 786464 | tf_op jit(solution)/shard_map/all_to_all | solution.py:123
  36.3 9.8 %all-to-all-start.1 = ((bf16[128,2,2,384]{3,2,1,0:T(2,128)(2,1)}), bf16[128,2,2,384]{3,2,1,0:T(2,128)(2,1)S(1)}, u32[]{:S(2)}, u32[]{:S(2)}) async-start(bf16[128,2,2,384]{3,2,1,0:T(2,128)(2,1)} %bitcast.105), calls=%async_computation.1 | async-start | bytes 786432 | tf_op jit(solution)/shard_map/all_to_all | solution.py:128
  49.4 4.9 %fusion.91 = (f32[16,6,32]{2,1,0:T(8,128)S(1)}, f32[16,6,32,32]{2,3,1,0:T(8,128)}) fusion(pred[6,384]{1,0:T(8,128)(4,1)S(1)} %iota_compare_fusion, bf16[16,32,384]{2,1,0:T(8,128)(2,1)} %get-tuple-element.20, pred[16,32,32]{1,2,0:T(8,128)(4,1)S(1)} %compare_or_fusion, bf16[16,32,1152]{2,1,0:T(8,128)(2,1)} %bitcast.111), kind=kOutput, calls=%fused_computation.102 | convolution fusion | flops 77070368 | bytes 1210624 | tf_op jit(solution)/shard_map/sub | solution.py:51
  54.2 4.2 %all-to-all-done.1 = bf16[128,2,2,384]{3,2,1,0:T(2,128)(2,1)S(1)} async-done(((bf16[128,2,2,384]{3,2,1,0:T(2,128)(2,1)}), bf16[128,2,2,384]{3,2,1,0:T(2,128)(2,1)S(1)}, u32[]{:S(2)}, u32[]{:S(2)}) %all-to-all-start.1) | async-done | bytes 393248 | tf_op jit(solution)/shard_map/all_to_all | solution.py:128
  58.6 4.8 %fusion.4 = f32[16,6,32,32]{2,3,1,0:T(8,128)} fusion(pred[6,384]{1,0:T(8,128)(4,1)S(1)} %iota_compare_fusion, bf16[16,32,384]{2,1,0:T(8,128)(2,1)S(1)} %bitcast.113, bf16[16,32,1152]{2,1,0:T(8,128)(2,1)} %bitcast.112), kind=kOutput, calls=%fused_computation.5 | convolution fusion | flops 76677120 | bytes 1181952 | tf_op jit(solution)/shard_map/bhid,bjd->bhij/dot_general | solution.py:57
  65.0 4.6 %fusion.49 = bf16[16,32,384]{2,1,0:T(8,128)(2,1)} fusion(pred[6,384]{1,0:T(8,128)(4,1)S(1)} %iota_compare_fusion, bf16[16,32,384]{2,1,0:T(8,128)(2,1)S(1)} %copy-done.8, f32[16,6,32,32]{2,3,1,0:T(8,128)} %fusion.4, f32[16,6,32,32]{2,3,1,0:T(8,128)} %get-tuple-element.22, f32[16,6,32]{2,1,0:T(8,128)S(1)} %get-tuple-element.21), kind=kOutput, calls=%fused_computation.44 | convolution fusion | flops 77564960 | bytes 1587456 | tf_op jit(solution)/shard_map/bhij,bhid->bjd/dot_general | solution.py:65
  69.5 4.6 %fusion.43 = bf16[16,32,384]{2,1,0:T(8,128)(2,1)} fusion(pred[6,384]{1,0:T(8,128)(4,1)S(1)} %iota_compare_fusion, bf16[16,32,384]{2,1,0:T(8,128)(2,1)S(1)} %get-tuple-element.19, f32[16,6,32,32]{2,3,1,0:T(8,128)} %fusion.4, f32[16,6,32,32]{2,3,1,0:T(8,128)} %get-tuple-element.22, f32[16,6,32]{2,1,0:T(8,128)S(1)} %get-tuple-element.21), kind=kOutput, calls=%fused_computation.42 | convolution fusion | flops 77564960 | bytes 1587456 | tf_op jit(solution)/shard_map/bhij,bhjd->bid/dot_general | solution.py:62
  74.1 2.5 %fusion.23 = (f32[16,32]{1,0:T(8,128)S(1)}, f32[16,32,768]{2,1,0:T(8,128)S(1)}) fusion(bf16[16,32,768]{2,1,0:T(8,128)(2,1)S(1)} %bitcast.97, f32[16,32]{1,0:T(8,128)S(1)} %add_rsqrt_fusion, bf16[768,1152]{1,0:T(8,128)(2,1)S(1)} %copy-done, bf16[16,32,384]{2,1,0:T(8,128)(2,1)S(1)} %copy-done.11, bf16[16,32,384]{2,1,0:T(8,128)(2,1)} %fusion.49, ...), kind=kOutput, calls=%fused_computation.29 | convolution fusion | flops 911080960 | bytes 5312512 | tf_op jit(solution)/shard_map/dot_general | solution.py:77
  78.3 1.7 %copy.41 = bf16[2,8,32,768]{3,1,0,2:T(8,128)(2,1)} copy(bf16[2,8,32,768]{3,2,1,0:T(8,128)(2,1)S(1)} %bitcast.102) | data formatting | bytes 1572864 | tf_op jit(solution)/shard_map/reshape | solution.py:138
  80.1 3.1 %collective-permute-start = (f32[4,2,48,1152]{3,2,1,0:T(8,128)S(1)}, f32[4,2,48,1152]{3,2,1,0:T(8,128)}, u32[]{:S(2)}, u32[]{:S(2)}) collective-permute-start(f32[4,2,48,1152]{3,2,1,0:T(8,128)S(1)} %dynamic-slice_bitcast_fusion), channel_id=1, source_target_pairs={{0,1},{1,0},{2,3},{3,2},{4,5},{5,4},{6,7},{7,6},{8,9},{9,8},{10,11... | collective-permute-start | bytes 5308424 | tf_op jit(solution)/shard_map/ppermute | solution.py:96
  83.3 4.9 %all-to-all-start.2 = ((bf16[2,32,8,768]{3,2,0,1:T(8,128)(2,1)}), bf16[2,32,8,768]{3,2,0,1:T(8,128)(2,1)}, u32[]{:S(2)}, u32[]{:S(2)}) async-start(bf16[2,32,8,768]{3,2,0,1:T(8,128)(2,1)} %bitcast.92), calls=%async_computation.2 | async-start | bytes 1572864 | tf_op jit(solution)/shard_map/all_to_all | solution.py:140
  88.2 2.2 %bitcast_add_fusion = f32[4,2,48,1152]{3,2,1,0:T(8,128)S(1)} fusion(f32[4,2,48,1152]{3,2,1,0:T(8,128)} %collective-permute-done, f32[4,2,2,48,1152]{4,3,2,1,0:T(8,128)} %bitcast.100, s32[]{:T(128)S(6)} %select_n.98), kind=kLoop, calls=%fused_computation.24 | loop fusion | flops 442368 | bytes 5308420 | tf_op jit(solution)/shard_map/add | solution.py:97
  91.2 4.5 %collective-permute-start.3 = (bf16[2,48,1152]{2,1,0:T(8,128)(2,1)}, bf16[2,48,1152]{2,1,0:T(8,128)(2,1)}, u32[]{:S(2)}, u32[]{:S(2)}) collective-permute-start(bf16[2,48,1152]{2,1,0:T(8,128)(2,1)} %get-tuple-element.17), channel_id=1, source_target_pairs={{0,12},{1,13},{2,14},{3,15},{4,0},{5,1},{6,2},{7,3},{8,4},{9,5},{1... | collective-permute-start | bytes 663560 | tf_op jit(solution)/shard_map/ppermute | solution.py:96
  95.8 3.6 %collective-permute-start.2 = (bf16[2,48,1152]{2,1,0:T(8,128)(2,1)}, bf16[2,48,1152]{2,1,0:T(8,128)(2,1)}, u32[]{:S(2)}, u32[]{:S(2)}) collective-permute-start(bf16[2,48,1152]{2,1,0:T(8,128)(2,1)} %get-tuple-element.18), channel_id=1, source_target_pairs={{0,8},{1,9},{2,10},{3,11},{4,12},{5,13},{6,14},{7,15},{8,0},{9,1},... | collective-permute-start | bytes 663560 | tf_op jit(solution)/shard_map/ppermute | solution.py:96
  99.4 1.9 %collective-permute-start.1 = (bf16[2,48,1152]{2,1,0:T(8,128)(2,1)}, bf16[2,48,1152]{2,1,0:T(8,128)(2,1)}, u32[]{:S(2)}, u32[]{:S(2)}) collective-permute-start(bf16[2,48,1152]{2,1,0:T(8,128)(2,1)} %get-tuple-element.16), channel_id=1, source_target_pairs={{0,4},{1,5},{2,6},{3,7},{4,8},{5,9},{6,10},{7,11},{8,12},{9,13},{1... | collective-permute-start | bytes 663560 | tf_op jit(solution)/shard_map/ppermute | solution.py:96
  101.4 3.7 %collective-permute-done.3 = bf16[2,48,1152]{2,1,0:T(8,128)(2,1)} collective-permute-done((bf16[2,48,1152]{2,1,0:T(8,128)(2,1)}, bf16[2,48,1152]{2,1,0:T(8,128)(2,1)}, u32[]{:S(2)}, u32[]{:S(2)}) %collective-permute-start.3) | collective-permute-done | bytes 221216 | tf_op jit(solution)/shard_map/ppermute | solution.py:96
  105.0 3.0 %collective-permute-done.2 = bf16[2,48,1152]{2,1,0:T(8,128)(2,1)} collective-permute-done((bf16[2,48,1152]{2,1,0:T(8,128)(2,1)}, bf16[2,48,1152]{2,1,0:T(8,128)(2,1)}, u32[]{:S(2)}, u32[]{:S(2)}) %collective-permute-start.2) | collective-permute-done | bytes 221216 | tf_op jit(solution)/shard_map/ppermute | solution.py:96
  108.1 5.2 %collective-permute-done.1 = bf16[2,48,1152]{2,1,0:T(8,128)(2,1)} collective-permute-done((bf16[2,48,1152]{2,1,0:T(8,128)(2,1)}, bf16[2,48,1152]{2,1,0:T(8,128)(2,1)}, u32[]{:S(2)}, u32[]{:S(2)}) %collective-permute-start.1) | collective-permute-done | bytes 221216 | tf_op jit(solution)/shard_map/ppermute | solution.py:96
  115.3 5.7 %collective-permute-start.4 = (f32[48,1152]{1,0:T(8,128)S(1)}, f32[48,1152]{1,0:T(8,128)S(1)}, u32[]{:S(2)}, u32[]{:S(2)}) collective-permute-start(f32[48,1152]{1,0:T(8,128)S(1)} %dynamic-slice_bitcast_fusion.1), channel_id=1, source_target_pairs={{0,2},{1,3},{2,0},{3,1},{4,6},{5,7},{6,4},{7,5},{8,10},{9,11},{10,... | collective-permute-start | bytes 663560 | tf_op jit(solution)/shard_map/ppermute | solution.py:96
  121.0 2.1 %copy.40 = bf16[2,2,16,8,768]{4,3,2,1,0:T(8,128)(2,1)} copy(bf16[2,2,16,8,768]{4,3,0,1,2:T(8,128)(2,1)} %bitcast.37) | data formatting | bytes 1572864 | tf_op jit(solution)/shard_map/all_to_all | solution.py:140
  123.0 4.7 %collective-permute-done.4 = f32[48,1152]{1,0:T(8,128)S(1)} collective-permute-done((f32[48,1152]{1,0:T(8,128)S(1)}, f32[48,1152]{1,0:T(8,128)S(1)}, u32[]{:S(2)}, u32[]{:S(2)}) %collective-permute-start.4) | collective-permute-done | bytes 221216 | tf_op jit(solution)/shard_map/ppermute | solution.py:96
  129.9 25.4 %all_to_all.59 = f32[32,1,1728]{2,1,0:T(1,128)S(1)} all-to-all(f32[32,1,1728]{2,1,0:T(1,128)S(1)} %reshape.111), channel_id=1, replica_groups=mesh['dp'=32,'band'=16] {'dp'}, dimensions={0} | all-to-all | bytes 442368 | tf_op jit(solution)/shard_map/all_to_all | solution.py:117
  (62 shorter events, 16.9 us)
Async XLA Ops:
  0.6 45.6 %copy-start = (bf16[768,1152]{1,0:T(8,128)(2,1)S(1)}, bf16[768,1152]{1,0:T(8,128)(2,1)}, u32[]{:S(2)}) copy-start(bf16[768,1152]{1,0:T(8,128)(2,1)} %param.7) | copy-start | bytes 5308420
  0.6 17.4 %copy-start.7 = (bf16[2,2,128,384]{3,2,1,0:T(8,128)(2,1)S(1)}, bf16[2,2,128,384]{3,2,1,0:T(8,128)(2,1)}, u32[]{:S(2)}) copy-start(bf16[2,2,128,384]{3,2,1,0:T(8,128)(2,1)} %param.5) | copy-start | bytes 1179652
  3.6 15.6 %copy-start.9 = (s32[2,8,32]{2,1,0:T(8,128)S(1)}, s32[2,8,32]{2,1,0:T(8,128)}, u32[]{:S(2)}) copy-start(s32[2,8,32]{2,1,0:T(8,128)} %param.6) | copy-start | bytes 6148
  3.6 31.4 %all-to-all-start = ((bf16[2,2,128,768]{3,1,0,2:T(2,128)(2,1)}), bf16[2,2,128,768]{3,1,0,2:T(2,128)(2,1)S(1)}, u32[]{:S(2)}, u32[]{:S(2)}) async-start(bf16[2,2,128,768]{3,1,0,2:T(2,128)(2,1)} %copy.17), calls=%async_computation | async-start | bytes 1572864 | tf_op jit(solution)/shard_map/all_to_all | solution.py:123
  36.3 22.1 %all-to-all-start.1 = ((bf16[128,2,2,384]{3,2,1,0:T(2,128)(2,1)}), bf16[128,2,2,384]{3,2,1,0:T(2,128)(2,1)S(1)}, u32[]{:S(2)}, u32[]{:S(2)}) async-start(bf16[128,2,2,384]{3,2,1,0:T(2,128)(2,1)} %bitcast.105), calls=%async_computation.1 | async-start | bytes 786432 | tf_op jit(solution)/shard_map/all_to_all | solution.py:128
  46.2 1.2 copy-start.4
  47.5 1.0 copy-start.6
  58.6 4.8 %copy-start.10 = (f32[16,6,32,32]{2,3,1,0:T(8,128)S(1)}, f32[16,6,32,32]{2,3,1,0:T(8,128)}, u32[]{:S(2)}) copy-start(f32[16,6,32,32]{2,3,1,0:T(8,128)} %get-tuple-element.22) | copy-start | bytes 1179652
  63.4 1.6 copy-start.8
  69.5 4.6 %copy-start.11 = (bf16[16,32,384]{2,1,0:T(8,128)(2,1)S(1)}, bf16[16,32,384]{2,1,0:T(8,128)(2,1)}, u32[]{:S(2)}) copy-start(bf16[16,32,384]{2,1,0:T(8,128)(2,1)} %fusion.46) | copy-start | bytes 1179652
  74.1 2.6 %copy-start.5 = (bf16[16,32,768]{2,1,0:T(8,128)(2,1)S(1)}, bf16[16,32,768]{2,1,0:T(8,128)(2,1)}, u32[]{:S(2)}) copy-start(bf16[16,32,768]{2,1,0:T(8,128)(2,1)} %copy-done.4) | copy-start | bytes 2359300
  74.1 2.6 %copy-start.12 = (bf16[16,32,384]{2,1,0:T(8,128)(2,1)S(1)}, bf16[16,32,384]{2,1,0:T(8,128)(2,1)}, u32[]{:S(2)}) copy-start(bf16[16,32,384]{2,1,0:T(8,128)(2,1)} %fusion.49) | copy-start | bytes 1179652
  74.1 2.6 %copy-start.13 = (bf16[16,32,384]{2,1,0:T(8,128)(2,1)S(1)}, bf16[16,32,384]{2,1,0:T(8,128)(2,1)}, u32[]{:S(2)}) copy-start(bf16[16,32,384]{2,1,0:T(8,128)(2,1)} %fusion.43) | copy-start | bytes 1179652
  77.9 2.0 %copy-start.1 = (f32[768,1152]{1,0:T(8,128)}, f32[768,1152]{1,0:T(8,128)S(1)}, u32[]{:S(2)}) copy-start(f32[768,1152]{1,0:T(8,128)S(1)} %convolution_bitcast_fusion) | copy-start | bytes 10616836
  80.1 8.1 %collective-permute-start = (f32[4,2,48,1152]{3,2,1,0:T(8,128)S(1)}, f32[4,2,48,1152]{3,2,1,0:T(8,128)}, u32[]{:S(2)}, u32[]{:S(2)}) collective-permute-start(f32[4,2,48,1152]{3,2,1,0:T(8,128)S(1)} %dynamic-slice_bitcast_fusion), channel_id=1, source_target_pairs={{0,1},{1,0},{2,3},{3,2},{4,5},{5,4},{6,7},{7,6},{8,9},{9,8},{10,11... | collective-permute-start | bytes 5308424 | tf_op jit(solution)/shard_map/ppermute | solution.py:96
  83.3 37.7 %all-to-all-start.2 = ((bf16[2,32,8,768]{3,2,0,1:T(8,128)(2,1)}), bf16[2,32,8,768]{3,2,0,1:T(8,128)(2,1)}, u32[]{:S(2)}, u32[]{:S(2)}) async-start(bf16[2,32,8,768]{3,2,0,1:T(8,128)(2,1)} %bitcast.92), calls=%async_computation.2 | async-start | bytes 1572864 | tf_op jit(solution)/shard_map/all_to_all | solution.py:140
  91.2 13.8 %collective-permute-start.3 = (bf16[2,48,1152]{2,1,0:T(8,128)(2,1)}, bf16[2,48,1152]{2,1,0:T(8,128)(2,1)}, u32[]{:S(2)}, u32[]{:S(2)}) collective-permute-start(bf16[2,48,1152]{2,1,0:T(8,128)(2,1)} %get-tuple-element.17), channel_id=1, source_target_pairs={{0,12},{1,13},{2,14},{3,15},{4,0},{5,1},{6,2},{7,3},{8,4},{9,5},{1... | collective-permute-start | bytes 663560 | tf_op jit(solution)/shard_map/ppermute | solution.py:96
  95.8 12.3 %collective-permute-start.2 = (bf16[2,48,1152]{2,1,0:T(8,128)(2,1)}, bf16[2,48,1152]{2,1,0:T(8,128)(2,1)}, u32[]{:S(2)}, u32[]{:S(2)}) collective-permute-start(bf16[2,48,1152]{2,1,0:T(8,128)(2,1)} %get-tuple-element.18), channel_id=1, source_target_pairs={{0,8},{1,9},{2,10},{3,11},{4,12},{5,13},{6,14},{7,15},{8,0},{9,1},... | collective-permute-start | bytes 663560 | tf_op jit(solution)/shard_map/ppermute | solution.py:96
  99.4 13.9 %collective-permute-start.1 = (bf16[2,48,1152]{2,1,0:T(8,128)(2,1)}, bf16[2,48,1152]{2,1,0:T(8,128)(2,1)}, u32[]{:S(2)}, u32[]{:S(2)}) collective-permute-start(bf16[2,48,1152]{2,1,0:T(8,128)(2,1)} %get-tuple-element.16), channel_id=1, source_target_pairs={{0,4},{1,5},{2,6},{3,7},{4,8},{5,9},{6,10},{7,11},{8,12},{9,13},{1... | collective-permute-start | bytes 663560 | tf_op jit(solution)/shard_map/ppermute | solution.py:96
  114.5 0.8 copy-start.2
  115.3 12.5 %copy-start.3 = (f32[2,48,1152]{2,1,0:T(8,128)S(1)}, f32[2,48,1152]{2,1,0:T(8,128)}, u32[]{:S(2)}) copy-start(f32[2,48,1152]{2,1,0:T(8,128)} %copy-done.2) | copy-start | bytes 1327108
  115.3 12.5 %collective-permute-start.4 = (f32[48,1152]{1,0:T(8,128)S(1)}, f32[48,1152]{1,0:T(8,128)S(1)}, u32[]{:S(2)}, u32[]{:S(2)}) collective-permute-start(f32[48,1152]{1,0:T(8,128)S(1)} %dynamic-slice_bitcast_fusion.1), channel_id=1, source_target_pairs={{0,2},{1,3},{2,0},{3,1},{4,6},{5,7},{6,4},{7,5},{8,10},{9,11},{10,... | collective-permute-start | bytes 663560 | tf_op jit(solution)/shard_map/ppermute | solution.py:96

commit v9 on v8

--- a/solution.py
+++ b/solution.py
@@ -114,8 +114,8 @@
     rows, d_out = blocks.shape
     cols = d_out // n_dp
     blocks = blocks.reshape(rows, n_dp, cols).transpose(1, 0, 2)
-    blocks = lax.all_to_all(blocks, "dp", 0, 0, tiled=True)
-    return blocks.sum(axis=0)
+    blocks = lax.all_to_all(blocks.astype(jnp.bfloat16), "dp", 0, 0, tiled=True)
+    return blocks.astype(jnp.float32).sum(axis=0)
 
 
 def body(cell_states, head_grads, group_ids, proj_weights):

time: 159 us -> 157 us (0.987)
    convert_element_type x0 -> x2, local copies, waits for them, and re-layouts: none -> 1.61 us  [dp_stage(): blocks = lax.all_to_all(blocks.astype(jnp.bfloat16), 'dp', 0, 0, tiled=True)]
  transfers between devices with their start and end apart: 8 -> 8, of which waited for: 6 -> 6; matrix products, arithmetic and copies ran while one was open for 9% -> 10% of each run, Pallas kernels for 0% -> 0%
where the time goes in v9:
time: 157 us; the launch traced here: 155 us
  starting transfers between devices  47.8 us (30%)
  waiting for transfers between devices  36.5 us (23%)
  matrix products  25.3 us (16%)
  blocking collectives  24.4 us (16%)
  local copies, waits for them, and re-layouts  15.1 us (10%)
  other arithmetic  5.12 us (3%)
    all_to_all x1, blocking collectives, dp_stage(): blocks = lax.all_to_all(blocks.astype(jnp.bfloat16), 'dp', 0, 0, tiled=True)  24.4 us
    ppermute x5, starting transfers between devices, exchange(): got = lax.ppermute(part.astype(wire), 'band', pairs)  18.8 us
    ppermute x5, waiting for transfers between devices, exchange(): got = lax.ppermute(part.astype(wire), 'band', pairs)  16.6 us
    all_to_all x1, waiting for transfers between devices, body(): lax.all_to_all(cell_states, 'band', split_axis=2, concat_axis=1, tiled=True)  15.6 us
    all_to_all x1, starting transfers between devices, body(): lax.all_to_all(cell_states, 'band', split_axis=2, concat_axis=1, tiled=True)  14.4 us
    all_to_all x1, starting transfers between devices, body(): lax.all_to_all(grads_by_col, 'band', split_axis=0, concat_axis=2, tiled=T...  9.75 us
    unnamed x32, local copies, waits for them, and re-layouts  6.79 us
    all_to_all x1, starting transfers between devices, body(): lax.all_to_all(input_cols, 'band', split_axis=1, concat_axis=2, tiled=True)  4.89 us
  transfers between devices with their start and end apart: 8, of which 6 were waited for; matrix products, arithmetic and copies ran while one was open for 10% of the time, Pallas kernels for 0%

profile of v9, /device:TPU:1, one launch (start us, length us, event | category | flops | bytes accessed | tf_op | source)
XLA Modules:
  0.0 155.3 jit_solution(5666797228746811855)
XLA Ops:
  0.7 3.0 %copy.29 = bf16[2,2,128,768]{3,1,0,2:T(2,128)(2,1)} copy(bf16[2,2,128,768]{3,2,1,0:T(8,128)(2,1)} %param.4) | data formatting | bytes 1572864 | tf_op args[0]
  3.6 14.4 %all-to-all-start = ((bf16[2,2,128,768]{3,1,0,2:T(2,128)(2,1)}), bf16[2,2,128,768]{3,1,0,2:T(2,128)(2,1)S(1)}, u32[]{:S(2)}, u32[]{:S(2)}) async-start(bf16[2,2,128,768]{3,1,0,2:T(2,128)(2,1)} %copy.29), calls=%async_computation | async-start | bytes 1572864 | tf_op jit(solution)/shard_map/all_to_all | solution.py:123
  19.4 15.6 %all-to-all-done = bf16[2,2,128,768]{3,1,0,2:T(2,128)(2,1)S(1)} async-done(((bf16[2,2,128,768]{3,1,0,2:T(2,128)(2,1)}), bf16[2,2,128,768]{3,1,0,2:T(2,128)(2,1)S(1)}, u32[]{:S(2)}, u32[]{:S(2)}) %all-to-all-start) | async-done | bytes 786464 | tf_op jit(solution)/shard_map/all_to_all | solution.py:123
  36.3 9.8 %all-to-all-start.1 = ((bf16[128,2,2,384]{3,2,1,0:T(2,128)(2,1)}), bf16[128,2,2,384]{3,2,1,0:T(2,128)(2,1)S(1)}, u32[]{:S(2)}, u32[]{:S(2)}) async-start(bf16[128,2,2,384]{3,2,1,0:T(2,128)(2,1)} %bitcast.102), calls=%async_computation.1 | async-start | bytes 786432 | tf_op jit(solution)/shard_map/all_to_all | solution.py:128
  49.4 4.9 %fusion.91 = (f32[16,6,32]{2,1,0:T(8,128)S(1)}, f32[16,6,32,32]{2,3,1,0:T(8,128)}) fusion(pred[6,384]{1,0:T(8,128)(4,1)S(1)} %iota_compare_fusion, bf16[16,32,384]{2,1,0:T(8,128)(2,1)} %get-tuple-element.22, pred[16,32,32]{1,2,0:T(8,128)(4,1)S(1)} %compare_or_fusion, bf16[16,32,1152]{2,1,0:T(8,128)(2,1)} %bitcast.111), kind=kOutput, calls=%fused_computation.103 | convolution fusion | flops 77070368 | bytes 1210624 | tf_op jit(solution)/shard_map/sub | solution.py:51
  54.3 4.2 %all-to-all-done.1 = bf16[128,2,2,384]{3,2,1,0:T(2,128)(2,1)S(1)} async-done(((bf16[128,2,2,384]{3,2,1,0:T(2,128)(2,1)}), bf16[128,2,2,384]{3,2,1,0:T(2,128)(2,1)S(1)}, u32[]{:S(2)}, u32[]{:S(2)}) %all-to-all-start.1) | async-done | bytes 393248 | tf_op jit(solution)/shard_map/all_to_all | solution.py:128
  58.6 4.8 %fusion.4 = f32[16,6,32,32]{2,3,1,0:T(8,128)} fusion(pred[6,384]{1,0:T(8,128)(4,1)S(1)} %iota_compare_fusion, bf16[16,32,384]{2,1,0:T(8,128)(2,1)S(1)} %bitcast.113, bf16[16,32,1152]{2,1,0:T(8,128)(2,1)} %bitcast.112), kind=kOutput, calls=%fused_computation.5 | convolution fusion | flops 76677120 | bytes 1181952 | tf_op jit(solution)/shard_map/bhid,bjd->bhij/dot_general | solution.py:57
  65.0 4.5 %fusion.49 = bf16[16,32,384]{2,1,0:T(8,128)(2,1)} fusion(pred[6,384]{1,0:T(8,128)(4,1)S(1)} %iota_compare_fusion, bf16[16,32,384]{2,1,0:T(8,128)(2,1)S(1)} %copy-done.8, f32[16,6,32,32]{2,3,1,0:T(8,128)} %fusion.4, f32[16,6,32,32]{2,3,1,0:T(8,128)} %get-tuple-element.24, f32[16,6,32]{2,1,0:T(8,128)S(1)} %get-tuple-element.23), kind=kOutput, calls=%fused_computation.44 | convolution fusion | flops 77564960 | bytes 1587456 | tf_op jit(solution)/shard_map/bhij,bhid->bjd/dot_general | solution.py:65
  69.5 4.6 %fusion.43 = bf16[16,32,384]{2,1,0:T(8,128)(2,1)} fusion(pred[6,384]{1,0:T(8,128)(4,1)S(1)} %iota_compare_fusion, bf16[16,32,384]{2,1,0:T(8,128)(2,1)S(1)} %get-tuple-element.21, f32[16,6,32,32]{2,3,1,0:T(8,128)} %fusion.4, f32[16,6,32,32]{2,3,1,0:T(8,128)} %get-tuple-element.24, f32[16,6,32]{2,1,0:T(8,128)S(1)} %get-tuple-element.23), kind=kOutput, calls=%fused_computation.42 | convolution fusion | flops 77564960 | bytes 1587456 | tf_op jit(solution)/shard_map/bhij,bhjd->bid/dot_general | solution.py:62
  74.1 2.5 %fusion.23 = (f32[16,32]{1,0:T(8,128)S(1)}, f32[16,32,768]{2,1,0:T(8,128)S(1)}) fusion(bf16[16,32,768]{2,1,0:T(8,128)(2,1)S(1)} %bitcast.96, f32[16,32]{1,0:T(8,128)S(1)} %add_rsqrt_fusion, bf16[768,1152]{1,0:T(8,128)(2,1)S(1)} %copy-done, bf16[16,32,384]{2,1,0:T(8,128)(2,1)S(1)} %copy-done.11, bf16[16,32,384]{2,1,0:T(8,128)(2,1)} %fusion.49, ...), kind=kOutput, calls=%fused_computation.29 | convolution fusion | flops 911080960 | bytes 5312512 | tf_op jit(solution)/shard_map/dot_general | solution.py:77
  78.3 1.7 %copy.55 = bf16[2,8,32,768]{3,1,0,2:T(8,128)(2,1)} copy(bf16[2,8,32,768]{3,2,1,0:T(8,128)(2,1)S(1)} %bitcast.101) | data formatting | bytes 1572864 | tf_op jit(solution)/shard_map/reshape | solution.py:138
  80.1 3.1 %collective-permute-start = (f32[4,2,48,1152]{3,2,1,0:T(8,128)S(1)}, f32[4,2,48,1152]{3,2,1,0:T(8,128)}, u32[]{:S(2)}, u32[]{:S(2)}) collective-permute-start(f32[4,2,48,1152]{3,2,1,0:T(8,128)S(1)} %dynamic-slice_bitcast_fusion), channel_id=1, source_target_pairs={{0,1},{1,0},{2,3},{3,2},{4,5},{5,4},{6,7},{7,6},{8,9},{9,8},{10,11... | collective-permute-start | bytes 5308424 | tf_op jit(solution)/shard_map/ppermute | solution.py:96
  83.2 4.9 %all-to-all-start.2 = ((bf16[2,32,8,768]{3,2,0,1:T(8,128)(2,1)}), bf16[2,32,8,768]{3,2,0,1:T(8,128)(2,1)}, u32[]{:S(2)}, u32[]{:S(2)}) async-start(bf16[2,32,8,768]{3,2,0,1:T(8,128)(2,1)} %bitcast.91), calls=%async_computation.2 | async-start | bytes 1572864 | tf_op jit(solution)/shard_map/all_to_all | solution.py:140
  88.1 2.2 %bitcast_add_fusion = f32[4,2,48,1152]{3,2,1,0:T(8,128)S(1)} fusion(f32[4,2,48,1152]{3,2,1,0:T(8,128)} %collective-permute-done, f32[4,2,2,48,1152]{4,3,2,1,0:T(8,128)} %bitcast.99, s32[]{:T(128)S(6)} %select_n.98), kind=kLoop, calls=%fused_computation.24 | loop fusion | flops 442368 | bytes 5308420 | tf_op jit(solution)/shard_map/add | solution.py:97
  91.2 4.5 %collective-permute-start.3 = (bf16[2,48,1152]{2,1,0:T(8,128)(2,1)}, bf16[2,48,1152]{2,1,0:T(8,128)(2,1)}, u32[]{:S(2)}, u32[]{:S(2)}) collective-permute-start(bf16[2,48,1152]{2,1,0:T(8,128)(2,1)} %get-tuple-element.19), channel_id=1, source_target_pairs={{0,12},{1,13},{2,14},{3,15},{4,0},{5,1},{6,2},{7,3},{8,4},{9,5},{1... | collective-permute-start | bytes 663560 | tf_op jit(solution)/shard_map/ppermute | solution.py:96
  95.7 3.6 %collective-permute-start.2 = (bf16[2,48,1152]{2,1,0:T(8,128)(2,1)}, bf16[2,48,1152]{2,1,0:T(8,128)(2,1)}, u32[]{:S(2)}, u32[]{:S(2)}) collective-permute-start(bf16[2,48,1152]{2,1,0:T(8,128)(2,1)} %get-tuple-element.20), channel_id=1, source_target_pairs={{0,8},{1,9},{2,10},{3,11},{4,12},{5,13},{6,14},{7,15},{8,0},{9,1},... | collective-permute-start | bytes 663560 | tf_op jit(solution)/shard_map/ppermute | solution.py:96
  99.3 1.9 %collective-permute-start.1 = (bf16[2,48,1152]{2,1,0:T(8,128)(2,1)}, bf16[2,48,1152]{2,1,0:T(8,128)(2,1)}, u32[]{:S(2)}, u32[]{:S(2)}) collective-permute-start(bf16[2,48,1152]{2,1,0:T(8,128)(2,1)} %get-tuple-element.18), channel_id=1, source_target_pairs={{0,4},{1,5},{2,6},{3,7},{4,8},{5,9},{6,10},{7,11},{8,12},{9,13},{1... | collective-permute-start | bytes 663560 | tf_op jit(solution)/shard_map/ppermute | solution.py:96
  101.3 3.7 %collective-permute-done.3 = bf16[2,48,1152]{2,1,0:T(8,128)(2,1)} collective-permute-done((bf16[2,48,1152]{2,1,0:T(8,128)(2,1)}, bf16[2,48,1152]{2,1,0:T(8,128)(2,1)}, u32[]{:S(2)}, u32[]{:S(2)}) %collective-permute-start.3) | collective-permute-done | bytes 221216 | tf_op jit(solution)/shard_map/ppermute | solution.py:96
  105.0 3.0 %collective-permute-done.2 = bf16[2,48,1152]{2,1,0:T(8,128)(2,1)} collective-permute-done((bf16[2,48,1152]{2,1,0:T(8,128)(2,1)}, bf16[2,48,1152]{2,1,0:T(8,128)(2,1)}, u32[]{:S(2)}, u32[]{:S(2)}) %collective-permute-start.2) | collective-permute-done | bytes 221216 | tf_op jit(solution)/shard_map/ppermute | solution.py:96
  108.0 5.2 %collective-permute-done.1 = bf16[2,48,1152]{2,1,0:T(8,128)(2,1)} collective-permute-done((bf16[2,48,1152]{2,1,0:T(8,128)(2,1)}, bf16[2,48,1152]{2,1,0:T(8,128)(2,1)}, u32[]{:S(2)}, u32[]{:S(2)}) %collective-permute-start.1) | collective-permute-done | bytes 221216 | tf_op jit(solution)/shard_map/ppermute | solution.py:96
  115.3 5.7 %collective-permute-start.4 = (f32[48,1152]{1,0:T(8,128)S(1)}, f32[48,1152]{1,0:T(8,128)S(1)}, u32[]{:S(2)}, u32[]{:S(2)}) collective-permute-start(f32[48,1152]{1,0:T(8,128)S(1)} %dynamic-slice_bitcast_fusion.1), channel_id=1, source_target_pairs={{0,2},{1,3},{2,0},{3,1},{4,6},{5,7},{6,4},{7,5},{8,10},{9,11},{10,... | collective-permute-start | bytes 663560 | tf_op jit(solution)/shard_map/ppermute | solution.py:96
  120.9 2.1 %copy.54 = bf16[2,2,16,8,768]{4,3,2,1,0:T(8,128)(2,1)} copy(bf16[2,2,16,8,768]{4,3,0,1,2:T(8,128)(2,1)} %bitcast.37) | data formatting | bytes 1572864 | tf_op jit(solution)/shard_map/all_to_all | solution.py:140
  123.0 4.7 %collective-permute-done.4 = f32[48,1152]{1,0:T(8,128)S(1)} collective-permute-done((f32[48,1152]{1,0:T(8,128)S(1)}, f32[48,1152]{1,0:T(8,128)S(1)}, u32[]{:S(2)}, u32[]{:S(2)}) %collective-permute-start.4) | collective-permute-done | bytes 221216 | tf_op jit(solution)/shard_map/ppermute | solution.py:96
  129.8 24.4 %all_to_all.59 = bf16[32,2,864]{2,1,0:T(2,128)(2,1)S(1)} all-to-all(bf16[32,2,864]{2,1,0:T(2,128)(2,1)S(1)} %reshape.109), channel_id=1, replica_groups=mesh['dp'=32,'band'=16] {'dp'}, dimensions={0} | all-to-all | bytes 221184 | tf_op jit(solution)/shard_map/all_to_all | solution.py:117
  (60 shorter events, 15.3 us)
Async XLA Ops:
  0.6 45.6 %copy-start = (bf16[768,1152]{1,0:T(8,128)(2,1)S(1)}, bf16[768,1152]{1,0:T(8,128)(2,1)}, u32[]{:S(2)}) copy-start(bf16[768,1152]{1,0:T(8,128)(2,1)} %param.7) | copy-start | bytes 5308420
  0.6 17.4 %copy-start.7 = (bf16[2,2,128,384]{3,2,1,0:T(8,128)(2,1)S(1)}, bf16[2,2,128,384]{3,2,1,0:T(8,128)(2,1)}, u32[]{:S(2)}) copy-start(bf16[2,2,128,384]{3,2,1,0:T(8,128)(2,1)} %param.5) | copy-start | bytes 1179652
  3.6 15.6 %copy-start.9 = (s32[2,8,32]{2,1,0:T(8,128)S(1)}, s32[2,8,32]{2,1,0:T(8,128)}, u32[]{:S(2)}) copy-start(s32[2,8,32]{2,1,0:T(8,128)} %param.6) | copy-start | bytes 6148
  3.6 31.4 %all-to-all-start = ((bf16[2,2,128,768]{3,1,0,2:T(2,128)(2,1)}), bf16[2,2,128,768]{3,1,0,2:T(2,128)(2,1)S(1)}, u32[]{:S(2)}, u32[]{:S(2)}) async-start(bf16[2,2,128,768]{3,1,0,2:T(2,128)(2,1)} %copy.29), calls=%async_computation | async-start | bytes 1572864 | tf_op jit(solution)/shard_map/all_to_all | solution.py:123
  36.3 22.1 %all-to-all-start.1 = ((bf16[128,2,2,384]{3,2,1,0:T(2,128)(2,1)}), bf16[128,2,2,384]{3,2,1,0:T(2,128)(2,1)S(1)}, u32[]{:S(2)}, u32[]{:S(2)}) async-start(bf16[128,2,2,384]{3,2,1,0:T(2,128)(2,1)} %bitcast.102), calls=%async_computation.1 | async-start | bytes 786432 | tf_op jit(solution)/shard_map/all_to_all | solution.py:128
  46.2 1.2 copy-start.4
  47.5 1.0 copy-start.6
  58.6 4.8 %copy-start.10 = (f32[16,6,32,32]{2,3,1,0:T(8,128)S(1)}, f32[16,6,32,32]{2,3,1,0:T(8,128)}, u32[]{:S(2)}) copy-start(f32[16,6,32,32]{2,3,1,0:T(8,128)} %get-tuple-element.24) | copy-start | bytes 1179652
  63.4 1.6 %copy-start.8 = (bf16[16,32,384]{2,1,0:T(8,128)(2,1)S(1)}, bf16[16,32,384]{2,1,0:T(8,128)(2,1)}, u32[]{:S(2)}) copy-start(bf16[16,32,384]{2,1,0:T(8,128)(2,1)} %get-tuple-element.22) | copy-start | bytes 1179652
  69.5 4.6 %copy-start.11 = (bf16[16,32,384]{2,1,0:T(8,128)(2,1)S(1)}, bf16[16,32,384]{2,1,0:T(8,128)(2,1)}, u32[]{:S(2)}) copy-start(bf16[16,32,384]{2,1,0:T(8,128)(2,1)} %fusion.46) | copy-start | bytes 1179652
  74.1 2.6 %copy-start.5 = (bf16[16,32,768]{2,1,0:T(8,128)(2,1)S(1)}, bf16[16,32,768]{2,1,0:T(8,128)(2,1)}, u32[]{:S(2)}) copy-start(bf16[16,32,768]{2,1,0:T(8,128)(2,1)} %copy-done.4) | copy-start | bytes 2359300
  74.1 2.6 %copy-start.12 = (bf16[16,32,384]{2,1,0:T(8,128)(2,1)S(1)}, bf16[16,32,384]{2,1,0:T(8,128)(2,1)}, u32[]{:S(2)}) copy-start(bf16[16,32,384]{2,1,0:T(8,128)(2,1)} %fusion.49) | copy-start | bytes 1179652
  74.1 2.6 %copy-start.13 = (bf16[16,32,384]{2,1,0:T(8,128)(2,1)S(1)}, bf16[16,32,384]{2,1,0:T(8,128)(2,1)}, u32[]{:S(2)}) copy-start(bf16[16,32,384]{2,1,0:T(8,128)(2,1)} %fusion.43) | copy-start | bytes 1179652
  77.9 2.0 %copy-start.1 = (f32[768,1152]{1,0:T(8,128)}, f32[768,1152]{1,0:T(8,128)S(1)}, u32[]{:S(2)}) copy-start(f32[768,1152]{1,0:T(8,128)S(1)} %convolution_bitcast_fusion) | copy-start | bytes 10616836
  80.1 8.1 %collective-permute-start = (f32[4,2,48,1152]{3,2,1,0:T(8,128)S(1)}, f32[4,2,48,1152]{3,2,1,0:T(8,128)}, u32[]{:S(2)}, u32[]{:S(2)}) collective-permute-start(f32[4,2,48,1152]{3,2,1,0:T(8,128)S(1)} %dynamic-slice_bitcast_fusion), channel_id=1, source_target_pairs={{0,1},{1,0},{2,3},{3,2},{4,5},{5,4},{6,7},{7,6},{8,9},{9,8},{10,11... | collective-permute-start | bytes 5308424 | tf_op jit(solution)/shard_map/ppermute | solution.py:96
  83.2 37.7 %all-to-all-start.2 = ((bf16[2,32,8,768]{3,2,0,1:T(8,128)(2,1)}), bf16[2,32,8,768]{3,2,0,1:T(8,128)(2,1)}, u32[]{:S(2)}, u32[]{:S(2)}) async-start(bf16[2,32,8,768]{3,2,0,1:T(8,128)(2,1)} %bitcast.91), calls=%async_computation.2 | async-start | bytes 1572864 | tf_op jit(solution)/shard_map/all_to_all | solution.py:140
  91.2 13.8 %collective-permute-start.3 = (bf16[2,48,1152]{2,1,0:T(8,128)(2,1)}, bf16[2,48,1152]{2,1,0:T(8,128)(2,1)}, u32[]{:S(2)}, u32[]{:S(2)}) collective-permute-start(bf16[2,48,1152]{2,1,0:T(8,128)(2,1)} %get-tuple-element.19), channel_id=1, source_target_pairs={{0,12},{1,13},{2,14},{3,15},{4,0},{5,1},{6,2},{7,3},{8,4},{9,5},{1... | collective-permute-start | bytes 663560 | tf_op jit(solution)/shard_map/ppermute | solution.py:96
  95.7 12.3 %collective-permute-start.2 = (bf16[2,48,1152]{2,1,0:T(8,128)(2,1)}, bf16[2,48,1152]{2,1,0:T(8,128)(2,1)}, u32[]{:S(2)}, u32[]{:S(2)}) collective-permute-start(bf16[2,48,1152]{2,1,0:T(8,128)(2,1)} %get-tuple-element.20), channel_id=1, source_target_pairs={{0,8},{1,9},{2,10},{3,11},{4,12},{5,13},{6,14},{7,15},{8,0},{9,1},... | collective-permute-start | bytes 663560 | tf_op jit(solution)/shard_map/ppermute | solution.py:96
  99.3 13.9 %collective-permute-start.1 = (bf16[2,48,1152]{2,1,0:T(8,128)(2,1)}, bf16[2,48,1152]{2,1,0:T(8,128)(2,1)}, u32[]{:S(2)}, u32[]{:S(2)}) collective-permute-start(bf16[2,48,1152]{2,1,0:T(8,128)(2,1)} %get-tuple-element.18), channel_id=1, source_target_pairs={{0,4},{1,5},{2,6},{3,7},{4,8},{5,9},{6,10},{7,11},{8,12},{9,13},{1... | collective-permute-start | bytes 663560 | tf_op jit(solution)/shard_map/ppermute | solution.py:96
  114.5 0.8 copy-start.2
  115.2 12.5 %copy-start.3 = (f32[2,48,1152]{2,1,0:T(8,128)S(1)}, f32[2,48,1152]{2,1,0:T(8,128)}, u32[]{:S(2)}) copy-start(f32[2,48,1152]{2,1,0:T(8,128)} %copy-done.2) | copy-start | bytes 1327108
  115.3 12.5 %collective-permute-start.4 = (f32[48,1152]{1,0:T(8,128)S(1)}, f32[48,1152]{1,0:T(8,128)S(1)}, u32[]{:S(2)}, u32[]{:S(2)}) collective-permute-start(f32[48,1152]{1,0:T(8,128)S(1)} %dynamic-slice_bitcast_fusion.1), channel_id=1, source_target_pairs={{0,2},{1,3},{2,0},{3,1},{4,6},{5,7},{6,4},{7,5},{8,10},{9,11},{10,... | collective-permute-start | bytes 663560 | tf_op jit(solution)/shard_map/ppermute | solution.py:96

commit v10 on v9

--- a/solution.py
+++ b/solution.py
@@ -105,17 +105,18 @@
     band = lax.axis_index("band")
     blocks = partial_w.reshape(n_band // 4, 2, 2, rows, d_out)
     blocks = exchange(blocks, 2, band % 2, 1, 2)
-    blocks = exchange(blocks, 0, band // 4, 4, n_band // 4, jnp.bfloat16)
-    return exchange(blocks, 0, (band // 2) % 2, 2, 2)
+    return exchange(blocks, 0, band // 4, 4, n_band // 4, jnp.bfloat16)
 
 
 def dp_stage(blocks):
     n_dp = lax.axis_size("dp")
-    rows, d_out = blocks.shape
+    halves, rows, d_out = blocks.shape
     cols = d_out // n_dp
-    blocks = blocks.reshape(rows, n_dp, cols).transpose(1, 0, 2)
+    blocks = blocks.reshape(halves, rows, n_dp, cols).transpose(2, 0, 1, 3)
     blocks = lax.all_to_all(blocks.astype(jnp.bfloat16), "dp", 0, 0, tiled=True)
-    return blocks.astype(jnp.float32).sum(axis=0)
+    blocks = blocks.astype(jnp.float32).sum(axis=0)
+    band = lax.axis_index("band")
+    return exchange(blocks, 0, (band // 2) % 2, 2, 2)
 
 
 def body(cell_states, head_grads, group_ids, proj_weights):

time: 157 us -> 159 us (1.013)
  blocking collectives: 24.4 us -> 0 us
  starting transfers between devices: 47.8 us -> 62 us
  waiting for transfers between devices: 36.5 us -> 44.2 us
  local copies, waits for them, and re-layouts: 15.1 us -> 18.2 us
    all_to_all x1 -> x0, blocking collectives: 24.4 us -> none  [dp_stage(): blocks = lax.all_to_all(blocks.astype(jnp.bfloat16), 'dp', 0, 0, tiled=True)]
    all_to_all x0 -> x1, starting transfers between devices: none -> 14.8 us  [dp_stage(): blocks = lax.all_to_all(blocks.astype(jnp.bfloat16), 'dp', 0, 0, tiled=True)]
    all_to_all x0 -> x1, waiting for transfers between devices: none -> 11.1 us  [dp_stage(): blocks = lax.all_to_all(blocks.astype(jnp.bfloat16), 'dp', 0, 0, tiled=True)]
    ppermute x5, waiting for transfers between devices: 16.6 us -> 9.71 us  [exchange(): got = lax.ppermute(part.astype(wire), 'band', pairs)]
    all_to_all x1, waiting for transfers between devices: 0.01 us -> 3.53 us  [body(): lax.all_to_all(input_cols, 'band', split_axis=1, concat_axis=2, tiled=True)]
    convert_element_type x2, local copies, waits for them, and re-layouts: 1.61 us -> 3.98 us  [dp_stage(): blocks = lax.all_to_all(blocks.astype(jnp.bfloat16), 'dp', 0, 0, tiled=True)]
    unnamed x32 -> x28, local copies, waits for them, and re-layouts: 6.79 us -> 7.46 us
  transfers between devices with their start and end apart: 8 -> 9, of which waited for: 6 -> 7; matrix products, arithmetic and copies ran while one was open for 10% -> 9% of each run, Pallas kernels for 0% -> 0%
where the time goes in v10:
time: 159 us; the launch traced here: 157 us
  starting transfers between devices  62 us (39%)
  waiting for transfers between devices  44.2 us (28%)
  matrix products  25.4 us (16%)
  local copies, waits for them, and re-layouts  18.2 us (11%)
  other arithmetic  5.89 us (4%)
    ppermute x5, starting transfers between devices, exchange(): got = lax.ppermute(part.astype(wire), 'band', pairs)  18.2 us
    all_to_all x1, waiting for transfers between devices, body(): lax.all_to_all(cell_states, 'band', split_axis=2, concat_axis=1, tiled=True)  15.6 us
    all_to_all x1, starting transfers between devices, dp_stage(): blocks = lax.all_to_all(blocks.astype(jnp.bfloat16), 'dp', 0, 0, tiled=True)  14.8 us
    all_to_all x1, starting transfers between devices, body(): lax.all_to_all(cell_states, 'band', split_axis=2, concat_axis=1, tiled=True)  14.4 us
    all_to_all x1, waiting for transfers between devices, dp_stage(): blocks = lax.all_to_all(blocks.astype(jnp.bfloat16), 'dp', 0, 0, tiled=True)  11.1 us
    all_to_all x1, starting transfers between devices, body(): lax.all_to_all(grads_by_col, 'band', split_axis=0, concat_axis=2, tiled=T...  9.75 us
    ppermute x5, waiting for transfers between devices, exchange(): got = lax.ppermute(part.astype(wire), 'band', pairs)  9.71 us
    unnamed x28, local copies, waits for them, and re-layouts  7.46 us
  transfers between devices with their start and end apart: 9, of which 7 were waited for; matrix products, arithmetic and copies ran while one was open for 9% of the time, Pallas kernels for 0%

profile of v10, /device:TPU:1, one launch (start us, length us, event | category | flops | bytes accessed | tf_op | source)
XLA Modules:
  0.0 156.7 jit_solution(3404908527533947195)
XLA Ops:
  0.7 3.0 %copy.41 = bf16[2,2,128,768]{3,1,0,2:T(2,128)(2,1)} copy(bf16[2,2,128,768]{3,2,1,0:T(8,128)(2,1)} %param.4) | data formatting | bytes 1572864 | tf_op args[0]
  3.6 14.4 %all-to-all-start = ((bf16[2,2,128,768]{3,1,0,2:T(2,128)(2,1)}), bf16[2,2,128,768]{3,1,0,2:T(2,128)(2,1)S(1)}, u32[]{:S(2)}, u32[]{:S(2)}) async-start(bf16[2,2,128,768]{3,1,0,2:T(2,128)(2,1)} %copy.41), calls=%async_computation | async-start | bytes 1572864 | tf_op jit(solution)/shard_map/all_to_all | solution.py:124
  19.4 15.6 %all-to-all-done = bf16[2,2,128,768]{3,1,0,2:T(2,128)(2,1)S(1)} async-done(((bf16[2,2,128,768]{3,1,0,2:T(2,128)(2,1)}), bf16[2,2,128,768]{3,1,0,2:T(2,128)(2,1)S(1)}, u32[]{:S(2)}, u32[]{:S(2)}) %all-to-all-start) | async-done | bytes 786464 | tf_op jit(solution)/shard_map/all_to_all | solution.py:124
  36.3 9.8 %all-to-all-start.1 = ((bf16[128,2,2,384]{3,2,1,0:T(2,128)(2,1)}), bf16[128,2,2,384]{3,2,1,0:T(2,128)(2,1)S(1)}, u32[]{:S(2)}, u32[]{:S(2)}) async-start(bf16[128,2,2,384]{3,2,1,0:T(2,128)(2,1)} %bitcast.105), calls=%async_computation.1 | async-start | bytes 786432 | tf_op jit(solution)/shard_map/all_to_all | solution.py:129
  49.4 4.9 %fusion.91 = (f32[16,6,32]{2,1,0:T(8,128)S(1)}, f32[16,6,32,32]{2,3,1,0:T(8,128)}) fusion(pred[6,384]{1,0:T(8,128)(4,1)S(1)} %iota_compare_fusion, bf16[16,32,384]{2,1,0:T(8,128)(2,1)} %get-tuple-element.18, pred[16,32,32]{1,2,0:T(8,128)(4,1)S(1)} %compare_or_fusion, bf16[16,32,1152]{2,1,0:T(8,128)(2,1)} %bitcast.111), kind=kOutput, calls=%fused_computation.103 | convolution fusion | flops 77070368 | bytes 1210624 | tf_op jit(solution)/shard_map/sub | solution.py:51
  54.3 4.2 %all-to-all-done.1 = bf16[128,2,2,384]{3,2,1,0:T(2,128)(2,1)S(1)} async-done(((bf16[128,2,2,384]{3,2,1,0:T(2,128)(2,1)}), bf16[128,2,2,384]{3,2,1,0:T(2,128)(2,1)S(1)}, u32[]{:S(2)}, u32[]{:S(2)}) %all-to-all-start.1) | async-done | bytes 393248 | tf_op jit(solution)/shard_map/all_to_all | solution.py:129
  58.6 4.8 %fusion.4 = f32[16,6,32,32]{2,3,1,0:T(8,128)} fusion(pred[6,384]{1,0:T(8,128)(4,1)S(1)} %iota_compare_fusion, bf16[16,32,384]{2,1,0:T(8,128)(2,1)S(1)} %bitcast.113, bf16[16,32,1152]{2,1,0:T(8,128)(2,1)} %bitcast.112), kind=kOutput, calls=%fused_computation.5 | convolution fusion | flops 76677120 | bytes 1181952 | tf_op jit(solution)/shard_map/bhid,bjd->bhij/dot_general | solution.py:57
  65.0 4.5 %fusion.49 = bf16[16,32,384]{2,1,0:T(8,128)(2,1)} fusion(pred[6,384]{1,0:T(8,128)(4,1)S(1)} %iota_compare_fusion, bf16[16,32,384]{2,1,0:T(8,128)(2,1)S(1)} %copy-done.6, f32[16,6,32,32]{2,3,1,0:T(8,128)} %fusion.4, f32[16,6,32,32]{2,3,1,0:T(8,128)} %get-tuple-element.20, f32[16,6,32]{2,1,0:T(8,128)S(1)} %get-tuple-element.19), kind=kOutput, calls=%fused_computation.44 | convolution fusion | flops 77564960 | bytes 1587456 | tf_op jit(solution)/shard_map/bhij,bhid->bjd/dot_general | solution.py:65
  69.5 4.5 %fusion.43 = bf16[16,32,384]{2,1,0:T(8,128)(2,1)} fusion(pred[6,384]{1,0:T(8,128)(4,1)S(1)} %iota_compare_fusion, bf16[16,32,384]{2,1,0:T(8,128)(2,1)S(1)} %get-tuple-element.17, f32[16,6,32,32]{2,3,1,0:T(8,128)} %fusion.4, f32[16,6,32,32]{2,3,1,0:T(8,128)} %get-tuple-element.20, f32[16,6,32]{2,1,0:T(8,128)S(1)} %get-tuple-element.19), kind=kOutput, calls=%fused_computation.42 | convolution fusion | flops 77564960 | bytes 1587456 | tf_op jit(solution)/shard_map/bhij,bhjd->bid/dot_general | solution.py:62
  74.1 2.7 %fusion.23 = (f32[16,32]{1,0:T(8,128)S(1)}, f32[16,32,768]{2,1,0:T(8,128)S(1)}) fusion(bf16[16,32,768]{2,1,0:T(8,128)(2,1)S(1)} %bitcast.96, f32[16,32]{1,0:T(8,128)S(1)} %add_rsqrt_fusion, bf16[768,1152]{1,0:T(8,128)(2,1)S(1)} %copy-done, bf16[16,32,384]{2,1,0:T(8,128)(2,1)} %fusion.46, bf16[16,32,384]{2,1,0:T(8,128)(2,1)} %fusion.49, ...), kind=kOutput, calls=%fused_computation.29 | convolution fusion | flops 911080960 | bytes 5312512 | tf_op jit(solution)/shard_map/dot_general | solution.py:77
  80.2 3.1 %collective-permute-start = (f32[4,2,48,1152]{3,2,1,0:T(8,128)S(1)}, f32[4,2,48,1152]{3,2,1,0:T(8,128)}, u32[]{:S(2)}, u32[]{:S(2)}) collective-permute-start(f32[4,2,48,1152]{3,2,1,0:T(8,128)S(1)} %dynamic-slice_bitcast_fusion), channel_id=1, source_target_pairs={{0,1},{1,0},{2,3},{3,2},{4,5},{5,4},{6,7},{7,6},{8,9},{9,8},{10,11... | collective-permute-start | bytes 5308424 | tf_op jit(solution)/shard_map/ppermute | solution.py:96
  83.3 4.9 %all-to-all-start.2 = ((bf16[2,32,8,768]{3,2,0,1:T(8,128)(2,1)}), bf16[2,32,8,768]{3,2,0,1:T(8,128)(2,1)}, u32[]{:S(2)}, u32[]{:S(2)}) async-start(bf16[2,32,8,768]{3,2,0,1:T(8,128)(2,1)} %bitcast.91), calls=%async_computation.2 | async-start | bytes 1572864 | tf_op jit(solution)/shard_map/all_to_all | solution.py:141
  88.2 2.2 %bitcast_add_fusion = f32[4,2,48,1152]{3,2,1,0:T(8,128)S(1)} fusion(f32[4,2,48,1152]{3,2,1,0:T(8,128)} %collective-permute-done, f32[4,2,2,48,1152]{4,3,2,1,0:T(8,128)} %bitcast.99, s32[]{:T(128)S(6)} %select_n.98), kind=kLoop, calls=%fused_computation.24 | loop fusion | flops 442368 | bytes 5308420 | tf_op jit(solution)/shard_map/add | solution.py:97
  91.3 4.5 %collective-permute-start.3 = (bf16[2,48,1152]{2,1,0:T(8,128)(2,1)}, bf16[2,48,1152]{2,1,0:T(8,128)(2,1)}, u32[]{:S(2)}, u32[]{:S(2)}) collective-permute-start(bf16[2,48,1152]{2,1,0:T(8,128)(2,1)} %get-tuple-element.15), channel_id=1, source_target_pairs={{0,12},{1,13},{2,14},{3,15},{4,0},{5,1},{6,2},{7,3},{8,4},{9,5},{1... | collective-permute-start | bytes 663560 | tf_op jit(solution)/shard_map/ppermute | solution.py:96
  95.8 3.7 %collective-permute-start.2 = (bf16[2,48,1152]{2,1,0:T(8,128)(2,1)}, bf16[2,48,1152]{2,1,0:T(8,128)(2,1)}, u32[]{:S(2)}, u32[]{:S(2)}) collective-permute-start(bf16[2,48,1152]{2,1,0:T(8,128)(2,1)} %get-tuple-element.16), channel_id=1, source_target_pairs={{0,8},{1,9},{2,10},{3,11},{4,12},{5,13},{6,14},{7,15},{8,0},{9,1},... | collective-permute-start | bytes 663560 | tf_op jit(solution)/shard_map/ppermute | solution.py:96
  99.5 2.1 %collective-permute-start.1 = (bf16[2,48,1152]{2,1,0:T(8,128)(2,1)}, bf16[2,48,1152]{2,1,0:T(8,128)(2,1)}, u32[]{:S(2)}, u32[]{:S(2)}) collective-permute-start(bf16[2,48,1152]{2,1,0:T(8,128)(2,1)} %get-tuple-element.14), channel_id=1, source_target_pairs={{0,4},{1,5},{2,6},{3,7},{4,8},{5,9},{6,10},{7,11},{8,12},{9,13},{1... | collective-permute-start | bytes 663560 | tf_op jit(solution)/shard_map/ppermute | solution.py:96
  101.6 3.5 %all-to-all-done.2 = bf16[2,32,8,768]{3,2,0,1:T(8,128)(2,1)} async-done(((bf16[2,32,8,768]{3,2,0,1:T(8,128)(2,1)}), bf16[2,32,8,768]{3,2,0,1:T(8,128)(2,1)}, u32[]{:S(2)}, u32[]{:S(2)}) %all-to-all-start.2) | async-done | bytes 786464 | tf_op jit(solution)/shard_map/all_to_all | solution.py:141
  105.2 2.1 %copy.69 = bf16[2,2,16,8,768]{4,3,2,1,0:T(8,128)(2,1)} copy(bf16[2,2,16,8,768]{4,3,0,1,2:T(8,128)(2,1)} %bitcast.35) | data formatting | bytes 1572864 | tf_op jit(solution)/shard_map/all_to_all | solution.py:141
  108.0 5.2 %collective-permute-done.1 = bf16[2,48,1152]{2,1,0:T(8,128)(2,1)} collective-permute-done((bf16[2,48,1152]{2,1,0:T(8,128)(2,1)}, bf16[2,48,1152]{2,1,0:T(8,128)(2,1)}, u32[]{:S(2)}, u32[]{:S(2)}) %collective-permute-start.1) | collective-permute-done | bytes 221216 | tf_op jit(solution)/shard_map/ppermute | solution.py:96
  115.2 3.0 %convert_element_type.85 = bf16[2,48,32,36]{3,2,1,0:T(8,128)(2,1)S(1)} reshape(bf16[2,48,1152]{2,1,0:T(8,128)(2,1)} %fusion.70) | data formatting | bytes 442368 | tf_op jit(solution)/shard_map/convert_element_type | solution.py:116
  120.7 14.8 %all-to-all-start.3 = ((bf16[32,2,1728]{2,1,0:T(2,128)(2,1)}), bf16[32,2,1728]{2,1,0:T(2,128)(2,1)S(1)}, u32[]{:S(2)}, u32[]{:S(2)}) async-start(bf16[32,2,1728]{2,1,0:T(2,128)(2,1)} %reshape.109), calls=%async_computation.3 | async-start | bytes 458752 | tf_op jit(solution)/shard_map/all_to_all | solution.py:116
  135.6 11.1 %all-to-all-done.3 = bf16[32,2,1728]{2,1,0:T(2,128)(2,1)S(1)} async-done(((bf16[32,2,1728]{2,1,0:T(2,128)(2,1)}), bf16[32,2,1728]{2,1,0:T(2,128)(2,1)S(1)}, u32[]{:S(2)}, u32[]{:S(2)}) %all-to-all-start.3) | async-done | bytes 221216 | tf_op jit(solution)/shard_map/all_to_all | solution.py:116
  147.6 4.7 %collective-permute-start.4 = (f32[48,36]{0,1:T(8,128)S(1)}, f32[48,36]{0,1:T(8,128)S(1)}, u32[]{:S(2)}, u32[]{:S(2)}) collective-permute-start(f32[48,36]{0,1:T(8,128)S(1)} %dynamic-slice_bitcast_fusion.1), channel_id=1, source_target_pairs={{0,2},{1,3},{2,0},{3,1},{4,6},{5,7},{6,4},{7,5},{8,10},{9,11},{10,... | collective-permute-start | bytes 20744 | tf_op jit(solution)/shard_map/ppermute | solution.py:96
  152.4 3.7 %collective-permute-done.4 = f32[48,36]{0,1:T(8,128)S(1)} collective-permute-done((f32[48,36]{0,1:T(8,128)S(1)}, f32[48,36]{0,1:T(8,128)S(1)}, u32[]{:S(2)}, u32[]{:S(2)}) %collective-permute-start.4) | collective-permute-done | bytes 6944 | tf_op jit(solution)/shard_map/ppermute | solution.py:96
  (57 shorter events, 18.6 us)
Async XLA Ops:
  0.6 45.6 %copy-start = (bf16[768,1152]{1,0:T(8,128)(2,1)S(1)}, bf16[768,1152]{1,0:T(8,128)(2,1)}, u32[]{:S(2)}) copy-start(bf16[768,1152]{1,0:T(8,128)(2,1)} %param.7) | copy-start | bytes 5308420
  0.6 17.4 %copy-start.5 = (bf16[2,2,128,384]{3,2,1,0:T(8,128)(2,1)S(1)}, bf16[2,2,128,384]{3,2,1,0:T(8,128)(2,1)}, u32[]{:S(2)}) copy-start(bf16[2,2,128,384]{3,2,1,0:T(8,128)(2,1)} %param.5) | copy-start | bytes 1179652
  3.6 15.6 %copy-start.7 = (s32[2,8,32]{2,1,0:T(8,128)S(1)}, s32[2,8,32]{2,1,0:T(8,128)}, u32[]{:S(2)}) copy-start(s32[2,8,32]{2,1,0:T(8,128)} %param.6) | copy-start | bytes 6148
  3.6 31.4 %all-to-all-start = ((bf16[2,2,128,768]{3,1,0,2:T(2,128)(2,1)}), bf16[2,2,128,768]{3,1,0,2:T(2,128)(2,1)S(1)}, u32[]{:S(2)}, u32[]{:S(2)}) async-start(bf16[2,2,128,768]{3,1,0,2:T(2,128)(2,1)} %copy.41), calls=%async_computation | async-start | bytes 1572864 | tf_op jit(solution)/shard_map/all_to_all | solution.py:124
  36.3 22.1 %all-to-all-start.1 = ((bf16[128,2,2,384]{3,2,1,0:T(2,128)(2,1)}), bf16[128,2,2,384]{3,2,1,0:T(2,128)(2,1)S(1)}, u32[]{:S(2)}, u32[]{:S(2)}) async-start(bf16[128,2,2,384]{3,2,1,0:T(2,128)(2,1)} %bitcast.105), calls=%async_computation.1 | async-start | bytes 786432 | tf_op jit(solution)/shard_map/all_to_all | solution.py:129
  46.2 1.2 copy-start.2
  47.5 1.0 copy-start.4
  58.6 4.8 %copy-start.8 = (f32[16,6,32,32]{2,3,1,0:T(8,128)S(1)}, f32[16,6,32,32]{2,3,1,0:T(8,128)}, u32[]{:S(2)}) copy-start(f32[16,6,32,32]{2,3,1,0:T(8,128)} %get-tuple-element.20) | copy-start | bytes 1179652
  63.4 1.6 copy-start.6
  74.0 2.7 %copy-start.3 = (bf16[16,32,768]{2,1,0:T(8,128)(2,1)S(1)}, bf16[16,32,768]{2,1,0:T(8,128)(2,1)}, u32[]{:S(2)}) copy-start(bf16[16,32,768]{2,1,0:T(8,128)(2,1)} %copy-done.2) | copy-start | bytes 2359300
  74.0 2.7 %copy-start.9 = (bf16[16,32,384]{2,1,0:T(8,128)(2,1)S(1)}, bf16[16,32,384]{2,1,0:T(8,128)(2,1)}, u32[]{:S(2)}) copy-start(bf16[16,32,384]{2,1,0:T(8,128)(2,1)} %fusion.46) | copy-start | bytes 1179652
  74.1 2.7 %copy-start.10 = (bf16[16,32,384]{2,1,0:T(8,128)(2,1)S(1)}, bf16[16,32,384]{2,1,0:T(8,128)(2,1)}, u32[]{:S(2)}) copy-start(bf16[16,32,384]{2,1,0:T(8,128)(2,1)} %fusion.49) | copy-start | bytes 1179652
  74.1 2.7 %copy-start.11 = (bf16[16,32,384]{2,1,0:T(8,128)(2,1)S(1)}, bf16[16,32,384]{2,1,0:T(8,128)(2,1)}, u32[]{:S(2)}) copy-start(bf16[16,32,384]{2,1,0:T(8,128)(2,1)} %fusion.43) | copy-start | bytes 1179652
  78.0 2.0 %copy-start.1 = (f32[768,1152]{1,0:T(8,128)}, f32[768,1152]{1,0:T(8,128)S(1)}, u32[]{:S(2)}) copy-start(f32[768,1152]{1,0:T(8,128)S(1)} %convolution_bitcast_fusion) | copy-start | bytes 10616836
  80.2 8.0 %collective-permute-start = (f32[4,2,48,1152]{3,2,1,0:T(8,128)S(1)}, f32[4,2,48,1152]{3,2,1,0:T(8,128)}, u32[]{:S(2)}, u32[]{:S(2)}) collective-permute-start(f32[4,2,48,1152]{3,2,1,0:T(8,128)S(1)} %dynamic-slice_bitcast_fusion), channel_id=1, source_target_pairs={{0,1},{1,0},{2,3},{3,2},{4,5},{5,4},{6,7},{7,6},{8,9},{9,8},{10,11... | collective-permute-start | bytes 5308424 | tf_op jit(solution)/shard_map/ppermute | solution.py:96
  83.3 21.9 %all-to-all-start.2 = ((bf16[2,32,8,768]{3,2,0,1:T(8,128)(2,1)}), bf16[2,32,8,768]{3,2,0,1:T(8,128)(2,1)}, u32[]{:S(2)}, u32[]{:S(2)}) async-start(bf16[2,32,8,768]{3,2,0,1:T(8,128)(2,1)} %bitcast.91), calls=%async_computation.2 | async-start | bytes 1572864 | tf_op jit(solution)/shard_map/all_to_all | solution.py:141
  91.3 16.0 %collective-permute-start.3 = (bf16[2,48,1152]{2,1,0:T(8,128)(2,1)}, bf16[2,48,1152]{2,1,0:T(8,128)(2,1)}, u32[]{:S(2)}, u32[]{:S(2)}) collective-permute-start(bf16[2,48,1152]{2,1,0:T(8,128)(2,1)} %get-tuple-element.15), channel_id=1, source_target_pairs={{0,12},{1,13},{2,14},{3,15},{4,0},{5,1},{6,2},{7,3},{8,4},{9,5},{1... | collective-permute-start | bytes 663560 | tf_op jit(solution)/shard_map/ppermute | solution.py:96
  95.8 12.3 %collective-permute-start.2 = (bf16[2,48,1152]{2,1,0:T(8,128)(2,1)}, bf16[2,48,1152]{2,1,0:T(8,128)(2,1)}, u32[]{:S(2)}, u32[]{:S(2)}) collective-permute-start(bf16[2,48,1152]{2,1,0:T(8,128)(2,1)} %get-tuple-element.16), channel_id=1, source_target_pairs={{0,8},{1,9},{2,10},{3,11},{4,12},{5,13},{6,14},{7,15},{8,0},{9,1},... | collective-permute-start | bytes 663560 | tf_op jit(solution)/shard_map/ppermute | solution.py:96
  99.5 13.8 %collective-permute-start.1 = (bf16[2,48,1152]{2,1,0:T(8,128)(2,1)}, bf16[2,48,1152]{2,1,0:T(8,128)(2,1)}, u32[]{:S(2)}, u32[]{:S(2)}) collective-permute-start(bf16[2,48,1152]{2,1,0:T(8,128)(2,1)} %get-tuple-element.14), channel_id=1, source_target_pairs={{0,4},{1,5},{2,6},{3,7},{4,8},{5,9},{6,10},{7,11},{8,12},{9,13},{1... | collective-permute-start | bytes 663560 | tf_op jit(solution)/shard_map/ppermute | solution.py:96
  120.7 26.0 %all-to-all-start.3 = ((bf16[32,2,1728]{2,1,0:T(2,128)(2,1)}), bf16[32,2,1728]{2,1,0:T(2,128)(2,1)S(1)}, u32[]{:S(2)}, u32[]{:S(2)}) async-start(bf16[32,2,1728]{2,1,0:T(2,128)(2,1)} %reshape.109), calls=%async_computation.3 | async-start | bytes 458752 | tf_op jit(solution)/shard_map/all_to_all | solution.py:116
  147.6 8.4 %collective-permute-start.4 = (f32[48,36]{0,1:T(8,128)S(1)}, f32[48,36]{0,1:T(8,128)S(1)}, u32[]{:S(2)}, u32[]{:S(2)}) collective-permute-start(f32[48,36]{0,1:T(8,128)S(1)} %dynamic-slice_bitcast_fusion.1), channel_id=1, source_target_pairs={{0,2},{1,3},{2,0},{3,1},{4,6},{5,7},{6,4},{7,5},{8,10},{9,11},{10,... | collective-permute-start | bytes 20744 | tf_op jit(solution)/shard_map/ppermute | solution.py:96

commit v11 on v9

--- a/solution.py
+++ b/solution.py
@@ -39,31 +39,32 @@
 
     query_heads = by_head(query)
     key_heads = by_head(key)
+    value_heads = by_head(value)
     grad_heads = by_head(grads)
     scores = (
-        jnp.einsum("bhid,bjd->bhij", query_heads, key, preferred_element_type=jnp.float32)
+        jnp.einsum("bid,bhjd->bihj", query, key_heads, preferred_element_type=jnp.float32)
         * SCALE
     )
     header = lax.broadcasted_iota(jnp.int32, (rows, rows), 1) == 0
     visible = (groups[:, :, None] == groups[:, None, :]) | header
-    scores = jnp.where(visible[:, None], scores, -1e30)
+    scores = jnp.where(visible[:, :, None], scores, -1e30)
     peak = jnp.max(scores, axis=-1, keepdims=True)
     expsc = jnp.exp(scores - peak)
     probs = expsc / jnp.sum(expsc, axis=-1, keepdims=True)
     probs_low = probs.astype(jnp.bfloat16)
     value_grad = jnp.einsum(
-        "bhij,bhid->bjd", probs_low, grad_heads, preferred_element_type=jnp.float32
+        "bihj,bhid->bjd", probs_low, grad_heads, preferred_element_type=jnp.float32
     ).astype(jnp.bfloat16)
     prob_grad = jnp.einsum(
-        "bhid,bjd->bhij", grad_heads, value, preferred_element_type=jnp.float32
+        "bid,bhjd->bihj", grads, value_heads, preferred_element_type=jnp.float32
     )
     score_grad = probs * (prob_grad - jnp.sum(probs * prob_grad, axis=-1, keepdims=True))
     score_low = (score_grad * SCALE).astype(jnp.bfloat16)
     query_grad = jnp.einsum(
-        "bhij,bhjd->bid", score_low, key_heads, preferred_element_type=jnp.float32
+        "bihj,bhjd->bid", score_low, key_heads, preferred_element_type=jnp.float32
     ).astype(jnp.bfloat16)
     key_grad = jnp.einsum(
-        "bhij,bhid->bjd", score_low, query_heads, preferred_element_type=jnp.float32
+        "bihj,bhid->bjd", score_low, query_heads, preferred_element_type=jnp.float32
     ).astype(jnp.bfloat16)
     return (query_grad, key_grad, value_grad)
 

time: 157 us -> 155 us (0.987)
  matrix products: 25.3 us -> 21.8 us
  waiting for transfers between devices: 36.5 us -> 38.1 us
    sub x1, matrix products: 4.88 us -> 3.11 us  [attend_back(): expsc = jnp.exp(scores - peak)]
    dot_general x4, matrix products: 15.5 us -> 13.8 us  [the longest x1 4.59 us: attend_back(): jnp.einsum('bihj,bhid->bjd', score_low, query_heads, preferred_element_ty...]
    all_to_all x1, waiting for transfers between devices: 4.19 us -> 5.78 us  [body(): lax.all_to_all(grads_by_col, 'band', split_axis=0, concat_axis=2, tiled=T...]
    unnamed x32 -> x36, local copies, waits for them, and re-layouts: 6.79 us -> 6.79 us
  transfers between devices with their start and end apart: 8 -> 8, of which waited for: 6 -> 6; matrix products, arithmetic and copies ran while one was open for 10% -> 9% of each run, Pallas kernels for 0% -> 0%
where the time goes in v11:
time: 155 us; the launch traced here: 154 us
  starting transfers between devices  47.8 us (31%)
  waiting for transfers between devices  38.1 us (25%)
  blocking collectives  24.4 us (16%)
  matrix products  21.8 us (14%)
  local copies, waits for them, and re-layouts  15.6 us (10%)
  other arithmetic  5.12 us (3%)
    all_to_all x1, blocking collectives, dp_stage(): blocks = lax.all_to_all(blocks.astype(jnp.bfloat16), 'dp', 0, 0, tiled=True)  24.4 us
    ppermute x5, starting transfers between devices, exchange(): got = lax.ppermute(part.astype(wire), 'band', pairs)  18.7 us
    ppermute x5, waiting for transfers between devices, exchange(): got = lax.ppermute(part.astype(wire), 'band', pairs)  16.7 us
    all_to_all x1, waiting for transfers between devices, body(): lax.all_to_all(cell_states, 'band', split_axis=2, concat_axis=1, tiled=True)  15.6 us
    all_to_all x1, starting transfers between devices, body(): lax.all_to_all(cell_states, 'band', split_axis=2, concat_axis=1, tiled=True)  14.4 us
    all_to_all x1, starting transfers between devices, body(): lax.all_to_all(grads_by_col, 'band', split_axis=0, concat_axis=2, tiled=T...  9.75 us
    unnamed x36, local copies, waits for them, and re-layouts  6.79 us
    all_to_all x1, waiting for transfers between devices, body(): lax.all_to_all(grads_by_col, 'band', split_axis=0, concat_axis=2, tiled=T...  5.78 us
  transfers between devices with their start and end apart: 8, of which 6 were waited for; matrix products, arithmetic and copies ran while one was open for 9% of the time, Pallas kernels for 0%

profile of v11, /device:TPU:1, one launch (start us, length us, event | category | flops | bytes accessed | tf_op | source)
XLA Modules:
  0.0 153.9 jit_solution(5739302855184523979)
XLA Ops:
  0.7 3.0 %copy.24 = bf16[2,2,128,768]{3,1,0,2:T(2,128)(2,1)} copy(bf16[2,2,128,768]{3,2,1,0:T(8,128)(2,1)} %param.4) | data formatting | bytes 1572864 | tf_op args[0]
  3.6 14.4 %all-to-all-start = ((bf16[2,2,128,768]{3,1,0,2:T(2,128)(2,1)}), bf16[2,2,128,768]{3,1,0,2:T(2,128)(2,1)S(1)}, u32[]{:S(2)}, u32[]{:S(2)}) async-start(bf16[2,2,128,768]{3,1,0,2:T(2,128)(2,1)} %copy.24), calls=%async_computation | async-start | bytes 1572864 | tf_op jit(solution)/shard_map/all_to_all | solution.py:124
  19.4 15.6 %all-to-all-done = bf16[2,2,128,768]{3,1,0,2:T(2,128)(2,1)S(1)} async-done(((bf16[2,2,128,768]{3,1,0,2:T(2,128)(2,1)}), bf16[2,2,128,768]{3,1,0,2:T(2,128)(2,1)S(1)}, u32[]{:S(2)}, u32[]{:S(2)}) %all-to-all-start) | async-done | bytes 786464 | tf_op jit(solution)/shard_map/all_to_all | solution.py:124
  36.3 9.8 %all-to-all-start.1 = ((bf16[128,2,2,384]{3,2,1,0:T(2,128)(2,1)}), bf16[128,2,2,384]{3,2,1,0:T(2,128)(2,1)S(1)}, u32[]{:S(2)}, u32[]{:S(2)}) async-start(bf16[128,2,2,384]{3,2,1,0:T(2,128)(2,1)} %bitcast.101), calls=%async_computation.1 | async-start | bytes 786432 | tf_op jit(solution)/shard_map/all_to_all | solution.py:129
  49.5 3.1 %fusion.91 = (f32[16,32,6]{1,2,0:T(8,128)S(1)}, f32[16,32,6,32]{1,3,2,0:T(8,128)}) fusion(pred[6,384]{1,0:T(8,128)(4,1)S(1)} %iota_compare_fusion, bf16[16,32,384]{2,1,0:T(8,128)(2,1)S(1)} %get-tuple-element.22, pred[16,32,32]{1,2,0:T(8,128)(4,1)S(1)} %compare_or_fusion, bf16[16,32,1152]{2,1,0:T(8,128)(2,1)} %bitcast.107), kind=kOutput, calls=%fused_computation.101 | convolution fusion | flops 77070368 | bytes 1210624 | tf_op jit(solution)/shard_map/sub | solution.py:52
  52.7 5.8 %all-to-all-done.1 = bf16[128,2,2,384]{3,2,1,0:T(2,128)(2,1)S(1)} async-done(((bf16[128,2,2,384]{3,2,1,0:T(2,128)(2,1)}), bf16[128,2,2,384]{3,2,1,0:T(2,128)(2,1)S(1)}, u32[]{:S(2)}, u32[]{:S(2)}) %all-to-all-start.1) | async-done | bytes 393248 | tf_op jit(solution)/shard_map/all_to_all | solution.py:129
  58.9 3.0 %fusion.10 = f32[16,32,6,32]{1,3,2,0:T(8,128)} fusion(bf16[16,32,384,1]{2,1,3,0:T(8,128)(2,1)S(1)} %bitcast.110, pred[6,384]{1,0:T(8,128)(4,1)S(1)} %iota_compare_fusion, bf16[16,32,384]{2,1,0:T(8,128)(2,1)} %get-tuple-element.21), kind=kOutput, calls=%fused_computation.12 | convolution fusion | flops 76677120 | bytes 1181952 | tf_op jit(solution)/shard_map/bid,bhjd->bihj/dot_general | solution.py:58
  63.5 4.6 %fusion.43 = bf16[16,32,384]{2,1,0:T(8,128)(2,1)} fusion(pred[6,384]{1,0:T(8,128)(4,1)S(1)} %iota_compare_fusion, bf16[16,32,384]{2,1,0:T(8,128)(2,1)S(1)} %copy-done.9, f32[16,32,6,32]{1,3,2,0:T(8,128)} %fusion.10, f32[16,32,6,32]{1,3,2,0:T(8,128)} %get-tuple-element.25, f32[16,32,6]{1,2,0:T(8,128)S(1)} %get-tuple-element.24), kind=kOutput, calls=%fused_computation.42 | convolution fusion | flops 77564960 | bytes 1587456 | tf_op jit(solution)/shard_map/bihj,bhjd->bid/dot_general | solution.py:63
  68.1 4.6 %fusion.49 = bf16[16,32,384]{2,1,0:T(8,128)(2,1)} fusion(pred[6,384]{1,0:T(8,128)(4,1)S(1)} %iota_compare_fusion, bf16[16,32,384]{2,1,0:T(8,128)(2,1)S(1)} %copy-done.7, f32[16,32,6,32]{1,3,2,0:T(8,128)} %fusion.10, f32[16,32,6,32]{1,3,2,0:T(8,128)} %get-tuple-element.25, f32[16,32,6]{1,2,0:T(8,128)S(1)} %get-tuple-element.24), kind=kOutput, calls=%fused_computation.44 | convolution fusion | flops 77564960 | bytes 1587456 | tf_op jit(solution)/shard_map/bihj,bhid->bjd/dot_general | solution.py:66
  72.7 2.5 %fusion.23 = (f32[16,32]{1,0:T(8,128)S(1)}, f32[16,32,768]{2,1,0:T(8,128)S(1)}) fusion(bf16[16,32,768]{2,1,0:T(8,128)(2,1)S(1)} %bitcast.95, f32[16,32]{1,0:T(8,128)S(1)} %add_rsqrt_fusion, bf16[768,1152]{1,0:T(8,128)(2,1)S(1)} %copy-done, bf16[16,32,384]{2,1,0:T(8,128)(2,1)S(1)} %copy-done.13, bf16[16,32,384]{2,1,0:T(8,128)(2,1)} %fusion.49, ...), kind=kOutput, calls=%fused_computation.29 | convolution fusion | flops 911080960 | bytes 5312512 | tf_op jit(solution)/shard_map/dot_general | solution.py:78
  76.9 1.7 %copy.47 = bf16[2,8,32,768]{3,1,0,2:T(8,128)(2,1)} copy(bf16[2,8,32,768]{3,2,1,0:T(8,128)(2,1)S(1)} %bitcast.100) | data formatting | bytes 1572864 | tf_op jit(solution)/shard_map/reshape | solution.py:139
  78.6 3.1 %collective-permute-start = (f32[4,2,48,1152]{3,2,1,0:T(8,128)S(1)}, f32[4,2,48,1152]{3,2,1,0:T(8,128)}, u32[]{:S(2)}, u32[]{:S(2)}) collective-permute-start(f32[4,2,48,1152]{3,2,1,0:T(8,128)S(1)} %dynamic-slice_bitcast_fusion), channel_id=1, source_target_pairs={{0,1},{1,0},{2,3},{3,2},{4,5},{5,4},{6,7},{7,6},{8,9},{9,8},{10,11... | collective-permute-start | bytes 5308424 | tf_op jit(solution)/shard_map/ppermute | solution.py:97
  81.8 4.9 %all-to-all-start.2 = ((bf16[2,32,8,768]{3,2,0,1:T(8,128)(2,1)}), bf16[2,32,8,768]{3,2,0,1:T(8,128)(2,1)}, u32[]{:S(2)}, u32[]{:S(2)}) async-start(bf16[2,32,8,768]{3,2,0,1:T(8,128)(2,1)} %bitcast.91), calls=%async_computation.2 | async-start | bytes 1572864 | tf_op jit(solution)/shard_map/all_to_all | solution.py:141
  86.7 2.2 %bitcast_add_fusion = f32[4,2,48,1152]{3,2,1,0:T(8,128)S(1)} fusion(f32[4,2,48,1152]{3,2,1,0:T(8,128)} %collective-permute-done, f32[4,2,2,48,1152]{4,3,2,1,0:T(8,128)} %bitcast.98, s32[]{:T(128)S(6)} %select_n.104), kind=kLoop, calls=%fused_computation.24 | loop fusion | flops 442368 | bytes 5308420 | tf_op jit(solution)/shard_map/add | solution.py:98
  89.8 4.5 %collective-permute-start.3 = (bf16[2,48,1152]{2,1,0:T(8,128)(2,1)}, bf16[2,48,1152]{2,1,0:T(8,128)(2,1)}, u32[]{:S(2)}, u32[]{:S(2)}) collective-permute-start(bf16[2,48,1152]{2,1,0:T(8,128)(2,1)} %get-tuple-element.19), channel_id=1, source_target_pairs={{0,12},{1,13},{2,14},{3,15},{4,0},{5,1},{6,2},{7,3},{8,4},{9,5},{1... | collective-permute-start | bytes 663560 | tf_op jit(solution)/shard_map/ppermute | solution.py:97
  94.3 3.8 %collective-permute-start.2 = (bf16[2,48,1152]{2,1,0:T(8,128)(2,1)}, bf16[2,48,1152]{2,1,0:T(8,128)(2,1)}, u32[]{:S(2)}, u32[]{:S(2)}) collective-permute-start(bf16[2,48,1152]{2,1,0:T(8,128)(2,1)} %get-tuple-element.20), channel_id=1, source_target_pairs={{0,8},{1,9},{2,10},{3,11},{4,12},{5,13},{6,14},{7,15},{8,0},{9,1},... | collective-permute-start | bytes 663560 | tf_op jit(solution)/shard_map/ppermute | solution.py:97
  98.1 1.9 %collective-permute-start.1 = (bf16[2,48,1152]{2,1,0:T(8,128)(2,1)}, bf16[2,48,1152]{2,1,0:T(8,128)(2,1)}, u32[]{:S(2)}, u32[]{:S(2)}) collective-permute-start(bf16[2,48,1152]{2,1,0:T(8,128)(2,1)} %get-tuple-element.18), channel_id=1, source_target_pairs={{0,4},{1,5},{2,6},{3,7},{4,8},{5,9},{6,10},{7,11},{8,12},{9,13},{1... | collective-permute-start | bytes 663560 | tf_op jit(solution)/shard_map/ppermute | solution.py:97
  100.1 3.7 %collective-permute-done.3 = bf16[2,48,1152]{2,1,0:T(8,128)(2,1)} collective-permute-done((bf16[2,48,1152]{2,1,0:T(8,128)(2,1)}, bf16[2,48,1152]{2,1,0:T(8,128)(2,1)}, u32[]{:S(2)}, u32[]{:S(2)}) %collective-permute-start.3) | collective-permute-done | bytes 221216 | tf_op jit(solution)/shard_map/ppermute | solution.py:97
  103.8 2.8 %collective-permute-done.2 = bf16[2,48,1152]{2,1,0:T(8,128)(2,1)} collective-permute-done((bf16[2,48,1152]{2,1,0:T(8,128)(2,1)}, bf16[2,48,1152]{2,1,0:T(8,128)(2,1)}, u32[]{:S(2)}, u32[]{:S(2)}) %collective-permute-start.2) | collective-permute-done | bytes 221216 | tf_op jit(solution)/shard_map/ppermute | solution.py:97
  106.6 5.2 %collective-permute-done.1 = bf16[2,48,1152]{2,1,0:T(8,128)(2,1)} collective-permute-done((bf16[2,48,1152]{2,1,0:T(8,128)(2,1)}, bf16[2,48,1152]{2,1,0:T(8,128)(2,1)}, u32[]{:S(2)}, u32[]{:S(2)}) %collective-permute-start.1) | collective-permute-done | bytes 221216 | tf_op jit(solution)/shard_map/ppermute | solution.py:97
  113.8 5.4 %collective-permute-start.4 = (f32[48,1152]{1,0:T(8,128)S(1)}, f32[48,1152]{1,0:T(8,128)S(1)}, u32[]{:S(2)}, u32[]{:S(2)}) collective-permute-start(f32[48,1152]{1,0:T(8,128)S(1)} %dynamic-slice_bitcast_fusion.1), channel_id=1, source_target_pairs={{0,2},{1,3},{2,0},{3,1},{4,6},{5,7},{6,4},{7,5},{8,10},{9,11},{10,... | collective-permute-start | bytes 663560 | tf_op jit(solution)/shard_map/ppermute | solution.py:97
  119.3 2.1 %copy.46 = bf16[2,2,16,8,768]{4,3,2,1,0:T(8,128)(2,1)} copy(bf16[2,2,16,8,768]{4,3,0,1,2:T(8,128)(2,1)} %bitcast.37) | data formatting | bytes 1572864 | tf_op jit(solution)/shard_map/all_to_all | solution.py:141
  121.3 5.0 %collective-permute-done.4 = f32[48,1152]{1,0:T(8,128)S(1)} collective-permute-done((f32[48,1152]{1,0:T(8,128)S(1)}, f32[48,1152]{1,0:T(8,128)S(1)}, u32[]{:S(2)}, u32[]{:S(2)}) %collective-permute-start.4) | collective-permute-done | bytes 221216 | tf_op jit(solution)/shard_map/ppermute | solution.py:97
  128.4 24.4 %all_to_all.59 = bf16[32,2,864]{2,1,0:T(2,128)(2,1)S(1)} all-to-all(bf16[32,2,864]{2,1,0:T(2,128)(2,1)S(1)} %reshape.114), channel_id=1, replica_groups=mesh['dp'=32,'band'=16] {'dp'}, dimensions={0} | all-to-all | bytes 221184 | tf_op jit(solution)/shard_map/all_to_all | solution.py:118
  (63 shorter events, 15.8 us)
Async XLA Ops:
  0.6 45.6 %copy-start = (bf16[768,1152]{1,0:T(8,128)(2,1)S(1)}, bf16[768,1152]{1,0:T(8,128)(2,1)}, u32[]{:S(2)}) copy-start(bf16[768,1152]{1,0:T(8,128)(2,1)} %param.7) | copy-start | bytes 5308420
  0.6 17.4 %copy-start.10 = (bf16[2,2,128,384]{3,2,1,0:T(8,128)(2,1)S(1)}, bf16[2,2,128,384]{3,2,1,0:T(8,128)(2,1)}, u32[]{:S(2)}) copy-start(bf16[2,2,128,384]{3,2,1,0:T(8,128)(2,1)} %param.5) | copy-start | bytes 1179652
  3.6 15.6 %copy-start.11 = (s32[2,8,32]{2,1,0:T(8,128)S(1)}, s32[2,8,32]{2,1,0:T(8,128)}, u32[]{:S(2)}) copy-start(s32[2,8,32]{2,1,0:T(8,128)} %param.6) | copy-start | bytes 6148
  3.6 31.4 %all-to-all-start = ((bf16[2,2,128,768]{3,1,0,2:T(2,128)(2,1)}), bf16[2,2,128,768]{3,1,0,2:T(2,128)(2,1)S(1)}, u32[]{:S(2)}, u32[]{:S(2)}) async-start(bf16[2,2,128,768]{3,1,0,2:T(2,128)(2,1)} %copy.24), calls=%async_computation | async-start | bytes 1572864 | tf_op jit(solution)/shard_map/all_to_all | solution.py:124
  36.3 22.1 %all-to-all-start.1 = ((bf16[128,2,2,384]{3,2,1,0:T(2,128)(2,1)}), bf16[128,2,2,384]{3,2,1,0:T(2,128)(2,1)S(1)}, u32[]{:S(2)}, u32[]{:S(2)}) async-start(bf16[128,2,2,384]{3,2,1,0:T(2,128)(2,1)} %bitcast.101), calls=%async_computation.1 | async-start | bytes 786432 | tf_op jit(solution)/shard_map/all_to_all | solution.py:129
  46.2 1.2 copy-start.5
  47.5 1.0 copy-start.4
  49.5 3.1 %copy-start.8 = (bf16[16,32,384]{2,1,0:T(8,128)(2,1)}, bf16[16,32,384]{2,1,0:T(8,128)(2,1)S(1)}, u32[]{:S(2)}) copy-start(bf16[16,32,384]{2,1,0:T(8,128)(2,1)S(1)} %get-tuple-element.22) | copy-start | bytes 1179652
  58.9 3.0 %copy-start.12 = (f32[16,32,6,32]{1,3,2,0:T(8,128)S(1)}, f32[16,32,6,32]{1,3,2,0:T(8,128)}, u32[]{:S(2)}) copy-start(f32[16,32,6,32]{1,3,2,0:T(8,128)} %get-tuple-element.25) | copy-start | bytes 1179652
  61.9 1.6 %copy-start.9 = (bf16[16,32,384]{2,1,0:T(8,128)(2,1)S(1)}, bf16[16,32,384]{2,1,0:T(8,128)(2,1)}, u32[]{:S(2)}) copy-start(bf16[16,32,384]{2,1,0:T(8,128)(2,1)} %copy-done.8) | copy-start | bytes 1179652
  63.5 4.6 %copy-start.7 = (bf16[16,32,384]{2,1,0:T(8,128)(2,1)S(1)}, bf16[16,32,384]{2,1,0:T(8,128)(2,1)}, u32[]{:S(2)}) copy-start(bf16[16,32,384]{2,1,0:T(8,128)(2,1)} %get-tuple-element.23) | copy-start | bytes 1179652
  68.1 4.6 %copy-start.13 = (bf16[16,32,384]{2,1,0:T(8,128)(2,1)S(1)}, bf16[16,32,384]{2,1,0:T(8,128)(2,1)}, u32[]{:S(2)}) copy-start(bf16[16,32,384]{2,1,0:T(8,128)(2,1)} %fusion.46) | copy-start | bytes 1179652
  72.7 2.6 %copy-start.6 = (bf16[16,32,768]{2,1,0:T(8,128)(2,1)S(1)}, bf16[16,32,768]{2,1,0:T(8,128)(2,1)}, u32[]{:S(2)}) copy-start(bf16[16,32,768]{2,1,0:T(8,128)(2,1)} %copy-done.5) | copy-start | bytes 2359300
  72.7 2.6 %copy-start.14 = (bf16[16,32,384]{2,1,0:T(8,128)(2,1)S(1)}, bf16[16,32,384]{2,1,0:T(8,128)(2,1)}, u32[]{:S(2)}) copy-start(bf16[16,32,384]{2,1,0:T(8,128)(2,1)} %fusion.43) | copy-start | bytes 1179652
  72.7 2.6 %copy-start.15 = (bf16[16,32,384]{2,1,0:T(8,128)(2,1)S(1)}, bf16[16,32,384]{2,1,0:T(8,128)(2,1)}, u32[]{:S(2)}) copy-start(bf16[16,32,384]{2,1,0:T(8,128)(2,1)} %fusion.49) | copy-start | bytes 1179652
  76.5 2.0 %copy-start.1 = (f32[768,1152]{1,0:T(8,128)}, f32[768,1152]{1,0:T(8,128)S(1)}, u32[]{:S(2)}) copy-start(f32[768,1152]{1,0:T(8,128)S(1)} %convolution_bitcast_fusion) | copy-start | bytes 10616836
  78.6 8.1 %collective-permute-start = (f32[4,2,48,1152]{3,2,1,0:T(8,128)S(1)}, f32[4,2,48,1152]{3,2,1,0:T(8,128)}, u32[]{:S(2)}, u32[]{:S(2)}) collective-permute-start(f32[4,2,48,1152]{3,2,1,0:T(8,128)S(1)} %dynamic-slice_bitcast_fusion), channel_id=1, source_target_pairs={{0,1},{1,0},{2,3},{3,2},{4,5},{5,4},{6,7},{7,6},{8,9},{9,8},{10,11... | collective-permute-start | bytes 5308424 | tf_op jit(solution)/shard_map/ppermute | solution.py:97
  81.8 37.5 %all-to-all-start.2 = ((bf16[2,32,8,768]{3,2,0,1:T(8,128)(2,1)}), bf16[2,32,8,768]{3,2,0,1:T(8,128)(2,1)}, u32[]{:S(2)}, u32[]{:S(2)}) async-start(bf16[2,32,8,768]{3,2,0,1:T(8,128)(2,1)} %bitcast.91), calls=%async_computation.2 | async-start | bytes 1572864 | tf_op jit(solution)/shard_map/all_to_all | solution.py:141
  89.8 14.0 %collective-permute-start.3 = (bf16[2,48,1152]{2,1,0:T(8,128)(2,1)}, bf16[2,48,1152]{2,1,0:T(8,128)(2,1)}, u32[]{:S(2)}, u32[]{:S(2)}) collective-permute-start(bf16[2,48,1152]{2,1,0:T(8,128)(2,1)} %get-tuple-element.19), channel_id=1, source_target_pairs={{0,12},{1,13},{2,14},{3,15},{4,0},{5,1},{6,2},{7,3},{8,4},{9,5},{1... | collective-permute-start | bytes 663560 | tf_op jit(solution)/shard_map/ppermute | solution.py:97
  94.3 12.3 %collective-permute-start.2 = (bf16[2,48,1152]{2,1,0:T(8,128)(2,1)}, bf16[2,48,1152]{2,1,0:T(8,128)(2,1)}, u32[]{:S(2)}, u32[]{:S(2)}) collective-permute-start(bf16[2,48,1152]{2,1,0:T(8,128)(2,1)} %get-tuple-element.20), channel_id=1, source_target_pairs={{0,8},{1,9},{2,10},{3,11},{4,12},{5,13},{6,14},{7,15},{8,0},{9,1},... | collective-permute-start | bytes 663560 | tf_op jit(solution)/shard_map/ppermute | solution.py:97
  98.1 13.7 %collective-permute-start.1 = (bf16[2,48,1152]{2,1,0:T(8,128)(2,1)}, bf16[2,48,1152]{2,1,0:T(8,128)(2,1)}, u32[]{:S(2)}, u32[]{:S(2)}) collective-permute-start(bf16[2,48,1152]{2,1,0:T(8,128)(2,1)} %get-tuple-element.18), channel_id=1, source_target_pairs={{0,4},{1,5},{2,6},{3,7},{4,8},{5,9},{6,10},{7,11},{8,12},{9,13},{1... | collective-permute-start | bytes 663560 | tf_op jit(solution)/shard_map/ppermute | solution.py:97
  113.0 0.8 copy-start.2
  113.8 12.5 %copy-start.3 = (f32[2,48,1152]{2,1,0:T(8,128)S(1)}, f32[2,48,1152]{2,1,0:T(8,128)}, u32[]{:S(2)}) copy-start(f32[2,48,1152]{2,1,0:T(8,128)} %copy-done.2) | copy-start | bytes 1327108
  113.8 12.5 %collective-permute-start.4 = (f32[48,1152]{1,0:T(8,128)S(1)}, f32[48,1152]{1,0:T(8,128)S(1)}, u32[]{:S(2)}, u32[]{:S(2)}) collective-permute-start(f32[48,1152]{1,0:T(8,128)S(1)} %dynamic-slice_bitcast_fusion.1), channel_id=1, source_target_pairs={{0,2},{1,3},{2,0},{3,1},{4,6},{5,7},{6,4},{7,5},{8,10},{9,11},{10,... | collective-permute-start | bytes 663560 | tf_op jit(solution)/shard_map/ppermute | solution.py:97

commit v12 on v11

--- a/solution.py
+++ b/solution.py
@@ -121,13 +121,12 @@
 
 def body(cell_states, head_grads, group_ids, proj_weights):
     width = cell_states.shape[-1]
-    states_cols = lax.all_to_all(cell_states, "band", split_axis=2, concat_axis=1, tiled=True)
-    tables, rows, cols, _ = states_cols.shape
-    states_cols = states_cols.transpose(0, 2, 1, 3).reshape(tables * cols, rows, width)
-    grads_by_col = head_grads.transpose(2, 0, 1, 3)
-    states_cols, grads_by_col = lax.optimization_barrier((states_cols, grads_by_col))
-    grad_cols = lax.all_to_all(grads_by_col, "band", split_axis=0, concat_axis=2, tiled=True)
-    grad_cols = grad_cols.transpose(1, 0, 2, 3).reshape(tables * cols, rows, -1)
+    both = jnp.concatenate((cell_states, head_grads), axis=-1).transpose(2, 0, 1, 3)
+    both_cols = lax.all_to_all(both, "band", split_axis=0, concat_axis=2, tiled=True)
+    cols, tables, rows, _ = both_cols.shape
+    both_cols = both_cols.transpose(1, 0, 2, 3).reshape(tables * cols, rows, -1)
+    states_cols = both_cols[..., :width]
+    grad_cols = both_cols[..., width:]
     groups = group_ids.reshape(tables * cols, rows)
     scaled, inverse, normed = normalize(states_cols)
     query_cols, key_cols, value_cols = project(normed, proj_weights)

time: 155 us -> 161 us (1.039)
  blocking collectives: 24.4 us -> 33.7 us
  starting transfers between devices: 47.8 us -> 39.3 us
  local copies, waits for them, and re-layouts: 15.6 us -> 18.9 us
  other arithmetic: 5.12 us -> 7.21 us
    all_to_all x2 -> x1, starting transfers between devices: 24.1 us -> 14.4 us  [body(): lax.all_to_all(both, 'band', split_axis=0, concat_axis=2, tiled=True)]
    all_to_all x1, blocking collectives: 24.4 us -> 33.7 us  [dp_stage(): blocks = lax.all_to_all(blocks.astype(jnp.bfloat16), 'dp', 0, 0, tiled=True)]
    all_to_all x4 -> x2, local copies, waits for them, and re-layouts: 1.44 us -> 4.77 us  [body(): lax.all_to_all(both, 'band', split_axis=0, concat_axis=2, tiled=True)]
    transpose x0 -> x1, other arithmetic: none -> 2.08 us  [body(): jnp.concatenate((cell_states, head_grads), axis=-1).transpose(2, 0, 1, 3)]
    unnamed x36 -> x26, local copies, waits for them, and re-layouts: 6.79 us -> 6.12 us
    all_to_all x2 -> x1, waiting for transfers between devices: 21.4 us -> 21 us  [body(): lax.all_to_all(both, 'band', split_axis=0, concat_axis=2, tiled=True)]
  transfers between devices with their start and end apart: 8 -> 7, of which waited for: 6 -> 5; matrix products, arithmetic and copies ran while one was open for 9% -> 4% of each run, Pallas kernels for 0% -> 0%
where the time goes in v12:
time: 161 us; the launch traced here: 160 us
  starting transfers between devices  39.3 us (24%)
  waiting for transfers between devices  37.5 us (23%)
  blocking collectives  33.7 us (21%)
  matrix products  22.3 us (14%)
  local copies, waits for them, and re-layouts  18.9 us (12%)
  other arithmetic  7.21 us (4%)
    all_to_all x1, blocking collectives, dp_stage(): blocks = lax.all_to_all(blocks.astype(jnp.bfloat16), 'dp', 0, 0, tiled=True)  33.7 us
    all_to_all x1, waiting for transfers between devices, body(): lax.all_to_all(both, 'band', split_axis=0, concat_axis=2, tiled=True)  21 us
    ppermute x5, starting transfers between devices, exchange(): got = lax.ppermute(part.astype(wire), 'band', pairs)  18.5 us
    ppermute x5, waiting for transfers between devices, exchange(): got = lax.ppermute(part.astype(wire), 'band', pairs)  16.5 us
    all_to_all x1, starting transfers between devices, body(): lax.all_to_all(both, 'band', split_axis=0, concat_axis=2, tiled=True)  14.4 us
    all_to_all x1, starting transfers between devices, body(): lax.all_to_all(input_cols, 'band', split_axis=1, concat_axis=2, tiled=True)  6.36 us
    unnamed x26, local copies, waits for them, and re-layouts  6.12 us
    all_to_all x2, local copies, waits for them, and re-layouts, body(): lax.all_to_all(both, 'band', split_axis=0, concat_axis=2, tiled=True)  4.77 us
  transfers between devices with their start and end apart: 7, of which 5 were waited for; matrix products, arithmetic and copies ran while one was open for 4% of the time, Pallas kernels for 0%

profile of v12, /device:TPU:1, one launch (start us, length us, event | category | flops | bytes accessed | tf_op | source)
XLA Modules:
  0.0 160.0 jit_solution(14875815462200212349)
XLA Ops:
  2.2 1.9 %copy.21 = bf16[2,2,128,768]{3,1,0,2:T(2,128)(2,1)S(1)} copy(bf16[2,2,128,768]{3,2,1,0:T(8,128)(2,1)} %param.4) | data formatting | bytes 1572864 | tf_op args[0]
  4.1 2.1 %maximum_bitcast_fusion = bf16[128,2,2,1152]{3,2,1,0:T(2,128)(2,1)} fusion(bf16[2,2,128,384]{3,1,0,2:T(2,128)(2,1)S(1)} %copy.22, bf16[2,2,128,768]{3,1,0,2:T(2,128)(2,1)S(1)} %copy.21), kind=kLoop, calls=%fused_computation.45 | loop fusion | flops 2359296 | bytes 2359296 | tf_op jit(solution)/shard_map/transpose | solution.py:124
  6.2 14.4 %all-to-all-start = ((bf16[128,2,2,1152]{3,2,1,0:T(2,128)(2,1)}), bf16[128,2,2,1152]{3,2,1,0:T(2,128)(2,1)S(1)}, u32[]{:S(2)}, u32[]{:S(2)}) async-start(bf16[128,2,2,1152]{3,2,1,0:T(2,128)(2,1)} %maximum_bitcast_fusion), calls=%async_computation | async-start | bytes 2359296 | tf_op jit(solution)/shard_map/all_to_all | solution.py:125
  20.8 21.0 %all-to-all-done = bf16[128,2,2,1152]{3,2,1,0:T(2,128)(2,1)S(1)} async-done(((bf16[128,2,2,1152]{3,2,1,0:T(2,128)(2,1)}), bf16[128,2,2,1152]{3,2,1,0:T(2,128)(2,1)S(1)}, u32[]{:S(2)}, u32[]{:S(2)}) %all-to-all-start) | async-done | bytes 1179680 | tf_op jit(solution)/shard_map/all_to_all | solution.py:125
  43.7 2.9 %all_to_all.32 = bf16[8,2,32,1152]{3,2,0,1:T(8,128)(2,1)S(1)} reshape(bf16[8,2,16,2,1152]{4,3,2,0,1:T(2,128)(2,1)} %copy.23) | data formatting | bytes 2359296 | tf_op jit(solution)/shard_map/all_to_all | solution.py:125
  51.1 1.9 %fusion.10 = f32[16,32,6,32]{1,3,2,0:T(8,128)} fusion(pred[6,384]{1,0:T(8,128)(4,1)S(1)} %iota_compare_fusion, bf16[16,32,384]{2,1,0:T(8,128)(2,1)S(1)} %get-tuple-element.17, bf16[16,32,1152]{2,1,0:T(8,128)(2,1)S(1)} %bitcast.87), kind=kOutput, calls=%fused_computation.12 | convolution fusion | flops 76677120 | bytes 1182720 | tf_op jit(solution)/shard_map/bid,bhjd->bihj/dot_general | solution.py:58
  53.0 3.1 %fusion.93 = (f32[16,32,6]{1,2,0:T(8,128)S(1)}, f32[16,32,6,32]{1,3,2,0:T(8,128)}) fusion(pred[6,384]{1,0:T(8,128)(4,1)S(1)} %iota_compare_fusion, bf16[16,32,384]{2,1,0:T(8,128)(2,1)} %get-tuple-element.18, pred[16,32,32]{1,2,0:T(8,128)(4,1)S(1)} %compare_or_fusion, bf16[16,32,1152]{2,1,0:T(8,128)(2,1)} %bitcast.98), kind=kOutput, calls=%fused_computation.103 | convolution fusion | flops 77070368 | bytes 1210624 | tf_op jit(solution)/shard_map/sub | solution.py:52
  56.1 3.0 %fusion.46 = bf16[16,32,384]{2,1,0:T(8,128)(2,1)} fusion(pred[6,384]{1,0:T(8,128)(4,1)S(1)} %iota_compare_fusion, bf16[16,32,384]{2,1,0:T(8,128)(2,1)} %slice.23, f32[16,32,6,32]{1,3,2,0:T(8,128)} %get-tuple-element.21, f32[16,32,6]{1,2,0:T(8,128)S(1)} %get-tuple-element.20), kind=kOutput, calls=%fused_computation.43 | convolution fusion | flops 77070336 | bytes 1194240 | tf_op jit(solution)/shard_map/bihj,bhid->bjd/dot_general | solution.py:55
  59.1 4.7 %fusion.43 = bf16[16,32,384]{2,1,0:T(8,128)(2,1)} fusion(pred[6,384]{1,0:T(8,128)(4,1)S(1)} %iota_compare_fusion, bf16[16,32,384]{2,1,0:T(8,128)(2,1)} %get-tuple-element.18, f32[16,32,6,32]{1,3,2,0:T(8,128)} %fusion.10, f32[16,32,6,32]{1,3,2,0:T(8,128)} %get-tuple-element.21, f32[16,32,6]{1,2,0:T(8,128)S(1)} %get-tuple-element.20), kind=kOutput, calls=%fused_computation.42 | convolution fusion | flops 77564960 | bytes 1587456 | tf_op jit(solution)/shard_map/bihj,bhjd->bid/dot_general | solution.py:63
  63.8 4.5 %fusion.49 = bf16[16,32,384]{2,1,0:T(8,128)(2,1)} fusion(pred[6,384]{1,0:T(8,128)(4,1)S(1)} %iota_compare_fusion, bf16[16,32,384]{2,1,0:T(8,128)(2,1)S(1)} %get-tuple-element.19, f32[16,32,6,32]{1,3,2,0:T(8,128)} %fusion.10, f32[16,32,6,32]{1,3,2,0:T(8,128)} %get-tuple-element.21, f32[16,32,6]{1,2,0:T(8,128)S(1)} %get-tuple-element.20), kind=kOutput, calls=%fused_computation.44 | convolution fusion | flops 77564960 | bytes 1587456 | tf_op jit(solution)/shard_map/bihj,bhid->bjd/dot_general | solution.py:66
  68.3 2.7 %fusion.23 = (f32[16,32]{1,0:T(8,128)S(1)}, f32[16,32,768]{2,1,0:T(8,128)S(1)}) fusion(f32[16,32]{1,0:T(8,128)S(1)} %add_rsqrt_fusion, bf16[16,32,1152]{2,1,0:T(8,128)(2,1)S(1)} %bitcast.88, bf16[768,1152]{1,0:T(8,128)(2,1)S(1)} %copy-done, bf16[16,32,384]{2,1,0:T(8,128)(2,1)} %fusion.46, bf16[16,32,384]{2,1,0:T(8,128)(2,1)} %fusion.49, ...), kind=kOutput, calls=%fused_computation.29 | convolution fusion | flops 911080960 | bytes 5312512 | tf_op jit(solution)/shard_map/dot_general | solution.py:78
  74.4 2.7 %collective-permute-start = (f32[4,2,48,1152]{3,2,1,0:T(8,128)S(1)}, f32[4,2,48,1152]{3,2,1,0:T(8,128)}, u32[]{:S(2)}, u32[]{:S(2)}) collective-permute-start(f32[4,2,48,1152]{3,2,1,0:T(8,128)S(1)} %dynamic-slice_bitcast_fusion), channel_id=1, source_target_pairs={{0,1},{1,0},{2,3},{3,2},{4,5},{5,4},{6,7},{7,6},{8,9},{9,8},{10,11... | collective-permute-start | bytes 5308424 | tf_op jit(solution)/shard_map/ppermute | solution.py:97
  77.2 6.4 %all-to-all-start.1 = ((bf16[2,32,8,768]{3,2,0,1:T(8,128)(2,1)}), bf16[2,32,8,768]{3,2,0,1:T(8,128)(2,1)}, u32[]{:S(2)}, u32[]{:S(2)}) async-start(bf16[2,32,8,768]{3,2,0,1:T(8,128)(2,1)} %bitcast.83), calls=%async_computation.1 | async-start | bytes 1572864 | tf_op jit(solution)/shard_map/all_to_all | solution.py:140
  83.6 2.2 %bitcast_add_fusion = f32[4,2,48,1152]{3,2,1,0:T(8,128)S(1)} fusion(f32[4,2,48,1152]{3,2,1,0:T(8,128)} %collective-permute-done, f32[4,2,2,48,1152]{4,3,2,1,0:T(8,128)} %bitcast.92, s32[]{:T(128)S(6)} %select_n.104), kind=kLoop, calls=%fused_computation.24 | loop fusion | flops 442368 | bytes 5308420 | tf_op jit(solution)/shard_map/add | solution.py:98
  86.7 4.5 %collective-permute-start.3 = (bf16[2,48,1152]{2,1,0:T(8,128)(2,1)}, bf16[2,48,1152]{2,1,0:T(8,128)(2,1)}, u32[]{:S(2)}, u32[]{:S(2)}) collective-permute-start(bf16[2,48,1152]{2,1,0:T(8,128)(2,1)} %get-tuple-element.15), channel_id=1, source_target_pairs={{0,12},{1,13},{2,14},{3,15},{4,0},{5,1},{6,2},{7,3},{8,4},{9,5},{1... | collective-permute-start | bytes 663560 | tf_op jit(solution)/shard_map/ppermute | solution.py:97
  91.2 3.6 %collective-permute-start.2 = (bf16[2,48,1152]{2,1,0:T(8,128)(2,1)}, bf16[2,48,1152]{2,1,0:T(8,128)(2,1)}, u32[]{:S(2)}, u32[]{:S(2)}) collective-permute-start(bf16[2,48,1152]{2,1,0:T(8,128)(2,1)} %get-tuple-element.16), channel_id=1, source_target_pairs={{0,8},{1,9},{2,10},{3,11},{4,12},{5,13},{6,14},{7,15},{8,0},{9,1},... | collective-permute-start | bytes 663560 | tf_op jit(solution)/shard_map/ppermute | solution.py:97
  94.8 1.9 %collective-permute-start.1 = (bf16[2,48,1152]{2,1,0:T(8,128)(2,1)}, bf16[2,48,1152]{2,1,0:T(8,128)(2,1)}, u32[]{:S(2)}, u32[]{:S(2)}) collective-permute-start(bf16[2,48,1152]{2,1,0:T(8,128)(2,1)} %get-tuple-element.14), channel_id=1, source_target_pairs={{0,4},{1,5},{2,6},{3,7},{4,8},{5,9},{6,10},{7,11},{8,12},{9,13},{1... | collective-permute-start | bytes 663560 | tf_op jit(solution)/shard_map/ppermute | solution.py:97
  96.8 3.7 %collective-permute-done.3 = bf16[2,48,1152]{2,1,0:T(8,128)(2,1)} collective-permute-done((bf16[2,48,1152]{2,1,0:T(8,128)(2,1)}, bf16[2,48,1152]{2,1,0:T(8,128)(2,1)}, u32[]{:S(2)}, u32[]{:S(2)}) %collective-permute-start.3) | collective-permute-done | bytes 221216 | tf_op jit(solution)/shard_map/ppermute | solution.py:97
  100.5 2.8 %collective-permute-done.2 = bf16[2,48,1152]{2,1,0:T(8,128)(2,1)} collective-permute-done((bf16[2,48,1152]{2,1,0:T(8,128)(2,1)}, bf16[2,48,1152]{2,1,0:T(8,128)(2,1)}, u32[]{:S(2)}, u32[]{:S(2)}) %collective-permute-start.2) | collective-permute-done | bytes 221216 | tf_op jit(solution)/shard_map/ppermute | solution.py:97
  103.3 5.3 %collective-permute-done.1 = bf16[2,48,1152]{2,1,0:T(8,128)(2,1)} collective-permute-done((bf16[2,48,1152]{2,1,0:T(8,128)(2,1)}, bf16[2,48,1152]{2,1,0:T(8,128)(2,1)}, u32[]{:S(2)}, u32[]{:S(2)}) %collective-permute-start.1) | collective-permute-done | bytes 221216 | tf_op jit(solution)/shard_map/ppermute | solution.py:97
  110.6 5.8 %collective-permute-start.4 = (f32[48,1152]{1,0:T(8,128)S(1)}, f32[48,1152]{1,0:T(8,128)S(1)}, u32[]{:S(2)}, u32[]{:S(2)}) collective-permute-start(f32[48,1152]{1,0:T(8,128)S(1)} %dynamic-slice_bitcast_fusion.1), channel_id=1, source_target_pairs={{0,2},{1,3},{2,0},{3,1},{4,6},{5,7},{6,4},{7,5},{8,10},{9,11},{10,... | collective-permute-start | bytes 663560 | tf_op jit(solution)/shard_map/ppermute | solution.py:97
  116.4 2.1 %copy.41 = bf16[2,2,16,8,768]{4,3,2,1,0:T(8,128)(2,1)} copy(bf16[2,2,16,8,768]{4,3,0,1,2:T(8,128)(2,1)} %bitcast.33) | data formatting | bytes 1572864 | tf_op jit(solution)/shard_map/all_to_all | solution.py:140
  118.5 4.6 %collective-permute-done.4 = f32[48,1152]{1,0:T(8,128)S(1)} collective-permute-done((f32[48,1152]{1,0:T(8,128)S(1)}, f32[48,1152]{1,0:T(8,128)S(1)}, u32[]{:S(2)}, u32[]{:S(2)}) %collective-permute-start.4) | collective-permute-done | bytes 221216 | tf_op jit(solution)/shard_map/ppermute | solution.py:97
  125.2 33.7 %all_to_all.41 = bf16[32,2,864]{2,1,0:T(2,128)(2,1)S(1)} all-to-all(bf16[32,2,864]{2,1,0:T(2,128)(2,1)S(1)} %reshape.110), channel_id=1, replica_groups=mesh['dp'=32,'band'=16] {'dp'}, dimensions={0} | all-to-all | bytes 221184 | tf_op jit(solution)/shard_map/all_to_all | solution.py:118
  (51 shorter events, 17.3 us)
Async XLA Ops:
  0.6 47.3 %copy-start = (bf16[768,1152]{1,0:T(8,128)(2,1)S(1)}, bf16[768,1152]{1,0:T(8,128)(2,1)}, u32[]{:S(2)}) copy-start(bf16[768,1152]{1,0:T(8,128)(2,1)} %param.7) | copy-start | bytes 5308420
  6.2 14.4 %copy-start.7 = (s32[2,8,32]{2,1,0:T(8,128)S(1)}, s32[2,8,32]{2,1,0:T(8,128)}, u32[]{:S(2)}) copy-start(s32[2,8,32]{2,1,0:T(8,128)} %param.6) | copy-start | bytes 6148
  6.2 35.6 %all-to-all-start = ((bf16[128,2,2,1152]{3,2,1,0:T(2,128)(2,1)}), bf16[128,2,2,1152]{3,2,1,0:T(2,128)(2,1)S(1)}, u32[]{:S(2)}, u32[]{:S(2)}) async-start(bf16[128,2,2,1152]{3,2,1,0:T(2,128)(2,1)} %maximum_bitcast_fusion), calls=%async_computation | async-start | bytes 2359296 | tf_op jit(solution)/shard_map/all_to_all | solution.py:125
  47.9 1.2 copy-start.5
  49.1 1.0 copy-start.4
  68.3 2.7 %copy-start.6 = (bf16[16,32,768]{2,1,0:T(8,128)(2,1)S(1)}, bf16[16,32,768]{2,1,0:T(8,128)(2,1)}, u32[]{:S(2)}) copy-start(bf16[16,32,768]{2,1,0:T(8,128)(2,1)} %copy-done.5) | copy-start | bytes 2359300
  68.3 2.7 %copy-start.8 = (bf16[16,32,384]{2,1,0:T(8,128)(2,1)S(1)}, bf16[16,32,384]{2,1,0:T(8,128)(2,1)}, u32[]{:S(2)}) copy-start(bf16[16,32,384]{2,1,0:T(8,128)(2,1)} %fusion.46) | copy-start | bytes 1179652
  68.3 2.7 %copy-start.9 = (bf16[16,32,384]{2,1,0:T(8,128)(2,1)S(1)}, bf16[16,32,384]{2,1,0:T(8,128)(2,1)}, u32[]{:S(2)}) copy-start(bf16[16,32,384]{2,1,0:T(8,128)(2,1)} %fusion.43) | copy-start | bytes 1179652
  68.3 2.7 %copy-start.10 = (bf16[16,32,384]{2,1,0:T(8,128)(2,1)S(1)}, bf16[16,32,384]{2,1,0:T(8,128)(2,1)}, u32[]{:S(2)}) copy-start(bf16[16,32,384]{2,1,0:T(8,128)(2,1)} %fusion.49) | copy-start | bytes 1179652
  72.2 2.0 %copy-start.1 = (f32[768,1152]{1,0:T(8,128)}, f32[768,1152]{1,0:T(8,128)S(1)}, u32[]{:S(2)}) copy-start(f32[768,1152]{1,0:T(8,128)S(1)} %convolution_bitcast_fusion) | copy-start | bytes 10616836
  74.4 9.2 %collective-permute-start = (f32[4,2,48,1152]{3,2,1,0:T(8,128)S(1)}, f32[4,2,48,1152]{3,2,1,0:T(8,128)}, u32[]{:S(2)}, u32[]{:S(2)}) collective-permute-start(f32[4,2,48,1152]{3,2,1,0:T(8,128)S(1)} %dynamic-slice_bitcast_fusion), channel_id=1, source_target_pairs={{0,1},{1,0},{2,3},{3,2},{4,5},{5,4},{6,7},{7,6},{8,9},{9,8},{10,11... | collective-permute-start | bytes 5308424 | tf_op jit(solution)/shard_map/ppermute | solution.py:97
  77.2 39.2 %all-to-all-start.1 = ((bf16[2,32,8,768]{3,2,0,1:T(8,128)(2,1)}), bf16[2,32,8,768]{3,2,0,1:T(8,128)(2,1)}, u32[]{:S(2)}, u32[]{:S(2)}) async-start(bf16[2,32,8,768]{3,2,0,1:T(8,128)(2,1)} %bitcast.83), calls=%async_computation.1 | async-start | bytes 1572864 | tf_op jit(solution)/shard_map/all_to_all | solution.py:140
  86.7 13.8 %collective-permute-start.3 = (bf16[2,48,1152]{2,1,0:T(8,128)(2,1)}, bf16[2,48,1152]{2,1,0:T(8,128)(2,1)}, u32[]{:S(2)}, u32[]{:S(2)}) collective-permute-start(bf16[2,48,1152]{2,1,0:T(8,128)(2,1)} %get-tuple-element.15), channel_id=1, source_target_pairs={{0,12},{1,13},{2,14},{3,15},{4,0},{5,1},{6,2},{7,3},{8,4},{9,5},{1... | collective-permute-start | bytes 663560 | tf_op jit(solution)/shard_map/ppermute | solution.py:97
  91.2 12.1 %collective-permute-start.2 = (bf16[2,48,1152]{2,1,0:T(8,128)(2,1)}, bf16[2,48,1152]{2,1,0:T(8,128)(2,1)}, u32[]{:S(2)}, u32[]{:S(2)}) collective-permute-start(bf16[2,48,1152]{2,1,0:T(8,128)(2,1)} %get-tuple-element.16), channel_id=1, source_target_pairs={{0,8},{1,9},{2,10},{3,11},{4,12},{5,13},{6,14},{7,15},{8,0},{9,1},... | collective-permute-start | bytes 663560 | tf_op jit(solution)/shard_map/ppermute | solution.py:97
  94.8 13.8 %collective-permute-start.1 = (bf16[2,48,1152]{2,1,0:T(8,128)(2,1)}, bf16[2,48,1152]{2,1,0:T(8,128)(2,1)}, u32[]{:S(2)}, u32[]{:S(2)}) collective-permute-start(bf16[2,48,1152]{2,1,0:T(8,128)(2,1)} %get-tuple-element.14), channel_id=1, source_target_pairs={{0,4},{1,5},{2,6},{3,7},{4,8},{5,9},{6,10},{7,11},{8,12},{9,13},{1... | collective-permute-start | bytes 663560 | tf_op jit(solution)/shard_map/ppermute | solution.py:97
  109.8 0.8 copy-start.2
  110.6 12.5 %copy-start.3 = (f32[2,48,1152]{2,1,0:T(8,128)S(1)}, f32[2,48,1152]{2,1,0:T(8,128)}, u32[]{:S(2)}) copy-start(f32[2,48,1152]{2,1,0:T(8,128)} %copy-done.2) | copy-start | bytes 1327108
  110.6 12.5 %collective-permute-start.4 = (f32[48,1152]{1,0:T(8,128)S(1)}, f32[48,1152]{1,0:T(8,128)S(1)}, u32[]{:S(2)}, u32[]{:S(2)}) collective-permute-start(f32[48,1152]{1,0:T(8,128)S(1)} %dynamic-slice_bitcast_fusion.1), channel_id=1, source_target_pairs={{0,2},{1,3},{2,0},{3,1},{4,6},{5,7},{6,4},{7,5},{8,10},{9,11},{10,... | collective-permute-start | bytes 663560 | tf_op jit(solution)/shard_map/ppermute | solution.py:97

commit v13 on v11

--- a/solution.py
+++ b/solution.py
@@ -107,7 +107,7 @@
     blocks = partial_w.reshape(n_band // 4, 2, 2, rows, d_out)
     blocks = exchange(blocks, 2, band % 2, 1, 2)
     blocks = exchange(blocks, 0, band // 4, 4, n_band // 4, jnp.bfloat16)
-    return exchange(blocks, 0, (band // 2) % 2, 2, 2)
+    return exchange(blocks, 0, (band // 2) % 2, 2, 2, jnp.bfloat16)
 
 
 def dp_stage(blocks):

time: 155 us -> 153 us (0.987)
  waiting for transfers between devices: 38.1 us -> 35.7 us
    ppermute x5, waiting for transfers between devices: 16.7 us -> 14.3 us  [exchange(): got = lax.ppermute(part.astype(wire), 'band', pairs)]
where the time goes in v13:
time: 153 us; the launch traced here: 152 us
  starting transfers between devices  47.8 us (31%)
  waiting for transfers between devices  35.7 us (23%)
  blocking collectives  24.4 us (16%)
  matrix products  21.8 us (14%)
  local copies, waits for them, and re-layouts  15.6 us (10%)
  other arithmetic  5.11 us (3%)
    all_to_all x1, blocking collectives, dp_stage(): blocks = lax.all_to_all(blocks.astype(jnp.bfloat16), 'dp', 0, 0, tiled=True)  24.4 us
    ppermute x5, starting transfers between devices, exchange(): got = lax.ppermute(part.astype(wire), 'band', pairs)  18.7 us
    all_to_all x1, waiting for transfers between devices, body(): lax.all_to_all(cell_states, 'band', split_axis=2, concat_axis=1, tiled=True)  15.6 us
    all_to_all x1, starting transfers between devices, body(): lax.all_to_all(cell_states, 'band', split_axis=2, concat_axis=1, tiled=True)  14.4 us
    ppermute x5, waiting for transfers between devices, exchange(): got = lax.ppermute(part.astype(wire), 'band', pairs)  14.3 us
    all_to_all x1, starting transfers between devices, body(): lax.all_to_all(grads_by_col, 'band', split_axis=0, concat_axis=2, tiled=T...  9.75 us
    unnamed x36, local copies, waits for them, and re-layouts  6.79 us
    all_to_all x1, waiting for transfers between devices, body(): lax.all_to_all(grads_by_col, 'band', split_axis=0, concat_axis=2, tiled=T...  5.78 us
  transfers between devices with their start and end apart: 8, of which 6 were waited for; matrix products, arithmetic and copies ran while one was open for 9% of the time, Pallas kernels for 0%

profile of v13, /device:TPU:1, one launch (start us, length us, event | category | flops | bytes accessed | tf_op | source)
XLA Modules:
  0.0 151.5 jit_solution(7618267147864943870)
XLA Ops:
  0.7 3.0 %copy.24 = bf16[2,2,128,768]{3,1,0,2:T(2,128)(2,1)} copy(bf16[2,2,128,768]{3,2,1,0:T(8,128)(2,1)} %param.4) | data formatting | bytes 1572864 | tf_op args[0]
  3.6 14.4 %all-to-all-start = ((bf16[2,2,128,768]{3,1,0,2:T(2,128)(2,1)}), bf16[2,2,128,768]{3,1,0,2:T(2,128)(2,1)S(1)}, u32[]{:S(2)}, u32[]{:S(2)}) async-start(bf16[2,2,128,768]{3,1,0,2:T(2,128)(2,1)} %copy.24), calls=%async_computation | async-start | bytes 1572864 | tf_op jit(solution)/shard_map/all_to_all | solution.py:124
  19.4 15.6 %all-to-all-done = bf16[2,2,128,768]{3,1,0,2:T(2,128)(2,1)S(1)} async-done(((bf16[2,2,128,768]{3,1,0,2:T(2,128)(2,1)}), bf16[2,2,128,768]{3,1,0,2:T(2,128)(2,1)S(1)}, u32[]{:S(2)}, u32[]{:S(2)}) %all-to-all-start) | async-done | bytes 786464 | tf_op jit(solution)/shard_map/all_to_all | solution.py:124
  36.3 9.8 %all-to-all-start.1 = ((bf16[128,2,2,384]{3,2,1,0:T(2,128)(2,1)}), bf16[128,2,2,384]{3,2,1,0:T(2,128)(2,1)S(1)}, u32[]{:S(2)}, u32[]{:S(2)}) async-start(bf16[128,2,2,384]{3,2,1,0:T(2,128)(2,1)} %bitcast.101), calls=%async_computation.1 | async-start | bytes 786432 | tf_op jit(solution)/shard_map/all_to_all | solution.py:129
  49.5 3.1 %fusion.92 = (f32[16,32,6]{1,2,0:T(8,128)S(1)}, f32[16,32,6,32]{1,3,2,0:T(8,128)}) fusion(pred[6,384]{1,0:T(8,128)(4,1)S(1)} %iota_compare_fusion, bf16[16,32,384]{2,1,0:T(8,128)(2,1)S(1)} %get-tuple-element.22, pred[16,32,32]{1,2,0:T(8,128)(4,1)S(1)} %compare_or_fusion, bf16[16,32,1152]{2,1,0:T(8,128)(2,1)} %bitcast.107), kind=kOutput, calls=%fused_computation.102 | convolution fusion | flops 77070368 | bytes 1210624 | tf_op jit(solution)/shard_map/sub | solution.py:52
  52.7 5.8 %all-to-all-done.1 = bf16[128,2,2,384]{3,2,1,0:T(2,128)(2,1)S(1)} async-done(((bf16[128,2,2,384]{3,2,1,0:T(2,128)(2,1)}), bf16[128,2,2,384]{3,2,1,0:T(2,128)(2,1)S(1)}, u32[]{:S(2)}, u32[]{:S(2)}) %all-to-all-start.1) | async-done | bytes 393248 | tf_op jit(solution)/shard_map/all_to_all | solution.py:129
  58.9 3.0 %fusion.10 = f32[16,32,6,32]{1,3,2,0:T(8,128)} fusion(bf16[16,32,384,1]{2,1,3,0:T(8,128)(2,1)S(1)} %bitcast.110, pred[6,384]{1,0:T(8,128)(4,1)S(1)} %iota_compare_fusion, bf16[16,32,384]{2,1,0:T(8,128)(2,1)} %get-tuple-element.21), kind=kOutput, calls=%fused_computation.12 | convolution fusion | flops 76677120 | bytes 1181952 | tf_op jit(solution)/shard_map/bid,bhjd->bihj/dot_general | solution.py:58
  63.5 4.6 %fusion.43 = bf16[16,32,384]{2,1,0:T(8,128)(2,1)} fusion(pred[6,384]{1,0:T(8,128)(4,1)S(1)} %iota_compare_fusion, bf16[16,32,384]{2,1,0:T(8,128)(2,1)S(1)} %copy-done.9, f32[16,32,6,32]{1,3,2,0:T(8,128)} %fusion.10, f32[16,32,6,32]{1,3,2,0:T(8,128)} %get-tuple-element.25, f32[16,32,6]{1,2,0:T(8,128)S(1)} %get-tuple-element.24), kind=kOutput, calls=%fused_computation.42 | convolution fusion | flops 77564960 | bytes 1587456 | tf_op jit(solution)/shard_map/bihj,bhjd->bid/dot_general | solution.py:63
  68.1 4.6 %fusion.49 = bf16[16,32,384]{2,1,0:T(8,128)(2,1)} fusion(pred[6,384]{1,0:T(8,128)(4,1)S(1)} %iota_compare_fusion, bf16[16,32,384]{2,1,0:T(8,128)(2,1)S(1)} %copy-done.7, f32[16,32,6,32]{1,3,2,0:T(8,128)} %fusion.10, f32[16,32,6,32]{1,3,2,0:T(8,128)} %get-tuple-element.25, f32[16,32,6]{1,2,0:T(8,128)S(1)} %get-tuple-element.24), kind=kOutput, calls=%fused_computation.44 | convolution fusion | flops 77564960 | bytes 1587456 | tf_op jit(solution)/shard_map/bihj,bhid->bjd/dot_general | solution.py:66
  72.7 2.5 %fusion.23 = (f32[16,32]{1,0:T(8,128)S(1)}, f32[16,32,768]{2,1,0:T(8,128)S(1)}) fusion(bf16[16,32,768]{2,1,0:T(8,128)(2,1)S(1)} %bitcast.95, f32[16,32]{1,0:T(8,128)S(1)} %add_rsqrt_fusion, bf16[768,1152]{1,0:T(8,128)(2,1)S(1)} %copy-done, bf16[16,32,384]{2,1,0:T(8,128)(2,1)S(1)} %copy-done.13, bf16[16,32,384]{2,1,0:T(8,128)(2,1)} %fusion.49, ...), kind=kOutput, calls=%fused_computation.29 | convolution fusion | flops 911080960 | bytes 5312512 | tf_op jit(solution)/shard_map/dot_general | solution.py:78
  76.9 1.7 %copy.47 = bf16[2,8,32,768]{3,1,0,2:T(8,128)(2,1)} copy(bf16[2,8,32,768]{3,2,1,0:T(8,128)(2,1)S(1)} %bitcast.100) | data formatting | bytes 1572864 | tf_op jit(solution)/shard_map/reshape | solution.py:139
  78.6 3.1 %collective-permute-start = (f32[4,2,48,1152]{3,2,1,0:T(8,128)S(1)}, f32[4,2,48,1152]{3,2,1,0:T(8,128)}, u32[]{:S(2)}, u32[]{:S(2)}) collective-permute-start(f32[4,2,48,1152]{3,2,1,0:T(8,128)S(1)} %dynamic-slice_bitcast_fusion), channel_id=1, source_target_pairs={{0,1},{1,0},{2,3},{3,2},{4,5},{5,4},{6,7},{7,6},{8,9},{9,8},{10,11... | collective-permute-start | bytes 5308424 | tf_op jit(solution)/shard_map/ppermute | solution.py:97
  81.8 4.9 %all-to-all-start.2 = ((bf16[2,32,8,768]{3,2,0,1:T(8,128)(2,1)}), bf16[2,32,8,768]{3,2,0,1:T(8,128)(2,1)}, u32[]{:S(2)}, u32[]{:S(2)}) async-start(bf16[2,32,8,768]{3,2,0,1:T(8,128)(2,1)} %bitcast.91), calls=%async_computation.2 | async-start | bytes 1572864 | tf_op jit(solution)/shard_map/all_to_all | solution.py:141
  86.7 2.2 %bitcast_add_fusion = f32[4,2,48,1152]{3,2,1,0:T(8,128)S(1)} fusion(f32[4,2,48,1152]{3,2,1,0:T(8,128)} %collective-permute-done, f32[4,2,2,48,1152]{4,3,2,1,0:T(8,128)} %bitcast.98, s32[]{:T(128)S(6)} %select_n.104), kind=kLoop, calls=%fused_computation.24 | loop fusion | flops 442368 | bytes 5308420 | tf_op jit(solution)/shard_map/add | solution.py:98
  89.8 4.5 %collective-permute-start.3 = (bf16[2,48,1152]{2,1,0:T(8,128)(2,1)}, bf16[2,48,1152]{2,1,0:T(8,128)(2,1)}, u32[]{:S(2)}, u32[]{:S(2)}) collective-permute-start(bf16[2,48,1152]{2,1,0:T(8,128)(2,1)} %get-tuple-element.19), channel_id=1, source_target_pairs={{0,12},{1,13},{2,14},{3,15},{4,0},{5,1},{6,2},{7,3},{8,4},{9,5},{1... | collective-permute-start | bytes 663560 | tf_op jit(solution)/shard_map/ppermute | solution.py:97
  94.3 3.8 %collective-permute-start.2 = (bf16[2,48,1152]{2,1,0:T(8,128)(2,1)}, bf16[2,48,1152]{2,1,0:T(8,128)(2,1)}, u32[]{:S(2)}, u32[]{:S(2)}) collective-permute-start(bf16[2,48,1152]{2,1,0:T(8,128)(2,1)} %get-tuple-element.20), channel_id=1, source_target_pairs={{0,8},{1,9},{2,10},{3,11},{4,12},{5,13},{6,14},{7,15},{8,0},{9,1},... | collective-permute-start | bytes 663560 | tf_op jit(solution)/shard_map/ppermute | solution.py:97
  98.1 1.9 %collective-permute-start.1 = (bf16[2,48,1152]{2,1,0:T(8,128)(2,1)}, bf16[2,48,1152]{2,1,0:T(8,128)(2,1)}, u32[]{:S(2)}, u32[]{:S(2)}) collective-permute-start(bf16[2,48,1152]{2,1,0:T(8,128)(2,1)} %get-tuple-element.18), channel_id=1, source_target_pairs={{0,4},{1,5},{2,6},{3,7},{4,8},{5,9},{6,10},{7,11},{8,12},{9,13},{1... | collective-permute-start | bytes 663560 | tf_op jit(solution)/shard_map/ppermute | solution.py:97
  100.1 3.7 %collective-permute-done.3 = bf16[2,48,1152]{2,1,0:T(8,128)(2,1)} collective-permute-done((bf16[2,48,1152]{2,1,0:T(8,128)(2,1)}, bf16[2,48,1152]{2,1,0:T(8,128)(2,1)}, u32[]{:S(2)}, u32[]{:S(2)}) %collective-permute-start.3) | collective-permute-done | bytes 221216 | tf_op jit(solution)/shard_map/ppermute | solution.py:97
  103.8 2.8 %collective-permute-done.2 = bf16[2,48,1152]{2,1,0:T(8,128)(2,1)} collective-permute-done((bf16[2,48,1152]{2,1,0:T(8,128)(2,1)}, bf16[2,48,1152]{2,1,0:T(8,128)(2,1)}, u32[]{:S(2)}, u32[]{:S(2)}) %collective-permute-start.2) | collective-permute-done | bytes 221216 | tf_op jit(solution)/shard_map/ppermute | solution.py:97
  106.6 5.2 %collective-permute-done.1 = bf16[2,48,1152]{2,1,0:T(8,128)(2,1)} collective-permute-done((bf16[2,48,1152]{2,1,0:T(8,128)(2,1)}, bf16[2,48,1152]{2,1,0:T(8,128)(2,1)}, u32[]{:S(2)}, u32[]{:S(2)}) %collective-permute-start.1) | collective-permute-done | bytes 221216 | tf_op jit(solution)/shard_map/ppermute | solution.py:97
  113.8 5.4 %collective-permute-start.4 = (bf16[48,1152]{1,0:T(8,128)(2,1)S(1)}, bf16[48,1152]{1,0:T(8,128)(2,1)S(1)}, u32[]{:S(2)}, u32[]{:S(2)}) collective-permute-start(bf16[48,1152]{1,0:T(8,128)(2,1)S(1)} %fusion.75), channel_id=1, source_target_pairs={{0,2},{1,3},{2,0},{3,1},{4,6},{5,7},{6,4},{7,5},{8,10},{9,11},{10,... | collective-permute-start | bytes 331784 | tf_op jit(solution)/shard_map/ppermute | solution.py:97
  119.3 2.1 %copy.46 = bf16[2,2,16,8,768]{4,3,2,1,0:T(8,128)(2,1)} copy(bf16[2,2,16,8,768]{4,3,0,1,2:T(8,128)(2,1)} %bitcast.37) | data formatting | bytes 1572864 | tf_op jit(solution)/shard_map/all_to_all | solution.py:141
  121.3 2.6 %collective-permute-done.4 = bf16[48,1152]{1,0:T(8,128)(2,1)S(1)} collective-permute-done((bf16[48,1152]{1,0:T(8,128)(2,1)S(1)}, bf16[48,1152]{1,0:T(8,128)(2,1)S(1)}, u32[]{:S(2)}, u32[]{:S(2)}) %collective-permute-start.4) | collective-permute-done | bytes 110624 | tf_op jit(solution)/shard_map/ppermute | solution.py:97
  126.0 24.4 %all_to_all.59 = bf16[32,2,864]{2,1,0:T(2,128)(2,1)S(1)} all-to-all(bf16[32,2,864]{2,1,0:T(2,128)(2,1)S(1)} %reshape.115), channel_id=1, replica_groups=mesh['dp'=32,'band'=16] {'dp'}, dimensions={0} | all-to-all | bytes 221184 | tf_op jit(solution)/shard_map/all_to_all | solution.py:118
  (63 shorter events, 15.8 us)
Async XLA Ops:
  0.6 45.6 %copy-start = (bf16[768,1152]{1,0:T(8,128)(2,1)S(1)}, bf16[768,1152]{1,0:T(8,128)(2,1)}, u32[]{:S(2)}) copy-start(bf16[768,1152]{1,0:T(8,128)(2,1)} %param.7) | copy-start | bytes 5308420
  0.6 17.4 %copy-start.10 = (bf16[2,2,128,384]{3,2,1,0:T(8,128)(2,1)S(1)}, bf16[2,2,128,384]{3,2,1,0:T(8,128)(2,1)}, u32[]{:S(2)}) copy-start(bf16[2,2,128,384]{3,2,1,0:T(8,128)(2,1)} %param.5) | copy-start | bytes 1179652
  3.6 15.6 %copy-start.11 = (s32[2,8,32]{2,1,0:T(8,128)S(1)}, s32[2,8,32]{2,1,0:T(8,128)}, u32[]{:S(2)}) copy-start(s32[2,8,32]{2,1,0:T(8,128)} %param.6) | copy-start | bytes 6148
  3.6 31.4 %all-to-all-start = ((bf16[2,2,128,768]{3,1,0,2:T(2,128)(2,1)}), bf16[2,2,128,768]{3,1,0,2:T(2,128)(2,1)S(1)}, u32[]{:S(2)}, u32[]{:S(2)}) async-start(bf16[2,2,128,768]{3,1,0,2:T(2,128)(2,1)} %copy.24), calls=%async_computation | async-start | bytes 1572864 | tf_op jit(solution)/shard_map/all_to_all | solution.py:124
  36.3 22.1 %all-to-all-start.1 = ((bf16[128,2,2,384]{3,2,1,0:T(2,128)(2,1)}), bf16[128,2,2,384]{3,2,1,0:T(2,128)(2,1)S(1)}, u32[]{:S(2)}, u32[]{:S(2)}) async-start(bf16[128,2,2,384]{3,2,1,0:T(2,128)(2,1)} %bitcast.101), calls=%async_computation.1 | async-start | bytes 786432 | tf_op jit(solution)/shard_map/all_to_all | solution.py:129
  46.2 1.2 copy-start.5
  47.5 1.0 copy-start.4
  49.5 3.1 %copy-start.8 = (bf16[16,32,384]{2,1,0:T(8,128)(2,1)}, bf16[16,32,384]{2,1,0:T(8,128)(2,1)S(1)}, u32[]{:S(2)}) copy-start(bf16[16,32,384]{2,1,0:T(8,128)(2,1)S(1)} %get-tuple-element.22) | copy-start | bytes 1179652
  58.9 3.0 %copy-start.12 = (f32[16,32,6,32]{1,3,2,0:T(8,128)S(1)}, f32[16,32,6,32]{1,3,2,0:T(8,128)}, u32[]{:S(2)}) copy-start(f32[16,32,6,32]{1,3,2,0:T(8,128)} %get-tuple-element.25) | copy-start | bytes 1179652
  61.9 1.6 %copy-start.9 = (bf16[16,32,384]{2,1,0:T(8,128)(2,1)S(1)}, bf16[16,32,384]{2,1,0:T(8,128)(2,1)}, u32[]{:S(2)}) copy-start(bf16[16,32,384]{2,1,0:T(8,128)(2,1)} %copy-done.8) | copy-start | bytes 1179652
  63.5 4.6 %copy-start.7 = (bf16[16,32,384]{2,1,0:T(8,128)(2,1)S(1)}, bf16[16,32,384]{2,1,0:T(8,128)(2,1)}, u32[]{:S(2)}) copy-start(bf16[16,32,384]{2,1,0:T(8,128)(2,1)} %get-tuple-element.23) | copy-start | bytes 1179652
  68.1 4.6 %copy-start.13 = (bf16[16,32,384]{2,1,0:T(8,128)(2,1)S(1)}, bf16[16,32,384]{2,1,0:T(8,128)(2,1)}, u32[]{:S(2)}) copy-start(bf16[16,32,384]{2,1,0:T(8,128)(2,1)} %fusion.46) | copy-start | bytes 1179652
  72.7 2.6 %copy-start.6 = (bf16[16,32,768]{2,1,0:T(8,128)(2,1)S(1)}, bf16[16,32,768]{2,1,0:T(8,128)(2,1)}, u32[]{:S(2)}) copy-start(bf16[16,32,768]{2,1,0:T(8,128)(2,1)} %copy-done.5) | copy-start | bytes 2359300
  72.7 2.6 %copy-start.14 = (bf16[16,32,384]{2,1,0:T(8,128)(2,1)S(1)}, bf16[16,32,384]{2,1,0:T(8,128)(2,1)}, u32[]{:S(2)}) copy-start(bf16[16,32,384]{2,1,0:T(8,128)(2,1)} %fusion.43) | copy-start | bytes 1179652
  72.7 2.6 %copy-start.15 = (bf16[16,32,384]{2,1,0:T(8,128)(2,1)S(1)}, bf16[16,32,384]{2,1,0:T(8,128)(2,1)}, u32[]{:S(2)}) copy-start(bf16[16,32,384]{2,1,0:T(8,128)(2,1)} %fusion.49) | copy-start | bytes 1179652
  76.5 2.0 %copy-start.1 = (f32[768,1152]{1,0:T(8,128)}, f32[768,1152]{1,0:T(8,128)S(1)}, u32[]{:S(2)}) copy-start(f32[768,1152]{1,0:T(8,128)S(1)} %convolution_bitcast_fusion) | copy-start | bytes 10616836
  78.6 8.1 %collective-permute-start = (f32[4,2,48,1152]{3,2,1,0:T(8,128)S(1)}, f32[4,2,48,1152]{3,2,1,0:T(8,128)}, u32[]{:S(2)}, u32[]{:S(2)}) collective-permute-start(f32[4,2,48,1152]{3,2,1,0:T(8,128)S(1)} %dynamic-slice_bitcast_fusion), channel_id=1, source_target_pairs={{0,1},{1,0},{2,3},{3,2},{4,5},{5,4},{6,7},{7,6},{8,9},{9,8},{10,11... | collective-permute-start | bytes 5308424 | tf_op jit(solution)/shard_map/ppermute | solution.py:97
  81.8 37.5 %all-to-all-start.2 = ((bf16[2,32,8,768]{3,2,0,1:T(8,128)(2,1)}), bf16[2,32,8,768]{3,2,0,1:T(8,128)(2,1)}, u32[]{:S(2)}, u32[]{:S(2)}) async-start(bf16[2,32,8,768]{3,2,0,1:T(8,128)(2,1)} %bitcast.91), calls=%async_computation.2 | async-start | bytes 1572864 | tf_op jit(solution)/shard_map/all_to_all | solution.py:141
  89.8 14.0 %collective-permute-start.3 = (bf16[2,48,1152]{2,1,0:T(8,128)(2,1)}, bf16[2,48,1152]{2,1,0:T(8,128)(2,1)}, u32[]{:S(2)}, u32[]{:S(2)}) collective-permute-start(bf16[2,48,1152]{2,1,0:T(8,128)(2,1)} %get-tuple-element.19), channel_id=1, source_target_pairs={{0,12},{1,13},{2,14},{3,15},{4,0},{5,1},{6,2},{7,3},{8,4},{9,5},{1... | collective-permute-start | bytes 663560 | tf_op jit(solution)/shard_map/ppermute | solution.py:97
  94.3 12.3 %collective-permute-start.2 = (bf16[2,48,1152]{2,1,0:T(8,128)(2,1)}, bf16[2,48,1152]{2,1,0:T(8,128)(2,1)}, u32[]{:S(2)}, u32[]{:S(2)}) collective-permute-start(bf16[2,48,1152]{2,1,0:T(8,128)(2,1)} %get-tuple-element.20), channel_id=1, source_target_pairs={{0,8},{1,9},{2,10},{3,11},{4,12},{5,13},{6,14},{7,15},{8,0},{9,1},... | collective-permute-start | bytes 663560 | tf_op jit(solution)/shard_map/ppermute | solution.py:97
  98.1 13.7 %collective-permute-start.1 = (bf16[2,48,1152]{2,1,0:T(8,128)(2,1)}, bf16[2,48,1152]{2,1,0:T(8,128)(2,1)}, u32[]{:S(2)}, u32[]{:S(2)}) collective-permute-start(bf16[2,48,1152]{2,1,0:T(8,128)(2,1)} %get-tuple-element.18), channel_id=1, source_target_pairs={{0,4},{1,5},{2,6},{3,7},{4,8},{5,9},{6,10},{7,11},{8,12},{9,13},{1... | collective-permute-start | bytes 663560 | tf_op jit(solution)/shard_map/ppermute | solution.py:97
  113.0 0.8 copy-start.2
  113.8 10.1 %copy-start.3 = (f32[2,48,1152]{2,1,0:T(8,128)S(1)}, f32[2,48,1152]{2,1,0:T(8,128)}, u32[]{:S(2)}) copy-start(f32[2,48,1152]{2,1,0:T(8,128)} %copy-done.2) | copy-start | bytes 1327108
  113.8 10.1 %collective-permute-start.4 = (bf16[48,1152]{1,0:T(8,128)(2,1)S(1)}, bf16[48,1152]{1,0:T(8,128)(2,1)S(1)}, u32[]{:S(2)}, u32[]{:S(2)}) collective-permute-start(bf16[48,1152]{1,0:T(8,128)(2,1)S(1)} %fusion.75), channel_id=1, source_target_pairs={{0,2},{1,3},{2,0},{3,1},{4,6},{5,7},{6,4},{7,5},{8,10},{9,11},{10,... | collective-permute-start | bytes 331784 | tf_op jit(solution)/shard_map/ppermute | solution.py:97

commit v14 on v13

--- a/solution.py
+++ b/solution.py
@@ -137,7 +137,6 @@
     all_grads = jnp.concatenate((query_grad, key_grad, value_grad), axis=-1)
     partial_w, input_cols = finish(scaled, inverse, normed, all_grads, proj_weights)
     input_cols = input_cols.reshape(tables, cols, rows, width).transpose(0, 2, 1, 3)
-    input_cols, partial_w = lax.optimization_barrier((input_cols, partial_w))
     input_grad = lax.all_to_all(input_cols, "band", split_axis=1, concat_axis=2, tiled=True)
     reduced = band_stages(partial_w)
     reduced, input_grad = lax.optimization_barrier((reduced, input_grad))

time: 153 us -> 157 us (1.026)
  the two profiles are of different devices: /device:TPU:1 before, /device:TPU:2 now
where the time goes in v14:
time: 157 us; the launch traced here: 156 us
  waiting for transfers between devices  42.4 us (27%)
  starting transfers between devices  39 us (25%)
  blocking collectives  26 us (17%)
  local copies, waits for them, and re-layouts  21.4 us (14%)
  matrix products  20.7 us (13%)
  other arithmetic  5.23 us (3%)
    all_to_all x1, blocking collectives, dp_stage(): blocks = lax.all_to_all(blocks.astype(jnp.bfloat16), 'dp', 0, 0, tiled=True)  26 us
    all_to_all x1, waiting for transfers between devices, body(): lax.all_to_all(cell_states, 'band', split_axis=2, concat_axis=1, tiled=True)  22.1 us
    ppermute x5, starting transfers between devices, exchange(): got = lax.ppermute(part.astype(wire), 'band', pairs)  17.1 us
    all_to_all x1, starting transfers between devices, body(): lax.all_to_all(cell_states, 'band', split_axis=2, concat_axis=1, tiled=True)  13.4 us
    ppermute x5, waiting for transfers between devices, exchange(): got = lax.ppermute(part.astype(wire), 'band', pairs)  13.3 us
    unnamed x22, local copies, waits for them, and re-layouts  8.7 us
    all_to_all x1, waiting for transfers between devices, body(): lax.all_to_all(grads_by_col, 'band', split_axis=0, concat_axis=2, tiled=T...  6.97 us
    all_to_all x1, starting transfers between devices, body(): lax.all_to_all(input_cols, 'band', split_axis=1, concat_axis=2, tiled=True)  4.37 us
  transfers between devices with their start and end apart: 8, of which 6 were waited for; matrix products, arithmetic and copies ran while one was open for 12% of the time, Pallas kernels for 0%

profile of v14, /device:TPU:2, one launch (start us, length us, event | category | flops | bytes accessed | tf_op | source)
XLA Modules:
  0.0 155.7 jit_solution(10954652491954820315)
XLA Ops:
  0.7 3.0 %copy.27 = bf16[2,2,128,768]{3,1,0,2:T(2,128)(2,1)} copy(bf16[2,2,128,768]{3,2,1,0:T(8,128)(2,1)} %param.4) | data formatting | bytes 1572864 | tf_op args[0]
  3.6 13.4 %all-to-all-start = ((bf16[2,2,128,768]{3,1,0,2:T(2,128)(2,1)}), bf16[2,2,128,768]{3,1,0,2:T(2,128)(2,1)S(1)}, u32[]{:S(2)}, u32[]{:S(2)}) async-start(bf16[2,2,128,768]{3,1,0,2:T(2,128)(2,1)} %copy.27), calls=%async_computation | async-start | bytes 1572864 | tf_op jit(solution)/shard_map/all_to_all | solution.py:124
  18.4 22.1 %all-to-all-done = bf16[2,2,128,768]{3,1,0,2:T(2,128)(2,1)S(1)} async-done(((bf16[2,2,128,768]{3,1,0,2:T(2,128)(2,1)}), bf16[2,2,128,768]{3,1,0,2:T(2,128)(2,1)S(1)}, u32[]{:S(2)}, u32[]{:S(2)}) %all-to-all-start) | async-done | bytes 786464 | tf_op jit(solution)/shard_map/all_to_all | solution.py:124
  42.0 4.1 %all-to-all-start.1 = ((bf16[128,2,2,384]{3,2,1,0:T(2,128)(2,1)}), bf16[128,2,2,384]{3,2,1,0:T(2,128)(2,1)}, u32[]{:S(2)}, u32[]{:S(2)}) async-start(bf16[128,2,2,384]{3,2,1,0:T(2,128)(2,1)} %bitcast.109), calls=%async_computation.1 | async-start | bytes 786432 | tf_op jit(solution)/shard_map/all_to_all | solution.py:129
  50.5 3.0 %fusion.90 = (f32[16,32,6]{1,2,0:T(8,128)S(1)}, f32[16,32,6,32]{1,3,2,0:T(8,128)}) fusion(pred[6,384]{1,0:T(8,128)(4,1)S(1)} %iota_compare_fusion, bf16[16,32,384]{2,1,0:T(8,128)(2,1)S(1)} %get-tuple-element.18, pred[16,32,32]{1,2,0:T(8,128)(4,1)S(1)} %compare_or_fusion, bf16[16,32,1152]{2,1,0:T(8,128)(2,1)} %bitcast.114), kind=kOutput, calls=%fused_computation.99 | convolution fusion | flops 77070368 | bytes 1210624 | tf_op jit(solution)/shard_map/sub | solution.py:52
  53.5 7.0 %all-to-all-done.1 = bf16[128,2,2,384]{3,2,1,0:T(2,128)(2,1)} async-done(((bf16[128,2,2,384]{3,2,1,0:T(2,128)(2,1)}), bf16[128,2,2,384]{3,2,1,0:T(2,128)(2,1)}, u32[]{:S(2)}, u32[]{:S(2)}) %all-to-all-start.1) | async-done | bytes 393248 | tf_op jit(solution)/shard_map/all_to_all | solution.py:129
  62.6 3.0 %fusion.10 = f32[16,32,6,32]{1,3,2,0:T(8,128)} fusion(bf16[16,32,384,1]{2,1,3,0:T(8,128)(2,1)} %bitcast.116, pred[6,384]{1,0:T(8,128)(4,1)S(1)} %iota_compare_fusion, bf16[16,32,384]{2,1,0:T(8,128)(2,1)} %get-tuple-element.17), kind=kOutput, calls=%fused_computation.11 | convolution fusion | flops 76677120 | bytes 1181952 | tf_op jit(solution)/shard_map/bid,bhjd->bihj/dot_general | solution.py:58
  65.6 3.8 %fusion.43 = bf16[16,32,384]{2,1,0:T(8,128)(2,1)S(1)} fusion(pred[6,384]{1,0:T(8,128)(4,1)S(1)} %iota_compare_fusion, bf16[16,32,384]{2,1,0:T(8,128)(2,1)S(1)} %get-tuple-element.18, f32[16,32,6,32]{1,3,2,0:T(8,128)} %fusion.10, f32[16,32,6,32]{1,3,2,0:T(8,128)} %get-tuple-element.21, f32[16,32,6]{1,2,0:T(8,128)S(1)} %get-tuple-element.20), kind=kOutput, calls=%fused_computation.41 | convolution fusion | flops 77564960 | bytes 1587456 | tf_op jit(solution)/shard_map/bihj,bhjd->bid/dot_general | solution.py:63
  69.4 3.9 %fusion.49 = bf16[16,32,384]{2,1,0:T(8,128)(2,1)S(1)} fusion(pred[6,384]{1,0:T(8,128)(4,1)S(1)} %iota_compare_fusion, bf16[16,32,384]{2,1,0:T(8,128)(2,1)} %get-tuple-element.19, f32[16,32,6,32]{1,3,2,0:T(8,128)} %fusion.10, f32[16,32,6,32]{1,3,2,0:T(8,128)} %get-tuple-element.21, f32[16,32,6]{1,2,0:T(8,128)S(1)} %get-tuple-element.20), kind=kOutput, calls=%fused_computation.43 | convolution fusion | flops 77564960 | bytes 1587456 | tf_op jit(solution)/shard_map/bihj,bhid->bjd/dot_general | solution.py:66
  73.3 2.3 %fusion.46 = bf16[16,32,384]{2,1,0:T(8,128)(2,1)S(1)} fusion(pred[6,384]{1,0:T(8,128)(4,1)S(1)} %iota_compare_fusion, bf16[16,32,384]{2,1,0:T(8,128)(2,1)} %bitcast.117, f32[16,32,6,32]{1,3,2,0:T(8,128)} %get-tuple-element.21, f32[16,32,6]{1,2,0:T(8,128)S(1)} %get-tuple-element.20), kind=kOutput, calls=%fused_computation.42 | convolution fusion | flops 77070336 | bytes 1194240 | tf_op jit(solution)/shard_map/bihj,bhid->bjd/dot_general | solution.py:55
  80.4 1.9 %collective-permute-start = (f32[4,2,48,1152]{3,2,1,0:T(8,128)}, f32[4,2,48,1152]{3,2,1,0:T(8,128)}, u32[]{:S(2)}, u32[]{:S(2)}) collective-permute-start(f32[4,2,48,1152]{3,2,1,0:T(8,128)} %dynamic-slice_bitcast_fusion), channel_id=1, source_target_pairs={{0,1},{1,0},{2,3},{3,2},{4,5},{5,4},{6,7},{7,6},{8,9},{9,8},{10,11... | collective-permute-start | bytes 5308424 | tf_op jit(solution)/shard_map/ppermute | solution.py:97
  82.4 2.3 %fusion.23 = (f32[16,32]{1,0:T(8,128)S(1)}, f32[16,32,768]{2,1,0:T(8,128)S(1)}) fusion(bf16[16,32,768]{2,1,0:T(8,128)(2,1)S(1)} %bitcast.101, f32[16,32]{1,0:T(8,128)S(1)} %add_rsqrt_fusion, bf16[768,1152]{1,0:T(8,128)(2,1)S(1)} %copy-done, bf16[16,32,384]{2,1,0:T(8,128)(2,1)} %copy-done.6, bf16[16,32,384]{2,1,0:T(8,128)(2,1)S(1)} %fusion.49, ...), kind=kOutput, calls=%fused_computation.28 | convolution fusion | flops 911080960 | bytes 5312512 | tf_op jit(solution)/shard_map/dot_general | solution.py:78
  86.4 4.4 %all-to-all-start.2 = ((bf16[2,32,8,768]{3,2,0,1:T(8,128)(2,1)}), bf16[2,32,8,768]{3,2,0,1:T(8,128)(2,1)}, u32[]{:S(2)}, u32[]{:S(2)}) async-start(bf16[2,32,8,768]{3,2,0,1:T(8,128)(2,1)} %bitcast.97), calls=%async_computation.2 | async-start | bytes 1572864 | tf_op jit(solution)/shard_map/all_to_all | solution.py:140
  90.8 2.2 %bitcast_add_fusion = f32[4,2,48,1152]{3,2,1,0:T(8,128)S(1)} fusion(f32[4,2,48,1152]{3,2,1,0:T(8,128)} %collective-permute-done, f32[4,2,2,48,1152]{4,3,2,1,0:T(8,128)} %copy-done.1, s32[]{:T(128)S(6)} %select_n.104), kind=kLoop, calls=%fused_computation.25 | loop fusion | flops 442368 | bytes 5308420 | tf_op jit(solution)/shard_map/add | solution.py:98
  93.9 2.4 %collective-permute-start.1 = (bf16[2,48,1152]{2,1,0:T(8,128)(2,1)}, bf16[2,48,1152]{2,1,0:T(8,128)(2,1)}, u32[]{:S(2)}, u32[]{:S(2)}) collective-permute-start(bf16[2,48,1152]{2,1,0:T(8,128)(2,1)} %get-tuple-element.14), channel_id=1, source_target_pairs={{0,4},{1,5},{2,6},{3,7},{4,8},{5,9},{6,10},{7,11},{8,12},{9,13},{1... | collective-permute-start | bytes 663560 | tf_op jit(solution)/shard_map/ppermute | solution.py:97
  96.3 2.7 %collective-permute-start.2 = (bf16[2,48,1152]{2,1,0:T(8,128)(2,1)}, bf16[2,48,1152]{2,1,0:T(8,128)(2,1)}, u32[]{:S(2)}, u32[]{:S(2)}) collective-permute-start(bf16[2,48,1152]{2,1,0:T(8,128)(2,1)} %get-tuple-element.16), channel_id=1, source_target_pairs={{0,8},{1,9},{2,10},{3,11},{4,12},{5,13},{6,14},{7,15},{8,0},{9,1},... | collective-permute-start | bytes 663560 | tf_op jit(solution)/shard_map/ppermute | solution.py:97
  99.0 4.4 %collective-permute-start.3 = (bf16[2,48,1152]{2,1,0:T(8,128)(2,1)}, bf16[2,48,1152]{2,1,0:T(8,128)(2,1)}, u32[]{:S(2)}, u32[]{:S(2)}) collective-permute-start(bf16[2,48,1152]{2,1,0:T(8,128)(2,1)} %get-tuple-element.15), channel_id=1, source_target_pairs={{0,12},{1,13},{2,14},{3,15},{4,0},{5,1},{6,2},{7,3},{8,4},{9,5},{1... | collective-permute-start | bytes 663560 | tf_op jit(solution)/shard_map/ppermute | solution.py:97
  103.4 3.8 %collective-permute-done.1 = bf16[2,48,1152]{2,1,0:T(8,128)(2,1)} collective-permute-done((bf16[2,48,1152]{2,1,0:T(8,128)(2,1)}, bf16[2,48,1152]{2,1,0:T(8,128)(2,1)}, u32[]{:S(2)}, u32[]{:S(2)}) %collective-permute-start.1) | collective-permute-done | bytes 221216 | tf_op jit(solution)/shard_map/ppermute | solution.py:97
  107.2 2.1 %collective-permute-done.2 = bf16[2,48,1152]{2,1,0:T(8,128)(2,1)} collective-permute-done((bf16[2,48,1152]{2,1,0:T(8,128)(2,1)}, bf16[2,48,1152]{2,1,0:T(8,128)(2,1)}, u32[]{:S(2)}, u32[]{:S(2)}) %collective-permute-start.2) | collective-permute-done | bytes 221216 | tf_op jit(solution)/shard_map/ppermute | solution.py:97
  109.3 4.4 %collective-permute-done.3 = bf16[2,48,1152]{2,1,0:T(8,128)(2,1)} collective-permute-done((bf16[2,48,1152]{2,1,0:T(8,128)(2,1)}, bf16[2,48,1152]{2,1,0:T(8,128)(2,1)}, u32[]{:S(2)}, u32[]{:S(2)}) %collective-permute-start.3) | collective-permute-done | bytes 221216 | tf_op jit(solution)/shard_map/ppermute | solution.py:97
  115.7 5.7 %collective-permute-start.4 = (bf16[48,1152]{1,0:T(8,128)(2,1)S(1)}, bf16[48,1152]{1,0:T(8,128)(2,1)S(1)}, u32[]{:S(2)}, u32[]{:S(2)}) collective-permute-start(bf16[48,1152]{1,0:T(8,128)(2,1)S(1)} %fusion.75), channel_id=1, source_target_pairs={{0,2},{1,3},{2,0},{3,1},{4,6},{5,7},{6,4},{7,5},{8,10},{9,11},{10,... | collective-permute-start | bytes 331784 | tf_op jit(solution)/shard_map/ppermute | solution.py:97
  121.4 2.1 %copy.51 = bf16[2,2,16,8,768]{4,3,2,1,0:T(8,128)(2,1)} copy(bf16[2,2,16,8,768]{4,3,0,1,2:T(8,128)(2,1)} %bitcast.40) | data formatting | bytes 1572864 | tf_op jit(solution)/shard_map/all_to_all | solution.py:140
  123.5 3.1 %collective-permute-done.4 = bf16[48,1152]{1,0:T(8,128)(2,1)S(1)} collective-permute-done((bf16[48,1152]{1,0:T(8,128)(2,1)S(1)}, bf16[48,1152]{1,0:T(8,128)(2,1)S(1)}, u32[]{:S(2)}, u32[]{:S(2)}) %collective-permute-start.4) | collective-permute-done | bytes 110624 | tf_op jit(solution)/shard_map/ppermute | solution.py:97
  128.6 26.0 %all_to_all.59 = bf16[32,2,864]{2,1,0:T(2,128)(2,1)S(1)} all-to-all(bf16[32,2,864]{2,1,0:T(2,128)(2,1)S(1)} %reshape.116), channel_id=1, replica_groups=mesh['dp'=32,'band'=16] {'dp'}, dimensions={0} | all-to-all | bytes 221184 | tf_op jit(solution)/shard_map/all_to_all | solution.py:118
  (51 shorter events, 21.8 us)
Async XLA Ops:
  0.6 46.6 %copy-start = (bf16[768,1152]{1,0:T(8,128)(2,1)S(1)}, bf16[768,1152]{1,0:T(8,128)(2,1)}, u32[]{:S(2)}) copy-start(bf16[768,1152]{1,0:T(8,128)(2,1)} %param.7) | copy-start | bytes 5308420
  0.6 16.4 %copy-start.7 = (bf16[2,2,128,384]{3,2,1,0:T(8,128)(2,1)S(1)}, bf16[2,2,128,384]{3,2,1,0:T(8,128)(2,1)}, u32[]{:S(2)}) copy-start(bf16[2,2,128,384]{3,2,1,0:T(8,128)(2,1)} %param.5) | copy-start | bytes 1179652
  3.6 14.6 %copy-start.8 = (s32[2,8,32]{2,1,0:T(8,128)S(1)}, s32[2,8,32]{2,1,0:T(8,128)}, u32[]{:S(2)}) copy-start(s32[2,8,32]{2,1,0:T(8,128)} %param.6) | copy-start | bytes 6148
  3.6 36.8 %all-to-all-start = ((bf16[2,2,128,768]{3,1,0,2:T(2,128)(2,1)}), bf16[2,2,128,768]{3,1,0,2:T(2,128)(2,1)S(1)}, u32[]{:S(2)}, u32[]{:S(2)}) async-start(bf16[2,2,128,768]{3,1,0,2:T(2,128)(2,1)} %copy.27), calls=%async_computation | async-start | bytes 1572864 | tf_op jit(solution)/shard_map/all_to_all | solution.py:124
  42.0 18.5 %all-to-all-start.1 = ((bf16[128,2,2,384]{3,2,1,0:T(2,128)(2,1)}), bf16[128,2,2,384]{3,2,1,0:T(2,128)(2,1)}, u32[]{:S(2)}, u32[]{:S(2)}) async-start(bf16[128,2,2,384]{3,2,1,0:T(2,128)(2,1)} %bitcast.109), calls=%async_computation.1 | async-start | bytes 786432 | tf_op jit(solution)/shard_map/all_to_all | solution.py:129
  48.4 1.0 copy-start.5
  75.6 0.8 copy-start.6
  75.6 1.3 copy-start.2
  78.1 2.3 %copy-start.1 = (f32[4,2,2,48,1152]{4,3,2,1,0:T(8,128)}, f32[4,2,2,48,1152]{4,3,2,1,0:T(8,128)S(1)}, u32[]{:S(2)}) copy-start(f32[4,2,2,48,1152]{4,3,2,1,0:T(8,128)S(1)} %fusion.95) | copy-start | bytes 10616836
  80.4 10.4 %collective-permute-start = (f32[4,2,48,1152]{3,2,1,0:T(8,128)}, f32[4,2,48,1152]{3,2,1,0:T(8,128)}, u32[]{:S(2)}, u32[]{:S(2)}) collective-permute-start(f32[4,2,48,1152]{3,2,1,0:T(8,128)} %dynamic-slice_bitcast_fusion), channel_id=1, source_target_pairs={{0,1},{1,0},{2,3},{3,2},{4,5},{5,4},{6,7},{7,6},{8,9},{9,8},{10,11... | collective-permute-start | bytes 5308424 | tf_op jit(solution)/shard_map/ppermute | solution.py:97
  86.4 35.0 %all-to-all-start.2 = ((bf16[2,32,8,768]{3,2,0,1:T(8,128)(2,1)}), bf16[2,32,8,768]{3,2,0,1:T(8,128)(2,1)}, u32[]{:S(2)}, u32[]{:S(2)}) async-start(bf16[2,32,8,768]{3,2,0,1:T(8,128)(2,1)} %bitcast.97), calls=%async_computation.2 | async-start | bytes 1572864 | tf_op jit(solution)/shard_map/all_to_all | solution.py:140
  93.9 13.3 %collective-permute-start.1 = (bf16[2,48,1152]{2,1,0:T(8,128)(2,1)}, bf16[2,48,1152]{2,1,0:T(8,128)(2,1)}, u32[]{:S(2)}, u32[]{:S(2)}) collective-permute-start(bf16[2,48,1152]{2,1,0:T(8,128)(2,1)} %get-tuple-element.14), channel_id=1, source_target_pairs={{0,4},{1,5},{2,6},{3,7},{4,8},{5,9},{6,10},{7,11},{8,12},{9,13},{1... | collective-permute-start | bytes 663560 | tf_op jit(solution)/shard_map/ppermute | solution.py:97
  96.3 13.0 %collective-permute-start.2 = (bf16[2,48,1152]{2,1,0:T(8,128)(2,1)}, bf16[2,48,1152]{2,1,0:T(8,128)(2,1)}, u32[]{:S(2)}, u32[]{:S(2)}) collective-permute-start(bf16[2,48,1152]{2,1,0:T(8,128)(2,1)} %get-tuple-element.16), channel_id=1, source_target_pairs={{0,8},{1,9},{2,10},{3,11},{4,12},{5,13},{6,14},{7,15},{8,0},{9,1},... | collective-permute-start | bytes 663560 | tf_op jit(solution)/shard_map/ppermute | solution.py:97
  99.0 14.7 %collective-permute-start.3 = (bf16[2,48,1152]{2,1,0:T(8,128)(2,1)}, bf16[2,48,1152]{2,1,0:T(8,128)(2,1)}, u32[]{:S(2)}, u32[]{:S(2)}) collective-permute-start(bf16[2,48,1152]{2,1,0:T(8,128)(2,1)} %get-tuple-element.15), channel_id=1, source_target_pairs={{0,12},{1,13},{2,14},{3,15},{4,0},{5,1},{6,2},{7,3},{8,4},{9,5},{1... | collective-permute-start | bytes 663560 | tf_op jit(solution)/shard_map/ppermute | solution.py:97
  114.9 0.8 copy-start.3
  115.7 10.9 %copy-start.4 = (f32[2,48,1152]{2,1,0:T(8,128)S(1)}, f32[2,48,1152]{2,1,0:T(8,128)}, u32[]{:S(2)}) copy-start(f32[2,48,1152]{2,1,0:T(8,128)} %copy-done.3) | copy-start | bytes 1327108
  115.7 10.9 %collective-permute-start.4 = (bf16[48,1152]{1,0:T(8,128)(2,1)S(1)}, bf16[48,1152]{1,0:T(8,128)(2,1)S(1)}, u32[]{:S(2)}, u32[]{:S(2)}) collective-permute-start(bf16[48,1152]{1,0:T(8,128)(2,1)S(1)} %fusion.75), channel_id=1, source_target_pairs={{0,2},{1,3},{2,0},{3,1},{4,6},{5,7},{6,4},{7,5},{8,10},{9,11},{10,... | collective-permute-start | bytes 331784 | tf_op jit(solution)/shard_map/ppermute | solution.py:97

commit v15 on v13

--- a/solution.py
+++ b/solution.py
@@ -114,9 +114,12 @@
     n_dp = lax.axis_size("dp")
     rows, d_out = blocks.shape
     cols = d_out // n_dp
-    blocks = blocks.reshape(rows, n_dp, cols).transpose(1, 0, 2)
+    blocks = blocks.reshape(rows, n_dp, cols).transpose(1, 0, 2).reshape(n_dp, rows * cols)
+    lanes = -(-rows * cols // 128) * 128
+    blocks = jnp.pad(blocks, ((0, 0), (0, lanes - rows * cols))).reshape(n_dp, lanes // 128, 128)
     blocks = lax.all_to_all(blocks.astype(jnp.bfloat16), "dp", 0, 0, tiled=True)
-    return blocks.astype(jnp.float32).sum(axis=0)
+    total = blocks.astype(jnp.float32).sum(axis=0).reshape(lanes)
+    return total[: rows * cols].reshape(rows, cols)
 
 
 def body(cell_states, head_grads, group_ids, proj_weights):

time: 153 us -> 152 us (level)
    unnamed x36 -> x35, local copies, waits for them, and re-layouts: 6.79 us -> 6.66 us
where the time goes in v15:
time: 152 us; the launch traced here: 151 us
  starting transfers between devices  47.8 us (31%)
  waiting for transfers between devices  35.7 us (23%)
  blocking collectives  24.5 us (16%)
  matrix products  21.8 us (14%)
  local copies, waits for them, and re-layouts  15.6 us (10%)
  other arithmetic  4.45 us (3%)
    all_to_all x1, blocking collectives, dp_stage(): blocks = lax.all_to_all(blocks.astype(jnp.bfloat16), 'dp', 0, 0, tiled=True)  24.5 us
    ppermute x5, starting transfers between devices, exchange(): got = lax.ppermute(part.astype(wire), 'band', pairs)  18.7 us
    all_to_all x1, waiting for transfers between devices, body(): lax.all_to_all(cell_states, 'band', split_axis=2, concat_axis=1, tiled=True)  15.6 us
    all_to_all x1, starting transfers between devices, body(): lax.all_to_all(cell_states, 'band', split_axis=2, concat_axis=1, tiled=True)  14.4 us
    ppermute x5, waiting for transfers between devices, exchange(): got = lax.ppermute(part.astype(wire), 'band', pairs)  14.3 us
    all_to_all x1, starting transfers between devices, body(): lax.all_to_all(grads_by_col, 'band', split_axis=0, concat_axis=2, tiled=T...  9.75 us
    unnamed x35, local copies, waits for them, and re-layouts  6.66 us
    all_to_all x1, waiting for transfers between devices, body(): lax.all_to_all(grads_by_col, 'band', split_axis=0, concat_axis=2, tiled=T...  5.78 us
  transfers between devices with their start and end apart: 8, of which 6 were waited for; matrix products, arithmetic and copies ran while one was open for 9% of the time, Pallas kernels for 0%

profile of v15, /device:TPU:1, one launch (start us, length us, event | category | flops | bytes accessed | tf_op | source)
XLA Modules:
  0.0 151.0 jit_solution(10160814804244844969)
XLA Ops:
  0.7 3.0 %copy.16 = bf16[2,2,128,768]{3,1,0,2:T(2,128)(2,1)} copy(bf16[2,2,128,768]{3,2,1,0:T(8,128)(2,1)} %param.4) | data formatting | bytes 1572864 | tf_op args[0]
  3.6 14.4 %all-to-all-start = ((bf16[2,2,128,768]{3,1,0,2:T(2,128)(2,1)}), bf16[2,2,128,768]{3,1,0,2:T(2,128)(2,1)S(1)}, u32[]{:S(2)}, u32[]{:S(2)}) async-start(bf16[2,2,128,768]{3,1,0,2:T(2,128)(2,1)} %copy.16), calls=%async_computation | async-start | bytes 1572864 | tf_op jit(solution)/shard_map/all_to_all | solution.py:127
  19.4 15.6 %all-to-all-done = bf16[2,2,128,768]{3,1,0,2:T(2,128)(2,1)S(1)} async-done(((bf16[2,2,128,768]{3,1,0,2:T(2,128)(2,1)}), bf16[2,2,128,768]{3,1,0,2:T(2,128)(2,1)S(1)}, u32[]{:S(2)}, u32[]{:S(2)}) %all-to-all-start) | async-done | bytes 786464 | tf_op jit(solution)/shard_map/all_to_all | solution.py:127
  36.3 9.8 %all-to-all-start.1 = ((bf16[128,2,2,384]{3,2,1,0:T(2,128)(2,1)}), bf16[128,2,2,384]{3,2,1,0:T(2,128)(2,1)S(1)}, u32[]{:S(2)}, u32[]{:S(2)}) async-start(bf16[128,2,2,384]{3,2,1,0:T(2,128)(2,1)} %bitcast.101), calls=%async_computation.1 | async-start | bytes 786432 | tf_op jit(solution)/shard_map/all_to_all | solution.py:132
  49.5 3.1 %fusion.92 = (f32[16,32,6]{1,2,0:T(8,128)S(1)}, f32[16,32,6,32]{1,3,2,0:T(8,128)}) fusion(pred[6,384]{1,0:T(8,128)(4,1)S(1)} %iota_compare_fusion, bf16[16,32,384]{2,1,0:T(8,128)(2,1)S(1)} %get-tuple-element.22, pred[16,32,32]{1,2,0:T(8,128)(4,1)S(1)} %compare_or_fusion, bf16[16,32,1152]{2,1,0:T(8,128)(2,1)} %bitcast.105), kind=kOutput, calls=%fused_computation.102 | convolution fusion | flops 77070368 | bytes 1210624 | tf_op jit(solution)/shard_map/sub | solution.py:52
  52.7 5.8 %all-to-all-done.1 = bf16[128,2,2,384]{3,2,1,0:T(2,128)(2,1)S(1)} async-done(((bf16[128,2,2,384]{3,2,1,0:T(2,128)(2,1)}), bf16[128,2,2,384]{3,2,1,0:T(2,128)(2,1)S(1)}, u32[]{:S(2)}, u32[]{:S(2)}) %all-to-all-start.1) | async-done | bytes 393248 | tf_op jit(solution)/shard_map/all_to_all | solution.py:132
  58.9 3.0 %fusion.10 = f32[16,32,6,32]{1,3,2,0:T(8,128)} fusion(bf16[16,32,384,1]{2,1,3,0:T(8,128)(2,1)S(1)} %bitcast.108, pred[6,384]{1,0:T(8,128)(4,1)S(1)} %iota_compare_fusion, bf16[16,32,384]{2,1,0:T(8,128)(2,1)} %get-tuple-element.21), kind=kOutput, calls=%fused_computation.12 | convolution fusion | flops 76677120 | bytes 1181952 | tf_op jit(solution)/shard_map/bid,bhjd->bihj/dot_general | solution.py:58
  63.5 4.6 %fusion.43 = bf16[16,32,384]{2,1,0:T(8,128)(2,1)} fusion(pred[6,384]{1,0:T(8,128)(4,1)S(1)} %iota_compare_fusion, bf16[16,32,384]{2,1,0:T(8,128)(2,1)S(1)} %copy-done.9, f32[16,32,6,32]{1,3,2,0:T(8,128)} %fusion.10, f32[16,32,6,32]{1,3,2,0:T(8,128)} %get-tuple-element.25, f32[16,32,6]{1,2,0:T(8,128)S(1)} %get-tuple-element.24), kind=kOutput, calls=%fused_computation.42 | convolution fusion | flops 77564960 | bytes 1587456 | tf_op jit(solution)/shard_map/bihj,bhjd->bid/dot_general | solution.py:63
  68.1 4.6 %fusion.49 = bf16[16,32,384]{2,1,0:T(8,128)(2,1)} fusion(pred[6,384]{1,0:T(8,128)(4,1)S(1)} %iota_compare_fusion, bf16[16,32,384]{2,1,0:T(8,128)(2,1)S(1)} %copy-done.7, f32[16,32,6,32]{1,3,2,0:T(8,128)} %fusion.10, f32[16,32,6,32]{1,3,2,0:T(8,128)} %get-tuple-element.25, f32[16,32,6]{1,2,0:T(8,128)S(1)} %get-tuple-element.24), kind=kOutput, calls=%fused_computation.44 | convolution fusion | flops 77564960 | bytes 1587456 | tf_op jit(solution)/shard_map/bihj,bhid->bjd/dot_general | solution.py:66
  72.7 2.5 %fusion.23 = (f32[16,32]{1,0:T(8,128)S(1)}, f32[16,32,768]{2,1,0:T(8,128)S(1)}) fusion(bf16[16,32,768]{2,1,0:T(8,128)(2,1)S(1)} %bitcast.95, f32[16,32]{1,0:T(8,128)S(1)} %add_rsqrt_fusion, bf16[768,1152]{1,0:T(8,128)(2,1)S(1)} %copy-done, bf16[16,32,384]{2,1,0:T(8,128)(2,1)S(1)} %copy-done.13, bf16[16,32,384]{2,1,0:T(8,128)(2,1)} %fusion.49, ...), kind=kOutput, calls=%fused_computation.29 | convolution fusion | flops 911080960 | bytes 5312512 | tf_op jit(solution)/shard_map/dot_general | solution.py:78
  76.9 1.7 %copy.35 = bf16[2,8,32,768]{3,1,0,2:T(8,128)(2,1)} copy(bf16[2,8,32,768]{3,2,1,0:T(8,128)(2,1)S(1)} %bitcast.100) | data formatting | bytes 1572864 | tf_op jit(solution)/shard_map/reshape | solution.py:142
  78.6 3.1 %collective-permute-start = (f32[4,2,48,1152]{3,2,1,0:T(8,128)S(1)}, f32[4,2,48,1152]{3,2,1,0:T(8,128)}, u32[]{:S(2)}, u32[]{:S(2)}) collective-permute-start(f32[4,2,48,1152]{3,2,1,0:T(8,128)S(1)} %dynamic-slice_bitcast_fusion), channel_id=1, source_target_pairs={{0,1},{1,0},{2,3},{3,2},{4,5},{5,4},{6,7},{7,6},{8,9},{9,8},{10,11... | collective-permute-start | bytes 5308424 | tf_op jit(solution)/shard_map/ppermute | solution.py:97
  81.8 4.9 %all-to-all-start.2 = ((bf16[2,32,8,768]{3,2,0,1:T(8,128)(2,1)}), bf16[2,32,8,768]{3,2,0,1:T(8,128)(2,1)}, u32[]{:S(2)}, u32[]{:S(2)}) async-start(bf16[2,32,8,768]{3,2,0,1:T(8,128)(2,1)} %bitcast.90), calls=%async_computation.2 | async-start | bytes 1572864 | tf_op jit(solution)/shard_map/all_to_all | solution.py:144
  86.7 2.2 %bitcast_add_fusion = f32[4,2,48,1152]{3,2,1,0:T(8,128)S(1)} fusion(f32[4,2,48,1152]{3,2,1,0:T(8,128)} %collective-permute-done, f32[4,2,2,48,1152]{4,3,2,1,0:T(8,128)} %bitcast.98, s32[]{:T(128)S(6)} %select_n.104), kind=kLoop, calls=%fused_computation.24 | loop fusion | flops 442368 | bytes 5308420 | tf_op jit(solution)/shard_map/add | solution.py:98
  89.8 4.5 %collective-permute-start.3 = (bf16[2,48,1152]{2,1,0:T(8,128)(2,1)}, bf16[2,48,1152]{2,1,0:T(8,128)(2,1)}, u32[]{:S(2)}, u32[]{:S(2)}) collective-permute-start(bf16[2,48,1152]{2,1,0:T(8,128)(2,1)} %get-tuple-element.19), channel_id=1, source_target_pairs={{0,12},{1,13},{2,14},{3,15},{4,0},{5,1},{6,2},{7,3},{8,4},{9,5},{1... | collective-permute-start | bytes 663560 | tf_op jit(solution)/shard_map/ppermute | solution.py:97
  94.3 3.8 %collective-permute-start.2 = (bf16[2,48,1152]{2,1,0:T(8,128)(2,1)}, bf16[2,48,1152]{2,1,0:T(8,128)(2,1)}, u32[]{:S(2)}, u32[]{:S(2)}) collective-permute-start(bf16[2,48,1152]{2,1,0:T(8,128)(2,1)} %get-tuple-element.20), channel_id=1, source_target_pairs={{0,8},{1,9},{2,10},{3,11},{4,12},{5,13},{6,14},{7,15},{8,0},{9,1},... | collective-permute-start | bytes 663560 | tf_op jit(solution)/shard_map/ppermute | solution.py:97
  98.1 1.9 %collective-permute-start.1 = (bf16[2,48,1152]{2,1,0:T(8,128)(2,1)}, bf16[2,48,1152]{2,1,0:T(8,128)(2,1)}, u32[]{:S(2)}, u32[]{:S(2)}) collective-permute-start(bf16[2,48,1152]{2,1,0:T(8,128)(2,1)} %get-tuple-element.18), channel_id=1, source_target_pairs={{0,4},{1,5},{2,6},{3,7},{4,8},{5,9},{6,10},{7,11},{8,12},{9,13},{1... | collective-permute-start | bytes 663560 | tf_op jit(solution)/shard_map/ppermute | solution.py:97
  100.1 3.7 %collective-permute-done.3 = bf16[2,48,1152]{2,1,0:T(8,128)(2,1)} collective-permute-done((bf16[2,48,1152]{2,1,0:T(8,128)(2,1)}, bf16[2,48,1152]{2,1,0:T(8,128)(2,1)}, u32[]{:S(2)}, u32[]{:S(2)}) %collective-permute-start.3) | collective-permute-done | bytes 221216 | tf_op jit(solution)/shard_map/ppermute | solution.py:97
  103.8 2.8 %collective-permute-done.2 = bf16[2,48,1152]{2,1,0:T(8,128)(2,1)} collective-permute-done((bf16[2,48,1152]{2,1,0:T(8,128)(2,1)}, bf16[2,48,1152]{2,1,0:T(8,128)(2,1)}, u32[]{:S(2)}, u32[]{:S(2)}) %collective-permute-start.2) | collective-permute-done | bytes 221216 | tf_op jit(solution)/shard_map/ppermute | solution.py:97
  106.6 5.2 %collective-permute-done.1 = bf16[2,48,1152]{2,1,0:T(8,128)(2,1)} collective-permute-done((bf16[2,48,1152]{2,1,0:T(8,128)(2,1)}, bf16[2,48,1152]{2,1,0:T(8,128)(2,1)}, u32[]{:S(2)}, u32[]{:S(2)}) %collective-permute-start.1) | collective-permute-done | bytes 221216 | tf_op jit(solution)/shard_map/ppermute | solution.py:97
  113.8 5.4 %collective-permute-start.4 = (bf16[48,1152]{1,0:T(8,128)(2,1)S(1)}, bf16[48,1152]{1,0:T(8,128)(2,1)S(1)}, u32[]{:S(2)}, u32[]{:S(2)}) collective-permute-start(bf16[48,1152]{1,0:T(8,128)(2,1)S(1)} %fusion.75), channel_id=1, source_target_pairs={{0,2},{1,3},{2,0},{3,1},{4,6},{5,7},{6,4},{7,5},{8,10},{9,11},{10,... | collective-permute-start | bytes 331784 | tf_op jit(solution)/shard_map/ppermute | solution.py:97
  119.3 2.1 %copy.34 = bf16[2,2,16,8,768]{4,3,2,1,0:T(8,128)(2,1)} copy(bf16[2,2,16,8,768]{4,3,0,1,2:T(8,128)(2,1)} %bitcast.37) | data formatting | bytes 1572864 | tf_op jit(solution)/shard_map/all_to_all | solution.py:144
  121.3 2.6 %collective-permute-done.4 = bf16[48,1152]{1,0:T(8,128)(2,1)S(1)} collective-permute-done((bf16[48,1152]{1,0:T(8,128)(2,1)S(1)}, bf16[48,1152]{1,0:T(8,128)(2,1)S(1)}, u32[]{:S(2)}, u32[]{:S(2)}) %collective-permute-start.4) | collective-permute-done | bytes 110624 | tf_op jit(solution)/shard_map/ppermute | solution.py:97
  125.7 24.5 %all_to_all.59 = bf16[32,14,128]{2,1,0:T(8,128)(2,1)S(1)} all-to-all(bf16[32,14,128]{2,1,0:T(8,128)(2,1)S(1)} %convert_element_type.93), channel_id=1, replica_groups=mesh['dp'=32,'band'=16] {'dp'}, dimensions={0} | all-to-all | bytes 229376 | tf_op jit(solution)/shard_map/all_to_all | solution.py:120
  (66 shorter events, 15.2 us)
Async XLA Ops:
  0.6 45.6 %copy-start = (bf16[768,1152]{1,0:T(8,128)(2,1)S(1)}, bf16[768,1152]{1,0:T(8,128)(2,1)}, u32[]{:S(2)}) copy-start(bf16[768,1152]{1,0:T(8,128)(2,1)} %param.7) | copy-start | bytes 5308420
  0.6 17.4 %copy-start.10 = (bf16[2,2,128,384]{3,2,1,0:T(8,128)(2,1)S(1)}, bf16[2,2,128,384]{3,2,1,0:T(8,128)(2,1)}, u32[]{:S(2)}) copy-start(bf16[2,2,128,384]{3,2,1,0:T(8,128)(2,1)} %param.5) | copy-start | bytes 1179652
  3.6 15.6 %copy-start.11 = (s32[2,8,32]{2,1,0:T(8,128)S(1)}, s32[2,8,32]{2,1,0:T(8,128)}, u32[]{:S(2)}) copy-start(s32[2,8,32]{2,1,0:T(8,128)} %param.6) | copy-start | bytes 6148
  3.6 31.4 %all-to-all-start = ((bf16[2,2,128,768]{3,1,0,2:T(2,128)(2,1)}), bf16[2,2,128,768]{3,1,0,2:T(2,128)(2,1)S(1)}, u32[]{:S(2)}, u32[]{:S(2)}) async-start(bf16[2,2,128,768]{3,1,0,2:T(2,128)(2,1)} %copy.16), calls=%async_computation | async-start | bytes 1572864 | tf_op jit(solution)/shard_map/all_to_all | solution.py:127
  36.3 22.1 %all-to-all-start.1 = ((bf16[128,2,2,384]{3,2,1,0:T(2,128)(2,1)}), bf16[128,2,2,384]{3,2,1,0:T(2,128)(2,1)S(1)}, u32[]{:S(2)}, u32[]{:S(2)}) async-start(bf16[128,2,2,384]{3,2,1,0:T(2,128)(2,1)} %bitcast.101), calls=%async_computation.1 | async-start | bytes 786432 | tf_op jit(solution)/shard_map/all_to_all | solution.py:132
  46.2 1.2 copy-start.5
  47.5 1.0 copy-start.4
  49.5 3.1 %copy-start.8 = (bf16[16,32,384]{2,1,0:T(8,128)(2,1)}, bf16[16,32,384]{2,1,0:T(8,128)(2,1)S(1)}, u32[]{:S(2)}) copy-start(bf16[16,32,384]{2,1,0:T(8,128)(2,1)S(1)} %get-tuple-element.22) | copy-start | bytes 1179652
  58.9 3.0 %copy-start.12 = (f32[16,32,6,32]{1,3,2,0:T(8,128)S(1)}, f32[16,32,6,32]{1,3,2,0:T(8,128)}, u32[]{:S(2)}) copy-start(f32[16,32,6,32]{1,3,2,0:T(8,128)} %get-tuple-element.25) | copy-start | bytes 1179652
  61.9 1.6 %copy-start.9 = (bf16[16,32,384]{2,1,0:T(8,128)(2,1)S(1)}, bf16[16,32,384]{2,1,0:T(8,128)(2,1)}, u32[]{:S(2)}) copy-start(bf16[16,32,384]{2,1,0:T(8,128)(2,1)} %copy-done.8) | copy-start | bytes 1179652
  63.5 4.6 %copy-start.7 = (bf16[16,32,384]{2,1,0:T(8,128)(2,1)S(1)}, bf16[16,32,384]{2,1,0:T(8,128)(2,1)}, u32[]{:S(2)}) copy-start(bf16[16,32,384]{2,1,0:T(8,128)(2,1)} %get-tuple-element.23) | copy-start | bytes 1179652
  68.1 4.6 %copy-start.13 = (bf16[16,32,384]{2,1,0:T(8,128)(2,1)S(1)}, bf16[16,32,384]{2,1,0:T(8,128)(2,1)}, u32[]{:S(2)}) copy-start(bf16[16,32,384]{2,1,0:T(8,128)(2,1)} %fusion.46) | copy-start | bytes 1179652
  72.7 2.6 %copy-start.6 = (bf16[16,32,768]{2,1,0:T(8,128)(2,1)S(1)}, bf16[16,32,768]{2,1,0:T(8,128)(2,1)}, u32[]{:S(2)}) copy-start(bf16[16,32,768]{2,1,0:T(8,128)(2,1)} %copy-done.5) | copy-start | bytes 2359300
  72.7 2.6 %copy-start.14 = (bf16[16,32,384]{2,1,0:T(8,128)(2,1)S(1)}, bf16[16,32,384]{2,1,0:T(8,128)(2,1)}, u32[]{:S(2)}) copy-start(bf16[16,32,384]{2,1,0:T(8,128)(2,1)} %fusion.43) | copy-start | bytes 1179652
  72.7 2.6 %copy-start.15 = (bf16[16,32,384]{2,1,0:T(8,128)(2,1)S(1)}, bf16[16,32,384]{2,1,0:T(8,128)(2,1)}, u32[]{:S(2)}) copy-start(bf16[16,32,384]{2,1,0:T(8,128)(2,1)} %fusion.49) | copy-start | bytes 1179652
  76.5 2.0 %copy-start.1 = (f32[768,1152]{1,0:T(8,128)}, f32[768,1152]{1,0:T(8,128)S(1)}, u32[]{:S(2)}) copy-start(f32[768,1152]{1,0:T(8,128)S(1)} %convolution_bitcast_fusion) | copy-start | bytes 10616836
  78.6 8.1 %collective-permute-start = (f32[4,2,48,1152]{3,2,1,0:T(8,128)S(1)}, f32[4,2,48,1152]{3,2,1,0:T(8,128)}, u32[]{:S(2)}, u32[]{:S(2)}) collective-permute-start(f32[4,2,48,1152]{3,2,1,0:T(8,128)S(1)} %dynamic-slice_bitcast_fusion), channel_id=1, source_target_pairs={{0,1},{1,0},{2,3},{3,2},{4,5},{5,4},{6,7},{7,6},{8,9},{9,8},{10,11... | collective-permute-start | bytes 5308424 | tf_op jit(solution)/shard_map/ppermute | solution.py:97
  81.8 37.5 %all-to-all-start.2 = ((bf16[2,32,8,768]{3,2,0,1:T(8,128)(2,1)}), bf16[2,32,8,768]{3,2,0,1:T(8,128)(2,1)}, u32[]{:S(2)}, u32[]{:S(2)}) async-start(bf16[2,32,8,768]{3,2,0,1:T(8,128)(2,1)} %bitcast.90), calls=%async_computation.2 | async-start | bytes 1572864 | tf_op jit(solution)/shard_map/all_to_all | solution.py:144
  89.8 14.0 %collective-permute-start.3 = (bf16[2,48,1152]{2,1,0:T(8,128)(2,1)}, bf16[2,48,1152]{2,1,0:T(8,128)(2,1)}, u32[]{:S(2)}, u32[]{:S(2)}) collective-permute-start(bf16[2,48,1152]{2,1,0:T(8,128)(2,1)} %get-tuple-element.19), channel_id=1, source_target_pairs={{0,12},{1,13},{2,14},{3,15},{4,0},{5,1},{6,2},{7,3},{8,4},{9,5},{1... | collective-permute-start | bytes 663560 | tf_op jit(solution)/shard_map/ppermute | solution.py:97
  94.3 12.3 %collective-permute-start.2 = (bf16[2,48,1152]{2,1,0:T(8,128)(2,1)}, bf16[2,48,1152]{2,1,0:T(8,128)(2,1)}, u32[]{:S(2)}, u32[]{:S(2)}) collective-permute-start(bf16[2,48,1152]{2,1,0:T(8,128)(2,1)} %get-tuple-element.20), channel_id=1, source_target_pairs={{0,8},{1,9},{2,10},{3,11},{4,12},{5,13},{6,14},{7,15},{8,0},{9,1},... | collective-permute-start | bytes 663560 | tf_op jit(solution)/shard_map/ppermute | solution.py:97
  98.1 13.7 %collective-permute-start.1 = (bf16[2,48,1152]{2,1,0:T(8,128)(2,1)}, bf16[2,48,1152]{2,1,0:T(8,128)(2,1)}, u32[]{:S(2)}, u32[]{:S(2)}) collective-permute-start(bf16[2,48,1152]{2,1,0:T(8,128)(2,1)} %get-tuple-element.18), channel_id=1, source_target_pairs={{0,4},{1,5},{2,6},{3,7},{4,8},{5,9},{6,10},{7,11},{8,12},{9,13},{1... | collective-permute-start | bytes 663560 | tf_op jit(solution)/shard_map/ppermute | solution.py:97
  113.0 0.8 copy-start.2
  113.8 10.1 %copy-start.3 = (f32[2,48,1152]{2,1,0:T(8,128)S(1)}, f32[2,48,1152]{2,1,0:T(8,128)}, u32[]{:S(2)}) copy-start(f32[2,48,1152]{2,1,0:T(8,128)} %copy-done.2) | copy-start | bytes 1327108
  113.8 10.1 %collective-permute-start.4 = (bf16[48,1152]{1,0:T(8,128)(2,1)S(1)}, bf16[48,1152]{1,0:T(8,128)(2,1)S(1)}, u32[]{:S(2)}, u32[]{:S(2)}) collective-permute-start(bf16[48,1152]{1,0:T(8,128)(2,1)S(1)} %fusion.75), channel_id=1, source_target_pairs={{0,2},{1,3},{2,0},{3,1},{4,6},{5,7},{6,4},{7,5},{8,10},{9,11},{10,... | collective-permute-start | bytes 331784 | tf_op jit(solution)/shard_map/ppermute | solution.py:97

commit v16 on v15

--- a/solution.py
+++ b/solution.py
@@ -88,7 +88,7 @@
     mine = lax.dynamic_index_in_dim(blocks, digit, axis=dim, keepdims=False)
     total = mine.astype(jnp.float32)
     n_band = lax.axis_size("band")
-    for shift in range(1, n):
+    for shift in sorted(range(1, n), key=lambda k: -min(k, n - k)):
         part = lax.dynamic_index_in_dim(blocks, (digit + shift) % n, axis=dim, keepdims=False)
         pairs = []
         for source in range(n_band):

time: 152 us -> 152 us (level); the launches traced: 151 us -> 149 us
  starting transfers between devices: 47.8 us -> 45.8 us
  waiting for transfers between devices: 35.7 us -> 37.5 us
    ppermute x5, starting transfers between devices: 18.7 us -> 16.7 us  [exchange(): got = lax.ppermute(part.astype(wire), 'band', pairs)]
    ppermute x5, waiting for transfers between devices: 14.3 us -> 16.1 us  [exchange(): got = lax.ppermute(part.astype(wire), 'band', pairs)]
where the time goes in v16:
time: 152 us; the launch traced here: 149 us
  starting transfers between devices  45.8 us (30%)
  waiting for transfers between devices  37.5 us (25%)
  blocking collectives  23.2 us (15%)
  matrix products  21.8 us (14%)
  local copies, waits for them, and re-layouts  15.6 us (10%)
  other arithmetic  4.45 us (3%)
    all_to_all x1, blocking collectives, dp_stage(): blocks = lax.all_to_all(blocks.astype(jnp.bfloat16), 'dp', 0, 0, tiled=True)  23.2 us
    ppermute x5, starting transfers between devices, exchange(): got = lax.ppermute(part.astype(wire), 'band', pairs)  16.7 us
    ppermute x5, waiting for transfers between devices, exchange(): got = lax.ppermute(part.astype(wire), 'band', pairs)  16.1 us
    all_to_all x1, waiting for transfers between devices, body(): lax.all_to_all(cell_states, 'band', split_axis=2, concat_axis=1, tiled=True)  15.6 us
    all_to_all x1, starting transfers between devices, body(): lax.all_to_all(cell_states, 'band', split_axis=2, concat_axis=1, tiled=True)  14.4 us
    all_to_all x1, starting transfers between devices, body(): lax.all_to_all(grads_by_col, 'band', split_axis=0, concat_axis=2, tiled=T...  9.75 us
    unnamed x35, local copies, waits for them, and re-layouts  6.66 us
    all_to_all x1, waiting for transfers between devices, body(): lax.all_to_all(grads_by_col, 'band', split_axis=0, concat_axis=2, tiled=T...  5.78 us
  transfers between devices with their start and end apart: 8, of which 6 were waited for; matrix products, arithmetic and copies ran while one was open for 9% of the time, Pallas kernels for 0%

profile of v16, /device:TPU:1, one launch (start us, length us, event | category | flops | bytes accessed | tf_op | source)
XLA Modules:
  0.0 149.5 jit_solution(11912055227238534078)
XLA Ops:
  0.7 3.0 %copy.16 = bf16[2,2,128,768]{3,1,0,2:T(2,128)(2,1)} copy(bf16[2,2,128,768]{3,2,1,0:T(8,128)(2,1)} %param.4) | data formatting | bytes 1572864 | tf_op args[0]
  3.6 14.4 %all-to-all-start = ((bf16[2,2,128,768]{3,1,0,2:T(2,128)(2,1)}), bf16[2,2,128,768]{3,1,0,2:T(2,128)(2,1)S(1)}, u32[]{:S(2)}, u32[]{:S(2)}) async-start(bf16[2,2,128,768]{3,1,0,2:T(2,128)(2,1)} %copy.16), calls=%async_computation | async-start | bytes 1572864 | tf_op jit(solution)/shard_map/all_to_all | solution.py:127
  19.4 15.6 %all-to-all-done = bf16[2,2,128,768]{3,1,0,2:T(2,128)(2,1)S(1)} async-done(((bf16[2,2,128,768]{3,1,0,2:T(2,128)(2,1)}), bf16[2,2,128,768]{3,1,0,2:T(2,128)(2,1)S(1)}, u32[]{:S(2)}, u32[]{:S(2)}) %all-to-all-start) | async-done | bytes 786464 | tf_op jit(solution)/shard_map/all_to_all | solution.py:127
  36.3 9.8 %all-to-all-start.1 = ((bf16[128,2,2,384]{3,2,1,0:T(2,128)(2,1)}), bf16[128,2,2,384]{3,2,1,0:T(2,128)(2,1)S(1)}, u32[]{:S(2)}, u32[]{:S(2)}) async-start(bf16[128,2,2,384]{3,2,1,0:T(2,128)(2,1)} %bitcast.101), calls=%async_computation.1 | async-start | bytes 786432 | tf_op jit(solution)/shard_map/all_to_all | solution.py:132
  49.5 3.1 %fusion.92 = (f32[16,32,6]{1,2,0:T(8,128)S(1)}, f32[16,32,6,32]{1,3,2,0:T(8,128)}) fusion(pred[6,384]{1,0:T(8,128)(4,1)S(1)} %iota_compare_fusion, bf16[16,32,384]{2,1,0:T(8,128)(2,1)S(1)} %get-tuple-element.22, pred[16,32,32]{1,2,0:T(8,128)(4,1)S(1)} %compare_or_fusion, bf16[16,32,1152]{2,1,0:T(8,128)(2,1)} %bitcast.105), kind=kOutput, calls=%fused_computation.102 | convolution fusion | flops 77070368 | bytes 1210624 | tf_op jit(solution)/shard_map/sub | solution.py:52
  52.7 5.8 %all-to-all-done.1 = bf16[128,2,2,384]{3,2,1,0:T(2,128)(2,1)S(1)} async-done(((bf16[128,2,2,384]{3,2,1,0:T(2,128)(2,1)}), bf16[128,2,2,384]{3,2,1,0:T(2,128)(2,1)S(1)}, u32[]{:S(2)}, u32[]{:S(2)}) %all-to-all-start.1) | async-done | bytes 393248 | tf_op jit(solution)/shard_map/all_to_all | solution.py:132
  58.9 3.0 %fusion.10 = f32[16,32,6,32]{1,3,2,0:T(8,128)} fusion(bf16[16,32,384,1]{2,1,3,0:T(8,128)(2,1)S(1)} %bitcast.108, pred[6,384]{1,0:T(8,128)(4,1)S(1)} %iota_compare_fusion, bf16[16,32,384]{2,1,0:T(8,128)(2,1)} %get-tuple-element.21), kind=kOutput, calls=%fused_computation.12 | convolution fusion | flops 76677120 | bytes 1181952 | tf_op jit(solution)/shard_map/bid,bhjd->bihj/dot_general | solution.py:58
  63.5 4.6 %fusion.43 = bf16[16,32,384]{2,1,0:T(8,128)(2,1)} fusion(pred[6,384]{1,0:T(8,128)(4,1)S(1)} %iota_compare_fusion, bf16[16,32,384]{2,1,0:T(8,128)(2,1)S(1)} %copy-done.9, f32[16,32,6,32]{1,3,2,0:T(8,128)} %fusion.10, f32[16,32,6,32]{1,3,2,0:T(8,128)} %get-tuple-element.25, f32[16,32,6]{1,2,0:T(8,128)S(1)} %get-tuple-element.24), kind=kOutput, calls=%fused_computation.42 | convolution fusion | flops 77564960 | bytes 1587456 | tf_op jit(solution)/shard_map/bihj,bhjd->bid/dot_general | solution.py:63
  68.1 4.6 %fusion.49 = bf16[16,32,384]{2,1,0:T(8,128)(2,1)} fusion(pred[6,384]{1,0:T(8,128)(4,1)S(1)} %iota_compare_fusion, bf16[16,32,384]{2,1,0:T(8,128)(2,1)S(1)} %copy-done.7, f32[16,32,6,32]{1,3,2,0:T(8,128)} %fusion.10, f32[16,32,6,32]{1,3,2,0:T(8,128)} %get-tuple-element.25, f32[16,32,6]{1,2,0:T(8,128)S(1)} %get-tuple-element.24), kind=kOutput, calls=%fused_computation.44 | convolution fusion | flops 77564960 | bytes 1587456 | tf_op jit(solution)/shard_map/bihj,bhid->bjd/dot_general | solution.py:66
  72.7 2.5 %fusion.23 = (f32[16,32]{1,0:T(8,128)S(1)}, f32[16,32,768]{2,1,0:T(8,128)S(1)}) fusion(bf16[16,32,768]{2,1,0:T(8,128)(2,1)S(1)} %bitcast.95, f32[16,32]{1,0:T(8,128)S(1)} %add_rsqrt_fusion, bf16[768,1152]{1,0:T(8,128)(2,1)S(1)} %copy-done, bf16[16,32,384]{2,1,0:T(8,128)(2,1)S(1)} %copy-done.13, bf16[16,32,384]{2,1,0:T(8,128)(2,1)} %fusion.49, ...), kind=kOutput, calls=%fused_computation.29 | convolution fusion | flops 911080960 | bytes 5312512 | tf_op jit(solution)/shard_map/dot_general | solution.py:78
  76.9 1.7 %copy.35 = bf16[2,8,32,768]{3,1,0,2:T(8,128)(2,1)} copy(bf16[2,8,32,768]{3,2,1,0:T(8,128)(2,1)S(1)} %bitcast.100) | data formatting | bytes 1572864 | tf_op jit(solution)/shard_map/reshape | solution.py:142
  78.6 3.1 %collective-permute-start = (f32[4,2,48,1152]{3,2,1,0:T(8,128)S(1)}, f32[4,2,48,1152]{3,2,1,0:T(8,128)}, u32[]{:S(2)}, u32[]{:S(2)}) collective-permute-start(f32[4,2,48,1152]{3,2,1,0:T(8,128)S(1)} %dynamic-slice_bitcast_fusion), channel_id=1, source_target_pairs={{0,1},{1,0},{2,3},{3,2},{4,5},{5,4},{6,7},{7,6},{8,9},{9,8},{10,11... | collective-permute-start | bytes 5308424 | tf_op jit(solution)/shard_map/ppermute | solution.py:97
  81.8 4.9 %all-to-all-start.2 = ((bf16[2,32,8,768]{3,2,0,1:T(8,128)(2,1)}), bf16[2,32,8,768]{3,2,0,1:T(8,128)(2,1)}, u32[]{:S(2)}, u32[]{:S(2)}) async-start(bf16[2,32,8,768]{3,2,0,1:T(8,128)(2,1)} %bitcast.90), calls=%async_computation.2 | async-start | bytes 1572864 | tf_op jit(solution)/shard_map/all_to_all | solution.py:144
  86.7 2.2 %bitcast_add_fusion = f32[4,2,48,1152]{3,2,1,0:T(8,128)S(1)} fusion(f32[4,2,48,1152]{3,2,1,0:T(8,128)} %collective-permute-done, f32[4,2,2,48,1152]{4,3,2,1,0:T(8,128)} %bitcast.98, s32[]{:T(128)S(6)} %select_n.104), kind=kLoop, calls=%fused_computation.24 | loop fusion | flops 442368 | bytes 5308420 | tf_op jit(solution)/shard_map/add | solution.py:98
  89.8 4.5 %collective-permute-start.3 = (bf16[2,48,1152]{2,1,0:T(8,128)(2,1)}, bf16[2,48,1152]{2,1,0:T(8,128)(2,1)}, u32[]{:S(2)}, u32[]{:S(2)}) collective-permute-start(bf16[2,48,1152]{2,1,0:T(8,128)(2,1)} %get-tuple-element.19), channel_id=1, source_target_pairs={{0,12},{1,13},{2,14},{3,15},{4,0},{5,1},{6,2},{7,3},{8,4},{9,5},{1... | collective-permute-start | bytes 663560 | tf_op jit(solution)/shard_map/ppermute | solution.py:97
  94.3 2.0 %collective-permute-start.2 = (bf16[2,48,1152]{2,1,0:T(8,128)(2,1)}, bf16[2,48,1152]{2,1,0:T(8,128)(2,1)}, u32[]{:S(2)}, u32[]{:S(2)}) collective-permute-start(bf16[2,48,1152]{2,1,0:T(8,128)(2,1)} %get-tuple-element.20), channel_id=1, source_target_pairs={{0,4},{1,5},{2,6},{3,7},{4,8},{5,9},{6,10},{7,11},{8,12},{9,13},{1... | collective-permute-start | bytes 663560 | tf_op jit(solution)/shard_map/ppermute | solution.py:97
  96.3 3.7 %collective-permute-start.1 = (bf16[2,48,1152]{2,1,0:T(8,128)(2,1)}, bf16[2,48,1152]{2,1,0:T(8,128)(2,1)}, u32[]{:S(2)}, u32[]{:S(2)}) collective-permute-start(bf16[2,48,1152]{2,1,0:T(8,128)(2,1)} %get-tuple-element.18), channel_id=1, source_target_pairs={{0,8},{1,9},{2,10},{3,11},{4,12},{5,13},{6,14},{7,15},{8,0},{9,1},... | collective-permute-start | bytes 663560 | tf_op jit(solution)/shard_map/ppermute | solution.py:97
  100.1 3.7 %collective-permute-done.3 = bf16[2,48,1152]{2,1,0:T(8,128)(2,1)} collective-permute-done((bf16[2,48,1152]{2,1,0:T(8,128)(2,1)}, bf16[2,48,1152]{2,1,0:T(8,128)(2,1)}, u32[]{:S(2)}, u32[]{:S(2)}) %collective-permute-start.3) | collective-permute-done | bytes 221216 | tf_op jit(solution)/shard_map/ppermute | solution.py:97
  103.8 2.8 %collective-permute-done.2 = bf16[2,48,1152]{2,1,0:T(8,128)(2,1)} collective-permute-done((bf16[2,48,1152]{2,1,0:T(8,128)(2,1)}, bf16[2,48,1152]{2,1,0:T(8,128)(2,1)}, u32[]{:S(2)}, u32[]{:S(2)}) %collective-permute-start.2) | collective-permute-done | bytes 221216 | tf_op jit(solution)/shard_map/ppermute | solution.py:97
  106.5 5.1 %collective-permute-done.1 = bf16[2,48,1152]{2,1,0:T(8,128)(2,1)} collective-permute-done((bf16[2,48,1152]{2,1,0:T(8,128)(2,1)}, bf16[2,48,1152]{2,1,0:T(8,128)(2,1)}, u32[]{:S(2)}, u32[]{:S(2)}) %collective-permute-start.1) | collective-permute-done | bytes 221216 | tf_op jit(solution)/shard_map/ppermute | solution.py:97
  113.7 3.5 %collective-permute-start.4 = (bf16[48,1152]{1,0:T(8,128)(2,1)S(1)}, bf16[48,1152]{1,0:T(8,128)(2,1)S(1)}, u32[]{:S(2)}, u32[]{:S(2)}) collective-permute-start(bf16[48,1152]{1,0:T(8,128)(2,1)S(1)} %fusion.75), channel_id=1, source_target_pairs={{0,2},{1,3},{2,0},{3,1},{4,6},{5,7},{6,4},{7,5},{8,10},{9,11},{10,... | collective-permute-start | bytes 331784 | tf_op jit(solution)/shard_map/ppermute | solution.py:97
  117.2 2.1 %copy.34 = bf16[2,2,16,8,768]{4,3,2,1,0:T(8,128)(2,1)} copy(bf16[2,2,16,8,768]{4,3,0,1,2:T(8,128)(2,1)} %bitcast.37) | data formatting | bytes 1572864 | tf_op jit(solution)/shard_map/all_to_all | solution.py:144
  119.2 4.5 %collective-permute-done.4 = bf16[48,1152]{1,0:T(8,128)(2,1)S(1)} collective-permute-done((bf16[48,1152]{1,0:T(8,128)(2,1)S(1)}, bf16[48,1152]{1,0:T(8,128)(2,1)S(1)}, u32[]{:S(2)}, u32[]{:S(2)}) %collective-permute-start.4) | collective-permute-done | bytes 110624 | tf_op jit(solution)/shard_map/ppermute | solution.py:97
  125.5 23.2 %all_to_all.59 = bf16[32,14,128]{2,1,0:T(8,128)(2,1)S(1)} all-to-all(bf16[32,14,128]{2,1,0:T(8,128)(2,1)S(1)} %convert_element_type.93), channel_id=1, replica_groups=mesh['dp'=32,'band'=16] {'dp'}, dimensions={0} | all-to-all | bytes 229376 | tf_op jit(solution)/shard_map/all_to_all | solution.py:120
  (66 shorter events, 15.2 us)
Async XLA Ops:
  0.6 45.6 %copy-start = (bf16[768,1152]{1,0:T(8,128)(2,1)S(1)}, bf16[768,1152]{1,0:T(8,128)(2,1)}, u32[]{:S(2)}) copy-start(bf16[768,1152]{1,0:T(8,128)(2,1)} %param.7) | copy-start | bytes 5308420
  0.6 17.4 %copy-start.10 = (bf16[2,2,128,384]{3,2,1,0:T(8,128)(2,1)S(1)}, bf16[2,2,128,384]{3,2,1,0:T(8,128)(2,1)}, u32[]{:S(2)}) copy-start(bf16[2,2,128,384]{3,2,1,0:T(8,128)(2,1)} %param.5) | copy-start | bytes 1179652
  3.6 15.6 %copy-start.11 = (s32[2,8,32]{2,1,0:T(8,128)S(1)}, s32[2,8,32]{2,1,0:T(8,128)}, u32[]{:S(2)}) copy-start(s32[2,8,32]{2,1,0:T(8,128)} %param.6) | copy-start | bytes 6148
  3.6 31.4 %all-to-all-start = ((bf16[2,2,128,768]{3,1,0,2:T(2,128)(2,1)}), bf16[2,2,128,768]{3,1,0,2:T(2,128)(2,1)S(1)}, u32[]{:S(2)}, u32[]{:S(2)}) async-start(bf16[2,2,128,768]{3,1,0,2:T(2,128)(2,1)} %copy.16), calls=%async_computation | async-start | bytes 1572864 | tf_op jit(solution)/shard_map/all_to_all | solution.py:127
  36.3 22.1 %all-to-all-start.1 = ((bf16[128,2,2,384]{3,2,1,0:T(2,128)(2,1)}), bf16[128,2,2,384]{3,2,1,0:T(2,128)(2,1)S(1)}, u32[]{:S(2)}, u32[]{:S(2)}) async-start(bf16[128,2,2,384]{3,2,1,0:T(2,128)(2,1)} %bitcast.101), calls=%async_computation.1 | async-start | bytes 786432 | tf_op jit(solution)/shard_map/all_to_all | solution.py:132
  46.2 1.2 copy-start.5
  47.5 1.0 copy-start.4
  49.5 3.1 %copy-start.8 = (bf16[16,32,384]{2,1,0:T(8,128)(2,1)}, bf16[16,32,384]{2,1,0:T(8,128)(2,1)S(1)}, u32[]{:S(2)}) copy-start(bf16[16,32,384]{2,1,0:T(8,128)(2,1)S(1)} %get-tuple-element.22) | copy-start | bytes 1179652
  58.9 3.0 %copy-start.12 = (f32[16,32,6,32]{1,3,2,0:T(8,128)S(1)}, f32[16,32,6,32]{1,3,2,0:T(8,128)}, u32[]{:S(2)}) copy-start(f32[16,32,6,32]{1,3,2,0:T(8,128)} %get-tuple-element.25) | copy-start | bytes 1179652
  61.9 1.6 %copy-start.9 = (bf16[16,32,384]{2,1,0:T(8,128)(2,1)S(1)}, bf16[16,32,384]{2,1,0:T(8,128)(2,1)}, u32[]{:S(2)}) copy-start(bf16[16,32,384]{2,1,0:T(8,128)(2,1)} %copy-done.8) | copy-start | bytes 1179652
  63.5 4.6 %copy-start.7 = (bf16[16,32,384]{2,1,0:T(8,128)(2,1)S(1)}, bf16[16,32,384]{2,1,0:T(8,128)(2,1)}, u32[]{:S(2)}) copy-start(bf16[16,32,384]{2,1,0:T(8,128)(2,1)} %get-tuple-element.23) | copy-start | bytes 1179652
  68.1 4.6 %copy-start.13 = (bf16[16,32,384]{2,1,0:T(8,128)(2,1)S(1)}, bf16[16,32,384]{2,1,0:T(8,128)(2,1)}, u32[]{:S(2)}) copy-start(bf16[16,32,384]{2,1,0:T(8,128)(2,1)} %fusion.46) | copy-start | bytes 1179652
  72.7 2.6 %copy-start.6 = (bf16[16,32,768]{2,1,0:T(8,128)(2,1)S(1)}, bf16[16,32,768]{2,1,0:T(8,128)(2,1)}, u32[]{:S(2)}) copy-start(bf16[16,32,768]{2,1,0:T(8,128)(2,1)} %copy-done.5) | copy-start | bytes 2359300
  72.7 2.6 %copy-start.14 = (bf16[16,32,384]{2,1,0:T(8,128)(2,1)S(1)}, bf16[16,32,384]{2,1,0:T(8,128)(2,1)}, u32[]{:S(2)}) copy-start(bf16[16,32,384]{2,1,0:T(8,128)(2,1)} %fusion.43) | copy-start | bytes 1179652
  72.7 2.6 %copy-start.15 = (bf16[16,32,384]{2,1,0:T(8,128)(2,1)S(1)}, bf16[16,32,384]{2,1,0:T(8,128)(2,1)}, u32[]{:S(2)}) copy-start(bf16[16,32,384]{2,1,0:T(8,128)(2,1)} %fusion.49) | copy-start | bytes 1179652
  76.5 2.0 %copy-start.1 = (f32[768,1152]{1,0:T(8,128)}, f32[768,1152]{1,0:T(8,128)S(1)}, u32[]{:S(2)}) copy-start(f32[768,1152]{1,0:T(8,128)S(1)} %convolution_bitcast_fusion) | copy-start | bytes 10616836
  78.6 8.1 %collective-permute-start = (f32[4,2,48,1152]{3,2,1,0:T(8,128)S(1)}, f32[4,2,48,1152]{3,2,1,0:T(8,128)}, u32[]{:S(2)}, u32[]{:S(2)}) collective-permute-start(f32[4,2,48,1152]{3,2,1,0:T(8,128)S(1)} %dynamic-slice_bitcast_fusion), channel_id=1, source_target_pairs={{0,1},{1,0},{2,3},{3,2},{4,5},{5,4},{6,7},{7,6},{8,9},{9,8},{10,11... | collective-permute-start | bytes 5308424 | tf_op jit(solution)/shard_map/ppermute | solution.py:97
  81.8 35.3 %all-to-all-start.2 = ((bf16[2,32,8,768]{3,2,0,1:T(8,128)(2,1)}), bf16[2,32,8,768]{3,2,0,1:T(8,128)(2,1)}, u32[]{:S(2)}, u32[]{:S(2)}) async-start(bf16[2,32,8,768]{3,2,0,1:T(8,128)(2,1)} %bitcast.90), calls=%async_computation.2 | async-start | bytes 1572864 | tf_op jit(solution)/shard_map/all_to_all | solution.py:144
  89.8 14.0 %collective-permute-start.3 = (bf16[2,48,1152]{2,1,0:T(8,128)(2,1)}, bf16[2,48,1152]{2,1,0:T(8,128)(2,1)}, u32[]{:S(2)}, u32[]{:S(2)}) collective-permute-start(bf16[2,48,1152]{2,1,0:T(8,128)(2,1)} %get-tuple-element.19), channel_id=1, source_target_pairs={{0,12},{1,13},{2,14},{3,15},{4,0},{5,1},{6,2},{7,3},{8,4},{9,5},{1... | collective-permute-start | bytes 663560 | tf_op jit(solution)/shard_map/ppermute | solution.py:97
  94.3 12.2 %collective-permute-start.2 = (bf16[2,48,1152]{2,1,0:T(8,128)(2,1)}, bf16[2,48,1152]{2,1,0:T(8,128)(2,1)}, u32[]{:S(2)}, u32[]{:S(2)}) collective-permute-start(bf16[2,48,1152]{2,1,0:T(8,128)(2,1)} %get-tuple-element.20), channel_id=1, source_target_pairs={{0,4},{1,5},{2,6},{3,7},{4,8},{5,9},{6,10},{7,11},{8,12},{9,13},{1... | collective-permute-start | bytes 663560 | tf_op jit(solution)/shard_map/ppermute | solution.py:97
  96.3 15.3 %collective-permute-start.1 = (bf16[2,48,1152]{2,1,0:T(8,128)(2,1)}, bf16[2,48,1152]{2,1,0:T(8,128)(2,1)}, u32[]{:S(2)}, u32[]{:S(2)}) collective-permute-start(bf16[2,48,1152]{2,1,0:T(8,128)(2,1)} %get-tuple-element.18), channel_id=1, source_target_pairs={{0,8},{1,9},{2,10},{3,11},{4,12},{5,13},{6,14},{7,15},{8,0},{9,1},... | collective-permute-start | bytes 663560 | tf_op jit(solution)/shard_map/ppermute | solution.py:97
  112.9 0.8 copy-start.2
  113.7 10.1 %copy-start.3 = (f32[2,48,1152]{2,1,0:T(8,128)S(1)}, f32[2,48,1152]{2,1,0:T(8,128)}, u32[]{:S(2)}) copy-start(f32[2,48,1152]{2,1,0:T(8,128)} %copy-done.2) | copy-start | bytes 1327108
  113.7 10.0 %collective-permute-start.4 = (bf16[48,1152]{1,0:T(8,128)(2,1)S(1)}, bf16[48,1152]{1,0:T(8,128)(2,1)S(1)}, u32[]{:S(2)}, u32[]{:S(2)}) collective-permute-start(bf16[48,1152]{1,0:T(8,128)(2,1)S(1)} %fusion.75), channel_id=1, source_target_pairs={{0,2},{1,3},{2,0},{3,1},{4,6},{5,7},{6,4},{7,5},{8,10},{9,11},{10,... | collective-permute-start | bytes 331784 | tf_op jit(solution)/shard_map/ppermute | solution.py:97

commit v17 on v16

--- a/solution.py
+++ b/solution.py
@@ -105,7 +105,7 @@
     rows = d_in // n_band
     band = lax.axis_index("band")
     blocks = partial_w.reshape(n_band // 4, 2, 2, rows, d_out)
-    blocks = exchange(blocks, 2, band % 2, 1, 2)
+    blocks = exchange(blocks, 2, band % 2, 1, 2, jnp.bfloat16)
     blocks = exchange(blocks, 0, band // 4, 4, n_band // 4, jnp.bfloat16)
     return exchange(blocks, 0, (band // 2) % 2, 2, 2, jnp.bfloat16)
 

time: 152 us -> 157 us (1.033)
  blocking collectives: 23.2 us -> 29.2 us
  waiting for transfers between devices: 37.5 us -> 35.2 us
    all_to_all x1, blocking collectives: 23.2 us -> 29.2 us  [dp_stage(): blocks = lax.all_to_all(blocks.astype(jnp.bfloat16), 'dp', 0, 0, tiled=True)]
    ppermute x5, waiting for transfers between devices: 16.1 us -> 13.8 us  [exchange(): got = lax.ppermute(part.astype(wire), 'band', pairs)]
    unnamed x35 -> x33, local copies, waits for them, and re-layouts: 6.66 us -> 6.66 us
  transfers between devices with their start and end apart: 8 -> 8, of which waited for: 6 -> 5; matrix products, arithmetic and copies ran while one was open for 9% -> 6% of each run, Pallas kernels for 0% -> 0%
where the time goes in v17:
time: 157 us; the launch traced here: 155 us
  starting transfers between devices  47.2 us (30%)
  waiting for transfers between devices  35.2 us (22%)
  blocking collectives  29.2 us (19%)
  matrix products  21.8 us (14%)
  local copies, waits for them, and re-layouts  15.6 us (10%)
  other arithmetic  5.1 us (3%)
    all_to_all x1, blocking collectives, dp_stage(): blocks = lax.all_to_all(blocks.astype(jnp.bfloat16), 'dp', 0, 0, tiled=True)  29.2 us
    ppermute x5, starting transfers between devices, exchange(): got = lax.ppermute(part.astype(wire), 'band', pairs)  18.1 us
    all_to_all x1, waiting for transfers between devices, body(): lax.all_to_all(cell_states, 'band', split_axis=2, concat_axis=1, tiled=True)  15.6 us
    all_to_all x1, starting transfers between devices, body(): lax.all_to_all(cell_states, 'band', split_axis=2, concat_axis=1, tiled=True)  14.4 us
    ppermute x5, waiting for transfers between devices, exchange(): got = lax.ppermute(part.astype(wire), 'band', pairs)  13.8 us
    all_to_all x1, starting transfers between devices, body(): lax.all_to_all(grads_by_col, 'band', split_axis=0, concat_axis=2, tiled=T...  9.75 us
    unnamed x33, local copies, waits for them, and re-layouts  6.66 us
    all_to_all x1, waiting for transfers between devices, body(): lax.all_to_all(grads_by_col, 'band', split_axis=0, concat_axis=2, tiled=T...  5.78 us
  transfers between devices with their start and end apart: 8, of which 5 were waited for; matrix products, arithmetic and copies ran while one was open for 6% of the time, Pallas kernels for 0%

profile of v17, /device:TPU:1, one launch (start us, length us, event | category | flops | bytes accessed | tf_op | source)
XLA Modules:
  0.0 155.2 jit_solution(14949308355018212822)
XLA Ops:
  0.7 3.0 %copy.17 = bf16[2,2,128,768]{3,1,0,2:T(2,128)(2,1)} copy(bf16[2,2,128,768]{3,2,1,0:T(8,128)(2,1)} %param.4) | data formatting | bytes 1572864 | tf_op args[0]
  3.6 14.4 %all-to-all-start = ((bf16[2,2,128,768]{3,1,0,2:T(2,128)(2,1)}), bf16[2,2,128,768]{3,1,0,2:T(2,128)(2,1)S(1)}, u32[]{:S(2)}, u32[]{:S(2)}) async-start(bf16[2,2,128,768]{3,1,0,2:T(2,128)(2,1)} %copy.17), calls=%async_computation | async-start | bytes 1572864 | tf_op jit(solution)/shard_map/all_to_all | solution.py:127
  19.4 15.6 %all-to-all-done = bf16[2,2,128,768]{3,1,0,2:T(2,128)(2,1)S(1)} async-done(((bf16[2,2,128,768]{3,1,0,2:T(2,128)(2,1)}), bf16[2,2,128,768]{3,1,0,2:T(2,128)(2,1)S(1)}, u32[]{:S(2)}, u32[]{:S(2)}) %all-to-all-start) | async-done | bytes 786464 | tf_op jit(solution)/shard_map/all_to_all | solution.py:127
  36.3 9.8 %all-to-all-start.1 = ((bf16[128,2,2,384]{3,2,1,0:T(2,128)(2,1)}), bf16[128,2,2,384]{3,2,1,0:T(2,128)(2,1)S(1)}, u32[]{:S(2)}, u32[]{:S(2)}) async-start(bf16[128,2,2,384]{3,2,1,0:T(2,128)(2,1)} %bitcast.106), calls=%async_computation.1 | async-start | bytes 786432 | tf_op jit(solution)/shard_map/all_to_all | solution.py:132
  49.6 3.1 %fusion.93 = (f32[16,32,6]{1,2,0:T(8,128)S(1)}, f32[16,32,6,32]{1,3,2,0:T(8,128)}) fusion(pred[6,384]{1,0:T(8,128)(4,1)S(1)} %iota_compare_fusion, bf16[16,32,384]{2,1,0:T(8,128)(2,1)S(1)} %get-tuple-element.22, pred[16,32,32]{1,2,0:T(8,128)(4,1)S(1)} %compare_or_fusion, bf16[16,32,1152]{2,1,0:T(8,128)(2,1)} %bitcast.110), kind=kOutput, calls=%fused_computation.103 | convolution fusion | flops 77070368 | bytes 1210624 | tf_op jit(solution)/shard_map/sub | solution.py:52
  52.7 5.8 %all-to-all-done.1 = bf16[128,2,2,384]{3,2,1,0:T(2,128)(2,1)S(1)} async-done(((bf16[128,2,2,384]{3,2,1,0:T(2,128)(2,1)}), bf16[128,2,2,384]{3,2,1,0:T(2,128)(2,1)S(1)}, u32[]{:S(2)}, u32[]{:S(2)}) %all-to-all-start.1) | async-done | bytes 393248 | tf_op jit(solution)/shard_map/all_to_all | solution.py:132
  58.9 3.0 %fusion.10 = f32[16,32,6,32]{1,3,2,0:T(8,128)} fusion(bf16[16,32,384,1]{2,1,3,0:T(8,128)(2,1)S(1)} %bitcast.113, pred[6,384]{1,0:T(8,128)(4,1)S(1)} %iota_compare_fusion, bf16[16,32,384]{2,1,0:T(8,128)(2,1)} %get-tuple-element.21), kind=kOutput, calls=%fused_computation.12 | convolution fusion | flops 76677120 | bytes 1181952 | tf_op jit(solution)/shard_map/bid,bhjd->bihj/dot_general | solution.py:58
  61.9 1.6 %fusion.46 = bf16[16,32,384]{2,1,0:T(8,128)(2,1)} fusion(pred[6,384]{1,0:T(8,128)(4,1)S(1)} %iota_compare_fusion, bf16[16,32,384]{2,1,0:T(8,128)(2,1)S(1)} %bitcast.114, f32[16,32,6,32]{1,3,2,0:T(8,128)S(1)} %copy-done.11, f32[16,32,6]{1,2,0:T(8,128)S(1)} %get-tuple-element.24), kind=kOutput, calls=%fused_computation.43 | convolution fusion | flops 77070336 | bytes 1194240 | tf_op jit(solution)/shard_map/bihj,bhid->bjd/dot_general | solution.py:55
  63.5 4.6 %fusion.43 = bf16[16,32,384]{2,1,0:T(8,128)(2,1)} fusion(pred[6,384]{1,0:T(8,128)(4,1)S(1)} %iota_compare_fusion, bf16[16,32,384]{2,1,0:T(8,128)(2,1)S(1)} %copy-done.8, f32[16,32,6,32]{1,3,2,0:T(8,128)} %fusion.10, f32[16,32,6,32]{1,3,2,0:T(8,128)} %get-tuple-element.25, f32[16,32,6]{1,2,0:T(8,128)S(1)} %get-tuple-element.24), kind=kOutput, calls=%fused_computation.42 | convolution fusion | flops 77564960 | bytes 1587456 | tf_op jit(solution)/shard_map/bihj,bhjd->bid/dot_general | solution.py:63
  68.1 4.6 %fusion.49 = bf16[16,32,384]{2,1,0:T(8,128)(2,1)} fusion(pred[6,384]{1,0:T(8,128)(4,1)S(1)} %iota_compare_fusion, bf16[16,32,384]{2,1,0:T(8,128)(2,1)S(1)} %copy-done.6, f32[16,32,6,32]{1,3,2,0:T(8,128)} %fusion.10, f32[16,32,6,32]{1,3,2,0:T(8,128)} %get-tuple-element.25, f32[16,32,6]{1,2,0:T(8,128)S(1)} %get-tuple-element.24), kind=kOutput, calls=%fused_computation.44 | convolution fusion | flops 77564960 | bytes 1587456 | tf_op jit(solution)/shard_map/bihj,bhid->bjd/dot_general | solution.py:66
  72.7 2.5 %fusion.23 = (f32[16,32]{1,0:T(8,128)S(1)}, f32[16,32,768]{2,1,0:T(8,128)S(1)}) fusion(bf16[16,32,768]{2,1,0:T(8,128)(2,1)S(1)} %bitcast.99, f32[16,32]{1,0:T(8,128)S(1)} %add_rsqrt_fusion, bf16[768,1152]{1,0:T(8,128)(2,1)S(1)} %copy-done, bf16[16,32,384]{2,1,0:T(8,128)(2,1)S(1)} %copy-done.12, bf16[16,32,384]{2,1,0:T(8,128)(2,1)} %fusion.49, ...), kind=kOutput, calls=%fused_computation.29 | convolution fusion | flops 911080960 | bytes 5312512 | tf_op jit(solution)/shard_map/dot_general | solution.py:78
  76.9 1.7 %copy.38 = bf16[2,8,32,768]{3,1,0,2:T(8,128)(2,1)} copy(bf16[2,8,32,768]{3,2,1,0:T(8,128)(2,1)S(1)} %bitcast.103) | data formatting | bytes 1572864 | tf_op jit(solution)/shard_map/reshape | solution.py:142
  78.6 3.1 %collective-permute-start = (bf16[4,2,48,1152]{3,2,1,0:T(8,128)(2,1)S(1)}, bf16[4,2,48,1152]{3,2,1,0:T(8,128)(2,1)}, u32[]{:S(2)}, u32[]{:S(2)}) collective-permute-start(bf16[4,2,48,1152]{3,2,1,0:T(8,128)(2,1)S(1)} %fusion.66), channel_id=1, source_target_pairs={{0,1},{1,0},{2,3},{3,2},{4,5},{5,4},{6,7},{7,6},{8,9},{9,8},{10,11... | collective-permute-start | bytes 2654216 | tf_op jit(solution)/shard_map/ppermute | solution.py:97
  81.8 2.1 %collective-permute-done = bf16[4,2,48,1152]{3,2,1,0:T(8,128)(2,1)} collective-permute-done((bf16[4,2,48,1152]{3,2,1,0:T(8,128)(2,1)S(1)}, bf16[4,2,48,1152]{3,2,1,0:T(8,128)(2,1)}, u32[]{:S(2)}, u32[]{:S(2)}) %collective-permute-start) | collective-permute-done | bytes 884768 | tf_op jit(solution)/shard_map/ppermute | solution.py:97
  83.9 1.9 %bitcast_add_fusion = f32[4,2,48,1152]{3,2,1,0:T(8,128)S(1)} fusion(bf16[4,2,48,1152]{3,2,1,0:T(8,128)(2,1)} %collective-permute-done, f32[4,2,2,48,1152]{4,3,2,1,0:T(8,128)} %bitcast.105, s32[]{:T(128)S(6)} %select_n.104), kind=kLoop, calls=%fused_computation.25 | loop fusion | flops 884736 | bytes 4423684 | tf_op jit(solution)/shard_map/add | solution.py:98
  86.7 2.5 %collective-permute-start.3 = (bf16[2,48,1152]{2,1,0:T(8,128)(2,1)}, bf16[2,48,1152]{2,1,0:T(8,128)(2,1)}, u32[]{:S(2)}, u32[]{:S(2)}) collective-permute-start(bf16[2,48,1152]{2,1,0:T(8,128)(2,1)} %get-tuple-element.19), channel_id=1, source_target_pairs={{0,12},{1,13},{2,14},{3,15},{4,0},{5,1},{6,2},{7,3},{8,4},{9,5},{1... | collective-permute-start | bytes 663560 | tf_op jit(solution)/shard_map/ppermute | solution.py:97
  89.1 4.7 %collective-permute-start.2 = (bf16[2,48,1152]{2,1,0:T(8,128)(2,1)}, bf16[2,48,1152]{2,1,0:T(8,128)(2,1)}, u32[]{:S(2)}, u32[]{:S(2)}) collective-permute-start(bf16[2,48,1152]{2,1,0:T(8,128)(2,1)} %get-tuple-element.20), channel_id=1, source_target_pairs={{0,4},{1,5},{2,6},{3,7},{4,8},{5,9},{6,10},{7,11},{8,12},{9,13},{1... | collective-permute-start | bytes 663560 | tf_op jit(solution)/shard_map/ppermute | solution.py:97
  93.9 3.7 %collective-permute-start.1 = (bf16[2,48,1152]{2,1,0:T(8,128)(2,1)}, bf16[2,48,1152]{2,1,0:T(8,128)(2,1)}, u32[]{:S(2)}, u32[]{:S(2)}) collective-permute-start(bf16[2,48,1152]{2,1,0:T(8,128)(2,1)} %get-tuple-element.18), channel_id=1, source_target_pairs={{0,8},{1,9},{2,10},{3,11},{4,12},{5,13},{6,14},{7,15},{8,0},{9,1},... | collective-permute-start | bytes 663560 | tf_op jit(solution)/shard_map/ppermute | solution.py:97
  97.6 5.0 %all-to-all-start.2 = ((bf16[2,32,8,768]{3,2,0,1:T(8,128)(2,1)}), bf16[2,32,8,768]{3,2,0,1:T(8,128)(2,1)}, u32[]{:S(2)}, u32[]{:S(2)}) async-start(bf16[2,32,8,768]{3,2,0,1:T(8,128)(2,1)} %bitcast.101), calls=%async_computation.2 | async-start | bytes 1572864 | tf_op jit(solution)/shard_map/all_to_all | solution.py:144
  102.6 3.1 %collective-permute-done.1 = bf16[2,48,1152]{2,1,0:T(8,128)(2,1)} collective-permute-done((bf16[2,48,1152]{2,1,0:T(8,128)(2,1)}, bf16[2,48,1152]{2,1,0:T(8,128)(2,1)}, u32[]{:S(2)}, u32[]{:S(2)}) %collective-permute-start.1) | collective-permute-done | bytes 221216 | tf_op jit(solution)/shard_map/ppermute | solution.py:97
  107.7 4.1 %collective-permute-start.4 = (bf16[48,1152]{1,0:T(8,128)(2,1)S(1)}, bf16[48,1152]{1,0:T(8,128)(2,1)S(1)}, u32[]{:S(2)}, u32[]{:S(2)}) collective-permute-start(bf16[48,1152]{1,0:T(8,128)(2,1)S(1)} %fusion.76), channel_id=1, source_target_pairs={{0,2},{1,3},{2,0},{3,1},{4,6},{5,7},{6,4},{7,5},{8,10},{9,11},{10,... | collective-permute-start | bytes 331784 | tf_op jit(solution)/shard_map/ppermute | solution.py:97
  111.8 8.6 %collective-permute-done.4 = bf16[48,1152]{1,0:T(8,128)(2,1)S(1)} collective-permute-done((bf16[48,1152]{1,0:T(8,128)(2,1)S(1)}, bf16[48,1152]{1,0:T(8,128)(2,1)S(1)}, u32[]{:S(2)}, u32[]{:S(2)}) %collective-permute-start.4) | collective-permute-done | bytes 110624 | tf_op jit(solution)/shard_map/ppermute | solution.py:97
  121.4 2.1 %copy.37 = bf16[2,2,16,8,768]{4,3,2,1,0:T(8,128)(2,1)} copy(bf16[2,2,16,8,768]{4,3,0,1,2:T(8,128)(2,1)} %bitcast.37) | data formatting | bytes 1572864 | tf_op jit(solution)/shard_map/all_to_all | solution.py:144
  125.2 29.2 %all_to_all.59 = bf16[32,14,128]{2,1,0:T(8,128)(2,1)S(1)} all-to-all(bf16[32,14,128]{2,1,0:T(8,128)(2,1)S(1)} %convert_element_type.105), channel_id=1, replica_groups=mesh['dp'=32,'band'=16] {'dp'}, dimensions={0} | all-to-all | bytes 229376 | tf_op jit(solution)/shard_map/all_to_all | solution.py:120
  (64 shorter events, 14.5 us)
Async XLA Ops:
  0.6 45.6 %copy-start = (bf16[768,1152]{1,0:T(8,128)(2,1)S(1)}, bf16[768,1152]{1,0:T(8,128)(2,1)}, u32[]{:S(2)}) copy-start(bf16[768,1152]{1,0:T(8,128)(2,1)} %param.7) | copy-start | bytes 5308420
  0.6 17.4 %copy-start.9 = (bf16[2,2,128,384]{3,2,1,0:T(8,128)(2,1)S(1)}, bf16[2,2,128,384]{3,2,1,0:T(8,128)(2,1)}, u32[]{:S(2)}) copy-start(bf16[2,2,128,384]{3,2,1,0:T(8,128)(2,1)} %param.5) | copy-start | bytes 1179652
  3.6 15.6 %copy-start.10 = (s32[2,8,32]{2,1,0:T(8,128)S(1)}, s32[2,8,32]{2,1,0:T(8,128)}, u32[]{:S(2)}) copy-start(s32[2,8,32]{2,1,0:T(8,128)} %param.6) | copy-start | bytes 6148
  3.6 31.4 %all-to-all-start = ((bf16[2,2,128,768]{3,1,0,2:T(2,128)(2,1)}), bf16[2,2,128,768]{3,1,0,2:T(2,128)(2,1)S(1)}, u32[]{:S(2)}, u32[]{:S(2)}) async-start(bf16[2,2,128,768]{3,1,0,2:T(2,128)(2,1)} %copy.17), calls=%async_computation | async-start | bytes 1572864 | tf_op jit(solution)/shard_map/all_to_all | solution.py:127
  36.3 22.1 %all-to-all-start.1 = ((bf16[128,2,2,384]{3,2,1,0:T(2,128)(2,1)}), bf16[128,2,2,384]{3,2,1,0:T(2,128)(2,1)S(1)}, u32[]{:S(2)}, u32[]{:S(2)}) async-start(bf16[128,2,2,384]{3,2,1,0:T(2,128)(2,1)} %bitcast.106), calls=%async_computation.1 | async-start | bytes 786432 | tf_op jit(solution)/shard_map/all_to_all | solution.py:132
  46.2 1.2 copy-start.4
  47.5 1.0 copy-start.3
  49.6 3.1 %copy-start.7 = (bf16[16,32,384]{2,1,0:T(8,128)(2,1)}, bf16[16,32,384]{2,1,0:T(8,128)(2,1)S(1)}, u32[]{:S(2)}) copy-start(bf16[16,32,384]{2,1,0:T(8,128)(2,1)S(1)} %get-tuple-element.22) | copy-start | bytes 1179652
  58.9 3.0 %copy-start.11 = (f32[16,32,6,32]{1,3,2,0:T(8,128)S(1)}, f32[16,32,6,32]{1,3,2,0:T(8,128)}, u32[]{:S(2)}) copy-start(f32[16,32,6,32]{1,3,2,0:T(8,128)} %get-tuple-element.25) | copy-start | bytes 1179652
  61.9 1.6 %copy-start.8 = (bf16[16,32,384]{2,1,0:T(8,128)(2,1)S(1)}, bf16[16,32,384]{2,1,0:T(8,128)(2,1)}, u32[]{:S(2)}) copy-start(bf16[16,32,384]{2,1,0:T(8,128)(2,1)} %copy-done.7) | copy-start | bytes 1179652
  63.5 4.6 %copy-start.6 = (bf16[16,32,384]{2,1,0:T(8,128)(2,1)S(1)}, bf16[16,32,384]{2,1,0:T(8,128)(2,1)}, u32[]{:S(2)}) copy-start(bf16[16,32,384]{2,1,0:T(8,128)(2,1)} %get-tuple-element.23) | copy-start | bytes 1179652
  68.1 4.6 %copy-start.12 = (bf16[16,32,384]{2,1,0:T(8,128)(2,1)S(1)}, bf16[16,32,384]{2,1,0:T(8,128)(2,1)}, u32[]{:S(2)}) copy-start(bf16[16,32,384]{2,1,0:T(8,128)(2,1)} %fusion.46) | copy-start | bytes 1179652
  72.7 2.6 %copy-start.5 = (bf16[16,32,768]{2,1,0:T(8,128)(2,1)S(1)}, bf16[16,32,768]{2,1,0:T(8,128)(2,1)}, u32[]{:S(2)}) copy-start(bf16[16,32,768]{2,1,0:T(8,128)(2,1)} %copy-done.4) | copy-start | bytes 2359300
  72.7 2.6 %copy-start.13 = (bf16[16,32,384]{2,1,0:T(8,128)(2,1)S(1)}, bf16[16,32,384]{2,1,0:T(8,128)(2,1)}, u32[]{:S(2)}) copy-start(bf16[16,32,384]{2,1,0:T(8,128)(2,1)} %fusion.43) | copy-start | bytes 1179652
  72.7 2.6 %copy-start.14 = (bf16[16,32,384]{2,1,0:T(8,128)(2,1)S(1)}, bf16[16,32,384]{2,1,0:T(8,128)(2,1)}, u32[]{:S(2)}) copy-start(bf16[16,32,384]{2,1,0:T(8,128)(2,1)} %fusion.49) | copy-start | bytes 1179652
  76.5 2.0 %copy-start.1 = (f32[768,1152]{1,0:T(8,128)}, f32[768,1152]{1,0:T(8,128)S(1)}, u32[]{:S(2)}) copy-start(f32[768,1152]{1,0:T(8,128)S(1)} %convolution_bitcast_fusion) | copy-start | bytes 10616836
  78.6 5.2 %collective-permute-start = (bf16[4,2,48,1152]{3,2,1,0:T(8,128)(2,1)S(1)}, bf16[4,2,48,1152]{3,2,1,0:T(8,128)(2,1)}, u32[]{:S(2)}, u32[]{:S(2)}) collective-permute-start(bf16[4,2,48,1152]{3,2,1,0:T(8,128)(2,1)S(1)} %fusion.66), channel_id=1, source_target_pairs={{0,1},{1,0},{2,3},{3,2},{4,5},{5,4},{6,7},{7,6},{8,9},{9,8},{10,11... | collective-permute-start | bytes 2654216 | tf_op jit(solution)/shard_map/ppermute | solution.py:97
  86.7 15.9 %collective-permute-start.3 = (bf16[2,48,1152]{2,1,0:T(8,128)(2,1)}, bf16[2,48,1152]{2,1,0:T(8,128)(2,1)}, u32[]{:S(2)}, u32[]{:S(2)}) collective-permute-start(bf16[2,48,1152]{2,1,0:T(8,128)(2,1)} %get-tuple-element.19), channel_id=1, source_target_pairs={{0,12},{1,13},{2,14},{3,15},{4,0},{5,1},{6,2},{7,3},{8,4},{9,5},{1... | collective-permute-start | bytes 663560 | tf_op jit(solution)/shard_map/ppermute | solution.py:97
  89.1 13.4 %collective-permute-start.2 = (bf16[2,48,1152]{2,1,0:T(8,128)(2,1)}, bf16[2,48,1152]{2,1,0:T(8,128)(2,1)}, u32[]{:S(2)}, u32[]{:S(2)}) collective-permute-start(bf16[2,48,1152]{2,1,0:T(8,128)(2,1)} %get-tuple-element.20), channel_id=1, source_target_pairs={{0,4},{1,5},{2,6},{3,7},{4,8},{5,9},{6,10},{7,11},{8,12},{9,13},{1... | collective-permute-start | bytes 663560 | tf_op jit(solution)/shard_map/ppermute | solution.py:97
  93.9 11.8 %collective-permute-start.1 = (bf16[2,48,1152]{2,1,0:T(8,128)(2,1)}, bf16[2,48,1152]{2,1,0:T(8,128)(2,1)}, u32[]{:S(2)}, u32[]{:S(2)}) collective-permute-start(bf16[2,48,1152]{2,1,0:T(8,128)(2,1)} %get-tuple-element.18), channel_id=1, source_target_pairs={{0,8},{1,9},{2,10},{3,11},{4,12},{5,13},{6,14},{7,15},{8,0},{9,1},... | collective-permute-start | bytes 663560 | tf_op jit(solution)/shard_map/ppermute | solution.py:97
  97.6 23.8 %all-to-all-start.2 = ((bf16[2,32,8,768]{3,2,0,1:T(8,128)(2,1)}), bf16[2,32,8,768]{3,2,0,1:T(8,128)(2,1)}, u32[]{:S(2)}, u32[]{:S(2)}) async-start(bf16[2,32,8,768]{3,2,0,1:T(8,128)(2,1)} %bitcast.101), calls=%async_computation.2 | async-start | bytes 1572864 | tf_op jit(solution)/shard_map/all_to_all | solution.py:144
  106.9 0.8 copy-start.2
  107.7 12.7 %collective-permute-start.4 = (bf16[48,1152]{1,0:T(8,128)(2,1)S(1)}, bf16[48,1152]{1,0:T(8,128)(2,1)S(1)}, u32[]{:S(2)}, u32[]{:S(2)}) collective-permute-start(bf16[48,1152]{1,0:T(8,128)(2,1)S(1)} %fusion.76), channel_id=1, source_target_pairs={{0,2},{1,3},{2,0},{3,1},{4,6},{5,7},{6,4},{7,5},{8,10},{9,11},{10,... | collective-permute-start | bytes 331784 | tf_op jit(solution)/shard_map/ppermute | solution.py:97
